TPU v7x, 32 devices: a whole 2x2x4 slice. The times are simulated.
32 devices in a mesh: groups: 2 (over y), tp: 16 (over z, x, core).
Axes of the slice: x: 2, y: 2, z: 4, core: 2. Of those that a mesh axis runs over, the one named last changes fastest.
Arguments:
- hidden_in: bfloat16 [32, 8, 512], P(('groups', 'tp')), parts along dimension 0, may hold values from -6 to 6
- norm_gain: float32 [8192], replicated, may hold values from 0.1 to 1.9
- q_blocks: bfloat16 [16, 16, 128, 2048], P('tp'), may hold values from -0.0625 to 0.0625
- o_blocks: bfloat16 [16, 2048, 16, 128], P('tp'), may hold values from -1.5 to 1.5
- kv_blocks: bfloat16 [2, 1024, 8192], P(None, None, 'tp'), may hold values from -0.0625 to 0.0625
- kv_assign: int32 [16], replicated, may hold values from 0 to 7, as said below
- key_cache: bfloat16 [32, 8, 2048, 128], P(('groups', 'tp')), parts along dimension 0, may hold values from -240 to 240
- value_cache: bfloat16 [32, 8, 2048, 128], P(('groups', 'tp')), parts along dimension 0, may hold values from -6 to 6
- lengths: int32 [32, 8], P(('groups', 'tp')), parts along dimension 0, may hold values from 1 to 2048, as said below
Outputs:
- attn_out: bfloat16 [32, 8, 512], P(('groups', 'tp')), parts along dimension 0
There are 2 independent parts, one for each index of `groups`. A program takes and returns all parts, laid end to end along the dimension named above; an argument that names none is the same for every part. Nothing has to cross between parts.
Inputs may be any that keep to these rules, and one draw needn't show every extreme that they name: `kv_assign`: entries 2m and 2m + 1 are equal, and each of the 8 key-value heads is named by exactly two entries. `lengths`: in every rank one row has all 2048 positions valid.
All inputs are finite; a program needn't handle non-finite values.
Results may differ from a plain program's by a relative error of at most 0.011.
The roundings to bfloat16 on the way count: a program that leaves them out, or rounds other values in their place, can miss the bound.
Values may be sent and summed in bfloat16 or wider, within the bound.
No kernel may reach another device: no remote copies, remote signals or barrier semaphores. Data moves between devices by JAX's collectives and lax.ppermute only.
A program may use at most 128 MiB of HBM per device.

v0:
```python
import jax
import jax.numpy as jnp
from jax import lax
from jax.sharding import PartitionSpec as P

D = 8192
KVH = 8
HD = 128
ROLL = 16
ROWS = 8
GR = 4
QG = 16
DS = 512


def from_partner(value, axis, bit):
    mask = 2**bit
    pairs = [(source, source ^ mask) for source in range(lax.axis_size(axis))]
    return lax.ppermute(value, axis, pairs)


def norm_rows(rows_float, norm_gain):
    mean_square = jnp.mean(rows_float * rows_float, axis=-1, keepdims=True)
    return (rows_float * lax.rsqrt(mean_square + 1e-05) * norm_gain[None, :]).astype(jnp.bfloat16)


def local(
    hidden_in, norm_gain, q_blocks, o_blocks, kv_blocks, kv_assign, key_cache, value_cache, lengths
):
    ranks = lax.axis_size("tp")
    my_index = lax.axis_index("tp")
    my_rank = my_index % ROLL
    my_half = my_rank % 2
    grid_cols = ranks // GR
    group_count = ranks // ROLL
    col_width = q_blocks.shape[3]
    key_width = kv_blocks.shape[2]
    grid_row = my_index // grid_cols
    grid_col = my_index % grid_cols
    dest_ids = jnp.arange(ranks, dtype=jnp.int32)
    dest_rank = dest_ids % ROLL
    dest_head = kv_assign[dest_rank]
    dest_group = 2 * dest_head + dest_rank % 2
    dest_copy = dest_ids // ROLL
    every_rows = lax.all_gather(hidden_in, "tp", axis=0, tiled=True)
    rows_float = (
        every_rows.reshape(group_count, ROLL, ROWS, DS)
        .transpose(0, 2, 1, 3)
        .reshape(group_count * ROWS, D)
        .astype(jnp.float32)
    )
    normed_every = norm_rows(rows_float, norm_gain)
    col_rows = lax.dynamic_slice_in_dim(normed_every, grid_col * col_width, col_width, 1)
    query_part = jnp.einsum(
        "rc,aec->rae", col_rows, q_blocks[0], preferred_element_type=jnp.float32
    )
    query_part = (
        query_part.reshape(group_count, ROWS, QG, HD)
        .transpose(0, 2, 1, 3)
        .reshape(group_count * QG, ROWS, HD)
    )
    query_pick = jnp.take(query_part, dest_copy * QG + dest_group, axis=0)
    slot_mask = (jnp.arange(GR, dtype=jnp.int32) == grid_row).astype(jnp.float32)
    query_term = (query_pick[:, :, None, :] * slot_mask[None, None, :, None]).reshape(
        ranks, ROWS, GR * HD
    )
    key_rows = lax.dynamic_slice_in_dim(normed_every, my_index * key_width, key_width, 1)
    keyval_part = jnp.einsum("rc,kfc->rkf", key_rows, kv_blocks, preferred_element_type=jnp.float32)
    keyval_part = (
        keyval_part.reshape(group_count, ROWS, 2, KVH, HD)
        .transpose(0, 3, 1, 2, 4)
        .reshape(group_count * KVH, ROWS, 2 * HD)
    )
    keyval_term = jnp.take(keyval_part, dest_copy * KVH + dest_head, axis=0)
    proj_term = jnp.concatenate([query_term, keyval_term], -1).reshape(ranks * ROWS, (GR + 2) * HD)
    projected = lax.psum_scatter(proj_term, "tp", scatter_dimension=0, tiled=True)
    queries = projected[:, : GR * HD].astype(jnp.bfloat16)
    keyval_new = projected[:, GR * HD :].astype(jnp.bfloat16)
    key_new = keyval_new[:, :HD]
    value_new = keyval_new[:, HD:]
    partner_queries = from_partner(queries, "tp", 0)
    both_queries = jnp.where(
        my_half == 0,
        jnp.concatenate([queries, partner_queries], 1),
        jnp.concatenate([partner_queries, queries], 1),
    )
    both_queries = both_queries.reshape(ROWS, 2 * GR, HD)
    scale = 1.0 / HD**0.5
    scores = (
        jnp.einsum("bhe,bte->bht", both_queries, key_cache[0], preferred_element_type=jnp.float32)
        * scale
    )
    positions = jnp.arange(scores.shape[2], dtype=jnp.int32)
    masked = positions[None, None, :] < lengths[0][:, None, None]
    new_score = (
        jnp.einsum("bhe,be->bh", both_queries, key_new, preferred_element_type=jnp.float32) * scale
    )
    new_score = jnp.where(my_half == 0, new_score, jnp.float32(-1e30))
    top = jnp.maximum(jnp.max(jnp.where(masked, scores, jnp.float32(-1e30)), axis=-1), new_score)
    weights = jnp.where(masked, jnp.exp(scores - top[..., None]), jnp.float32(0.0))
    new_weight = jnp.exp(new_score - top)
    total = jnp.sum(weights, axis=-1) + new_weight
    summed = jnp.einsum(
        "bht,bte->bhe",
        weights.astype(jnp.bfloat16),
        value_cache[0],
        preferred_element_type=jnp.float32,
    )
    new_rounded = lax.optimization_barrier(new_weight.astype(jnp.bfloat16)).astype(jnp.float32)
    summed = summed + new_rounded[..., None] * value_new.astype(jnp.float32)[:, None, :]
    top_split = top.reshape(ROWS, 2, GR)
    total_split = total.reshape(ROWS, 2, GR)
    summed_split = summed.reshape(ROWS, 2, GR, HD)
    first_half = my_half == 0
    own_top = jnp.where(first_half, top_split[:, 0], top_split[:, 1])
    own_total = jnp.where(first_half, total_split[:, 0], total_split[:, 1])
    own_summed = jnp.where(first_half, summed_split[:, 0], summed_split[:, 1])
    give_top = jnp.where(first_half, top_split[:, 1], top_split[:, 0])
    give_total = jnp.where(first_half, total_split[:, 1], total_split[:, 0])
    give_summed = jnp.where(first_half, summed_split[:, 1], summed_split[:, 0])
    got_top, got_total, got_summed = from_partner((give_top, give_total, give_summed), "tp", 0)
    joint = jnp.maximum(own_top, got_top)
    factor_own = jnp.exp(own_top - joint)
    factor_got = jnp.exp(got_top - joint)
    numer = own_summed * factor_own[..., None] + got_summed * factor_got[..., None]
    denom = own_total * factor_own + got_total * factor_got
    attention = (numer / denom[..., None]).astype(jnp.bfloat16).reshape(ROWS, GR * HD)
    every_attn = lax.all_gather(attention[None], "tp", axis=0, tiled=True)
    head_ids = jnp.arange(KVH, dtype=jnp.int32)
    pair_heads = kv_assign[0::2]
    inverse = jnp.sum(
        head_ids[None, :] * (pair_heads[None, :] == head_ids[:, None]).astype(jnp.int32), axis=1
    )
    slot_ids = jnp.arange(QG, dtype=jnp.int32)
    rank_of_slot = 2 * inverse[slot_ids // 2] + slot_ids % 2
    attn_grid = every_attn.reshape(group_count, ROLL, ROWS, GR, HD)
    row_slot = lax.dynamic_index_in_dim(attn_grid, grid_row, 3, keepdims=False)
    chosen = jnp.take(row_slot, rank_of_slot, axis=1)
    out_part = jnp.einsum("gabe,cae->gbc", chosen, o_blocks[0], preferred_element_type=jnp.float32)
    placed = jnp.zeros((group_count, ROWS, D), jnp.float32)
    placed = lax.dynamic_update_slice_in_dim(placed, out_part, grid_col * col_width, 2)
    out_term = (
        placed.reshape(group_count, ROWS, ROLL, DS).transpose(0, 2, 1, 3).reshape(ranks * ROWS, DS)
    )
    my_cols = lax.psum_scatter(out_term, "tp", scatter_dimension=0, tiled=True)
    return my_cols.astype(jnp.bfloat16)[None]


def solution(mesh):
    return jax.shard_map(
        local,
        mesh=mesh,
        in_specs=(
            P(("groups", "tp"), None, None),
            P(),
            P("tp", None, None, None),
            P("tp", None, None, None),
            P(None, None, "tp"),
            P(),
            P(("groups", "tp"), None, None, None),
            P(("groups", "tp"), None, None, None),
            P(("groups", "tp"), None),
        ),
        out_specs=P(("groups", "tp"), None, None),
        check_vma=False,
    )
```

profile of v0, /device:TPU:1, one launch (start us, length us, event | category | flops | bytes accessed | tf_op | source)
XLA Modules:
  0.0 192.1 jit_solution(7086260716293882496)
XLA Ops:
  6.5 23.7 %all_gather.6 = bf16[16,8,512]{2,1,0:T(8,128)(2,1)S(1)} all-gather(bf16[1,8,512]{2,1,0:T(8,128)(2,1)} %param.9), channel_id=1, replica_groups=mesh['groups'=2,'tp'=16] {'tp'}, dimensions={0}, use_global_device_ids=true | all-gather | bytes 139264 | tf_op jit(solution)/shard_map/all_gather | solution.py:45
  30.5 0.7 slice.41
  31.2 1.3 gather_fusion.1
  32.7 0.7 gather_fusion
  33.5 0.9 multiply_convert_fusion
  34.3 0.6 convolution_bitcast_fusion
  35.2 5.6 %fusion.17 = f32[16,8,128]{2,1,0:T(8,128)S(1)} fusion(bf16[1,16,128,2048]{3,2,1,0:T(8,128)(2,1)} %param.11, bf16[8,8192]{1,0:T(8,128)(2,1)S(1)} %multiply_convert_fusion, s32[]{:T(128)S(6)} %select_n.308), kind=kOutput, calls=%fused_computation.16 | convolution fusion | flops 67108864 | bytes 8486916 | tf_op jit(solution)/shard_map/rc,aec->rae/dot_general | solution.py:54
  40.8 0.6 gather_fusion.2
  41.6 0.6 gather_fusion.3
  42.2 0.8 pad_maximum_fusion
  43.2 50.4 %reduce-scatter.3.cloned.1.call-done = f32[8,768]{1,0:T(8,128)} async-done(((f32[128,768]{1,0:T(8,128)}), f32[8,768]{1,0:T(8,128)}) %reduce-scatter.3.cloned.1.call-update) | async-done | bytes 24592 | tf_op jit(solution)/shard_map/reduce_scatter | solution.py:76
  93.7 0.7 convert.7
  94.4 2.5 %collective-permute-start = (bf16[8,512]{1,0:T(8,128)(2,1)S(1)}, bf16[8,512]{1,0:T(8,128)(2,1)S(1)}, u32[]{:S(2)}, u32[]{:S(2)}) collective-permute-start(bf16[8,512]{1,0:T(8,128)(2,1)S(1)} %slice.61), channel_id=1, source_target_pairs={{0,1},{1,0},{2,3},{3,2},{4,5},{5,4},{6,7},{7,6},{8,9},{9,8},{10,11... | collective-permute-start | bytes 24584 | tf_op jit(solution)/shard_map/ppermute | solution.py:19
  97.0 0.8 collective-permute-done
  97.9 3.5 %select_reduce_fusion = (f32[8,8]{1,0:T(8,128)S(1)}, f32[8,8,2048]{2,1,0:T(8,128)S(1)}) fusion(pred[8,2048]{1,0:T(8,128)(4,1)S(1)} %iota_compare_fusion, bf16[1,8,2048,128]{3,2,1,0:T(8,128)(2,1)} %param.15, bf16[8,4,128]{2,1,0:T(4,128)(2,1)S(1)} %concatenate.18, bf16[8,4,128]{2,1,0:T(4,128)(2,1)S(1)} %concatenate.17, pred[]{:T(512)S(6)} %eq.39), kind=kOutput, calls=%fused_computation.20 | convolution fusion | flops 34021312 | bytes 4751617 | tf_op jit(solution)/shard_map/bhe,bte->bht/dot_general | solution.py:90
  102.3 2.9 %fusion.20 = f32[8,8,128]{2,1,0:T(8,128)S(1)} fusion(bf16[1,8,2048,128]{3,2,1,0:T(8,128)(2,1)} %param.16, f32[8,8,2048]{2,1,0:T(8,128)S(1)} %get-tuple-element.17, f32[8,8]{1,0:T(8,128)S(1)} %fusion.43, pred[8,2048]{1,0:T(8,128)(4,1)S(1)} %iota_compare_fusion, f32[8,128]{1,0:T(8,128)S(1)} %get-tuple-element.8, f32[8,8]{1,0:T(8,128)S(1)} %convert_element_type.57), kind=kOutput, calls=%fused_computation.18 | convolution fusion | flops 33964032 | bytes 4772352 | tf_op jit(solution)/shard_map/bht,bte->bhe/dot_general | solution.py:103
  105.3 0.4 collective-permute-start.2
  105.9 0.6 collective-permute-done.2
  106.6 19.9 %all_gather.7 = bf16[16,8,512]{2,1,0:T(8,128)(2,1)S(1)} all-gather(bf16[1,8,512]{2,1,0:T(8,128)(2,1)S(1)} %broadcast_in_dim_reshape.3), channel_id=1, replica_groups=mesh['groups'=2,'tp'=16] {'tp'}, dimensions={0}, use_global_device_ids=true | all-gather | bytes 139264 | tf_op jit(solution)/shard_map/all_gather | solution.py:128
  126.6 0.6 gather_fusion.4
  127.2 5.7 %fusion.14 = f32[1,8,8192]{2,1,0:T(8,128)S(1)} fusion(f32[1,8,8192]{2,1,0:T(8,128)S(1)} %broadcast_in_dim.78, s32[]{:T(128)S(6)} %select_n.308, bf16[2048,16,128]{2,1,0:T(8,128)(2,1)} %bitcast.146, bf16[16,8,128]{2,1,0:T(8,128)(2,1)S(1)} %gather_fusion.4, pred[16]{0:T(512)(128)(4,1)S(1)} %get-tuple-element.18), kind=kOutput, calls=%fused_computation.15 | convolution fusion | flops 67125248 | bytes 8487428 | tf_op jit(solution)/shard_map/gabe,cae->gbc/dot_general | solution.py:139
  132.8 0.7 copy-done.1
  133.6 50.4 %reduce-scatter.5.cloned.1.call-done = f32[8,512]{1,0:T(8,128)} async-done(((f32[128,512]{1,0:T(8,128)}), f32[8,512]{1,0:T(8,128)}) %reduce-scatter.5.cloned.1.call-update) | async-done | bytes 16400 | tf_op jit(solution)/shard_map/reduce_scatter | solution.py:145
  183.9 1.3 convert_bitcast_fusion
  (57 shorter events, 2.5 us)
Async XLA Ops:
  6.5 27.8 %copy-start = (bf16[2,1024,512]{2,1,0:T(8,128)(2,1)S(1)}, bf16[2,1024,512]{2,1,0:T(8,128)(2,1)}, u32[]{:S(2)}) copy-start(bf16[2,1024,512]{2,1,0:T(8,128)(2,1)} %param.13) | copy-start | bytes 6291460
  6.5 87.1 %reduce-scatter.3.cloned.1.call-start = ((), (), s32[]{:S(2)}) async-start(), calls=%async_computation.2 | async-start | bytes 417792 | tf_op jit(solution)/shard_map/reduce_scatter | solution.py:76
  35.2 8.0 %copy-start.2 = (s32[1,8]{1,0:T(1,128)S(1)}, s32[1,8]{1,0:T(1,128)}, u32[]{:S(2)}) copy-start(s32[1,8]{1,0:T(1,128)} %param.17) | copy-start | bytes 100
  43.0 140.9 %reduce-scatter.5.cloned.1.call-start = ((), (), s32[]{:S(2)}) async-start(), calls=%async_computation.3 | async-start | bytes 278528 | tf_op jit(solution)/shard_map/reduce_scatter | solution.py:145
  94.4 3.4 %collective-permute-start = (bf16[8,512]{1,0:T(8,128)(2,1)S(1)}, bf16[8,512]{1,0:T(8,128)(2,1)S(1)}, u32[]{:S(2)}, u32[]{:S(2)}) collective-permute-start(bf16[8,512]{1,0:T(8,128)(2,1)S(1)} %slice.61), channel_id=1, source_target_pairs={{0,1},{1,0},{2,3},{3,2},{4,5},{5,4},{6,7},{7,6},{8,9},{9,8},{10,11... | collective-permute-start | bytes 24584 | tf_op jit(solution)/shard_map/ppermute | solution.py:19
  101.5 4.2 %collective-permute-start.1 = (f32[8,4]{0,1:T(4,128)S(1)}, f32[8,4]{0,1:T(4,128)S(1)}, u32[]{:S(2)}, u32[]{:S(2)}) collective-permute-start(f32[8,4]{0,1:T(4,128)S(1)} %select_bitcast_fusion.2), channel_id=1, source_target_pairs={{0,1},{1,0},{2,3},{3,2},{4,5},{5,4},{6,7},{7,6},{8,9},{9,8},{10,11... | collective-permute-start | bytes 392 | tf_op jit(solution)/shard_map/ppermute | solution.py:19
  102.2 3.5 %collective-permute-start.3 = (f32[8,4]{0,1:T(4,128)S(1)}, f32[8,4]{0,1:T(4,128)S(1)}, u32[]{:S(2)}, u32[]{:S(2)}) collective-permute-start(f32[8,4]{0,1:T(4,128)S(1)} %select_bitcast_fusion.1), channel_id=1, source_target_pairs={{0,1},{1,0},{2,3},{3,2},{4,5},{5,4},{6,7},{7,6},{8,9},{9,8},{10,11... | collective-permute-start | bytes 392 | tf_op jit(solution)/shard_map/ppermute | solution.py:19
  105.3 1.2 collective-permute-start.2
  132.8 0.7 copy-start.1
Sparse Core Ops, SparseCore 0:
  43.1 50.4 reduce-scatter.2
  133.7 50.1 reduce-scatter.4
where the time goes:
time: 195 us; the launch traced here: 192 us
  waiting for transfers between devices  102 us (52%)
  blocking collectives  43.6 us (22%)
  matrix products  18.4 us (9%)
  between operations  13.7 us (7%)
  local copies, waits for them, and re-layouts  5.86 us (3%)
  other arithmetic  4.78 us (2%)
  starting transfers between devices  3.52 us (2%)
    reduce_scatter x1, waiting for transfers between devices, local(): lax.psum_scatter(proj_term, 'tp', scatter_dimension=0, tiled=True)  50.4 us
    reduce_scatter x1, waiting for transfers between devices, local(): my_cols = lax.psum_scatter(out_term, 'tp', scatter_dimension=0, tiled=True)  50.4 us
    all_gather x1, blocking collectives, local(): every_rows = lax.all_gather(hidden_in, 'tp', axis=0, tiled=True)  23.7 us
    all_gather x1, blocking collectives, local(): every_attn = lax.all_gather(attention[None], 'tp', axis=0, tiled=True)  19.9 us
    dot_general x1, matrix products, local(): jnp.einsum('gabe,cae->gbc', chosen, o_blocks[0], preferred_element_type=j...  5.65 us
    dot_general x1, matrix products, local(): jnp.einsum('rc,aec->rae', col_rows, q_blocks[0], preferred_element_type=j...  5.65 us
  transfers between devices with their start and end apart: 6, of which 4 were waited for; matrix products, arithmetic and copies ran while one was open for 2% of the time, Pallas kernels for 0%

commit v1 on v0

--- a/solution.py
+++ b/solution.py
@@ -17,6 +17,39 @@
     mask = 2**bit
     pairs = [(source, source ^ mask) for source in range(lax.axis_size(axis))]
     return lax.ppermute(value, axis, pairs)
+
+
+def xor_swap(value, axis, bit):
+    return from_partner(value, axis, bit)
+
+
+def gather_xor(value, axis):
+    n = lax.axis_size(axis)
+    me = lax.axis_index(axis)
+    held = value
+    for bit in range(n.bit_length() - 1):
+        other = xor_swap(held, axis, bit)
+        low = ((me >> bit) & 1) == 0
+        held = jnp.where(low, jnp.concatenate([held, other], 0), jnp.concatenate([other, held], 0))
+    return held
+
+
+def scatter_sum_xor(pieces, axis):
+    n = lax.axis_size(axis)
+    bits = n.bit_length() - 1
+    me = lax.axis_index(axis)
+    held = pieces.reshape((2,) * bits + pieces.shape[1:])
+    order = list(range(bits - 1, -1, -1))
+    for bit in range(bits):
+        pos = order.index(bit)
+        order.pop(pos)
+        low = ((me >> bit) & 1) == 0
+        first = lax.index_in_dim(held, 0, pos, keepdims=False)
+        second = lax.index_in_dim(held, 1, pos, keepdims=False)
+        keep = jnp.where(low, first, second)
+        give = jnp.where(low, second, first)
+        held = keep + xor_swap(give, axis, bit)
+    return held[None]
 
 
 def norm_rows(rows_float, norm_gain):
@@ -42,7 +75,7 @@
     dest_head = kv_assign[dest_rank]
     dest_group = 2 * dest_head + dest_rank % 2
     dest_copy = dest_ids // ROLL
-    every_rows = lax.all_gather(hidden_in, "tp", axis=0, tiled=True)
+    every_rows = gather_xor(hidden_in, "tp")
     rows_float = (
         every_rows.reshape(group_count, ROLL, ROWS, DS)
         .transpose(0, 2, 1, 3)
@@ -73,7 +106,7 @@
     )
     keyval_term = jnp.take(keyval_part, dest_copy * KVH + dest_head, axis=0)
     proj_term = jnp.concatenate([query_term, keyval_term], -1).reshape(ranks * ROWS, (GR + 2) * HD)
-    projected = lax.psum_scatter(proj_term, "tp", scatter_dimension=0, tiled=True)
+    projected = scatter_sum_xor(proj_term.reshape(ranks, ROWS, (GR + 2) * HD), "tp")[0]
     queries = projected[:, : GR * HD].astype(jnp.bfloat16)
     keyval_new = projected[:, GR * HD :].astype(jnp.bfloat16)
     key_new = keyval_new[:, :HD]
@@ -125,7 +158,7 @@
     numer = own_summed * factor_own[..., None] + got_summed * factor_got[..., None]
     denom = own_total * factor_own + got_total * factor_got
     attention = (numer / denom[..., None]).astype(jnp.bfloat16).reshape(ROWS, GR * HD)
-    every_attn = lax.all_gather(attention[None], "tp", axis=0, tiled=True)
+    every_attn = gather_xor(attention[None], "tp")
     head_ids = jnp.arange(KVH, dtype=jnp.int32)
     pair_heads = kv_assign[0::2]
     inverse = jnp.sum(
@@ -142,7 +175,7 @@
     out_term = (
         placed.reshape(group_count, ROWS, ROLL, DS).transpose(0, 2, 1, 3).reshape(ranks * ROWS, DS)
     )
-    my_cols = lax.psum_scatter(out_term, "tp", scatter_dimension=0, tiled=True)
+    my_cols = scatter_sum_xor(out_term.reshape(ranks, ROWS, DS), "tp")[0]
     return my_cols.astype(jnp.bfloat16)[None]
 
 

time: 195 us -> 88.9 us (0.46)
  the two profiles are of different devices: /device:TPU:1 before, /device:TPU:0 now
where the time goes in v1:
time: 88.9 us; the launch traced here: 88.5 us
  waiting for transfers between devices  31.1 us (35%)
  starting transfers between devices  29.9 us (34%)
  matrix products  18.4 us (21%)
  local copies, waits for them, and re-layouts  4.97 us (6%)
  other arithmetic  3.65 us (4%)
    ppermute x20, waiting for transfers between devices, from_partner(): return lax.ppermute(value, axis, pairs)  31.1 us
    ppermute x20, starting transfers between devices, from_partner(): return lax.ppermute(value, axis, pairs)  29.9 us
    dot_general x1, matrix products, local(): jnp.einsum('gabe,cae->gbc', chosen, o_blocks[0], preferred_element_type=j...  5.65 us
    dot_general x1, matrix products, local(): jnp.einsum('rc,aec->rae', col_rows, q_blocks[0], preferred_element_type=j...  5.65 us
    dot_general x1, matrix products, local(): jnp.einsum('bhe,bte->bht', both_queries, key_cache[0], preferred_element_...  3.46 us
    dot_general x1, matrix products, local(): jnp.einsum('bht,bte->bhe', weights.astype(jnp.bfloat16), value_cache[0],...  2.89 us
  transfers between devices with their start and end apart: 20, of which 17 were waited for; matrix products, arithmetic and copies ran while one was open for 7% of the time, Pallas kernels for 0%

profile of v1, /device:TPU:0, one launch (start us, length us, event | category | flops | bytes accessed | tf_op | source)
XLA Modules:
  0.0 88.5 jit_solution(16844129374900298633)
XLA Ops:
  4.5 2.5 %collective-permute-start.1 = (bf16[2,8,512]{2,1,0:T(8,128)(2,1)S(1)}, bf16[2,8,512]{2,1,0:T(8,128)(2,1)S(1)}, u32[]{:S(2)}, u32[]{:S(2)}) collective-permute-start(bf16[2,8,512]{2,1,0:T(8,128)(2,1)S(1)} %maximum_select_fusion.7), channel_id=1, source_target_pairs={{0,2},{1,3},{2,0},{3,1},{4,6},{5,7},{6,4},{7,5},{8,10},{9,11},{10,... | collective-permute-start | bytes 49160 | tf_op jit(solution)/shard_map/ppermute | solution.py:19
  8.7 2.2 %collective-permute-start.2 = (bf16[4,8,512]{2,1,0:T(8,128)(2,1)S(1)}, bf16[4,8,512]{2,1,0:T(8,128)(2,1)S(1)}, u32[]{:S(2)}, u32[]{:S(2)}) collective-permute-start(bf16[4,8,512]{2,1,0:T(8,128)(2,1)S(1)} %maximum_select_fusion.4), channel_id=1, source_target_pairs={{0,4},{1,5},{2,6},{3,7},{4,0},{5,1},{6,2},{7,3},{8,12},{9,13},{10,... | collective-permute-start | bytes 98312 | tf_op jit(solution)/shard_map/ppermute | solution.py:19
  10.9 1.9 %collective-permute-done.2 = bf16[4,8,512]{2,1,0:T(8,128)(2,1)S(1)} collective-permute-done((bf16[4,8,512]{2,1,0:T(8,128)(2,1)S(1)}, bf16[4,8,512]{2,1,0:T(8,128)(2,1)S(1)}, u32[]{:S(2)}, u32[]{:S(2)}) %collective-permute-start.2) | collective-permute-done | bytes 32800 | tf_op jit(solution)/shard_map/ppermute | solution.py:19
  12.8 3.1 %collective-permute-start.3 = (bf16[8,8,512]{2,1,0:T(8,128)(2,1)S(1)}, bf16[8,8,512]{2,1,0:T(8,128)(2,1)S(1)}, u32[]{:S(2)}, u32[]{:S(2)}) collective-permute-start(bf16[8,8,512]{2,1,0:T(8,128)(2,1)S(1)} %maximum_select_fusion.1), channel_id=1, source_target_pairs={{0,8},{1,9},{2,10},{3,11},{4,12},{5,13},{6,14},{7,15},{8,0},{9,1},... | collective-permute-start | bytes 196616 | tf_op jit(solution)/shard_map/ppermute | solution.py:19
  15.9 2.2 %collective-permute-done.3 = bf16[8,8,512]{2,1,0:T(8,128)(2,1)S(1)} collective-permute-done((bf16[8,8,512]{2,1,0:T(8,128)(2,1)S(1)}, bf16[8,8,512]{2,1,0:T(8,128)(2,1)S(1)}, u32[]{:S(2)}, u32[]{:S(2)}) %collective-permute-start.3) | collective-permute-done | bytes 65568 | tf_op jit(solution)/shard_map/ppermute | solution.py:19
  19.9 5.7 %fusion.17 = f32[16,8,128]{2,1,0:T(8,128)S(1)} fusion(bf16[1,16,128,2048]{3,2,1,0:T(8,128)(2,1)} %param.11, bf16[8,8192]{1,0:T(8,128)(2,1)S(1)} %multiply_convert_fusion, s32[]{:T(128)S(6)} %select_n.570), kind=kOutput, calls=%fused_computation.16 | convolution fusion | flops 67108864 | bytes 8486916 | tf_op jit(solution)/shard_map/rc,aec->rae/dot_general | solution.py:87
  28.6 1.9 %collective-permute-start.5 = (f32[2,2,8,768]{3,2,1,0:T(8,128)S(1)}, f32[2,2,8,768]{3,2,1,0:T(8,128)S(1)}, u32[]{:S(2)}, u32[]{:S(2)}) collective-permute-start(f32[2,2,8,768]{3,2,1,0:T(8,128)S(1)} %select_bitcast_fusion.2), channel_id=1, source_target_pairs={{0,2},{1,3},{2,0},{3,1},{4,6},{5,7},{6,4},{7,5},{8,10},{9,11},{10,... | collective-permute-start | bytes 294920 | tf_op jit(solution)/shard_map/ppermute | solution.py:19
  30.5 3.1 %collective-permute-done.5 = f32[2,2,8,768]{3,2,1,0:T(8,128)S(1)} collective-permute-done((f32[2,2,8,768]{3,2,1,0:T(8,128)S(1)}, f32[2,2,8,768]{3,2,1,0:T(8,128)S(1)}, u32[]{:S(2)}, u32[]{:S(2)}) %collective-permute-start.5) | collective-permute-done | bytes 98336 | tf_op jit(solution)/shard_map/ppermute | solution.py:19
  33.6 1.9 %collective-permute-start.6 = (f32[2,8,768]{2,1,0:T(8,128)S(1)}, f32[2,8,768]{2,1,0:T(8,128)S(1)}, u32[]{:S(2)}, u32[]{:S(2)}) collective-permute-start(f32[2,8,768]{2,1,0:T(8,128)S(1)} %select_bitcast_fusion.4), channel_id=1, source_target_pairs={{0,4},{1,5},{2,6},{3,7},{4,0},{5,1},{6,2},{7,3},{8,12},{9,13},{10,... | collective-permute-start | bytes 147464 | tf_op jit(solution)/shard_map/ppermute | solution.py:19
  35.6 2.2 %collective-permute-done.6 = f32[2,8,768]{2,1,0:T(8,128)S(1)} collective-permute-done((f32[2,8,768]{2,1,0:T(8,128)S(1)}, f32[2,8,768]{2,1,0:T(8,128)S(1)}, u32[]{:S(2)}, u32[]{:S(2)}) %collective-permute-start.6) | collective-permute-done | bytes 49184 | tf_op jit(solution)/shard_map/ppermute | solution.py:19
  37.8 3.0 %collective-permute-start.7 = (f32[8,768]{1,0:T(8,128)S(1)}, f32[8,768]{1,0:T(8,128)S(1)}, u32[]{:S(2)}, u32[]{:S(2)}) collective-permute-start(f32[8,768]{1,0:T(8,128)S(1)} %select_bitcast_fusion.6), channel_id=1, source_target_pairs={{0,8},{1,9},{2,10},{3,11},{4,12},{5,13},{6,14},{7,15},{8,0},{9,1},... | collective-permute-start | bytes 73736 | tf_op jit(solution)/shard_map/ppermute | solution.py:19
  40.8 1.8 %collective-permute-done.7 = f32[8,768]{1,0:T(8,128)S(1)} collective-permute-done((f32[8,768]{1,0:T(8,128)S(1)}, f32[8,768]{1,0:T(8,128)S(1)}, u32[]{:S(2)}, u32[]{:S(2)}) %collective-permute-start.7) | collective-permute-done | bytes 24608 | tf_op jit(solution)/shard_map/ppermute | solution.py:19
  44.0 3.5 %select_reduce_fusion = (f32[8,8]{1,0:T(8,128)S(1)}, f32[8,8,2048]{2,1,0:T(8,128)S(1)}) fusion(pred[8,2048]{1,0:T(8,128)(4,1)S(1)} %iota_compare_fusion, bf16[1,8,2048,128]{3,2,1,0:T(8,128)(2,1)} %param.15, bf16[8,4,128]{2,1,0:T(4,128)(2,1)S(1)} %copy.145, bf16[8,4,128]{2,1,0:T(4,128)(2,1)S(1)} %copy.144, pred[]{:T(512)S(6)} %eq.67), kind=kOutput, calls=%fused_computation.20 | convolution fusion | flops 34021312 | bytes 4751617 | tf_op jit(solution)/shard_map/bhe,bte->bht/dot_general | solution.py:123
  48.4 2.9 %fusion.20 = f32[8,8,128]{2,1,0:T(8,128)S(1)} fusion(bf16[1,8,2048,128]{3,2,1,0:T(8,128)(2,1)} %param.16, f32[8,8,2048]{2,1,0:T(8,128)S(1)} %get-tuple-element.19, f32[8,8]{1,0:T(8,128)S(1)} %fusion.63, pred[8,2048]{1,0:T(8,128)(4,1)S(1)} %iota_compare_fusion, f32[8,128]{1,0:T(8,128)S(1)} %get-tuple-element.10, f32[8,8]{1,0:T(8,128)S(1)} %convert_element_type.52), kind=kOutput, calls=%fused_computation.18 | convolution fusion | flops 33964032 | bytes 4772352 | tf_op jit(solution)/shard_map/bht,bte->bhe/dot_general | solution.py:136
  55.6 2.1 %collective-permute-done.13 = bf16[2,8,512]{2,1,0:T(8,128)(2,1)S(1)} collective-permute-done((bf16[2,8,512]{2,1,0:T(8,128)(2,1)S(1)}, bf16[2,8,512]{2,1,0:T(8,128)(2,1)S(1)}, u32[]{:S(2)}, u32[]{:S(2)}) %collective-permute-start.13) | collective-permute-done | bytes 16416 | tf_op jit(solution)/shard_map/ppermute | solution.py:19
  57.7 2.1 %collective-permute-start.14 = (bf16[4,8,512]{2,1,0:T(8,128)(2,1)S(1)}, bf16[4,8,512]{2,1,0:T(8,128)(2,1)S(1)}, u32[]{:S(2)}, u32[]{:S(2)}) collective-permute-start(bf16[4,8,512]{2,1,0:T(8,128)(2,1)S(1)} %maximum_select_fusion.6), channel_id=1, source_target_pairs={{0,4},{1,5},{2,6},{3,7},{4,0},{5,1},{6,2},{7,3},{8,12},{9,13},{10,... | collective-permute-start | bytes 98312 | tf_op jit(solution)/shard_map/ppermute | solution.py:19
  59.8 1.9 %collective-permute-done.14 = bf16[4,8,512]{2,1,0:T(8,128)(2,1)S(1)} collective-permute-done((bf16[4,8,512]{2,1,0:T(8,128)(2,1)S(1)}, bf16[4,8,512]{2,1,0:T(8,128)(2,1)S(1)}, u32[]{:S(2)}, u32[]{:S(2)}) %collective-permute-start.14) | collective-permute-done | bytes 32800 | tf_op jit(solution)/shard_map/ppermute | solution.py:19
  61.7 3.0 %collective-permute-start.15 = (bf16[8,8,512]{2,1,0:T(8,128)(2,1)S(1)}, bf16[8,8,512]{2,1,0:T(8,128)(2,1)S(1)}, u32[]{:S(2)}, u32[]{:S(2)}) collective-permute-start(bf16[8,8,512]{2,1,0:T(8,128)(2,1)S(1)} %maximum_select_fusion.3), channel_id=1, source_target_pairs={{0,8},{1,9},{2,10},{3,11},{4,12},{5,13},{6,14},{7,15},{8,0},{9,1},... | collective-permute-start | bytes 196616 | tf_op jit(solution)/shard_map/ppermute | solution.py:19
  64.7 2.2 %collective-permute-done.15 = bf16[8,8,512]{2,1,0:T(8,128)(2,1)S(1)} collective-permute-done((bf16[8,8,512]{2,1,0:T(8,128)(2,1)S(1)}, bf16[8,8,512]{2,1,0:T(8,128)(2,1)S(1)}, u32[]{:S(2)}, u32[]{:S(2)}) %collective-permute-start.15) | collective-permute-done | bytes 65568 | tf_op jit(solution)/shard_map/ppermute | solution.py:19
  67.5 5.7 %fusion.14 = f32[1,8,8192]{2,1,0:T(8,128)S(1)} fusion(f32[1,8,8192]{2,1,0:T(8,128)S(1)} %broadcast_in_dim.74, s32[]{:T(128)S(6)} %select_n.570, bf16[2048,16,128]{2,1,0:T(8,128)(2,1)} %bitcast.254, bf16[16,8,128]{2,1,0:T(8,128)(2,1)S(1)} %gather_fusion.4, pred[16]{0:T(512)(128)(4,1)S(1)} %get-tuple-element.21), kind=kOutput, calls=%fused_computation.15 | convolution fusion | flops 67125248 | bytes 8487428 | tf_op jit(solution)/shard_map/gabe,cae->gbc/dot_general | solution.py:172
  76.4 2.6 %collective-permute-done.17 = f32[2,2,8,512]{3,2,1,0:T(8,128)S(1)} collective-permute-done((f32[2,2,8,512]{3,2,1,0:T(8,128)S(1)}, f32[2,2,8,512]{3,2,1,0:T(8,128)S(1)}, u32[]{:S(2)}, u32[]{:S(2)}) %collective-permute-start.17) | collective-permute-done | bytes 65568 | tf_op jit(solution)/shard_map/ppermute | solution.py:19
  79.1 2.1 %collective-permute-start.18 = (f32[2,8,512]{2,1,0:T(8,128)S(1)}, f32[2,8,512]{2,1,0:T(8,128)S(1)}, u32[]{:S(2)}, u32[]{:S(2)}) collective-permute-start(f32[2,8,512]{2,1,0:T(8,128)S(1)} %select_bitcast_fusion.5), channel_id=1, source_target_pairs={{0,4},{1,5},{2,6},{3,7},{4,0},{5,1},{6,2},{7,3},{8,12},{9,13},{10,... | collective-permute-start | bytes 98312 | tf_op jit(solution)/shard_map/ppermute | solution.py:19
  81.1 1.9 %collective-permute-done.18 = f32[2,8,512]{2,1,0:T(8,128)S(1)} collective-permute-done((f32[2,8,512]{2,1,0:T(8,128)S(1)}, f32[2,8,512]{2,1,0:T(8,128)S(1)}, u32[]{:S(2)}, u32[]{:S(2)}) %collective-permute-start.18) | collective-permute-done | bytes 32800 | tf_op jit(solution)/shard_map/ppermute | solution.py:19
  83.1 3.1 %collective-permute-start.19 = (f32[8,512]{1,0:T(8,128)S(1)}, f32[8,512]{1,0:T(8,128)S(1)}, u32[]{:S(2)}, u32[]{:S(2)}) collective-permute-start(f32[8,512]{1,0:T(8,128)S(1)} %select_bitcast_fusion.7), channel_id=1, source_target_pairs={{0,8},{1,9},{2,10},{3,11},{4,12},{5,13},{6,14},{7,15},{8,0},{9,1},... | collective-permute-start | bytes 49160 | tf_op jit(solution)/shard_map/ppermute | solution.py:19
  (99 shorter events, 23.8 us)
Async XLA Ops:
  0.0 19.2 %copy-start = (bf16[2,1024,512]{2,1,0:T(8,128)(2,1)S(1)}, bf16[2,1024,512]{2,1,0:T(8,128)(2,1)}, u32[]{:S(2)}) copy-start(bf16[2,1024,512]{2,1,0:T(8,128)(2,1)} %param.13) | copy-start | bytes 6291460
  0.0 3.7 %collective-permute-start = (bf16[1,8,512]{2,1,0:T(8,128)(2,1)}, bf16[1,8,512]{2,1,0:T(8,128)(2,1)S(1)}, u32[]{:S(2)}, u32[]{:S(2)}) collective-permute-start(bf16[1,8,512]{2,1,0:T(8,128)(2,1)} %param.9), channel_id=1, source_target_pairs={{0,1},{1,0},{2,3},{3,2},{4,5},{5,4},{6,7},{7,6},{8,9},{9,8},{10,11... | collective-permute-start | bytes 24584 | tf_op jit(solution)/shard_map/ppermute | solution.py:19
  4.5 4.2 %collective-permute-start.1 = (bf16[2,8,512]{2,1,0:T(8,128)(2,1)S(1)}, bf16[2,8,512]{2,1,0:T(8,128)(2,1)S(1)}, u32[]{:S(2)}, u32[]{:S(2)}) collective-permute-start(bf16[2,8,512]{2,1,0:T(8,128)(2,1)S(1)} %maximum_select_fusion.7), channel_id=1, source_target_pairs={{0,2},{1,3},{2,0},{3,1},{4,6},{5,7},{6,4},{7,5},{8,10},{9,11},{10,... | collective-permute-start | bytes 49160 | tf_op jit(solution)/shard_map/ppermute | solution.py:19
  8.7 4.1 %collective-permute-start.2 = (bf16[4,8,512]{2,1,0:T(8,128)(2,1)S(1)}, bf16[4,8,512]{2,1,0:T(8,128)(2,1)S(1)}, u32[]{:S(2)}, u32[]{:S(2)}) collective-permute-start(bf16[4,8,512]{2,1,0:T(8,128)(2,1)S(1)} %maximum_select_fusion.4), channel_id=1, source_target_pairs={{0,4},{1,5},{2,6},{3,7},{4,0},{5,1},{6,2},{7,3},{8,12},{9,13},{10,... | collective-permute-start | bytes 98312 | tf_op jit(solution)/shard_map/ppermute | solution.py:19
  12.8 5.3 %collective-permute-start.3 = (bf16[8,8,512]{2,1,0:T(8,128)(2,1)S(1)}, bf16[8,8,512]{2,1,0:T(8,128)(2,1)S(1)}, u32[]{:S(2)}, u32[]{:S(2)}) collective-permute-start(bf16[8,8,512]{2,1,0:T(8,128)(2,1)S(1)} %maximum_select_fusion.1), channel_id=1, source_target_pairs={{0,8},{1,9},{2,10},{3,11},{4,12},{5,13},{6,14},{7,15},{8,0},{9,1},... | collective-permute-start | bytes 196616 | tf_op jit(solution)/shard_map/ppermute | solution.py:19
  19.9 15.6 %copy-start.1 = (s32[1,8]{1,0:T(1,128)S(1)}, s32[1,8]{1,0:T(1,128)}, u32[]{:S(2)}) copy-start(s32[1,8]{1,0:T(1,128)} %param.17) | copy-start | bytes 100
  27.0 1.5 %collective-permute-start.4 = (f32[2,2,2,8,768]{4,3,2,1,0:T(8,128)S(1)}, f32[2,2,2,8,768]{4,3,2,1,0:T(8,128)S(1)}, u32[]{:S(2)}, u32[]{:S(2)}) collective-permute-start(f32[2,2,2,8,768]{4,3,2,1,0:T(8,128)S(1)} %select_bitcast_fusion), channel_id=1, source_target_pairs={{0,1},{1,0},{2,3},{3,2},{4,5},{5,4},{6,7},{7,6},{8,9},{9,8},{10,11... | collective-permute-start | bytes 589832 | tf_op jit(solution)/shard_map/ppermute | solution.py:19
  28.6 5.0 %collective-permute-start.5 = (f32[2,2,8,768]{3,2,1,0:T(8,128)S(1)}, f32[2,2,8,768]{3,2,1,0:T(8,128)S(1)}, u32[]{:S(2)}, u32[]{:S(2)}) collective-permute-start(f32[2,2,8,768]{3,2,1,0:T(8,128)S(1)} %select_bitcast_fusion.2), channel_id=1, source_target_pairs={{0,2},{1,3},{2,0},{3,1},{4,6},{5,7},{6,4},{7,5},{8,10},{9,11},{10,... | collective-permute-start | bytes 294920 | tf_op jit(solution)/shard_map/ppermute | solution.py:19
  33.6 4.2 %collective-permute-start.6 = (f32[2,8,768]{2,1,0:T(8,128)S(1)}, f32[2,8,768]{2,1,0:T(8,128)S(1)}, u32[]{:S(2)}, u32[]{:S(2)}) collective-permute-start(f32[2,8,768]{2,1,0:T(8,128)S(1)} %select_bitcast_fusion.4), channel_id=1, source_target_pairs={{0,4},{1,5},{2,6},{3,7},{4,0},{5,1},{6,2},{7,3},{8,12},{9,13},{10,... | collective-permute-start | bytes 147464 | tf_op jit(solution)/shard_map/ppermute | solution.py:19
  37.8 4.9 %collective-permute-start.7 = (f32[8,768]{1,0:T(8,128)S(1)}, f32[8,768]{1,0:T(8,128)S(1)}, u32[]{:S(2)}, u32[]{:S(2)}) collective-permute-start(f32[8,768]{1,0:T(8,128)S(1)} %select_bitcast_fusion.6), channel_id=1, source_target_pairs={{0,8},{1,9},{2,10},{3,11},{4,12},{5,13},{6,14},{7,15},{8,0},{9,1},... | collective-permute-start | bytes 73736 | tf_op jit(solution)/shard_map/ppermute | solution.py:19
  42.6 1.2 %collective-permute-start.8 = (bf16[8,512]{1,0:T(8,128)(2,1)S(1)}, bf16[8,512]{1,0:T(8,128)(2,1)S(1)}, u32[]{:S(2)}, u32[]{:S(2)}) collective-permute-start(bf16[8,512]{1,0:T(8,128)(2,1)S(1)} %get-tuple-element.13), channel_id=1, source_target_pairs={{0,1},{1,0},{2,3},{3,2},{4,5},{5,4},{6,7},{7,6},{8,9},{9,8},{10,11... | collective-permute-start | bytes 24584 | tf_op jit(solution)/shard_map/ppermute | solution.py:19
  47.6 4.1 %collective-permute-start.9 = (f32[8,4]{0,1:T(4,128)S(1)}, f32[8,4]{0,1:T(4,128)S(1)}, u32[]{:S(2)}, u32[]{:S(2)}) collective-permute-start(f32[8,4]{0,1:T(4,128)S(1)} %select_bitcast_fusion.10), channel_id=1, source_target_pairs={{0,1},{1,0},{2,3},{3,2},{4,5},{5,4},{6,7},{7,6},{8,9},{9,8},{10,11... | collective-permute-start | bytes 392 | tf_op jit(solution)/shard_map/ppermute | solution.py:19
  48.1 3.5 %collective-permute-start.11 = (f32[8,4]{0,1:T(4,128)S(1)}, f32[8,4]{0,1:T(4,128)S(1)}, u32[]{:S(2)}, u32[]{:S(2)}) collective-permute-start(f32[8,4]{0,1:T(4,128)S(1)} %select_bitcast_fusion.9), channel_id=1, source_target_pairs={{0,1},{1,0},{2,3},{3,2},{4,5},{5,4},{6,7},{7,6},{8,9},{9,8},{10,11... | collective-permute-start | bytes 392 | tf_op jit(solution)/shard_map/ppermute | solution.py:19
  51.4 1.2 %collective-permute-start.10 = (f32[8,4,128]{2,0,1:T(8,128)S(1)}, f32[8,4,128]{2,0,1:T(8,128)S(1)}, u32[]{:S(2)}, u32[]{:S(2)}) collective-permute-start(f32[8,4,128]{2,0,1:T(8,128)S(1)} %select_bitcast_fusion.8), channel_id=1, source_target_pairs={{0,1},{1,0},{2,3},{3,2},{4,5},{5,4},{6,7},{7,6},{8,9},{9,8},{10,11... | collective-permute-start | bytes 49160 | tf_op jit(solution)/shard_map/ppermute | solution.py:19
  52.7 1.2 %collective-permute-start.12 = (bf16[1,8,512]{2,1,0:T(8,128)(2,1)S(1)}, bf16[1,8,512]{2,1,0:T(8,128)(2,1)S(1)}, u32[]{:S(2)}, u32[]{:S(2)}) collective-permute-start(bf16[1,8,512]{2,1,0:T(8,128)(2,1)S(1)} %bitcast.267), channel_id=1, source_target_pairs={{0,1},{1,0},{2,3},{3,2},{4,5},{5,4},{6,7},{7,6},{8,9},{9,8},{10,11... | collective-permute-start | bytes 24584 | tf_op jit(solution)/shard_map/ppermute | solution.py:19
  54.0 3.7 %collective-permute-start.13 = (bf16[2,8,512]{2,1,0:T(8,128)(2,1)S(1)}, bf16[2,8,512]{2,1,0:T(8,128)(2,1)S(1)}, u32[]{:S(2)}, u32[]{:S(2)}) collective-permute-start(bf16[2,8,512]{2,1,0:T(8,128)(2,1)S(1)} %maximum_select_fusion.10), channel_id=1, source_target_pairs={{0,2},{1,3},{2,0},{3,1},{4,6},{5,7},{6,4},{7,5},{8,10},{9,11},{10,... | collective-permute-start | bytes 49160 | tf_op jit(solution)/shard_map/ppermute | solution.py:19
  57.7 4.0 %collective-permute-start.14 = (bf16[4,8,512]{2,1,0:T(8,128)(2,1)S(1)}, bf16[4,8,512]{2,1,0:T(8,128)(2,1)S(1)}, u32[]{:S(2)}, u32[]{:S(2)}) collective-permute-start(bf16[4,8,512]{2,1,0:T(8,128)(2,1)S(1)} %maximum_select_fusion.6), channel_id=1, source_target_pairs={{0,4},{1,5},{2,6},{3,7},{4,0},{5,1},{6,2},{7,3},{8,12},{9,13},{10,... | collective-permute-start | bytes 98312 | tf_op jit(solution)/shard_map/ppermute | solution.py:19
  61.7 5.2 %collective-permute-start.15 = (bf16[8,8,512]{2,1,0:T(8,128)(2,1)S(1)}, bf16[8,8,512]{2,1,0:T(8,128)(2,1)S(1)}, u32[]{:S(2)}, u32[]{:S(2)}) collective-permute-start(bf16[8,8,512]{2,1,0:T(8,128)(2,1)S(1)} %maximum_select_fusion.3), channel_id=1, source_target_pairs={{0,8},{1,9},{2,10},{3,11},{4,12},{5,13},{6,14},{7,15},{8,0},{9,1},... | collective-permute-start | bytes 196616 | tf_op jit(solution)/shard_map/ppermute | solution.py:19
  73.2 1.4 %collective-permute-start.16 = (f32[2,2,2,8,512]{4,3,2,1,0:T(8,128)S(1)}, f32[2,2,2,8,512]{4,3,2,1,0:T(8,128)S(1)}, u32[]{:S(2)}, u32[]{:S(2)}) collective-permute-start(f32[2,2,2,8,512]{4,3,2,1,0:T(8,128)S(1)} %select_bitcast_fusion.1), channel_id=1, source_target_pairs={{0,1},{1,0},{2,3},{3,2},{4,5},{5,4},{6,7},{7,6},{8,9},{9,8},{10,11... | collective-permute-start | bytes 393224 | tf_op jit(solution)/shard_map/ppermute | solution.py:19
  74.7 4.3 %collective-permute-start.17 = (f32[2,2,8,512]{3,2,1,0:T(8,128)S(1)}, f32[2,2,8,512]{3,2,1,0:T(8,128)S(1)}, u32[]{:S(2)}, u32[]{:S(2)}) collective-permute-start(f32[2,2,8,512]{3,2,1,0:T(8,128)S(1)} %select_bitcast_fusion.3), channel_id=1, source_target_pairs={{0,2},{1,3},{2,0},{3,1},{4,6},{5,7},{6,4},{7,5},{8,10},{9,11},{10,... | collective-permute-start | bytes 196616 | tf_op jit(solution)/shard_map/ppermute | solution.py:19
  79.1 4.0 %collective-permute-start.18 = (f32[2,8,512]{2,1,0:T(8,128)S(1)}, f32[2,8,512]{2,1,0:T(8,128)S(1)}, u32[]{:S(2)}, u32[]{:S(2)}) collective-permute-start(f32[2,8,512]{2,1,0:T(8,128)S(1)} %select_bitcast_fusion.5), channel_id=1, source_target_pairs={{0,4},{1,5},{2,6},{3,7},{4,0},{5,1},{6,2},{7,3},{8,12},{9,13},{10,... | collective-permute-start | bytes 98312 | tf_op jit(solution)/shard_map/ppermute | solution.py:19
  83.1 4.8 %collective-permute-start.19 = (f32[8,512]{1,0:T(8,128)S(1)}, f32[8,512]{1,0:T(8,128)S(1)}, u32[]{:S(2)}, u32[]{:S(2)}) collective-permute-start(f32[8,512]{1,0:T(8,128)S(1)} %select_bitcast_fusion.7), channel_id=1, source_target_pairs={{0,8},{1,9},{2,10},{3,11},{4,12},{5,13},{6,14},{7,15},{8,0},{9,1},... | collective-permute-start | bytes 49160 | tf_op jit(solution)/shard_map/ppermute | solution.py:19

commit v2 on v1

--- a/solution.py
+++ b/solution.py
@@ -32,6 +32,20 @@
         low = ((me >> bit) & 1) == 0
         held = jnp.where(low, jnp.concatenate([held, other], 0), jnp.concatenate([other, held], 0))
     return held
+
+
+def scatter_rounds(held, order, axis, bits):
+    me = lax.axis_index(axis)
+    for bit in bits:
+        pos = order.index(bit)
+        order = order[:pos] + order[pos + 1 :]
+        low = ((me >> bit) & 1) == 0
+        first = lax.index_in_dim(held, 0, pos, keepdims=False)
+        second = lax.index_in_dim(held, 1, pos, keepdims=False)
+        keep = jnp.where(low, first, second)
+        give = jnp.where(low, second, first)
+        held = keep + xor_swap(give, axis, bit)
+    return held, order
 
 
 def scatter_sum_xor(pieces, axis):
@@ -93,10 +107,6 @@
         .reshape(group_count * QG, ROWS, HD)
     )
     query_pick = jnp.take(query_part, dest_copy * QG + dest_group, axis=0)
-    slot_mask = (jnp.arange(GR, dtype=jnp.int32) == grid_row).astype(jnp.float32)
-    query_term = (query_pick[:, :, None, :] * slot_mask[None, None, :, None]).reshape(
-        ranks, ROWS, GR * HD
-    )
     key_rows = lax.dynamic_slice_in_dim(normed_every, my_index * key_width, key_width, 1)
     keyval_part = jnp.einsum("rc,kfc->rkf", key_rows, kv_blocks, preferred_element_type=jnp.float32)
     keyval_part = (
@@ -105,8 +115,18 @@
         .reshape(group_count * KVH, ROWS, 2 * HD)
     )
     keyval_term = jnp.take(keyval_part, dest_copy * KVH + dest_head, axis=0)
-    proj_term = jnp.concatenate([query_term, keyval_term], -1).reshape(ranks * ROWS, (GR + 2) * HD)
-    projected = scatter_sum_xor(proj_term.reshape(ranks, ROWS, (GR + 2) * HD), "tp")[0]
+    bits = ranks.bit_length() - 1
+    col_bits = grid_cols.bit_length() - 1
+    compact = jnp.concatenate([query_pick, keyval_term], -1)
+    held, order = scatter_rounds(
+        compact.reshape((2,) * bits + (ROWS, 3 * HD)), list(range(bits - 1, -1, -1)), "tp", range(col_bits)
+    )
+    slot_here = jnp.arange(GR, dtype=jnp.int32) == grid_row
+    query_slots = jnp.where(
+        slot_here[:, None], held[..., None, :HD], jnp.zeros((), jnp.float32)
+    ).reshape(held.shape[:-1] + (GR * HD,))
+    held = jnp.concatenate([query_slots, held[..., HD:]], -1)
+    projected, _ = scatter_rounds(held, order, "tp", range(col_bits, bits))
     queries = projected[:, : GR * HD].astype(jnp.bfloat16)
     keyval_new = projected[:, GR * HD :].astype(jnp.bfloat16)
     key_new = keyval_new[:, :HD]
@@ -151,7 +171,9 @@
     give_top = jnp.where(first_half, top_split[:, 1], top_split[:, 0])
     give_total = jnp.where(first_half, total_split[:, 1], total_split[:, 0])
     give_summed = jnp.where(first_half, summed_split[:, 1], summed_split[:, 0])
-    got_top, got_total, got_summed = from_partner((give_top, give_total, give_summed), "tp", 0)
+    give = jnp.concatenate([give_summed, give_top[..., None], give_total[..., None]], -1)
+    got = from_partner(give, "tp", 0)
+    got_summed, got_top, got_total = got[..., :HD], got[..., HD], got[..., HD + 1]
     joint = jnp.maximum(own_top, got_top)
     factor_own = jnp.exp(own_top - joint)
     factor_got = jnp.exp(got_top - joint)
@@ -170,12 +192,25 @@
     row_slot = lax.dynamic_index_in_dim(attn_grid, grid_row, 3, keepdims=False)
     chosen = jnp.take(row_slot, rank_of_slot, axis=1)
     out_part = jnp.einsum("gabe,cae->gbc", chosen, o_blocks[0], preferred_element_type=jnp.float32)
-    placed = jnp.zeros((group_count, ROWS, D), jnp.float32)
-    placed = lax.dynamic_update_slice_in_dim(placed, out_part, grid_col * col_width, 2)
-    out_term = (
-        placed.reshape(group_count, ROWS, ROLL, DS).transpose(0, 2, 1, 3).reshape(ranks * ROWS, DS)
-    )
-    my_cols = scatter_sum_xor(out_term.reshape(ranks, ROWS, DS), "tp")[0]
+    if group_count == 1 and grid_cols == GR and col_width == GR * DS:
+        col_bits = grid_cols.bit_length() - 1
+        row_bits = GR.bit_length() - 1
+        pieces = out_part[0].reshape(ROWS, GR, DS).transpose(1, 0, 2)
+        held, _ = scatter_rounds(
+            pieces.reshape((2,) * row_bits + (ROWS, DS)),
+            list(range(col_bits + row_bits - 1, col_bits - 1, -1)),
+            "tp",
+            range(col_bits, col_bits + row_bits),
+        )
+        pairs = [(i * grid_cols + j, j * grid_cols + i) for i in range(GR) for j in range(grid_cols)]
+        my_cols = lax.ppermute(held, "tp", pairs)
+    else:
+        placed = jnp.zeros((group_count, ROWS, D), jnp.float32)
+        placed = lax.dynamic_update_slice_in_dim(placed, out_part, grid_col * col_width, 2)
+        out_term = (
+            placed.reshape(group_count, ROWS, ROLL, DS).transpose(0, 2, 1, 3).reshape(ranks * ROWS, DS)
+        )
+        my_cols = scatter_sum_xor(out_term.reshape(ranks, ROWS, DS), "tp")[0]
     return my_cols.astype(jnp.bfloat16)[None]
 
 

time: 88.9 us -> 88.6 us (level)
  the two profiles are of different devices: /device:TPU:0 before, /device:TPU:24 now
where the time goes in v2:
time: 88.6 us; the launch traced here: 88.2 us
  waiting for transfers between devices  51.9 us (59%)
  matrix products  18.4 us (21%)
  starting transfers between devices  8.35 us (9%)
  local copies, waits for them, and re-layouts  5.38 us (6%)
  other arithmetic  3.81 us (4%)
    ppermute x16, waiting for transfers between devices, from_partner(): return lax.ppermute(value, axis, pairs)  46.1 us
    ppermute x16, starting transfers between devices, from_partner(): return lax.ppermute(value, axis, pairs)  6.44 us
    ppermute x1, waiting for transfers between devices, local(): my_cols = lax.ppermute(held, 'tp', pairs)  5.74 us
    dot_general x1, matrix products, local(): jnp.einsum('gabe,cae->gbc', chosen, o_blocks[0], preferred_element_type=j...  5.65 us
    dot_general x1, matrix products, local(): jnp.einsum('rc,aec->rae', col_rows, q_blocks[0], preferred_element_type=j...  5.65 us
    dot_general x1, matrix products, local(): jnp.einsum('bhe,bte->bht', both_queries, key_cache[0], preferred_element_...  3.46 us
    dot_general x1, matrix products, local(): jnp.einsum('bht,bte->bhe', weights.astype(jnp.bfloat16), value_cache[0],...  2.9 us
    ppermute x1, starting transfers between devices, local(): my_cols = lax.ppermute(held, 'tp', pairs)  1.91 us
  transfers between devices with their start and end apart: 17, of which 16 were waited for; matrix products, arithmetic and copies ran while one was open for 4% of the time, Pallas kernels for 0%

profile of v2, /device:TPU:24, one launch (start us, length us, event | category | flops | bytes accessed | tf_op | source)
XLA Modules:
  0.0 88.2 jit_solution(10002211991404673152)
XLA Ops:
  0.0 1.5 %gather_fusion.1 = s32[16]{0:T(128)S(1)} fusion(s32[16]{0:T(128)} %param.14, s32[1024]{0:T(1024)S(1)} %pad_clamp_fusion.3), kind=kCustom, calls=%fused_computation.1 | custom fusion | bytes 192 | tf_op jit(solution)/shard_map/gather | solution.py:89
  3.2 1.5 %collective-permute-start.1 = (bf16[2,8,512]{2,1,0:T(8,128)(2,1)S(1)}, bf16[2,8,512]{2,1,0:T(8,128)(2,1)S(1)}, u32[]{:S(2)}, u32[]{:S(2)}) collective-permute-start(bf16[2,8,512]{2,1,0:T(8,128)(2,1)S(1)} %maximum_select_fusion.7), channel_id=1, source_target_pairs={{0,2},{1,3},{2,0},{3,1},{4,6},{5,7},{6,4},{7,5},{8,10},{9,11},{10,... | collective-permute-start | bytes 49160 | tf_op jit(solution)/shard_map/ppermute | solution.py:19
  4.7 2.2 %collective-permute-done.1 = bf16[2,8,512]{2,1,0:T(8,128)(2,1)S(1)} collective-permute-done((bf16[2,8,512]{2,1,0:T(8,128)(2,1)S(1)}, bf16[2,8,512]{2,1,0:T(8,128)(2,1)S(1)}, u32[]{:S(2)}, u32[]{:S(2)}) %collective-permute-start.1) | collective-permute-done | bytes 16416 | tf_op jit(solution)/shard_map/ppermute | solution.py:19
  7.5 3.5 %collective-permute-done.2 = bf16[4,8,512]{2,1,0:T(8,128)(2,1)S(1)} collective-permute-done((bf16[4,8,512]{2,1,0:T(8,128)(2,1)S(1)}, bf16[4,8,512]{2,1,0:T(8,128)(2,1)S(1)}, u32[]{:S(2)}, u32[]{:S(2)}) %collective-permute-start.2) | collective-permute-done | bytes 32800 | tf_op jit(solution)/shard_map/ppermute | solution.py:19
  11.3 5.4 %collective-permute-done.3 = bf16[8,8,512]{2,1,0:T(8,128)(2,1)S(1)} collective-permute-done((bf16[8,8,512]{2,1,0:T(8,128)(2,1)S(1)}, bf16[8,8,512]{2,1,0:T(8,128)(2,1)S(1)}, u32[]{:S(2)}, u32[]{:S(2)}) %collective-permute-start.3) | collective-permute-done | bytes 65568 | tf_op jit(solution)/shard_map/ppermute | solution.py:19
  19.2 5.6 %fusion.11 = f32[16,8,128]{2,1,0:T(8,128)S(1)} fusion(bf16[1,16,128,2048]{3,2,1,0:T(8,128)(2,1)} %param.11, bf16[8,8192]{1,0:T(8,128)(2,1)S(1)} %multiply_convert_fusion, s32[]{:T(128)S(6)} %select_n.568), kind=kOutput, calls=%fused_computation.14 | convolution fusion | flops 67108864 | bytes 8486916 | tf_op jit(solution)/shard_map/rc,aec->rae/dot_general | solution.py:101
  25.8 1.1 %collective-permute-done.4 = f32[2,2,2,8,384]{4,3,2,1,0:T(8,128)S(1)} collective-permute-done((f32[2,2,2,8,384]{4,3,2,1,0:T(8,128)S(1)}, f32[2,2,2,8,384]{4,3,2,1,0:T(8,128)S(1)}, u32[]{:S(2)}, u32[]{:S(2)}) %collective-permute-start.4) | collective-permute-done | bytes 98336 | tf_op jit(solution)/shard_map/ppermute | solution.py:19
  26.9 1.6 %collective-permute-start.5 = (f32[2,2,8,384]{3,2,1,0:T(8,128)S(1)}, f32[2,2,8,384]{3,2,1,0:T(8,128)S(1)}, u32[]{:S(2)}, u32[]{:S(2)}) collective-permute-start(f32[2,2,8,384]{3,2,1,0:T(8,128)S(1)} %select_bitcast_fusion.3), channel_id=1, source_target_pairs={{0,2},{1,3},{2,0},{3,1},{4,6},{5,7},{6,4},{7,5},{8,10},{9,11},{10,... | collective-permute-start | bytes 147464 | tf_op jit(solution)/shard_map/ppermute | solution.py:19
  28.6 2.5 %collective-permute-done.5 = f32[2,2,8,384]{3,2,1,0:T(8,128)S(1)} collective-permute-done((f32[2,2,8,384]{3,2,1,0:T(8,128)S(1)}, f32[2,2,8,384]{3,2,1,0:T(8,128)S(1)}, u32[]{:S(2)}, u32[]{:S(2)}) %collective-permute-start.5) | collective-permute-done | bytes 49184 | tf_op jit(solution)/shard_map/ppermute | solution.py:19
  31.9 3.4 %collective-permute-done.6 = f32[2,8,768]{2,1,0:T(8,128)S(1)} collective-permute-done((f32[2,8,768]{2,1,0:T(8,128)S(1)}, f32[2,8,768]{2,1,0:T(8,128)S(1)}, u32[]{:S(2)}, u32[]{:S(2)}) %collective-permute-start.6) | collective-permute-done | bytes 49184 | tf_op jit(solution)/shard_map/ppermute | solution.py:19
  35.4 4.7 %collective-permute-done.7 = f32[8,768]{1,0:T(8,128)S(1)} collective-permute-done((f32[8,768]{1,0:T(8,128)S(1)}, f32[8,768]{1,0:T(8,128)S(1)}, u32[]{:S(2)}, u32[]{:S(2)}) %collective-permute-start.7) | collective-permute-done | bytes 24608 | tf_op jit(solution)/shard_map/ppermute | solution.py:19
  40.2 1.1 %collective-permute-done.8 = bf16[8,512]{1,0:T(8,128)(2,1)S(1)} collective-permute-done((bf16[8,512]{1,0:T(8,128)(2,1)S(1)}, bf16[8,512]{1,0:T(8,128)(2,1)S(1)}, u32[]{:S(2)}, u32[]{:S(2)}) %collective-permute-start.8) | collective-permute-done | bytes 8224 | tf_op jit(solution)/shard_map/ppermute | solution.py:19
  41.5 3.5 %select_reduce_fusion = (f32[8,8]{1,0:T(8,128)S(1)}, f32[8,8,2048]{2,1,0:T(8,128)S(1)}) fusion(pred[8,2048]{1,0:T(8,128)(4,1)S(1)} %iota_compare_fusion, bf16[1,8,2048,128]{3,2,1,0:T(8,128)(2,1)} %param.15, bf16[8,4,128]{2,1,0:T(4,128)(2,1)S(1)} %concatenate.179, bf16[8,4,128]{2,1,0:T(4,128)(2,1)S(1)} %concatenate.178, pred[]{:T(512)S(6)} %eq.61), kind=kOutput, calls=%fused_computation.18 | convolution fusion | flops 34021312 | bytes 4751617 | tf_op jit(solution)/shard_map/bhe,bte->bht/dot_general | solution.py:143
  45.3 2.9 %fusion.14 = f32[8,8,128]{2,1,0:T(8,128)S(1)} fusion(bf16[1,8,2048,128]{3,2,1,0:T(8,128)(2,1)} %param.16, f32[8,8,2048]{2,1,0:T(8,128)S(1)} %get-tuple-element.22, f32[8,8]{1,0:T(8,128)S(1)} %fusion.48, pred[8,2048]{1,0:T(8,128)(4,1)S(1)} %iota_compare_fusion, f32[8,128]{1,0:T(8,128)S(1)} %get-tuple-element.13, f32[8,8]{1,0:T(8,128)S(1)} %convert_element_type.44), kind=kOutput, calls=%fused_computation.16 | convolution fusion | flops 33964032 | bytes 4772352 | tf_op jit(solution)/shard_map/bht,bte->bhe/dot_general | solution.py:156
  49.1 1.4 %collective-permute-done.9 = f32[8,4,130]{0,1,2:T(4,128)S(1)} collective-permute-done((f32[8,4,130]{0,1,2:T(4,128)S(1)}, f32[8,4,130]{0,1,2:T(4,128)S(1)}, u32[]{:S(2)}, u32[]{:S(2)}) %collective-permute-start.9) | collective-permute-done | bytes 16672 | tf_op jit(solution)/shard_map/ppermute | solution.py:19
  51.9 1.5 %collective-permute-start.11 = (bf16[2,8,512]{2,1,0:T(8,128)(2,1)S(1)}, bf16[2,8,512]{2,1,0:T(8,128)(2,1)S(1)}, u32[]{:S(2)}, u32[]{:S(2)}) collective-permute-start(bf16[2,8,512]{2,1,0:T(8,128)(2,1)S(1)} %maximum_select_fusion.10), channel_id=1, source_target_pairs={{0,2},{1,3},{2,0},{3,1},{4,6},{5,7},{6,4},{7,5},{8,10},{9,11},{10,... | collective-permute-start | bytes 49160 | tf_op jit(solution)/shard_map/ppermute | solution.py:19
  53.4 2.2 %collective-permute-done.11 = bf16[2,8,512]{2,1,0:T(8,128)(2,1)S(1)} collective-permute-done((bf16[2,8,512]{2,1,0:T(8,128)(2,1)S(1)}, bf16[2,8,512]{2,1,0:T(8,128)(2,1)S(1)}, u32[]{:S(2)}, u32[]{:S(2)}) %collective-permute-start.11) | collective-permute-done | bytes 16416 | tf_op jit(solution)/shard_map/ppermute | solution.py:19
  55.7 3.9 %collective-permute-done.12 = bf16[4,8,512]{2,1,0:T(8,128)(2,1)S(1)} collective-permute-done((bf16[4,8,512]{2,1,0:T(8,128)(2,1)S(1)}, bf16[4,8,512]{2,1,0:T(8,128)(2,1)S(1)}, u32[]{:S(2)}, u32[]{:S(2)}) %collective-permute-start.12) | collective-permute-done | bytes 32800 | tf_op jit(solution)/shard_map/ppermute | solution.py:19
  59.7 5.3 %collective-permute-done.13 = bf16[8,8,512]{2,1,0:T(8,128)(2,1)S(1)} collective-permute-done((bf16[8,8,512]{2,1,0:T(8,128)(2,1)S(1)}, bf16[8,8,512]{2,1,0:T(8,128)(2,1)S(1)}, u32[]{:S(2)}, u32[]{:S(2)}) %collective-permute-start.13) | collective-permute-done | bytes 65568 | tf_op jit(solution)/shard_map/ppermute | solution.py:19
  65.6 5.6 %fusion.2 = f32[8,4,512,1]{2,0,3,1:T(8,128)S(1)} fusion(bf16[4,512,16,128]{3,2,1,0:T(8,128)(2,1)} %bitcast.205, bf16[16,8,128]{2,1,0:T(8,128)(2,1)S(1)} %gather_fusion.4, pred[16]{0:T(512)(128)(4,1)S(1)} %compare_and_fusion.2), kind=kOutput, calls=%fused_computation.7 | convolution fusion | flops 67125248 | bytes 8486928 | tf_op jit(solution)/shard_map/gabe,cae->gbc/dot_general | solution.py:194
  71.4 3.9 %collective-permute-done.14 = f32[2,8,512]{2,1,0:T(8,128)S(1)} collective-permute-done((f32[2,8,512]{2,1,0:T(8,128)S(1)}, f32[2,8,512]{2,1,0:T(8,128)S(1)}, u32[]{:S(2)}, u32[]{:S(2)}) %collective-permute-start.14) | collective-permute-done | bytes 32800 | tf_op jit(solution)/shard_map/ppermute | solution.py:19
  75.4 4.6 %collective-permute-done.15 = f32[8,512]{1,0:T(8,128)S(1)} collective-permute-done((f32[8,512]{1,0:T(8,128)S(1)}, f32[8,512]{1,0:T(8,128)S(1)}, u32[]{:S(2)}, u32[]{:S(2)}) %collective-permute-start.15) | collective-permute-done | bytes 16416 | tf_op jit(solution)/shard_map/ppermute | solution.py:19
  80.0 1.9 %collective-permute-start.16 = (bf16[8,512]{1,0:T(8,128)(2,1)S(1)}, bf16[8,512]{1,0:T(8,128)(2,1)S(1)}, u32[]{:S(2)}, u32[]{:S(2)}) collective-permute-start(bf16[8,512]{1,0:T(8,128)(2,1)S(1)} %bitcast_add_fusion.3), channel_id=1, source_target_pairs={{0,0},{1,4},{2,8},{3,12},{4,1},{5,5},{6,9},{7,13},{8,2},{9,6},{10,... | collective-permute-start | bytes 24584 | tf_op jit(solution)/shard_map/ppermute | solution.py:206
  81.9 5.7 %collective-permute-done.16 = bf16[8,512]{1,0:T(8,128)(2,1)S(1)} collective-permute-done((bf16[8,512]{1,0:T(8,128)(2,1)S(1)}, bf16[8,512]{1,0:T(8,128)(2,1)S(1)}, u32[]{:S(2)}, u32[]{:S(2)}) %collective-permute-start.16) | collective-permute-done | bytes 8224 | tf_op jit(solution)/shard_map/ppermute | solution.py:206
  (95 shorter events, 11.3 us)
Async XLA Ops:
  0.0 17.8 %copy-start = (bf16[2,1024,512]{2,1,0:T(8,128)(2,1)S(1)}, bf16[2,1024,512]{2,1,0:T(8,128)(2,1)}, u32[]{:S(2)}) copy-start(bf16[2,1024,512]{2,1,0:T(8,128)(2,1)} %param.13) | copy-start | bytes 6291460
  0.0 2.4 %collective-permute-start = (bf16[1,8,512]{2,1,0:T(8,128)(2,1)}, bf16[1,8,512]{2,1,0:T(8,128)(2,1)S(1)}, u32[]{:S(2)}, u32[]{:S(2)}) collective-permute-start(bf16[1,8,512]{2,1,0:T(8,128)(2,1)} %param.9), channel_id=1, source_target_pairs={{0,1},{1,0},{2,3},{3,2},{4,5},{5,4},{6,7},{7,6},{8,9},{9,8},{10,11... | collective-permute-start | bytes 24584 | tf_op jit(solution)/shard_map/ppermute | solution.py:19
  3.2 3.7 %collective-permute-start.1 = (bf16[2,8,512]{2,1,0:T(8,128)(2,1)S(1)}, bf16[2,8,512]{2,1,0:T(8,128)(2,1)S(1)}, u32[]{:S(2)}, u32[]{:S(2)}) collective-permute-start(bf16[2,8,512]{2,1,0:T(8,128)(2,1)S(1)} %maximum_select_fusion.7), channel_id=1, source_target_pairs={{0,2},{1,3},{2,0},{3,1},{4,6},{5,7},{6,4},{7,5},{8,10},{9,11},{10,... | collective-permute-start | bytes 49160 | tf_op jit(solution)/shard_map/ppermute | solution.py:19
  6.9 4.0 %collective-permute-start.2 = (bf16[4,8,512]{2,1,0:T(8,128)(2,1)S(1)}, bf16[4,8,512]{2,1,0:T(8,128)(2,1)S(1)}, u32[]{:S(2)}, u32[]{:S(2)}) collective-permute-start(bf16[4,8,512]{2,1,0:T(8,128)(2,1)S(1)} %maximum_select_fusion.4), channel_id=1, source_target_pairs={{0,4},{1,5},{2,6},{3,7},{4,0},{5,1},{6,2},{7,3},{8,12},{9,13},{10,... | collective-permute-start | bytes 98312 | tf_op jit(solution)/shard_map/ppermute | solution.py:19
  10.9 5.8 %collective-permute-start.3 = (bf16[8,8,512]{2,1,0:T(8,128)(2,1)S(1)}, bf16[8,8,512]{2,1,0:T(8,128)(2,1)S(1)}, u32[]{:S(2)}, u32[]{:S(2)}) collective-permute-start(bf16[8,8,512]{2,1,0:T(8,128)(2,1)S(1)} %maximum_select_fusion.1), channel_id=1, source_target_pairs={{0,8},{1,9},{2,10},{3,11},{4,12},{5,13},{6,14},{7,15},{8,0},{9,1},... | collective-permute-start | bytes 196616 | tf_op jit(solution)/shard_map/ppermute | solution.py:19
  19.2 6.5 %copy-start.1 = (s32[16]{0:T(128)S(1)}, s32[16]{0:T(128)}, u32[]{:S(2)}) copy-start(s32[16]{0:T(128)} %param.14) | copy-start | bytes 196
  25.5 1.4 %collective-permute-start.4 = (f32[2,2,2,8,384]{4,3,2,1,0:T(8,128)S(1)}, f32[2,2,2,8,384]{4,3,2,1,0:T(8,128)S(1)}, u32[]{:S(2)}, u32[]{:S(2)}) collective-permute-start(f32[2,2,2,8,384]{4,3,2,1,0:T(8,128)S(1)} %select_bitcast_fusion.1), channel_id=1, source_target_pairs={{0,1},{1,0},{2,3},{3,2},{4,5},{5,4},{6,7},{7,6},{8,9},{9,8},{10,11... | collective-permute-start | bytes 294920 | tf_op jit(solution)/shard_map/ppermute | solution.py:19
  26.9 4.2 %collective-permute-start.5 = (f32[2,2,8,384]{3,2,1,0:T(8,128)S(1)}, f32[2,2,8,384]{3,2,1,0:T(8,128)S(1)}, u32[]{:S(2)}, u32[]{:S(2)}) collective-permute-start(f32[2,2,8,384]{3,2,1,0:T(8,128)S(1)} %select_bitcast_fusion.3), channel_id=1, source_target_pairs={{0,2},{1,3},{2,0},{3,1},{4,6},{5,7},{6,4},{7,5},{8,10},{9,11},{10,... | collective-permute-start | bytes 147464 | tf_op jit(solution)/shard_map/ppermute | solution.py:19
  31.1 4.2 %collective-permute-start.6 = (f32[2,8,768]{2,1,0:T(8,128)S(1)}, f32[2,8,768]{2,1,0:T(8,128)S(1)}, u32[]{:S(2)}, u32[]{:S(2)}) collective-permute-start(f32[2,8,768]{2,1,0:T(8,128)S(1)} %select_bitcast_fusion.2), channel_id=1, source_target_pairs={{0,4},{1,5},{2,6},{3,7},{4,0},{5,1},{6,2},{7,3},{8,12},{9,13},{10,... | collective-permute-start | bytes 147464 | tf_op jit(solution)/shard_map/ppermute | solution.py:19
  35.3 4.8 %collective-permute-start.7 = (f32[8,768]{1,0:T(8,128)S(1)}, f32[8,768]{1,0:T(8,128)S(1)}, u32[]{:S(2)}, u32[]{:S(2)}) collective-permute-start(f32[8,768]{1,0:T(8,128)S(1)} %select_bitcast_fusion.5), channel_id=1, source_target_pairs={{0,8},{1,9},{2,10},{3,11},{4,12},{5,13},{6,14},{7,15},{8,0},{9,1},... | collective-permute-start | bytes 73736 | tf_op jit(solution)/shard_map/ppermute | solution.py:19
  40.1 1.2 %collective-permute-start.8 = (bf16[8,512]{1,0:T(8,128)(2,1)S(1)}, bf16[8,512]{1,0:T(8,128)(2,1)S(1)}, u32[]{:S(2)}, u32[]{:S(2)}) collective-permute-start(bf16[8,512]{1,0:T(8,128)(2,1)S(1)} %slice.139), channel_id=1, source_target_pairs={{0,1},{1,0},{2,3},{3,2},{4,5},{5,4},{6,7},{7,6},{8,9},{9,8},{10,11... | collective-permute-start | bytes 24584 | tf_op jit(solution)/shard_map/ppermute | solution.py:19
  48.8 1.6 %collective-permute-start.9 = (f32[8,4,130]{0,1,2:T(4,128)S(1)}, f32[8,4,130]{0,1,2:T(4,128)S(1)}, u32[]{:S(2)}, u32[]{:S(2)}) collective-permute-start(f32[8,4,130]{0,1,2:T(4,128)S(1)} %pad_maximum_fusion), channel_id=1, source_target_pairs={{0,1},{1,0},{2,3},{3,2},{4,5},{5,4},{6,7},{7,6},{8,9},{9,8},{10,11... | collective-permute-start | bytes 49928 | tf_op jit(solution)/shard_map/ppermute | solution.py:19
  50.7 1.2 %collective-permute-start.10 = (bf16[1,8,512]{2,1,0:T(8,128)(2,1)S(1)}, bf16[1,8,512]{2,1,0:T(8,128)(2,1)S(1)}, u32[]{:S(2)}, u32[]{:S(2)}) collective-permute-start(bf16[1,8,512]{2,1,0:T(8,128)(2,1)S(1)} %bitcast.225), channel_id=1, source_target_pairs={{0,1},{1,0},{2,3},{3,2},{4,5},{5,4},{6,7},{7,6},{8,9},{9,8},{10,11... | collective-permute-start | bytes 24584 | tf_op jit(solution)/shard_map/ppermute | solution.py:19
  51.9 3.7 %collective-permute-start.11 = (bf16[2,8,512]{2,1,0:T(8,128)(2,1)S(1)}, bf16[2,8,512]{2,1,0:T(8,128)(2,1)S(1)}, u32[]{:S(2)}, u32[]{:S(2)}) collective-permute-start(bf16[2,8,512]{2,1,0:T(8,128)(2,1)S(1)} %maximum_select_fusion.10), channel_id=1, source_target_pairs={{0,2},{1,3},{2,0},{3,1},{4,6},{5,7},{6,4},{7,5},{8,10},{9,11},{10,... | collective-permute-start | bytes 49160 | tf_op jit(solution)/shard_map/ppermute | solution.py:19
  55.6 4.0 %collective-permute-start.12 = (bf16[4,8,512]{2,1,0:T(8,128)(2,1)S(1)}, bf16[4,8,512]{2,1,0:T(8,128)(2,1)S(1)}, u32[]{:S(2)}, u32[]{:S(2)}) collective-permute-start(bf16[4,8,512]{2,1,0:T(8,128)(2,1)S(1)} %maximum_select_fusion.6), channel_id=1, source_target_pairs={{0,4},{1,5},{2,6},{3,7},{4,0},{5,1},{6,2},{7,3},{8,12},{9,13},{10,... | collective-permute-start | bytes 98312 | tf_op jit(solution)/shard_map/ppermute | solution.py:19
  59.6 5.4 %collective-permute-start.13 = (bf16[8,8,512]{2,1,0:T(8,128)(2,1)S(1)}, bf16[8,8,512]{2,1,0:T(8,128)(2,1)S(1)}, u32[]{:S(2)}, u32[]{:S(2)}) collective-permute-start(bf16[8,8,512]{2,1,0:T(8,128)(2,1)S(1)} %maximum_select_fusion.3), channel_id=1, source_target_pairs={{0,8},{1,9},{2,10},{3,11},{4,12},{5,13},{6,14},{7,15},{8,0},{9,1},... | collective-permute-start | bytes 196616 | tf_op jit(solution)/shard_map/ppermute | solution.py:19
  71.3 4.0 %collective-permute-start.14 = (f32[2,8,512]{2,1,0:T(8,128)S(1)}, f32[2,8,512]{2,1,0:T(8,128)S(1)}, u32[]{:S(2)}, u32[]{:S(2)}) collective-permute-start(f32[2,8,512]{2,1,0:T(8,128)S(1)} %select_bitcast_fusion.4), channel_id=1, source_target_pairs={{0,4},{1,5},{2,6},{3,7},{4,0},{5,1},{6,2},{7,3},{8,12},{9,13},{10,... | collective-permute-start | bytes 98312 | tf_op jit(solution)/shard_map/ppermute | solution.py:19
  75.3 4.7 %collective-permute-start.15 = (f32[8,512]{1,0:T(8,128)S(1)}, f32[8,512]{1,0:T(8,128)S(1)}, u32[]{:S(2)}, u32[]{:S(2)}) collective-permute-start(f32[8,512]{1,0:T(8,128)S(1)} %select_bitcast_fusion.6), channel_id=1, source_target_pairs={{0,8},{1,9},{2,10},{3,11},{4,12},{5,13},{6,14},{7,15},{8,0},{9,1},... | collective-permute-start | bytes 49160 | tf_op jit(solution)/shard_map/ppermute | solution.py:19
  80.0 7.7 %collective-permute-start.16 = (bf16[8,512]{1,0:T(8,128)(2,1)S(1)}, bf16[8,512]{1,0:T(8,128)(2,1)S(1)}, u32[]{:S(2)}, u32[]{:S(2)}) collective-permute-start(bf16[8,512]{1,0:T(8,128)(2,1)S(1)} %bitcast_add_fusion.3), channel_id=1, source_target_pairs={{0,0},{1,4},{2,8},{3,12},{4,1},{5,5},{6,9},{7,13},{8,2},{9,6},{10,... | collective-permute-start | bytes 24584 | tf_op jit(solution)/shard_map/ppermute | solution.py:206

commit v3 on v2

--- a/solution.py
+++ b/solution.py
@@ -64,6 +64,36 @@
         give = jnp.where(low, second, first)
         held = keep + xor_swap(give, axis, bit)
     return held[None]
+
+
+def pick(table, idx):
+    hit = idx[:, None] == jnp.arange(table.shape[0], dtype=idx.dtype)[None, :]
+    hit = hit.reshape(hit.shape + (1,) * (table.ndim - 1))
+    return jnp.sum(jnp.where(hit, table[None], jnp.zeros((), table.dtype)), axis=1)
+
+
+def gather_rounds(held, axis, bits):
+    me = lax.axis_index(axis)
+    for bit in bits:
+        other = xor_swap(held, axis, bit)
+        low = ((me >> bit) & 1) == 0
+        held = jnp.where(low, jnp.concatenate([held, other], 0), jnp.concatenate([other, held], 0))
+    return held
+
+
+def exchange_rounds(held, axis, bits):
+    me = lax.axis_index(axis)
+    count = len(bits)
+    for done, bit in enumerate(bits):
+        low = ((me >> bit) & 1) == 0
+        first = lax.index_in_dim(held, 0, 0, keepdims=False)
+        second = lax.index_in_dim(held, 1, 0, keepdims=False)
+        keep = jnp.where(low, first, second)
+        give = jnp.where(low, second, first)
+        got = xor_swap(give, axis, bit)
+        at = count - done - 1 + done
+        held = jnp.where(low, jnp.stack([keep, got], at), jnp.stack([got, keep], at))
+    return held
 
 
 def norm_rows(rows_float, norm_gain):
@@ -106,7 +136,7 @@
         .transpose(0, 2, 1, 3)
         .reshape(group_count * QG, ROWS, HD)
     )
-    query_pick = jnp.take(query_part, dest_copy * QG + dest_group, axis=0)
+    query_pick = pick(query_part, dest_copy * QG + dest_group)
     key_rows = lax.dynamic_slice_in_dim(normed_every, my_index * key_width, key_width, 1)
     keyval_part = jnp.einsum("rc,kfc->rkf", key_rows, kv_blocks, preferred_element_type=jnp.float32)
     keyval_part = (
@@ -114,7 +144,7 @@
         .transpose(0, 3, 1, 2, 4)
         .reshape(group_count * KVH, ROWS, 2 * HD)
     )
-    keyval_term = jnp.take(keyval_part, dest_copy * KVH + dest_head, axis=0)
+    keyval_term = pick(keyval_part, dest_copy * KVH + dest_head)
     bits = ranks.bit_length() - 1
     col_bits = grid_cols.bit_length() - 1
     compact = jnp.concatenate([query_pick, keyval_term], -1)
@@ -179,8 +209,15 @@
     factor_got = jnp.exp(got_top - joint)
     numer = own_summed * factor_own[..., None] + got_summed * factor_got[..., None]
     denom = own_total * factor_own + got_total * factor_got
-    attention = (numer / denom[..., None]).astype(jnp.bfloat16).reshape(ROWS, GR * HD)
-    every_attn = gather_xor(attention[None], "tp")
+    attention = (numer / denom[..., None]).astype(jnp.bfloat16)
+    bits = ranks.bit_length() - 1
+    col_bits = grid_cols.bit_length() - 1
+    row_bits = GR.bit_length() - 1
+    by_row = attention.transpose(1, 0, 2).reshape((2,) * row_bits + (ROWS, HD))
+    by_row = exchange_rounds(by_row, "tp", list(range(bits - 1, col_bits - 1, -1)))
+    by_row = by_row.reshape(GR, ROWS, HD)
+    every_slot = gather_rounds(by_row[None], "tp", range(col_bits))
+    every_slot = every_slot.transpose(1, 0, 2, 3).reshape(group_count, ROLL, ROWS, HD)
     head_ids = jnp.arange(KVH, dtype=jnp.int32)
     pair_heads = kv_assign[0::2]
     inverse = jnp.sum(
@@ -188,9 +225,7 @@
     )
     slot_ids = jnp.arange(QG, dtype=jnp.int32)
     rank_of_slot = 2 * inverse[slot_ids // 2] + slot_ids % 2
-    attn_grid = every_attn.reshape(group_count, ROLL, ROWS, GR, HD)
-    row_slot = lax.dynamic_index_in_dim(attn_grid, grid_row, 3, keepdims=False)
-    chosen = jnp.take(row_slot, rank_of_slot, axis=1)
+    chosen = jax.vmap(lambda per_group: pick(per_group, rank_of_slot))(every_slot)
     out_part = jnp.einsum("gabe,cae->gbc", chosen, o_blocks[0], preferred_element_type=jnp.float32)
     if group_count == 1 and grid_cols == GR and col_width == GR * DS:
         col_bits = grid_cols.bit_length() - 1
@@ -203,7 +238,7 @@
             range(col_bits, col_bits + row_bits),
         )
         pairs = [(i * grid_cols + j, j * grid_cols + i) for i in range(GR) for j in range(grid_cols)]
-        my_cols = lax.ppermute(held, "tp", pairs)
+        my_cols = lax.ppermute(held.astype(jnp.bfloat16), "tp", pairs)
     else:
         placed = jnp.zeros((group_count, ROWS, D), jnp.float32)
         placed = lax.dynamic_update_slice_in_dim(placed, out_part, grid_col * col_width, 2)

time: 88.6 us -> 87.2 us (0.984)
  local copies, waits for them, and re-layouts: 5.38 us -> 3.55 us
    gather x3 -> x0, local copies, waits for them, and re-layouts: 1.74 us -> none  [the longest x1 0.58 us: local(): keyval_term = jnp.take(keyval_part, dest_copy * KVH + dest_head, axis=0)]
    reduce_sum x0 -> x3, other arithmetic: none -> 0.89 us  [pick(): jnp.sum(jnp.where(hit, table[None], jnp.zeros((), table.dtype)), axis=1)]
  transfers between devices with their start and end apart: 17 -> 17, of which waited for: 16 -> 16; matrix products, arithmetic and copies ran while one was open for 4% -> 3% of each run, Pallas kernels for 0% -> 0%
where the time goes in v3:
time: 87.2 us; the launch traced here: 86.9 us
  waiting for transfers between devices  52.1 us (60%)
  matrix products  18.5 us (21%)
  starting transfers between devices  8.23 us (9%)
  other arithmetic  4.14 us (5%)
  local copies, waits for them, and re-layouts  3.55 us (4%)
    ppermute x16, waiting for transfers between devices, from_partner(): return lax.ppermute(value, axis, pairs)  46.3 us
    ppermute x16, starting transfers between devices, from_partner(): return lax.ppermute(value, axis, pairs)  6.32 us
    ppermute x1, waiting for transfers between devices, local(): my_cols = lax.ppermute(held.astype(jnp.bfloat16), 'tp', pairs)  5.74 us
    dot_general x1, matrix products, local(): jnp.einsum('rc,aec->rae', col_rows, q_blocks[0], preferred_element_type=j...  5.65 us
    dot_general x1, matrix products, local(): jnp.einsum('gabe,cae->gbc', chosen, o_blocks[0], preferred_element_type=j...  5.65 us
    dot_general x1, matrix products, local(): jnp.einsum('bhe,bte->bht', both_queries, key_cache[0], preferred_element_...  3.46 us
    dot_general x1, matrix products, local(): jnp.einsum('bht,bte->bhe', weights.astype(jnp.bfloat16), value_cache[0],...  2.93 us
    ppermute x1, starting transfers between devices, local(): my_cols = lax.ppermute(held.astype(jnp.bfloat16), 'tp', pairs)  1.91 us
  transfers between devices with their start and end apart: 17, of which 16 were waited for; matrix products, arithmetic and copies ran while one was open for 3% of the time, Pallas kernels for 0%

profile of v3, /device:TPU:24, one launch (start us, length us, event | category | flops | bytes accessed | tf_op | source)
XLA Modules:
  0.0 86.9 jit_solution(13688694294881849631)
XLA Ops:
  0.0 1.5 %gather_fusion.1 = s32[16]{0:T(128)S(1)} fusion(s32[16]{0:T(128)} %param.14, s32[1024]{0:T(1024)S(1)} %pad_clamp_fusion), kind=kCustom, calls=%fused_computation.1 | custom fusion | bytes 192 | tf_op jit(solution)/shard_map/gather | solution.py:119
  2.3 1.5 %collective-permute-start.1 = (bf16[2,8,512]{2,1,0:T(8,128)(2,1)S(1)}, bf16[2,8,512]{2,1,0:T(8,128)(2,1)S(1)}, u32[]{:S(2)}, u32[]{:S(2)}) collective-permute-start(bf16[2,8,512]{2,1,0:T(8,128)(2,1)S(1)} %maximum_select_fusion.4), channel_id=1, source_target_pairs={{0,2},{1,3},{2,0},{3,1},{4,6},{5,7},{6,4},{7,5},{8,10},{9,11},{10,... | collective-permute-start | bytes 49160 | tf_op jit(solution)/shard_map/ppermute | solution.py:19
  3.8 2.2 %collective-permute-done.1 = bf16[2,8,512]{2,1,0:T(8,128)(2,1)S(1)} collective-permute-done((bf16[2,8,512]{2,1,0:T(8,128)(2,1)S(1)}, bf16[2,8,512]{2,1,0:T(8,128)(2,1)S(1)}, u32[]{:S(2)}, u32[]{:S(2)}) %collective-permute-start.1) | collective-permute-done | bytes 16416 | tf_op jit(solution)/shard_map/ppermute | solution.py:19
  6.6 3.4 %collective-permute-done.2 = bf16[4,8,512]{2,1,0:T(8,128)(2,1)S(1)} collective-permute-done((bf16[4,8,512]{2,1,0:T(8,128)(2,1)S(1)}, bf16[4,8,512]{2,1,0:T(8,128)(2,1)S(1)}, u32[]{:S(2)}, u32[]{:S(2)}) %collective-permute-start.2) | collective-permute-done | bytes 32800 | tf_op jit(solution)/shard_map/ppermute | solution.py:19
  10.5 5.3 %collective-permute-done.3 = bf16[8,8,512]{2,1,0:T(8,128)(2,1)S(1)} collective-permute-done((bf16[8,8,512]{2,1,0:T(8,128)(2,1)S(1)}, bf16[8,8,512]{2,1,0:T(8,128)(2,1)S(1)}, u32[]{:S(2)}, u32[]{:S(2)}) %collective-permute-start.3) | collective-permute-done | bytes 65568 | tf_op jit(solution)/shard_map/ppermute | solution.py:19
  17.6 5.7 %fusion.11 = f32[16,8,128]{2,1,0:T(8,128)S(1)} fusion(bf16[1,16,128,2048]{3,2,1,0:T(8,128)(2,1)} %param.11, bf16[8,8192]{1,0:T(8,128)(2,1)S(1)} %multiply_convert_fusion, s32[]{:T(128)S(6)} %select_n.497), kind=kOutput, calls=%fused_computation.11 | convolution fusion | flops 67108864 | bytes 8486916 | tf_op jit(solution)/shard_map/rc,aec->rae/dot_general | solution.py:131
  24.0 1.3 %collective-permute-done.4 = f32[2,2,2,8,384]{4,3,2,1,0:T(8,128)S(1)} collective-permute-done((f32[2,2,2,8,384]{4,3,2,1,0:T(8,128)S(1)}, f32[2,2,2,8,384]{4,3,2,1,0:T(8,128)S(1)}, u32[]{:S(2)}, u32[]{:S(2)}) %collective-permute-start.4) | collective-permute-done | bytes 98336 | tf_op jit(solution)/shard_map/ppermute | solution.py:19
  25.3 1.6 %collective-permute-start.5 = (f32[2,2,8,384]{3,2,1,0:T(8,128)S(1)}, f32[2,2,8,384]{3,2,1,0:T(8,128)S(1)}, u32[]{:S(2)}, u32[]{:S(2)}) collective-permute-start(f32[2,2,8,384]{3,2,1,0:T(8,128)S(1)} %select_bitcast_fusion.3), channel_id=1, source_target_pairs={{0,2},{1,3},{2,0},{3,1},{4,6},{5,7},{6,4},{7,5},{8,10},{9,11},{10,... | collective-permute-start | bytes 147464 | tf_op jit(solution)/shard_map/ppermute | solution.py:19
  26.9 2.5 %collective-permute-done.5 = f32[2,2,8,384]{3,2,1,0:T(8,128)S(1)} collective-permute-done((f32[2,2,8,384]{3,2,1,0:T(8,128)S(1)}, f32[2,2,8,384]{3,2,1,0:T(8,128)S(1)}, u32[]{:S(2)}, u32[]{:S(2)}) %collective-permute-start.5) | collective-permute-done | bytes 49184 | tf_op jit(solution)/shard_map/ppermute | solution.py:19
  29.6 4.1 %collective-permute-done.6 = f32[2,8,768]{2,1,0:T(8,128)S(1)} collective-permute-done((f32[2,8,768]{2,1,0:T(8,128)S(1)}, f32[2,8,768]{2,1,0:T(8,128)S(1)}, u32[]{:S(2)}, u32[]{:S(2)}) %collective-permute-start.6) | collective-permute-done | bytes 49184 | tf_op jit(solution)/shard_map/ppermute | solution.py:19
  33.9 4.6 %collective-permute-done.7 = f32[8,768]{1,0:T(8,128)S(1)} collective-permute-done((f32[8,768]{1,0:T(8,128)S(1)}, f32[8,768]{1,0:T(8,128)S(1)}, u32[]{:S(2)}, u32[]{:S(2)}) %collective-permute-start.7) | collective-permute-done | bytes 24608 | tf_op jit(solution)/shard_map/ppermute | solution.py:19
  39.8 3.5 %select_reduce_fusion.3 = (f32[8,8]{1,0:T(8,128)S(1)}, f32[8,8,2048]{2,1,0:T(8,128)S(1)}) fusion(pred[8,2048]{1,0:T(8,128)(4,1)S(1)} %iota_compare_fusion, bf16[1,8,2048,128]{3,2,1,0:T(8,128)(2,1)} %param.15, bf16[8,4,128]{2,1,0:T(4,128)(2,1)S(1)} %concatenate.106, bf16[8,4,128]{2,1,0:T(4,128)(2,1)S(1)} %concatenate.105, pred[]{:T(512)S(6)} %eq.114), kind=kOutput, calls=%fused_computation.18 | convolution fusion | flops 34021312 | bytes 4751617 | tf_op jit(solution)/shard_map/bhe,bte->bht/dot_general | solution.py:173
  43.7 2.9 %fusion.14 = f32[8,8,128]{2,1,0:T(8,128)S(1)} fusion(bf16[1,8,2048,128]{3,2,1,0:T(8,128)(2,1)} %param.16, f32[8,8,2048]{2,1,0:T(8,128)S(1)} %get-tuple-element.22, f32[8,8]{1,0:T(8,128)S(1)} %fusion.44, pred[8,2048]{1,0:T(8,128)(4,1)S(1)} %iota_compare_fusion, f32[8,128]{1,0:T(8,128)S(1)} %get-tuple-element.13, f32[8,8]{1,0:T(8,128)S(1)} %convert_element_type.46), kind=kOutput, calls=%fused_computation.13 | convolution fusion | flops 33964032 | bytes 4772352 | tf_op jit(solution)/shard_map/bht,bte->bhe/dot_general | solution.py:186
  47.5 1.3 %collective-permute-done.9 = f32[8,4,130]{0,1,2:T(4,128)S(1)} collective-permute-done((f32[8,4,130]{0,1,2:T(4,128)S(1)}, f32[8,4,130]{0,1,2:T(4,128)S(1)}, u32[]{:S(2)}, u32[]{:S(2)}) %collective-permute-start.9) | collective-permute-done | bytes 16672 | tf_op jit(solution)/shard_map/ppermute | solution.py:19
  49.4 5.7 %collective-permute-done.10 = bf16[2,8,128]{1,0,2:T(2,128)(2,1)S(1)} collective-permute-done((bf16[2,8,128]{1,0,2:T(2,128)(2,1)S(1)}, bf16[2,8,128]{1,0,2:T(2,128)(2,1)S(1)}, u32[]{:S(2)}, u32[]{:S(2)}) %collective-permute-start.10) | collective-permute-done | bytes 4128 | tf_op jit(solution)/shard_map/ppermute | solution.py:19
  55.9 2.9 %collective-permute-done.11 = bf16[2,8,128]{2,1,0:T(8,128)(2,1)S(1)} collective-permute-done((bf16[2,8,128]{2,1,0:T(8,128)(2,1)S(1)}, bf16[2,8,128]{2,1,0:T(8,128)(2,1)S(1)}, u32[]{:S(2)}, u32[]{:S(2)}) %collective-permute-start.11) | collective-permute-done | bytes 4128 | tf_op jit(solution)/shard_map/ppermute | solution.py:19
  59.0 1.1 %collective-permute-done.12 = bf16[1,4,8,128]{3,2,1,0:T(8,128)(2,1)S(1)} collective-permute-done((bf16[1,4,8,128]{3,2,1,0:T(8,128)(2,1)S(1)}, bf16[1,4,8,128]{3,2,1,0:T(8,128)(2,1)S(1)}, u32[]{:S(2)}, u32[]{:S(2)}) %collective-permute-start.12) | collective-permute-done | bytes 8224 | tf_op jit(solution)/shard_map/ppermute | solution.py:19
  60.1 1.5 %collective-permute-start.13 = (bf16[2,4,8,128]{3,2,1,0:T(8,128)(2,1)S(1)}, bf16[2,4,8,128]{3,2,1,0:T(8,128)(2,1)S(1)}, u32[]{:S(2)}, u32[]{:S(2)}) collective-permute-start(bf16[2,4,8,128]{3,2,1,0:T(8,128)(2,1)S(1)} %maximum_select_fusion.6), channel_id=1, source_target_pairs={{0,2},{1,3},{2,0},{3,1},{4,6},{5,7},{6,4},{7,5},{8,10},{9,11},{10,... | collective-permute-start | bytes 49160 | tf_op jit(solution)/shard_map/ppermute | solution.py:19
  61.7 2.2 %collective-permute-done.13 = bf16[2,4,8,128]{3,2,1,0:T(8,128)(2,1)S(1)} collective-permute-done((bf16[2,4,8,128]{3,2,1,0:T(8,128)(2,1)S(1)}, bf16[2,4,8,128]{3,2,1,0:T(8,128)(2,1)S(1)}, u32[]{:S(2)}, u32[]{:S(2)}) %collective-permute-start.13) | collective-permute-done | bytes 16416 | tf_op jit(solution)/shard_map/ppermute | solution.py:19
  64.2 5.6 %fusion.2 = f32[8,4,512,1]{2,0,3,1:T(8,128)S(1)} fusion(bf16[4,512,16,128]{3,2,1,0:T(8,128)(2,1)} %bitcast.187, bf16[16,8,128]{2,1,0:T(8,128)(2,1)S(1)} %select_reduce_fusion.2), kind=kOutput, calls=%fused_computation.4 | convolution fusion | flops 67108864 | bytes 8486912 | tf_op jit(solution)/shard_map/gabe,cae->gbc/dot_general | solution.py:229
  70.0 3.9 %collective-permute-done.14 = f32[2,8,512]{2,1,0:T(8,128)S(1)} collective-permute-done((f32[2,8,512]{2,1,0:T(8,128)S(1)}, f32[2,8,512]{2,1,0:T(8,128)S(1)}, u32[]{:S(2)}, u32[]{:S(2)}) %collective-permute-start.14) | collective-permute-done | bytes 32800 | tf_op jit(solution)/shard_map/ppermute | solution.py:19
  74.0 4.6 %collective-permute-done.15 = f32[8,512]{1,0:T(8,128)S(1)} collective-permute-done((f32[8,512]{1,0:T(8,128)S(1)}, f32[8,512]{1,0:T(8,128)S(1)}, u32[]{:S(2)}, u32[]{:S(2)}) %collective-permute-start.15) | collective-permute-done | bytes 16416 | tf_op jit(solution)/shard_map/ppermute | solution.py:19
  78.6 1.9 %collective-permute-start.16 = (bf16[8,512]{1,0:T(8,128)(2,1)S(1)}, bf16[8,512]{1,0:T(8,128)(2,1)S(1)}, u32[]{:S(2)}, u32[]{:S(2)}) collective-permute-start(bf16[8,512]{1,0:T(8,128)(2,1)S(1)} %fusion.39), channel_id=1, source_target_pairs={{0,0},{1,4},{2,8},{3,12},{4,1},{5,5},{6,9},{7,13},{8,2},{9,6},{10,... | collective-permute-start | bytes 24584 | tf_op jit(solution)/shard_map/ppermute | solution.py:241
  80.5 5.7 %collective-permute-done.16 = bf16[8,512]{1,0:T(8,128)(2,1)S(1)} collective-permute-done((bf16[8,512]{1,0:T(8,128)(2,1)S(1)}, bf16[8,512]{1,0:T(8,128)(2,1)S(1)}, u32[]{:S(2)}, u32[]{:S(2)}) %collective-permute-start.16) | collective-permute-done | bytes 8224 | tf_op jit(solution)/shard_map/ppermute | solution.py:241
  (93 shorter events, 9.9 us)
Async XLA Ops:
  0.0 16.9 %copy-start = (bf16[2,1024,512]{2,1,0:T(8,128)(2,1)S(1)}, bf16[2,1024,512]{2,1,0:T(8,128)(2,1)}, u32[]{:S(2)}) copy-start(bf16[2,1024,512]{2,1,0:T(8,128)(2,1)} %param.13) | copy-start | bytes 6291460
  0.0 1.5 %collective-permute-start = (bf16[1,8,512]{2,1,0:T(8,128)(2,1)}, bf16[1,8,512]{2,1,0:T(8,128)(2,1)S(1)}, u32[]{:S(2)}, u32[]{:S(2)}) collective-permute-start(bf16[1,8,512]{2,1,0:T(8,128)(2,1)} %param.9), channel_id=1, source_target_pairs={{0,1},{1,0},{2,3},{3,2},{4,5},{5,4},{6,7},{7,6},{8,9},{9,8},{10,11... | collective-permute-start | bytes 24584 | tf_op jit(solution)/shard_map/ppermute | solution.py:19
  2.3 3.7 %collective-permute-start.1 = (bf16[2,8,512]{2,1,0:T(8,128)(2,1)S(1)}, bf16[2,8,512]{2,1,0:T(8,128)(2,1)S(1)}, u32[]{:S(2)}, u32[]{:S(2)}) collective-permute-start(bf16[2,8,512]{2,1,0:T(8,128)(2,1)S(1)} %maximum_select_fusion.4), channel_id=1, source_target_pairs={{0,2},{1,3},{2,0},{3,1},{4,6},{5,7},{6,4},{7,5},{8,10},{9,11},{10,... | collective-permute-start | bytes 49160 | tf_op jit(solution)/shard_map/ppermute | solution.py:19
  6.0 4.0 %collective-permute-start.2 = (bf16[4,8,512]{2,1,0:T(8,128)(2,1)S(1)}, bf16[4,8,512]{2,1,0:T(8,128)(2,1)S(1)}, u32[]{:S(2)}, u32[]{:S(2)}) collective-permute-start(bf16[4,8,512]{2,1,0:T(8,128)(2,1)S(1)} %maximum_select_fusion.2), channel_id=1, source_target_pairs={{0,4},{1,5},{2,6},{3,7},{4,0},{5,1},{6,2},{7,3},{8,12},{9,13},{10,... | collective-permute-start | bytes 98312 | tf_op jit(solution)/shard_map/ppermute | solution.py:19
  10.0 5.8 %collective-permute-start.3 = (bf16[8,8,512]{2,1,0:T(8,128)(2,1)S(1)}, bf16[8,8,512]{2,1,0:T(8,128)(2,1)S(1)}, u32[]{:S(2)}, u32[]{:S(2)}) collective-permute-start(bf16[8,8,512]{2,1,0:T(8,128)(2,1)S(1)} %maximum_select_fusion.1), channel_id=1, source_target_pairs={{0,8},{1,9},{2,10},{3,11},{4,12},{5,13},{6,14},{7,15},{8,0},{9,1},... | collective-permute-start | bytes 196616 | tf_op jit(solution)/shard_map/ppermute | solution.py:19
  17.6 16.2 %copy-start.2 = (s32[1,8]{1,0:T(1,128)S(1)}, s32[1,8]{1,0:T(1,128)}, u32[]{:S(2)}) copy-start(s32[1,8]{1,0:T(1,128)} %param.17) | copy-start | bytes 100
  23.9 1.4 %collective-permute-start.4 = (f32[2,2,2,8,384]{4,3,2,1,0:T(8,128)S(1)}, f32[2,2,2,8,384]{4,3,2,1,0:T(8,128)S(1)}, u32[]{:S(2)}, u32[]{:S(2)}) collective-permute-start(f32[2,2,2,8,384]{4,3,2,1,0:T(8,128)S(1)} %select_bitcast_fusion.1), channel_id=1, source_target_pairs={{0,1},{1,0},{2,3},{3,2},{4,5},{5,4},{6,7},{7,6},{8,9},{9,8},{10,11... | collective-permute-start | bytes 294920 | tf_op jit(solution)/shard_map/ppermute | solution.py:19
  25.3 4.2 %collective-permute-start.5 = (f32[2,2,8,384]{3,2,1,0:T(8,128)S(1)}, f32[2,2,8,384]{3,2,1,0:T(8,128)S(1)}, u32[]{:S(2)}, u32[]{:S(2)}) collective-permute-start(f32[2,2,8,384]{3,2,1,0:T(8,128)S(1)} %select_bitcast_fusion.3), channel_id=1, source_target_pairs={{0,2},{1,3},{2,0},{3,1},{4,6},{5,7},{6,4},{7,5},{8,10},{9,11},{10,... | collective-permute-start | bytes 147464 | tf_op jit(solution)/shard_map/ppermute | solution.py:19
  29.5 4.2 %collective-permute-start.6 = (f32[2,8,768]{2,1,0:T(8,128)S(1)}, f32[2,8,768]{2,1,0:T(8,128)S(1)}, u32[]{:S(2)}, u32[]{:S(2)}) collective-permute-start(f32[2,8,768]{2,1,0:T(8,128)S(1)} %select_bitcast_fusion.2), channel_id=1, source_target_pairs={{0,4},{1,5},{2,6},{3,7},{4,0},{5,1},{6,2},{7,3},{8,12},{9,13},{10,... | collective-permute-start | bytes 147464 | tf_op jit(solution)/shard_map/ppermute | solution.py:19
  33.7 4.8 %collective-permute-start.7 = (f32[8,768]{1,0:T(8,128)S(1)}, f32[8,768]{1,0:T(8,128)S(1)}, u32[]{:S(2)}, u32[]{:S(2)}) collective-permute-start(f32[8,768]{1,0:T(8,128)S(1)} %select_bitcast_fusion.5), channel_id=1, source_target_pairs={{0,8},{1,9},{2,10},{3,11},{4,12},{5,13},{6,14},{7,15},{8,0},{9,1},... | collective-permute-start | bytes 73736 | tf_op jit(solution)/shard_map/ppermute | solution.py:19
  38.5 1.2 %collective-permute-start.8 = (bf16[8,512]{1,0:T(8,128)(2,1)S(1)}, bf16[8,512]{1,0:T(8,128)(2,1)S(1)}, u32[]{:S(2)}, u32[]{:S(2)}) collective-permute-start(bf16[8,512]{1,0:T(8,128)(2,1)S(1)} %slice.151), channel_id=1, source_target_pairs={{0,1},{1,0},{2,3},{3,2},{4,5},{5,4},{6,7},{7,6},{8,9},{9,8},{10,11... | collective-permute-start | bytes 24584 | tf_op jit(solution)/shard_map/ppermute | solution.py:19
  43.3 4.1 %copy-start.1 = (s32[16]{0:T(128)S(1)}, s32[16]{0:T(128)}, u32[]{:S(2)}) copy-start(s32[16]{0:T(128)} %param.14) | copy-start | bytes 196
  47.2 1.6 %collective-permute-start.9 = (f32[8,4,130]{0,1,2:T(4,128)S(1)}, f32[8,4,130]{0,1,2:T(4,128)S(1)}, u32[]{:S(2)}, u32[]{:S(2)}) collective-permute-start(f32[8,4,130]{0,1,2:T(4,128)S(1)} %pad_maximum_fusion), channel_id=1, source_target_pairs={{0,1},{1,0},{2,3},{3,2},{4,5},{5,4},{6,7},{7,6},{8,9},{9,8},{10,11... | collective-permute-start | bytes 49928 | tf_op jit(solution)/shard_map/ppermute | solution.py:19
  49.1 6.0 %collective-permute-start.10 = (bf16[2,8,128]{1,0,2:T(2,128)(2,1)S(1)}, bf16[2,8,128]{1,0,2:T(2,128)(2,1)S(1)}, u32[]{:S(2)}, u32[]{:S(2)}) collective-permute-start(bf16[2,8,128]{1,0,2:T(2,128)(2,1)S(1)} %get-tuple-element.10), channel_id=1, source_target_pairs={{0,8},{1,9},{2,10},{3,11},{4,12},{5,13},{6,14},{7,15},{8,0},{9,1},... | collective-permute-start | bytes 12296 | tf_op jit(solution)/shard_map/ppermute | solution.py:19
  55.2 3.7 %collective-permute-start.11 = (bf16[2,8,128]{2,1,0:T(8,128)(2,1)S(1)}, bf16[2,8,128]{2,1,0:T(8,128)(2,1)S(1)}, u32[]{:S(2)}, u32[]{:S(2)}) collective-permute-start(bf16[2,8,128]{2,1,0:T(8,128)(2,1)S(1)} %get-tuple-element.16), channel_id=1, source_target_pairs={{0,4},{1,5},{2,6},{3,7},{4,0},{5,1},{6,2},{7,3},{8,12},{9,13},{10,... | collective-permute-start | bytes 12296 | tf_op jit(solution)/shard_map/ppermute | solution.py:19
  58.9 1.2 %collective-permute-start.12 = (bf16[1,4,8,128]{3,2,1,0:T(8,128)(2,1)S(1)}, bf16[1,4,8,128]{3,2,1,0:T(8,128)(2,1)S(1)}, u32[]{:S(2)}, u32[]{:S(2)}) collective-permute-start(bf16[1,4,8,128]{3,2,1,0:T(8,128)(2,1)S(1)} %bitcast.205), channel_id=1, source_target_pairs={{0,1},{1,0},{2,3},{3,2},{4,5},{5,4},{6,7},{7,6},{8,9},{9,8},{10,11... | collective-permute-start | bytes 24584 | tf_op jit(solution)/shard_map/ppermute | solution.py:19
  60.1 3.7 %collective-permute-start.13 = (bf16[2,4,8,128]{3,2,1,0:T(8,128)(2,1)S(1)}, bf16[2,4,8,128]{3,2,1,0:T(8,128)(2,1)S(1)}, u32[]{:S(2)}, u32[]{:S(2)}) collective-permute-start(bf16[2,4,8,128]{3,2,1,0:T(8,128)(2,1)S(1)} %maximum_select_fusion.6), channel_id=1, source_target_pairs={{0,2},{1,3},{2,0},{3,1},{4,6},{5,7},{6,4},{7,5},{8,10},{9,11},{10,... | collective-permute-start | bytes 49160 | tf_op jit(solution)/shard_map/ppermute | solution.py:19
  69.9 4.0 %collective-permute-start.14 = (f32[2,8,512]{2,1,0:T(8,128)S(1)}, f32[2,8,512]{2,1,0:T(8,128)S(1)}, u32[]{:S(2)}, u32[]{:S(2)}) collective-permute-start(f32[2,8,512]{2,1,0:T(8,128)S(1)} %select_bitcast_fusion.4), channel_id=1, source_target_pairs={{0,4},{1,5},{2,6},{3,7},{4,0},{5,1},{6,2},{7,3},{8,12},{9,13},{10,... | collective-permute-start | bytes 98312 | tf_op jit(solution)/shard_map/ppermute | solution.py:19
  73.9 4.7 %collective-permute-start.15 = (f32[8,512]{1,0:T(8,128)S(1)}, f32[8,512]{1,0:T(8,128)S(1)}, u32[]{:S(2)}, u32[]{:S(2)}) collective-permute-start(f32[8,512]{1,0:T(8,128)S(1)} %select_bitcast_fusion.6), channel_id=1, source_target_pairs={{0,8},{1,9},{2,10},{3,11},{4,12},{5,13},{6,14},{7,15},{8,0},{9,1},... | collective-permute-start | bytes 49160 | tf_op jit(solution)/shard_map/ppermute | solution.py:19
  78.6 7.7 %collective-permute-start.16 = (bf16[8,512]{1,0:T(8,128)(2,1)S(1)}, bf16[8,512]{1,0:T(8,128)(2,1)S(1)}, u32[]{:S(2)}, u32[]{:S(2)}) collective-permute-start(bf16[8,512]{1,0:T(8,128)(2,1)S(1)} %fusion.39), channel_id=1, source_target_pairs={{0,0},{1,4},{2,8},{3,12},{4,1},{5,5},{6,9},{7,13},{8,2},{9,6},{10,... | collective-permute-start | bytes 24584 | tf_op jit(solution)/shard_map/ppermute | solution.py:241

commit v4 on v3

--- a/solution.py
+++ b/solution.py
@@ -228,17 +228,13 @@
     chosen = jax.vmap(lambda per_group: pick(per_group, rank_of_slot))(every_slot)
     out_part = jnp.einsum("gabe,cae->gbc", chosen, o_blocks[0], preferred_element_type=jnp.float32)
     if group_count == 1 and grid_cols == GR and col_width == GR * DS:
-        col_bits = grid_cols.bit_length() - 1
-        row_bits = GR.bit_length() - 1
-        pieces = out_part[0].reshape(ROWS, GR, DS).transpose(1, 0, 2)
-        held, _ = scatter_rounds(
-            pieces.reshape((2,) * row_bits + (ROWS, DS)),
-            list(range(col_bits + row_bits - 1, col_bits - 1, -1)),
-            "tp",
-            range(col_bits, col_bits + row_bits),
-        )
-        pairs = [(i * grid_cols + j, j * grid_cols + i) for i in range(GR) for j in range(grid_cols)]
-        my_cols = lax.ppermute(held.astype(jnp.bfloat16), "tp", pairs)
+        pieces = out_part[0].reshape(ROWS, GR, DS)
+        my_cols = None
+        for s in range(GR):
+            piece = lax.dynamic_index_in_dim(pieces, grid_row ^ s, 1, keepdims=False)
+            pairs = [(i * grid_cols + j, j * grid_cols + (i ^ s)) for i in range(GR) for j in range(grid_cols)]
+            got = lax.ppermute(piece, "tp", pairs)
+            my_cols = got if my_cols is None else my_cols + got
     else:
         placed = jnp.zeros((group_count, ROWS, D), jnp.float32)
         placed = lax.dynamic_update_slice_in_dim(placed, out_part, grid_col * col_width, 2)

time: 87.2 us -> 84.3 us (0.967)
  the two profiles are of different devices: /device:TPU:24 before, /device:TPU:1 now
where the time goes in v4:
time: 84.3 us; the launch traced here: 82.7 us
  starting transfers between devices  36.9 us (44%)
  waiting for transfers between devices  19.4 us (23%)
  matrix products  18.5 us (22%)
  other arithmetic  4.71 us (6%)
  local copies, waits for them, and re-layouts  2.96 us (4%)
    ppermute x14, starting transfers between devices, from_partner(): return lax.ppermute(value, axis, pairs)  27.6 us
    ppermute x14, waiting for transfers between devices, from_partner(): return lax.ppermute(value, axis, pairs)  15.3 us
    ppermute x4, starting transfers between devices, local(): got = lax.ppermute(piece, 'tp', pairs)  9.24 us
    dot_general x1, matrix products, local(): jnp.einsum('rc,aec->rae', col_rows, q_blocks[0], preferred_element_type=j...  5.65 us
    dot_general x1, matrix products, local(): jnp.einsum('gabe,cae->gbc', chosen, o_blocks[0], preferred_element_type=j...  5.65 us
    ppermute x4, waiting for transfers between devices, local(): got = lax.ppermute(piece, 'tp', pairs)  4.17 us
    dot_general x1, matrix products, local(): jnp.einsum('bhe,bte->bht', both_queries, key_cache[0], preferred_element_...  3.46 us
    dot_general x1, matrix products, local(): jnp.einsum('bht,bte->bhe', weights.astype(jnp.bfloat16), value_cache[0],...  2.93 us
  transfers between devices with their start and end apart: 18, of which 15 were waited for; matrix products, arithmetic and copies ran while one was open for 3% of the time, Pallas kernels for 0%

profile of v4, /device:TPU:1, one launch (start us, length us, event | category | flops | bytes accessed | tf_op | source)
XLA Modules:
  0.0 82.7 jit_solution(341056764785379183)
XLA Ops:
  0.1 1.4 %gather_fusion.1 = s32[16]{0:T(128)S(1)} fusion(s32[16]{0:T(128)} %param.14, s32[1024]{0:T(1024)S(1)} %pad_clamp_fusion), kind=kCustom, calls=%fused_computation.1 | custom fusion | bytes 192 | tf_op jit(solution)/shard_map/gather | solution.py:119
  2.3 2.5 %collective-permute-start.1 = (bf16[2,8,512]{2,1,0:T(8,128)(2,1)S(1)}, bf16[2,8,512]{2,1,0:T(8,128)(2,1)S(1)}, u32[]{:S(2)}, u32[]{:S(2)}) collective-permute-start(bf16[2,8,512]{2,1,0:T(8,128)(2,1)S(1)} %maximum_select_fusion.4), channel_id=1, source_target_pairs={{0,2},{1,3},{2,0},{3,1},{4,6},{5,7},{6,4},{7,5},{8,10},{9,11},{10,... | collective-permute-start | bytes 49160 | tf_op jit(solution)/shard_map/ppermute | solution.py:19
  6.0 1.6 %collective-permute-start.2 = (bf16[4,8,512]{2,1,0:T(8,128)(2,1)S(1)}, bf16[4,8,512]{2,1,0:T(8,128)(2,1)S(1)}, u32[]{:S(2)}, u32[]{:S(2)}) collective-permute-start(bf16[4,8,512]{2,1,0:T(8,128)(2,1)S(1)} %maximum_select_fusion.2), channel_id=1, source_target_pairs={{0,4},{1,5},{2,6},{3,7},{4,0},{5,1},{6,2},{7,3},{8,12},{9,13},{10,... | collective-permute-start | bytes 98312 | tf_op jit(solution)/shard_map/ppermute | solution.py:19
  8.9 2.5 %collective-permute-start.3 = (bf16[8,8,512]{2,1,0:T(8,128)(2,1)S(1)}, bf16[8,8,512]{2,1,0:T(8,128)(2,1)S(1)}, u32[]{:S(2)}, u32[]{:S(2)}) collective-permute-start(bf16[8,8,512]{2,1,0:T(8,128)(2,1)S(1)} %maximum_select_fusion.1), channel_id=1, source_target_pairs={{0,8},{1,9},{2,10},{3,11},{4,12},{5,13},{6,14},{7,15},{8,0},{9,1},... | collective-permute-start | bytes 196616 | tf_op jit(solution)/shard_map/ppermute | solution.py:19
  11.5 1.6 %collective-permute-done.3 = bf16[8,8,512]{2,1,0:T(8,128)(2,1)S(1)} collective-permute-done((bf16[8,8,512]{2,1,0:T(8,128)(2,1)S(1)}, bf16[8,8,512]{2,1,0:T(8,128)(2,1)S(1)}, u32[]{:S(2)}, u32[]{:S(2)}) %collective-permute-start.3) | collective-permute-done | bytes 65568 | tf_op jit(solution)/shard_map/ppermute | solution.py:19
  14.9 5.7 %fusion.14 = f32[16,8,128]{2,1,0:T(8,128)S(1)} fusion(bf16[1,16,128,2048]{3,2,1,0:T(8,128)(2,1)} %param.11, bf16[8,8192]{1,0:T(8,128)(2,1)S(1)} %multiply_convert_fusion, s32[]{:T(128)S(6)} %select_n.472), kind=kOutput, calls=%fused_computation.12 | convolution fusion | flops 67108864 | bytes 8486916 | tf_op jit(solution)/shard_map/rc,aec->rae/dot_general | solution.py:131
  21.1 3.4 %collective-permute-start.4 = (f32[2,2,2,8,384]{4,3,2,1,0:T(8,128)S(1)}, f32[2,2,2,8,384]{4,3,2,1,0:T(8,128)S(1)}, u32[]{:S(2)}, u32[]{:S(2)}) collective-permute-start(f32[2,2,2,8,384]{4,3,2,1,0:T(8,128)S(1)} %select_bitcast_fusion.1), channel_id=1, source_target_pairs={{0,1},{1,0},{2,3},{3,2},{4,5},{5,4},{6,7},{7,6},{8,9},{9,8},{10,11... | collective-permute-start | bytes 294920 | tf_op jit(solution)/shard_map/ppermute | solution.py:19
  25.5 1.6 %collective-permute-start.5 = (f32[2,2,8,384]{3,2,1,0:T(8,128)S(1)}, f32[2,2,8,384]{3,2,1,0:T(8,128)S(1)}, u32[]{:S(2)}, u32[]{:S(2)}) collective-permute-start(f32[2,2,8,384]{3,2,1,0:T(8,128)S(1)} %select_bitcast_fusion.3), channel_id=1, source_target_pairs={{0,2},{1,3},{2,0},{3,1},{4,6},{5,7},{6,4},{7,5},{8,10},{9,11},{10,... | collective-permute-start | bytes 147464 | tf_op jit(solution)/shard_map/ppermute | solution.py:19
  27.2 1.4 %collective-permute-done.5 = f32[2,2,8,384]{3,2,1,0:T(8,128)S(1)} collective-permute-done((f32[2,2,8,384]{3,2,1,0:T(8,128)S(1)}, f32[2,2,8,384]{3,2,1,0:T(8,128)S(1)}, u32[]{:S(2)}, u32[]{:S(2)}) %collective-permute-start.5) | collective-permute-done | bytes 49184 | tf_op jit(solution)/shard_map/ppermute | solution.py:19
  28.6 1.6 %collective-permute-start.6 = (f32[2,8,768]{2,1,0:T(8,128)S(1)}, f32[2,8,768]{2,1,0:T(8,128)S(1)}, u32[]{:S(2)}, u32[]{:S(2)}) collective-permute-start(f32[2,8,768]{2,1,0:T(8,128)S(1)} %select_bitcast_fusion.2), channel_id=1, source_target_pairs={{0,4},{1,5},{2,6},{3,7},{4,0},{5,1},{6,2},{7,3},{8,12},{9,13},{10,... | collective-permute-start | bytes 147464 | tf_op jit(solution)/shard_map/ppermute | solution.py:19
  30.2 1.5 %collective-permute-done.6 = f32[2,8,768]{2,1,0:T(8,128)S(1)} collective-permute-done((f32[2,8,768]{2,1,0:T(8,128)S(1)}, f32[2,8,768]{2,1,0:T(8,128)S(1)}, u32[]{:S(2)}, u32[]{:S(2)}) %collective-permute-start.6) | collective-permute-done | bytes 49184 | tf_op jit(solution)/shard_map/ppermute | solution.py:19
  31.8 3.0 %collective-permute-start.7 = (f32[8,768]{1,0:T(8,128)S(1)}, f32[8,768]{1,0:T(8,128)S(1)}, u32[]{:S(2)}, u32[]{:S(2)}) collective-permute-start(f32[8,768]{1,0:T(8,128)S(1)} %select_bitcast_fusion.4), channel_id=1, source_target_pairs={{0,8},{1,9},{2,10},{3,11},{4,12},{5,13},{6,14},{7,15},{8,0},{9,1},... | collective-permute-start | bytes 73736 | tf_op jit(solution)/shard_map/ppermute | solution.py:19
  36.0 3.3 %collective-permute-start.8 = (bf16[8,512]{1,0:T(8,128)(2,1)S(1)}, bf16[8,512]{1,0:T(8,128)(2,1)S(1)}, u32[]{:S(2)}, u32[]{:S(2)}) collective-permute-start(bf16[8,512]{1,0:T(8,128)(2,1)S(1)} %slice.135), channel_id=1, source_target_pairs={{0,1},{1,0},{2,3},{3,2},{4,5},{5,4},{6,7},{7,6},{8,9},{9,8},{10,11... | collective-permute-start | bytes 24584 | tf_op jit(solution)/shard_map/ppermute | solution.py:19
  40.2 3.5 %select_reduce_fusion.3 = (f32[8,8]{1,0:T(8,128)S(1)}, f32[8,8,2048]{2,1,0:T(8,128)S(1)}) fusion(pred[8,2048]{1,0:T(8,128)(4,1)S(1)} %iota_compare_fusion, bf16[1,8,2048,128]{3,2,1,0:T(8,128)(2,1)} %param.15, bf16[8,4,128]{2,1,0:T(4,128)(2,1)S(1)} %concatenate.106, bf16[8,4,128]{2,1,0:T(4,128)(2,1)S(1)} %concatenate.105, pred[]{:T(512)S(6)} %eq.112), kind=kOutput, calls=%fused_computation.19 | convolution fusion | flops 34021312 | bytes 4751617 | tf_op jit(solution)/shard_map/bhe,bte->bht/dot_general | solution.py:173
  44.1 2.9 %fusion.17 = f32[8,8,128]{2,1,0:T(8,128)S(1)} fusion(bf16[1,8,2048,128]{3,2,1,0:T(8,128)(2,1)} %param.16, f32[8,8,2048]{2,1,0:T(8,128)S(1)} %get-tuple-element.26, f32[8,8]{1,0:T(8,128)S(1)} %fusion.47, pred[8,2048]{1,0:T(8,128)(4,1)S(1)} %iota_compare_fusion, f32[8,128]{1,0:T(8,128)S(1)} %get-tuple-element.17, f32[8,8]{1,0:T(8,128)S(1)} %convert_element_type.46), kind=kOutput, calls=%fused_computation.14 | convolution fusion | flops 33964032 | bytes 4772352 | tf_op jit(solution)/shard_map/bht,bte->bhe/dot_general | solution.py:186
  49.5 2.7 %collective-permute-start.10 = (bf16[2,8,128]{1,0,2:T(2,128)(2,1)S(1)}, bf16[2,8,128]{1,0,2:T(2,128)(2,1)S(1)}, u32[]{:S(2)}, u32[]{:S(2)}) collective-permute-start(bf16[2,8,128]{1,0,2:T(2,128)(2,1)S(1)} %get-tuple-element.10), channel_id=1, source_target_pairs={{0,8},{1,9},{2,10},{3,11},{4,12},{5,13},{6,14},{7,15},{8,0},{9,1},... | collective-permute-start | bytes 12296 | tf_op jit(solution)/shard_map/ppermute | solution.py:19
  52.4 2.0 %collective-permute-done.10 = bf16[2,8,128]{1,0,2:T(2,128)(2,1)S(1)} collective-permute-done((bf16[2,8,128]{1,0,2:T(2,128)(2,1)S(1)}, bf16[2,8,128]{1,0,2:T(2,128)(2,1)S(1)}, u32[]{:S(2)}, u32[]{:S(2)}) %collective-permute-start.10) | collective-permute-done | bytes 4128 | tf_op jit(solution)/shard_map/ppermute | solution.py:19
  54.5 2.3 %collective-permute-start.11 = (bf16[2,8,128]{2,1,0:T(8,128)(2,1)S(1)}, bf16[2,8,128]{2,1,0:T(8,128)(2,1)S(1)}, u32[]{:S(2)}, u32[]{:S(2)}) collective-permute-start(bf16[2,8,128]{2,1,0:T(8,128)(2,1)S(1)} %get-tuple-element.20), channel_id=1, source_target_pairs={{0,4},{1,5},{2,6},{3,7},{4,0},{5,1},{6,2},{7,3},{8,12},{9,13},{10,... | collective-permute-start | bytes 12296 | tf_op jit(solution)/shard_map/ppermute | solution.py:19
  57.8 1.4 %collective-permute-start.12 = (bf16[1,4,8,128]{3,2,1,0:T(8,128)(2,1)S(1)}, bf16[1,4,8,128]{3,2,1,0:T(8,128)(2,1)S(1)}, u32[]{:S(2)}, u32[]{:S(2)}) collective-permute-start(bf16[1,4,8,128]{3,2,1,0:T(8,128)(2,1)S(1)} %bitcast.187), channel_id=1, source_target_pairs={{0,1},{1,0},{2,3},{3,2},{4,5},{5,4},{6,7},{7,6},{8,9},{9,8},{10,11... | collective-permute-start | bytes 24584 | tf_op jit(solution)/shard_map/ppermute | solution.py:19
  61.3 1.3 %collective-permute-done.13 = bf16[2,4,8,128]{3,2,1,0:T(8,128)(2,1)S(1)} collective-permute-done((bf16[2,4,8,128]{3,2,1,0:T(8,128)(2,1)S(1)}, bf16[2,4,8,128]{3,2,1,0:T(8,128)(2,1)S(1)}, u32[]{:S(2)}, u32[]{:S(2)}) %collective-permute-start.13) | collective-permute-done | bytes 16416 | tf_op jit(solution)/shard_map/ppermute | solution.py:19
  63.0 5.6 %fusion.11 = f32[8,4,512]{2,0,1:T(8,128)S(1)} fusion(bf16[4,512,16,128]{3,2,1,0:T(8,128)(2,1)} %bitcast.171, bf16[16,8,128]{2,1,0:T(8,128)(2,1)S(1)} %select_reduce_fusion.2), kind=kOutput, calls=%fused_computation.11 | convolution fusion | flops 67108864 | bytes 8486912 | tf_op jit(solution)/shard_map/gabe,cae->gbc/dot_general | solution.py:229
  68.7 5.0 %collective-permute-start.14 = (f32[8,512]{1,0:T(8,128)S(1)}, f32[8,512]{1,0:T(8,128)S(1)}, u32[]{:S(2)}, u32[]{:S(2)}) collective-permute-start(f32[8,512]{1,0:T(8,128)S(1)} %get-tuple-element.14), channel_id=1, source_target_pairs={{0,0},{1,4},{2,8},{3,12},{4,1},{5,5},{6,9},{7,13},{8,2},{9,6},{10,... | collective-permute-start | bytes 49160 | tf_op jit(solution)/shard_map/ppermute | solution.py:236
  73.8 3.3 %collective-permute-start.16 = (f32[8,512]{1,0:T(8,128)S(1)}, f32[8,512]{1,0:T(8,128)S(1)}, u32[]{:S(2)}, u32[]{:S(2)}) collective-permute-start(f32[8,512]{1,0:T(8,128)S(1)} %get-tuple-element.13), channel_id=1, source_target_pairs={{0,2},{1,6},{2,10},{3,14},{4,3},{5,7},{6,11},{7,15},{8,0},{9,4},{1... | collective-permute-start | bytes 49160 | tf_op jit(solution)/shard_map/ppermute | solution.py:236
  77.9 3.5 %collective-permute-done.16 = f32[8,512]{1,0:T(8,128)S(1)} collective-permute-done((f32[8,512]{1,0:T(8,128)S(1)}, f32[8,512]{1,0:T(8,128)S(1)}, u32[]{:S(2)}, u32[]{:S(2)}) %collective-permute-start.16) | collective-permute-done | bytes 16416 | tf_op jit(solution)/shard_map/ppermute | solution.py:236
  (92 shorter events, 17.7 us)
Async XLA Ops:
  0.0 14.2 %copy-start = (bf16[2,1024,512]{2,1,0:T(8,128)(2,1)S(1)}, bf16[2,1024,512]{2,1,0:T(8,128)(2,1)}, u32[]{:S(2)}) copy-start(bf16[2,1024,512]{2,1,0:T(8,128)(2,1)} %param.13) | copy-start | bytes 6291460
  0.0 1.5 %collective-permute-start = (bf16[1,8,512]{2,1,0:T(8,128)(2,1)}, bf16[1,8,512]{2,1,0:T(8,128)(2,1)S(1)}, u32[]{:S(2)}, u32[]{:S(2)}) collective-permute-start(bf16[1,8,512]{2,1,0:T(8,128)(2,1)} %param.9), channel_id=1, source_target_pairs={{0,1},{1,0},{2,3},{3,2},{4,5},{5,4},{6,7},{7,6},{8,9},{9,8},{10,11... | collective-permute-start | bytes 24584 | tf_op jit(solution)/shard_map/ppermute | solution.py:19
  2.3 3.7 %collective-permute-start.1 = (bf16[2,8,512]{2,1,0:T(8,128)(2,1)S(1)}, bf16[2,8,512]{2,1,0:T(8,128)(2,1)S(1)}, u32[]{:S(2)}, u32[]{:S(2)}) collective-permute-start(bf16[2,8,512]{2,1,0:T(8,128)(2,1)S(1)} %maximum_select_fusion.4), channel_id=1, source_target_pairs={{0,2},{1,3},{2,0},{3,1},{4,6},{5,7},{6,4},{7,5},{8,10},{9,11},{10,... | collective-permute-start | bytes 49160 | tf_op jit(solution)/shard_map/ppermute | solution.py:19
  6.0 2.9 %collective-permute-start.2 = (bf16[4,8,512]{2,1,0:T(8,128)(2,1)S(1)}, bf16[4,8,512]{2,1,0:T(8,128)(2,1)S(1)}, u32[]{:S(2)}, u32[]{:S(2)}) collective-permute-start(bf16[4,8,512]{2,1,0:T(8,128)(2,1)S(1)} %maximum_select_fusion.2), channel_id=1, source_target_pairs={{0,4},{1,5},{2,6},{3,7},{4,0},{5,1},{6,2},{7,3},{8,12},{9,13},{10,... | collective-permute-start | bytes 98312 | tf_op jit(solution)/shard_map/ppermute | solution.py:19
  8.9 4.2 %collective-permute-start.3 = (bf16[8,8,512]{2,1,0:T(8,128)(2,1)S(1)}, bf16[8,8,512]{2,1,0:T(8,128)(2,1)S(1)}, u32[]{:S(2)}, u32[]{:S(2)}) collective-permute-start(bf16[8,8,512]{2,1,0:T(8,128)(2,1)S(1)} %maximum_select_fusion.1), channel_id=1, source_target_pairs={{0,8},{1,9},{2,10},{3,11},{4,12},{5,13},{6,14},{7,15},{8,0},{9,1},... | collective-permute-start | bytes 196616 | tf_op jit(solution)/shard_map/ppermute | solution.py:19
  14.8 19.9 %copy-start.2 = (s32[1,8]{1,0:T(1,128)S(1)}, s32[1,8]{1,0:T(1,128)}, u32[]{:S(2)}) copy-start(s32[1,8]{1,0:T(1,128)} %param.17) | copy-start | bytes 100
  21.1 4.3 %collective-permute-start.4 = (f32[2,2,2,8,384]{4,3,2,1,0:T(8,128)S(1)}, f32[2,2,2,8,384]{4,3,2,1,0:T(8,128)S(1)}, u32[]{:S(2)}, u32[]{:S(2)}) collective-permute-start(f32[2,2,2,8,384]{4,3,2,1,0:T(8,128)S(1)} %select_bitcast_fusion.1), channel_id=1, source_target_pairs={{0,1},{1,0},{2,3},{3,2},{4,5},{5,4},{6,7},{7,6},{8,9},{9,8},{10,11... | collective-permute-start | bytes 294920 | tf_op jit(solution)/shard_map/ppermute | solution.py:19
  25.5 3.1 %collective-permute-start.5 = (f32[2,2,8,384]{3,2,1,0:T(8,128)S(1)}, f32[2,2,8,384]{3,2,1,0:T(8,128)S(1)}, u32[]{:S(2)}, u32[]{:S(2)}) collective-permute-start(f32[2,2,8,384]{3,2,1,0:T(8,128)S(1)} %select_bitcast_fusion.3), channel_id=1, source_target_pairs={{0,2},{1,3},{2,0},{3,1},{4,6},{5,7},{6,4},{7,5},{8,10},{9,11},{10,... | collective-permute-start | bytes 147464 | tf_op jit(solution)/shard_map/ppermute | solution.py:19
  28.6 3.1 %collective-permute-start.6 = (f32[2,8,768]{2,1,0:T(8,128)S(1)}, f32[2,8,768]{2,1,0:T(8,128)S(1)}, u32[]{:S(2)}, u32[]{:S(2)}) collective-permute-start(f32[2,8,768]{2,1,0:T(8,128)S(1)} %select_bitcast_fusion.2), channel_id=1, source_target_pairs={{0,4},{1,5},{2,6},{3,7},{4,0},{5,1},{6,2},{7,3},{8,12},{9,13},{10,... | collective-permute-start | bytes 147464 | tf_op jit(solution)/shard_map/ppermute | solution.py:19
  31.8 4.2 %collective-permute-start.7 = (f32[8,768]{1,0:T(8,128)S(1)}, f32[8,768]{1,0:T(8,128)S(1)}, u32[]{:S(2)}, u32[]{:S(2)}) collective-permute-start(f32[8,768]{1,0:T(8,128)S(1)} %select_bitcast_fusion.4), channel_id=1, source_target_pairs={{0,8},{1,9},{2,10},{3,11},{4,12},{5,13},{6,14},{7,15},{8,0},{9,1},... | collective-permute-start | bytes 73736 | tf_op jit(solution)/shard_map/ppermute | solution.py:19
  36.0 4.1 %collective-permute-start.8 = (bf16[8,512]{1,0:T(8,128)(2,1)S(1)}, bf16[8,512]{1,0:T(8,128)(2,1)S(1)}, u32[]{:S(2)}, u32[]{:S(2)}) collective-permute-start(bf16[8,512]{1,0:T(8,128)(2,1)S(1)} %slice.135), channel_id=1, source_target_pairs={{0,1},{1,0},{2,3},{3,2},{4,5},{5,4},{6,7},{7,6},{8,9},{9,8},{10,11... | collective-permute-start | bytes 24584 | tf_op jit(solution)/shard_map/ppermute | solution.py:19
  43.7 4.3 %copy-start.1 = (s32[16]{0:T(128)S(1)}, s32[16]{0:T(128)}, u32[]{:S(2)}) copy-start(s32[16]{0:T(128)} %param.14) | copy-start | bytes 196
  47.6 1.6 %collective-permute-start.9 = (f32[8,4,130]{0,1,2:T(4,128)S(1)}, f32[8,4,130]{0,1,2:T(4,128)S(1)}, u32[]{:S(2)}, u32[]{:S(2)}) collective-permute-start(f32[8,4,130]{0,1,2:T(4,128)S(1)} %pad_maximum_fusion), channel_id=1, source_target_pairs={{0,1},{1,0},{2,3},{3,2},{4,5},{5,4},{6,7},{7,6},{8,9},{9,8},{10,11... | collective-permute-start | bytes 49928 | tf_op jit(solution)/shard_map/ppermute | solution.py:19
  49.5 4.9 %collective-permute-start.10 = (bf16[2,8,128]{1,0,2:T(2,128)(2,1)S(1)}, bf16[2,8,128]{1,0,2:T(2,128)(2,1)S(1)}, u32[]{:S(2)}, u32[]{:S(2)}) collective-permute-start(bf16[2,8,128]{1,0,2:T(2,128)(2,1)S(1)} %get-tuple-element.10), channel_id=1, source_target_pairs={{0,8},{1,9},{2,10},{3,11},{4,12},{5,13},{6,14},{7,15},{8,0},{9,1},... | collective-permute-start | bytes 12296 | tf_op jit(solution)/shard_map/ppermute | solution.py:19
  54.5 3.3 %collective-permute-start.11 = (bf16[2,8,128]{2,1,0:T(8,128)(2,1)S(1)}, bf16[2,8,128]{2,1,0:T(8,128)(2,1)S(1)}, u32[]{:S(2)}, u32[]{:S(2)}) collective-permute-start(bf16[2,8,128]{2,1,0:T(8,128)(2,1)S(1)} %get-tuple-element.20), channel_id=1, source_target_pairs={{0,4},{1,5},{2,6},{3,7},{4,0},{5,1},{6,2},{7,3},{8,12},{9,13},{10,... | collective-permute-start | bytes 12296 | tf_op jit(solution)/shard_map/ppermute | solution.py:19
  57.8 2.3 %collective-permute-start.12 = (bf16[1,4,8,128]{3,2,1,0:T(8,128)(2,1)S(1)}, bf16[1,4,8,128]{3,2,1,0:T(8,128)(2,1)S(1)}, u32[]{:S(2)}, u32[]{:S(2)}) collective-permute-start(bf16[1,4,8,128]{3,2,1,0:T(8,128)(2,1)S(1)} %bitcast.187), channel_id=1, source_target_pairs={{0,1},{1,0},{2,3},{3,2},{4,5},{5,4},{6,7},{7,6},{8,9},{9,8},{10,11... | collective-permute-start | bytes 24584 | tf_op jit(solution)/shard_map/ppermute | solution.py:19
  60.0 2.6 %collective-permute-start.13 = (bf16[2,4,8,128]{3,2,1,0:T(8,128)(2,1)S(1)}, bf16[2,4,8,128]{3,2,1,0:T(8,128)(2,1)S(1)}, u32[]{:S(2)}, u32[]{:S(2)}) collective-permute-start(bf16[2,4,8,128]{3,2,1,0:T(8,128)(2,1)S(1)} %maximum_select_fusion.6), channel_id=1, source_target_pairs={{0,2},{1,3},{2,0},{3,1},{4,6},{5,7},{6,4},{7,5},{8,10},{9,11},{10,... | collective-permute-start | bytes 49160 | tf_op jit(solution)/shard_map/ppermute | solution.py:19
  68.7 9.3 %collective-permute-start.14 = (f32[8,512]{1,0:T(8,128)S(1)}, f32[8,512]{1,0:T(8,128)S(1)}, u32[]{:S(2)}, u32[]{:S(2)}) collective-permute-start(f32[8,512]{1,0:T(8,128)S(1)} %get-tuple-element.14), channel_id=1, source_target_pairs={{0,0},{1,4},{2,8},{3,12},{4,1},{5,5},{6,9},{7,13},{8,2},{9,6},{10,... | collective-permute-start | bytes 49160 | tf_op jit(solution)/shard_map/ppermute | solution.py:236
  73.7 4.2 %collective-permute-start.15 = (f32[8,512]{1,0:T(8,128)S(1)}, f32[8,512]{1,0:T(8,128)S(1)}, u32[]{:S(2)}, u32[]{:S(2)}) collective-permute-start(f32[8,512]{1,0:T(8,128)S(1)} %get-tuple-element.11), channel_id=1, source_target_pairs={{0,1},{1,5},{2,9},{3,13},{4,0},{5,4},{6,8},{7,12},{8,3},{9,7},{10,... | collective-permute-start | bytes 49160 | tf_op jit(solution)/shard_map/ppermute | solution.py:236
  73.8 7.7 %collective-permute-start.16 = (f32[8,512]{1,0:T(8,128)S(1)}, f32[8,512]{1,0:T(8,128)S(1)}, u32[]{:S(2)}, u32[]{:S(2)}) collective-permute-start(f32[8,512]{1,0:T(8,128)S(1)} %get-tuple-element.13), channel_id=1, source_target_pairs={{0,2},{1,6},{2,10},{3,14},{4,3},{5,7},{6,11},{7,15},{8,0},{9,4},{1... | collective-permute-start | bytes 49160 | tf_op jit(solution)/shard_map/ppermute | solution.py:236
  77.1 5.0 %collective-permute-start.17 = (f32[8,512]{1,0:T(8,128)S(1)}, f32[8,512]{1,0:T(8,128)S(1)}, u32[]{:S(2)}, u32[]{:S(2)}) collective-permute-start(f32[8,512]{1,0:T(8,128)S(1)} %get-tuple-element.12), channel_id=1, source_target_pairs={{0,3},{1,7},{2,11},{3,15},{4,2},{5,6},{6,10},{7,14},{8,1},{9,5},{1... | collective-permute-start | bytes 49160 | tf_op jit(solution)/shard_map/ppermute | solution.py:236

commit v5 on v4

--- a/solution.py
+++ b/solution.py
@@ -94,6 +94,11 @@
         at = count - done - 1 + done
         held = jnp.where(low, jnp.stack([keep, got], at), jnp.stack([got, keep], at))
     return held
+
+
+def swap_rows(value, axis, col_bits, s):
+    shift = s << col_bits
+    return lax.ppermute(value, axis, [(t, t ^ shift) for t in range(lax.axis_size(axis))])
 
 
 def norm_rows(rows_float, norm_gain):
@@ -119,7 +124,13 @@
     dest_head = kv_assign[dest_rank]
     dest_group = 2 * dest_head + dest_rank % 2
     dest_copy = dest_ids // ROLL
-    every_rows = gather_xor(hidden_in, "tp")
+    bits = ranks.bit_length() - 1
+    col_bits = grid_cols.bit_length() - 1
+    row_bits = GR.bit_length() - 1
+    row_order = jnp.arange(GR, dtype=jnp.int32) ^ grid_row
+    in_row = gather_rounds(hidden_in, "tp", range(col_bits))
+    from_rows = [in_row] + [swap_rows(in_row, "tp", col_bits, s) for s in range(1, GR)]
+    every_rows = pick(jnp.stack(from_rows), row_order).reshape(ranks, ROWS, DS)
     rows_float = (
         every_rows.reshape(group_count, ROLL, ROWS, DS)
         .transpose(0, 2, 1, 3)
@@ -145,18 +156,21 @@
         .reshape(group_count * KVH, ROWS, 2 * HD)
     )
     keyval_term = pick(keyval_part, dest_copy * KVH + dest_head)
-    bits = ranks.bit_length() - 1
-    col_bits = grid_cols.bit_length() - 1
     compact = jnp.concatenate([query_pick, keyval_term], -1)
-    held, order = scatter_rounds(
+    held, _ = scatter_rounds(
         compact.reshape((2,) * bits + (ROWS, 3 * HD)), list(range(bits - 1, -1, -1)), "tp", range(col_bits)
     )
-    slot_here = jnp.arange(GR, dtype=jnp.int32) == grid_row
-    query_slots = jnp.where(
-        slot_here[:, None], held[..., None, :HD], jnp.zeros((), jnp.float32)
-    ).reshape(held.shape[:-1] + (GR * HD,))
-    held = jnp.concatenate([query_slots, held[..., HD:]], -1)
-    projected, _ = scatter_rounds(held, order, "tp", range(col_bits, bits))
+    held = held.reshape(GR, ROWS, 3 * HD)
+    from_rows = [lax.dynamic_index_in_dim(held, grid_row, 0, keepdims=False)]
+    for s in range(1, GR):
+        piece = lax.dynamic_index_in_dim(held, grid_row ^ s, 0, keepdims=False)
+        from_rows.append(swap_rows(piece, "tp", col_bits, s))
+    query_slots = pick(jnp.stack([got[:, :HD] for got in from_rows]), row_order)
+    query_slots = query_slots.transpose(1, 0, 2).reshape(ROWS, GR * HD)
+    keyval_sum = from_rows[0][:, HD:]
+    for got in from_rows[1:]:
+        keyval_sum = keyval_sum + got[:, HD:]
+    projected = jnp.concatenate([query_slots, keyval_sum], -1)
     queries = projected[:, : GR * HD].astype(jnp.bfloat16)
     keyval_new = projected[:, GR * HD :].astype(jnp.bfloat16)
     key_new = keyval_new[:, :HD]
@@ -210,12 +224,11 @@
     numer = own_summed * factor_own[..., None] + got_summed * factor_got[..., None]
     denom = own_total * factor_own + got_total * factor_got
     attention = (numer / denom[..., None]).astype(jnp.bfloat16)
-    bits = ranks.bit_length() - 1
-    col_bits = grid_cols.bit_length() - 1
-    row_bits = GR.bit_length() - 1
-    by_row = attention.transpose(1, 0, 2).reshape((2,) * row_bits + (ROWS, HD))
-    by_row = exchange_rounds(by_row, "tp", list(range(bits - 1, col_bits - 1, -1)))
-    by_row = by_row.reshape(GR, ROWS, HD)
+    from_rows = [lax.dynamic_index_in_dim(attention, grid_row, 1, keepdims=False)]
+    for s in range(1, GR):
+        piece = lax.dynamic_index_in_dim(attention, grid_row ^ s, 1, keepdims=False)
+        from_rows.append(swap_rows(piece, "tp", col_bits, s))
+    by_row = pick(jnp.stack(from_rows), row_order)
     every_slot = gather_rounds(by_row[None], "tp", range(col_bits))
     every_slot = every_slot.transpose(1, 0, 2, 3).reshape(group_count, ROLL, ROWS, HD)
     head_ids = jnp.arange(KVH, dtype=jnp.int32)

time: 84.3 us -> 80.2 us (0.951); the launches traced: 82.7 us -> 79.8 us
  starting transfers between devices: 36.9 us -> 33.5 us
  other arithmetic: 4.71 us -> 5.68 us
  waiting for transfers between devices: 19.4 us -> 18.5 us
    ppermute x14 -> x8, starting transfers between devices: 27.6 us -> 13.7 us  [from_partner(): return lax.ppermute(value, axis, pairs)]
    ppermute x0 -> x9, starting transfers between devices: none -> 11.4 us  [swap_rows(): lax.ppermute(value, axis, [(t, t ^ shift) for t in range(lax.axis_size(ax...]
    ppermute x14 -> x8, waiting for transfers between devices: 15.3 us -> 6.81 us  [from_partner(): return lax.ppermute(value, axis, pairs)]
    ppermute x0 -> x9, waiting for transfers between devices: none -> 7.64 us  [swap_rows(): lax.ppermute(value, axis, [(t, t ^ shift) for t in range(lax.axis_size(ax...]
    ppermute x4, starting transfers between devices: 9.24 us -> 8.38 us  [local(): got = lax.ppermute(piece, 'tp', pairs)]
  transfers between devices with their start and end apart: 18 -> 21, of which waited for: 15 -> 15; matrix products, arithmetic and copies ran while one was open for 3% -> 5% of each run, Pallas kernels for 0% -> 0%
where the time goes in v5:
time: 80.2 us; the launch traced here: 79.8 us
  starting transfers between devices  33.5 us (42%)
  waiting for transfers between devices  18.5 us (23%)
  matrix products  18.4 us (23%)
  other arithmetic  5.68 us (7%)
  local copies, waits for them, and re-layouts  3.3 us (4%)
    ppermute x8, starting transfers between devices, from_partner(): return lax.ppermute(value, axis, pairs)  13.7 us
    ppermute x9, starting transfers between devices, swap_rows(): lax.ppermute(value, axis, [(t, t ^ shift) for t in range(lax.axis_size(ax...  11.4 us
    ppermute x4, starting transfers between devices, local(): got = lax.ppermute(piece, 'tp', pairs)  8.38 us
    ppermute x9, waiting for transfers between devices, swap_rows(): lax.ppermute(value, axis, [(t, t ^ shift) for t in range(lax.axis_size(ax...  7.64 us
    ppermute x8, waiting for transfers between devices, from_partner(): return lax.ppermute(value, axis, pairs)  6.81 us
    dot_general x1, matrix products, local(): jnp.einsum('rc,aec->rae', col_rows, q_blocks[0], preferred_element_type=j...  5.65 us
    dot_general x1, matrix products, local(): jnp.einsum('gabe,cae->gbc', chosen, o_blocks[0], preferred_element_type=j...  5.65 us
    ppermute x4, waiting for transfers between devices, local(): got = lax.ppermute(piece, 'tp', pairs)  4.06 us
  transfers between devices with their start and end apart: 21, of which 15 were waited for; matrix products, arithmetic and copies ran while one was open for 5% of the time, Pallas kernels for 0%

profile of v5, /device:TPU:1, one launch (start us, length us, event | category | flops | bytes accessed | tf_op | source)
XLA Modules:
  0.0 79.8 jit_solution(7924854314543923071)
XLA Ops:
  0.1 1.4 %gather_fusion.1 = s32[16]{0:T(128)S(1)} fusion(s32[16]{0:T(128)} %param.14, s32[1024]{0:T(1024)S(1)} %pad_clamp_fusion), kind=kCustom, calls=%fused_computation.1 | custom fusion | bytes 192 | tf_op jit(solution)/shard_map/gather | solution.py:124
  2.6 2.5 %collective-permute-start.1 = (bf16[2,8,512]{2,1,0:T(8,128)(2,1)S(1)}, bf16[2,8,512]{2,1,0:T(8,128)(2,1)S(1)}, u32[]{:S(2)}, u32[]{:S(2)}) collective-permute-start(bf16[2,8,512]{2,1,0:T(8,128)(2,1)S(1)} %maximum_select_fusion.3), channel_id=1, source_target_pairs={{0,2},{1,3},{2,0},{3,1},{4,6},{5,7},{6,4},{7,5},{8,10},{9,11},{10,... | collective-permute-start | bytes 49160 | tf_op jit(solution)/shard_map/ppermute | solution.py:19
  6.2 1.6 %collective-permute-start.2 = (bf16[4,8,512]{2,1,0:T(8,128)(2,1)S(1)}, bf16[4,8,512]{2,1,0:T(8,128)(2,1)S(1)}, u32[]{:S(2)}, u32[]{:S(2)}) collective-permute-start(bf16[4,8,512]{2,1,0:T(8,128)(2,1)S(1)} %maximum_select_fusion.1), channel_id=1, source_target_pairs={{0,4},{1,5},{2,6},{3,7},{4,0},{5,1},{6,2},{7,3},{8,12},{9,13},{10,... | collective-permute-start | bytes 98312 | tf_op jit(solution)/shard_map/ppermute | solution.py:101
  7.8 2.3 %collective-permute-start.3 = (bf16[4,8,512]{2,1,0:T(8,128)(2,1)S(1)}, bf16[4,8,512]{2,1,0:T(8,128)(2,1)S(1)}, u32[]{:S(2)}, u32[]{:S(2)}) collective-permute-start(bf16[4,8,512]{2,1,0:T(8,128)(2,1)S(1)} %maximum_select_fusion.1), channel_id=1, source_target_pairs={{0,8},{1,9},{2,10},{3,11},{4,12},{5,13},{6,14},{7,15},{8,0},{9,1},... | collective-permute-start | bytes 98312 | tf_op jit(solution)/shard_map/ppermute | solution.py:101
  10.2 1.7 %collective-permute-done.3 = bf16[4,8,512]{2,1,0:T(8,128)(2,1)S(1)} collective-permute-done((bf16[4,8,512]{2,1,0:T(8,128)(2,1)S(1)}, bf16[4,8,512]{2,1,0:T(8,128)(2,1)S(1)}, u32[]{:S(2)}, u32[]{:S(2)}) %collective-permute-start.3) | collective-permute-done | bytes 32800 | tf_op jit(solution)/shard_map/ppermute | solution.py:101
  11.8 2.9 %collective-permute-done.4 = bf16[4,8,512]{2,1,0:T(8,128)(2,1)S(1)} collective-permute-done((bf16[4,8,512]{2,1,0:T(8,128)(2,1)S(1)}, bf16[4,8,512]{2,1,0:T(8,128)(2,1)S(1)}, u32[]{:S(2)}, u32[]{:S(2)}) %collective-permute-start.4) | collective-permute-done | bytes 32800 | tf_op jit(solution)/shard_map/ppermute | solution.py:101
  16.6 5.7 %fusion.14 = f32[16,8,128]{2,1,0:T(8,128)S(1)} fusion(bf16[1,16,128,2048]{3,2,1,0:T(8,128)(2,1)} %param.11, bf16[8,8192]{1,0:T(8,128)(2,1)S(1)} %multiply_convert_fusion, s32[]{:T(128)S(6)} %select_n.375), kind=kOutput, calls=%fused_computation.12 | convolution fusion | flops 67108864 | bytes 8486916 | tf_op jit(solution)/shard_map/rc,aec->rae/dot_general | solution.py:142
  22.9 3.1 %collective-permute-start.5 = (f32[2,2,2,8,384]{4,3,2,1,0:T(8,128)S(1)}, f32[2,2,2,8,384]{4,3,2,1,0:T(8,128)S(1)}, u32[]{:S(2)}, u32[]{:S(2)}) collective-permute-start(f32[2,2,2,8,384]{4,3,2,1,0:T(8,128)S(1)} %select_bitcast_fusion.1), channel_id=1, source_target_pairs={{0,1},{1,0},{2,3},{3,2},{4,5},{5,4},{6,7},{7,6},{8,9},{9,8},{10,11... | collective-permute-start | bytes 294920 | tf_op jit(solution)/shard_map/ppermute | solution.py:19
  27.0 1.3 %collective-permute-start.6 = (f32[2,2,8,384]{3,2,1,0:T(8,128)S(1)}, f32[2,2,8,384]{3,2,1,0:T(8,128)S(1)}, u32[]{:S(2)}, u32[]{:S(2)}) collective-permute-start(f32[2,2,8,384]{3,2,1,0:T(8,128)S(1)} %select_bitcast_fusion.2), channel_id=1, source_target_pairs={{0,2},{1,3},{2,0},{3,1},{4,6},{5,7},{6,4},{7,5},{8,10},{9,11},{10,... | collective-permute-start | bytes 147464 | tf_op jit(solution)/shard_map/ppermute | solution.py:19
  28.5 1.5 %collective-permute-done.6 = f32[2,2,8,384]{3,2,1,0:T(8,128)S(1)} collective-permute-done((f32[2,2,8,384]{3,2,1,0:T(8,128)S(1)}, f32[2,2,8,384]{3,2,1,0:T(8,128)S(1)}, u32[]{:S(2)}, u32[]{:S(2)}) %collective-permute-start.6) | collective-permute-done | bytes 49184 | tf_op jit(solution)/shard_map/ppermute | solution.py:19
  30.2 3.5 %collective-permute-start.7 = (f32[8,384]{1,0:T(8,128)S(1)}, f32[8,384]{1,0:T(8,128)S(1)}, u32[]{:S(2)}, u32[]{:S(2)}) collective-permute-start(f32[8,384]{1,0:T(8,128)S(1)} %get-tuple-element.20), channel_id=1, source_target_pairs={{0,4},{1,5},{2,6},{3,7},{4,0},{5,1},{6,2},{7,3},{8,12},{9,13},{10,... | collective-permute-start | bytes 36872 | tf_op jit(solution)/shard_map/ppermute | solution.py:101
  34.8 3.0 %collective-permute-start.10 = (bf16[8,512]{1,0:T(8,128)(2,1)S(1)}, bf16[8,512]{1,0:T(8,128)(2,1)S(1)}, u32[]{:S(2)}, u32[]{:S(2)}) collective-permute-start(bf16[8,512]{1,0:T(8,128)(2,1)S(1)} %bitcast.196), channel_id=1, source_target_pairs={{0,1},{1,0},{2,3},{3,2},{4,5},{5,4},{6,7},{7,6},{8,9},{9,8},{10,11... | collective-permute-start | bytes 24584 | tf_op jit(solution)/shard_map/ppermute | solution.py:19
  38.8 3.5 %select_reduce_fusion.3 = (f32[8,8]{1,0:T(8,128)S(1)}, f32[8,8,2048]{2,1,0:T(8,128)S(1)}) fusion(pred[8,2048]{1,0:T(8,128)(4,1)S(1)} %iota_compare_fusion, bf16[1,8,2048,128]{3,2,1,0:T(8,128)(2,1)} %param.15, bf16[8,8,128]{2,0,1:T(8,128)(2,1)S(1)} %maximum_select_fusion.4), kind=kOutput, calls=%fused_computation.19 | convolution fusion | flops 33947584 | bytes 4751616 | tf_op jit(solution)/shard_map/bhe,bte->bht/dot_general | solution.py:187
  42.6 2.9 %fusion.17 = f32[8,8,128]{2,1,0:T(8,128)S(1)} fusion(bf16[1,8,2048,128]{3,2,1,0:T(8,128)(2,1)} %param.16, f32[8,8,2048]{2,1,0:T(8,128)S(1)} %get-tuple-element.30, f32[8,8]{1,0:T(8,128)S(1)} %fusion.45, pred[8,2048]{1,0:T(8,128)(4,1)S(1)} %iota_compare_fusion, f32[8,128]{1,0:T(8,128)S(1)} %get-tuple-element.25, f32[8,8]{1,0:T(8,128)S(1)} %convert_element_type.71), kind=kOutput, calls=%fused_computation.14 | convolution fusion | flops 33964032 | bytes 4772352 | tf_op jit(solution)/shard_map/bht,bte->bhe/dot_general | solution.py:200
  48.2 1.8 %collective-permute-start.12 = (bf16[8,128]{1,0:T(8,128)(2,1)S(1)}, bf16[8,128]{1,0:T(8,128)(2,1)S(1)}, u32[]{:S(2)}, u32[]{:S(2)}) collective-permute-start(bf16[8,128]{1,0:T(8,128)(2,1)S(1)} %bitcast.207), channel_id=1, source_target_pairs={{0,4},{1,5},{2,6},{3,7},{4,0},{5,1},{6,2},{7,3},{8,12},{9,13},{10,... | collective-permute-start | bytes 6152 | tf_op jit(solution)/shard_map/ppermute | solution.py:101
  50.8 1.5 %collective-permute-start.14 = (bf16[8,128]{1,0:T(8,128)(2,1)S(1)}, bf16[8,128]{1,0:T(8,128)(2,1)S(1)}, u32[]{:S(2)}, u32[]{:S(2)}) collective-permute-start(bf16[8,128]{1,0:T(8,128)(2,1)S(1)} %bitcast.209), channel_id=1, source_target_pairs={{0,12},{1,13},{2,14},{3,15},{4,8},{5,9},{6,10},{7,11},{8,4},{9,5},... | collective-permute-start | bytes 6152 | tf_op jit(solution)/shard_map/ppermute | solution.py:101
  53.4 1.6 %collective-permute-done.14 = bf16[8,128]{1,0:T(8,128)(2,1)S(1)} collective-permute-done((bf16[8,128]{1,0:T(8,128)(2,1)S(1)}, bf16[8,128]{1,0:T(8,128)(2,1)S(1)}, u32[]{:S(2)}, u32[]{:S(2)}) %collective-permute-start.14) | collective-permute-done | bytes 2080 | tf_op jit(solution)/shard_map/ppermute | solution.py:101
  55.1 2.1 %collective-permute-start.15 = (bf16[1,4,8,128]{3,2,1,0:T(8,128)(2,1)S(1)}, bf16[1,4,8,128]{3,2,1,0:T(8,128)(2,1)S(1)}, u32[]{:S(2)}, u32[]{:S(2)}) collective-permute-start(bf16[1,4,8,128]{3,2,1,0:T(8,128)(2,1)S(1)} %bitcast.198), channel_id=1, source_target_pairs={{0,1},{1,0},{2,3},{3,2},{4,5},{5,4},{6,7},{7,6},{8,9},{9,8},{10,11... | collective-permute-start | bytes 24584 | tf_op jit(solution)/shard_map/ppermute | solution.py:19
  59.4 1.3 %collective-permute-done.16 = bf16[2,4,8,128]{3,2,1,0:T(8,128)(2,1)S(1)} collective-permute-done((bf16[2,4,8,128]{3,2,1,0:T(8,128)(2,1)S(1)}, bf16[2,4,8,128]{3,2,1,0:T(8,128)(2,1)S(1)}, u32[]{:S(2)}, u32[]{:S(2)}) %collective-permute-start.16) | collective-permute-done | bytes 16416 | tf_op jit(solution)/shard_map/ppermute | solution.py:19
  61.0 5.6 %fusion.11 = f32[8,4,512]{2,0,1:T(8,128)S(1)} fusion(bf16[4,512,16,128]{3,2,1,0:T(8,128)(2,1)} %bitcast.183, bf16[16,8,128]{2,1,0:T(8,128)(2,1)S(1)} %select_reduce_fusion.2), kind=kOutput, calls=%fused_computation.11 | convolution fusion | flops 67108864 | bytes 8486912 | tf_op jit(solution)/shard_map/gabe,cae->gbc/dot_general | solution.py:242
  66.7 1.9 %collective-permute-start.17 = (f32[8,512]{1,0:T(8,128)S(1)}, f32[8,512]{1,0:T(8,128)S(1)}, u32[]{:S(2)}, u32[]{:S(2)}) collective-permute-start(f32[8,512]{1,0:T(8,128)S(1)} %get-tuple-element.16), channel_id=1, source_target_pairs={{0,0},{1,4},{2,8},{3,12},{4,1},{5,5},{6,9},{7,13},{8,2},{9,6},{10,... | collective-permute-start | bytes 49160 | tf_op jit(solution)/shard_map/ppermute | solution.py:249
  68.7 6.4 %collective-permute-start.19 = (f32[8,512]{1,0:T(8,128)S(1)}, f32[8,512]{1,0:T(8,128)S(1)}, u32[]{:S(2)}, u32[]{:S(2)}) collective-permute-start(f32[8,512]{1,0:T(8,128)S(1)} %get-tuple-element.15), channel_id=1, source_target_pairs={{0,2},{1,6},{2,10},{3,14},{4,3},{5,7},{6,11},{7,15},{8,0},{9,4},{1... | collective-permute-start | bytes 49160 | tf_op jit(solution)/shard_map/ppermute | solution.py:249
  75.1 1.3 %collective-permute-done.19 = f32[8,512]{1,0:T(8,128)S(1)} collective-permute-done((f32[8,512]{1,0:T(8,128)S(1)}, f32[8,512]{1,0:T(8,128)S(1)}, u32[]{:S(2)}, u32[]{:S(2)}) %collective-permute-start.19) | collective-permute-done | bytes 16416 | tf_op jit(solution)/shard_map/ppermute | solution.py:249
  76.4 2.8 %collective-permute-done.20 = f32[8,512]{1,0:T(8,128)S(1)} collective-permute-done((f32[8,512]{1,0:T(8,128)S(1)}, f32[8,512]{1,0:T(8,128)S(1)}, u32[]{:S(2)}, u32[]{:S(2)}) %collective-permute-start.20) | collective-permute-done | bytes 16416 | tf_op jit(solution)/shard_map/ppermute | solution.py:249
  (102 shorter events, 16.4 us)
Async XLA Ops:
  0.0 15.9 %copy-start = (bf16[2,1024,512]{2,1,0:T(8,128)(2,1)S(1)}, bf16[2,1024,512]{2,1,0:T(8,128)(2,1)}, u32[]{:S(2)}) copy-start(bf16[2,1024,512]{2,1,0:T(8,128)(2,1)} %param.13) | copy-start | bytes 6291460
  0.0 1.8 %collective-permute-start = (bf16[1,8,512]{2,1,0:T(8,128)(2,1)}, bf16[1,8,512]{2,1,0:T(8,128)(2,1)S(1)}, u32[]{:S(2)}, u32[]{:S(2)}) collective-permute-start(bf16[1,8,512]{2,1,0:T(8,128)(2,1)} %param.9), channel_id=1, source_target_pairs={{0,1},{1,0},{2,3},{3,2},{4,5},{5,4},{6,7},{7,6},{8,9},{9,8},{10,11... | collective-permute-start | bytes 24584 | tf_op jit(solution)/shard_map/ppermute | solution.py:19
  2.6 3.7 %collective-permute-start.1 = (bf16[2,8,512]{2,1,0:T(8,128)(2,1)S(1)}, bf16[2,8,512]{2,1,0:T(8,128)(2,1)S(1)}, u32[]{:S(2)}, u32[]{:S(2)}) collective-permute-start(bf16[2,8,512]{2,1,0:T(8,128)(2,1)S(1)} %maximum_select_fusion.3), channel_id=1, source_target_pairs={{0,2},{1,3},{2,0},{3,1},{4,6},{5,7},{6,4},{7,5},{8,10},{9,11},{10,... | collective-permute-start | bytes 49160 | tf_op jit(solution)/shard_map/ppermute | solution.py:19
  6.2 3.9 %collective-permute-start.2 = (bf16[4,8,512]{2,1,0:T(8,128)(2,1)S(1)}, bf16[4,8,512]{2,1,0:T(8,128)(2,1)S(1)}, u32[]{:S(2)}, u32[]{:S(2)}) collective-permute-start(bf16[4,8,512]{2,1,0:T(8,128)(2,1)S(1)} %maximum_select_fusion.1), channel_id=1, source_target_pairs={{0,4},{1,5},{2,6},{3,7},{4,0},{5,1},{6,2},{7,3},{8,12},{9,13},{10,... | collective-permute-start | bytes 98312 | tf_op jit(solution)/shard_map/ppermute | solution.py:101
  7.8 4.0 %collective-permute-start.3 = (bf16[4,8,512]{2,1,0:T(8,128)(2,1)S(1)}, bf16[4,8,512]{2,1,0:T(8,128)(2,1)S(1)}, u32[]{:S(2)}, u32[]{:S(2)}) collective-permute-start(bf16[4,8,512]{2,1,0:T(8,128)(2,1)S(1)} %maximum_select_fusion.1), channel_id=1, source_target_pairs={{0,8},{1,9},{2,10},{3,11},{4,12},{5,13},{6,14},{7,15},{8,0},{9,1},... | collective-permute-start | bytes 98312 | tf_op jit(solution)/shard_map/ppermute | solution.py:101
  10.1 4.6 %collective-permute-start.4 = (bf16[4,8,512]{2,1,0:T(8,128)(2,1)S(1)}, bf16[4,8,512]{2,1,0:T(8,128)(2,1)S(1)}, u32[]{:S(2)}, u32[]{:S(2)}) collective-permute-start(bf16[4,8,512]{2,1,0:T(8,128)(2,1)S(1)} %maximum_select_fusion.1), channel_id=1, source_target_pairs={{0,12},{1,13},{2,14},{3,15},{4,8},{5,9},{6,10},{7,11},{8,4},{9,5},... | collective-permute-start | bytes 98312 | tf_op jit(solution)/shard_map/ppermute | solution.py:101
  16.6 11.7 %copy-start.2 = (s32[1,8]{1,0:T(1,128)S(1)}, s32[1,8]{1,0:T(1,128)}, u32[]{:S(2)}) copy-start(s32[1,8]{1,0:T(1,128)} %param.17) | copy-start | bytes 100
  16.6 11.8 %copy-start.1 = (s32[16]{0:T(128)S(1)}, s32[16]{0:T(128)}, u32[]{:S(2)}) copy-start(s32[16]{0:T(128)} %param.14) | copy-start | bytes 196
  22.9 4.0 %collective-permute-start.5 = (f32[2,2,2,8,384]{4,3,2,1,0:T(8,128)S(1)}, f32[2,2,2,8,384]{4,3,2,1,0:T(8,128)S(1)}, u32[]{:S(2)}, u32[]{:S(2)}) collective-permute-start(f32[2,2,2,8,384]{4,3,2,1,0:T(8,128)S(1)} %select_bitcast_fusion.1), channel_id=1, source_target_pairs={{0,1},{1,0},{2,3},{3,2},{4,5},{5,4},{6,7},{7,6},{8,9},{9,8},{10,11... | collective-permute-start | bytes 294920 | tf_op jit(solution)/shard_map/ppermute | solution.py:19
  27.0 3.0 %collective-permute-start.6 = (f32[2,2,8,384]{3,2,1,0:T(8,128)S(1)}, f32[2,2,8,384]{3,2,1,0:T(8,128)S(1)}, u32[]{:S(2)}, u32[]{:S(2)}) collective-permute-start(f32[2,2,8,384]{3,2,1,0:T(8,128)S(1)} %select_bitcast_fusion.2), channel_id=1, source_target_pairs={{0,2},{1,3},{2,0},{3,1},{4,6},{5,7},{6,4},{7,5},{8,10},{9,11},{10,... | collective-permute-start | bytes 147464 | tf_op jit(solution)/shard_map/ppermute | solution.py:19
  30.0 4.4 %collective-permute-start.9 = (f32[8,384]{1,0:T(8,128)S(1)}, f32[8,384]{1,0:T(8,128)S(1)}, u32[]{:S(2)}, u32[]{:S(2)}) collective-permute-start(f32[8,384]{1,0:T(8,128)S(1)} %get-tuple-element.18), channel_id=1, source_target_pairs={{0,12},{1,13},{2,14},{3,15},{4,8},{5,9},{6,10},{7,11},{8,4},{9,5},... | collective-permute-start | bytes 36872 | tf_op jit(solution)/shard_map/ppermute | solution.py:101
  30.2 4.3 %collective-permute-start.8 = (f32[8,384]{1,0:T(8,128)S(1)}, f32[8,384]{1,0:T(8,128)S(1)}, u32[]{:S(2)}, u32[]{:S(2)}) collective-permute-start(f32[8,384]{1,0:T(8,128)S(1)} %get-tuple-element.19), channel_id=1, source_target_pairs={{0,8},{1,9},{2,10},{3,11},{4,12},{5,13},{6,14},{7,15},{8,0},{9,1},... | collective-permute-start | bytes 36872 | tf_op jit(solution)/shard_map/ppermute | solution.py:101
  30.2 4.5 %collective-permute-start.7 = (f32[8,384]{1,0:T(8,128)S(1)}, f32[8,384]{1,0:T(8,128)S(1)}, u32[]{:S(2)}, u32[]{:S(2)}) collective-permute-start(f32[8,384]{1,0:T(8,128)S(1)} %get-tuple-element.20), channel_id=1, source_target_pairs={{0,4},{1,5},{2,6},{3,7},{4,0},{5,1},{6,2},{7,3},{8,12},{9,13},{10,... | collective-permute-start | bytes 36872 | tf_op jit(solution)/shard_map/ppermute | solution.py:101
  34.8 3.8 %collective-permute-start.10 = (bf16[8,512]{1,0:T(8,128)(2,1)S(1)}, bf16[8,512]{1,0:T(8,128)(2,1)S(1)}, u32[]{:S(2)}, u32[]{:S(2)}) collective-permute-start(bf16[8,512]{1,0:T(8,128)(2,1)S(1)} %bitcast.196), channel_id=1, source_target_pairs={{0,1},{1,0},{2,3},{3,2},{4,5},{5,4},{6,7},{7,6},{8,9},{9,8},{10,11... | collective-permute-start | bytes 24584 | tf_op jit(solution)/shard_map/ppermute | solution.py:19
  46.1 1.6 %collective-permute-start.11 = (f32[8,4,130]{0,1,2:T(4,128)S(1)}, f32[8,4,130]{0,1,2:T(4,128)S(1)}, u32[]{:S(2)}, u32[]{:S(2)}) collective-permute-start(f32[8,4,130]{0,1,2:T(4,128)S(1)} %pad_maximum_fusion), channel_id=1, source_target_pairs={{0,1},{1,0},{2,3},{3,2},{4,5},{5,4},{6,7},{7,6},{8,9},{9,8},{10,11... | collective-permute-start | bytes 49928 | tf_op jit(solution)/shard_map/ppermute | solution.py:19
  48.2 4.8 %collective-permute-start.12 = (bf16[8,128]{1,0:T(8,128)(2,1)S(1)}, bf16[8,128]{1,0:T(8,128)(2,1)S(1)}, u32[]{:S(2)}, u32[]{:S(2)}) collective-permute-start(bf16[8,128]{1,0:T(8,128)(2,1)S(1)} %bitcast.207), channel_id=1, source_target_pairs={{0,4},{1,5},{2,6},{3,7},{4,0},{5,1},{6,2},{7,3},{8,12},{9,13},{10,... | collective-permute-start | bytes 6152 | tf_op jit(solution)/shard_map/ppermute | solution.py:101
  50.1 3.4 %collective-permute-start.13 = (bf16[8,128]{1,0:T(8,128)(2,1)S(1)}, bf16[8,128]{1,0:T(8,128)(2,1)S(1)}, u32[]{:S(2)}, u32[]{:S(2)}) collective-permute-start(bf16[8,128]{1,0:T(8,128)(2,1)S(1)} %bitcast.208), channel_id=1, source_target_pairs={{0,8},{1,9},{2,10},{3,11},{4,12},{5,13},{6,14},{7,15},{8,0},{9,1},... | collective-permute-start | bytes 6152 | tf_op jit(solution)/shard_map/ppermute | solution.py:101
  50.8 4.3 %collective-permute-start.14 = (bf16[8,128]{1,0:T(8,128)(2,1)S(1)}, bf16[8,128]{1,0:T(8,128)(2,1)S(1)}, u32[]{:S(2)}, u32[]{:S(2)}) collective-permute-start(bf16[8,128]{1,0:T(8,128)(2,1)S(1)} %bitcast.209), channel_id=1, source_target_pairs={{0,12},{1,13},{2,14},{3,15},{4,8},{5,9},{6,10},{7,11},{8,4},{9,5},... | collective-permute-start | bytes 6152 | tf_op jit(solution)/shard_map/ppermute | solution.py:101
  55.1 2.9 %collective-permute-start.15 = (bf16[1,4,8,128]{3,2,1,0:T(8,128)(2,1)S(1)}, bf16[1,4,8,128]{3,2,1,0:T(8,128)(2,1)S(1)}, u32[]{:S(2)}, u32[]{:S(2)}) collective-permute-start(bf16[1,4,8,128]{3,2,1,0:T(8,128)(2,1)S(1)} %bitcast.198), channel_id=1, source_target_pairs={{0,1},{1,0},{2,3},{3,2},{4,5},{5,4},{6,7},{7,6},{8,9},{9,8},{10,11... | collective-permute-start | bytes 24584 | tf_op jit(solution)/shard_map/ppermute | solution.py:19
  58.1 2.6 %collective-permute-start.16 = (bf16[2,4,8,128]{3,2,1,0:T(8,128)(2,1)S(1)}, bf16[2,4,8,128]{3,2,1,0:T(8,128)(2,1)S(1)}, u32[]{:S(2)}, u32[]{:S(2)}) collective-permute-start(bf16[2,4,8,128]{3,2,1,0:T(8,128)(2,1)S(1)} %maximum_select_fusion.5), channel_id=1, source_target_pairs={{0,2},{1,3},{2,0},{3,1},{4,6},{5,7},{6,4},{7,5},{8,10},{9,11},{10,... | collective-permute-start | bytes 49160 | tf_op jit(solution)/shard_map/ppermute | solution.py:19
  66.7 8.4 %collective-permute-start.17 = (f32[8,512]{1,0:T(8,128)S(1)}, f32[8,512]{1,0:T(8,128)S(1)}, u32[]{:S(2)}, u32[]{:S(2)}) collective-permute-start(f32[8,512]{1,0:T(8,128)S(1)} %get-tuple-element.16), channel_id=1, source_target_pairs={{0,0},{1,4},{2,8},{3,12},{4,1},{5,5},{6,9},{7,13},{8,2},{9,6},{10,... | collective-permute-start | bytes 49160 | tf_op jit(solution)/shard_map/ppermute | solution.py:249
  68.6 6.5 %collective-permute-start.18 = (f32[8,512]{1,0:T(8,128)S(1)}, f32[8,512]{1,0:T(8,128)S(1)}, u32[]{:S(2)}, u32[]{:S(2)}) collective-permute-start(f32[8,512]{1,0:T(8,128)S(1)} %get-tuple-element.13), channel_id=1, source_target_pairs={{0,1},{1,5},{2,9},{3,13},{4,0},{5,4},{6,8},{7,12},{8,3},{9,7},{10,... | collective-permute-start | bytes 49160 | tf_op jit(solution)/shard_map/ppermute | solution.py:249
  68.7 7.7 %collective-permute-start.19 = (f32[8,512]{1,0:T(8,128)S(1)}, f32[8,512]{1,0:T(8,128)S(1)}, u32[]{:S(2)}, u32[]{:S(2)}) collective-permute-start(f32[8,512]{1,0:T(8,128)S(1)} %get-tuple-element.15), channel_id=1, source_target_pairs={{0,2},{1,6},{2,10},{3,14},{4,3},{5,7},{6,11},{7,15},{8,0},{9,4},{1... | collective-permute-start | bytes 49160 | tf_op jit(solution)/shard_map/ppermute | solution.py:249
  75.1 4.1 %collective-permute-start.20 = (f32[8,512]{1,0:T(8,128)S(1)}, f32[8,512]{1,0:T(8,128)S(1)}, u32[]{:S(2)}, u32[]{:S(2)}) collective-permute-start(f32[8,512]{1,0:T(8,128)S(1)} %get-tuple-element.14), channel_id=1, source_target_pairs={{0,3},{1,7},{2,11},{3,15},{4,2},{5,6},{6,10},{7,14},{8,1},{9,5},{1... | collective-permute-start | bytes 49160 | tf_op jit(solution)/shard_map/ppermute | solution.py:249

commit v6 on v5

--- a/solution.py
+++ b/solution.py
@@ -99,6 +99,10 @@
 def swap_rows(value, axis, col_bits, s):
     shift = s << col_bits
     return lax.ppermute(value, axis, [(t, t ^ shift) for t in range(lax.axis_size(axis))])
+
+
+def swap_cols(value, axis, s):
+    return lax.ppermute(value, axis, [(t, t ^ s) for t in range(lax.axis_size(axis))])
 
 
 def norm_rows(rows_float, norm_gain):
@@ -128,7 +132,13 @@
     col_bits = grid_cols.bit_length() - 1
     row_bits = GR.bit_length() - 1
     row_order = jnp.arange(GR, dtype=jnp.int32) ^ grid_row
-    in_row = gather_rounds(hidden_in, "tp", range(col_bits))
+    col_order = jnp.arange(grid_cols, dtype=jnp.int32) ^ grid_col
+    direct_cols = grid_cols <= 4
+    if direct_cols:
+        from_cols = [hidden_in[0]] + [swap_cols(hidden_in[0], "tp", s) for s in range(1, grid_cols)]
+        in_row = pick(jnp.stack(from_cols), col_order)
+    else:
+        in_row = gather_rounds(hidden_in, "tp", range(col_bits))
     from_rows = [in_row] + [swap_rows(in_row, "tp", col_bits, s) for s in range(1, GR)]
     every_rows = pick(jnp.stack(from_rows), row_order).reshape(ranks, ROWS, DS)
     rows_float = (
@@ -147,7 +157,8 @@
         .transpose(0, 2, 1, 3)
         .reshape(group_count * QG, ROWS, HD)
     )
-    query_pick = pick(query_part, dest_copy * QG + dest_group)
+    pair_first = dest_copy * QG + 2 * dest_head
+    query_pick = jnp.concatenate([pick(query_part, pair_first), pick(query_part, pair_first + 1)], -1)
     key_rows = lax.dynamic_slice_in_dim(normed_every, my_index * key_width, key_width, 1)
     keyval_part = jnp.einsum("rc,kfc->rkf", key_rows, kv_blocks, preferred_element_type=jnp.float32)
     keyval_part = (
@@ -156,32 +167,32 @@
         .reshape(group_count * KVH, ROWS, 2 * HD)
     )
     keyval_term = pick(keyval_part, dest_copy * KVH + dest_head)
+    width = 4 * HD
     compact = jnp.concatenate([query_pick, keyval_term], -1)
-    held, _ = scatter_rounds(
-        compact.reshape((2,) * bits + (ROWS, 3 * HD)), list(range(bits - 1, -1, -1)), "tp", range(col_bits)
-    )
-    held = held.reshape(GR, ROWS, 3 * HD)
+    if direct_cols:
+        by_col = compact.reshape(GR, grid_cols, ROWS, width)
+        held = lax.dynamic_index_in_dim(by_col, grid_col, 1, keepdims=False)
+        for s in range(1, grid_cols):
+            held = held + swap_cols(lax.dynamic_index_in_dim(by_col, grid_col ^ s, 1, keepdims=False), "tp", s)
+    else:
+        held, _ = scatter_rounds(
+            compact.reshape((2,) * bits + (ROWS, width)), list(range(bits - 1, -1, -1)), "tp", range(col_bits)
+        )
+        held = held.reshape(GR, ROWS, width)
     from_rows = [lax.dynamic_index_in_dim(held, grid_row, 0, keepdims=False)]
     for s in range(1, GR):
         piece = lax.dynamic_index_in_dim(held, grid_row ^ s, 0, keepdims=False)
         from_rows.append(swap_rows(piece, "tp", col_bits, s))
-    query_slots = pick(jnp.stack([got[:, :HD] for got in from_rows]), row_order)
-    query_slots = query_slots.transpose(1, 0, 2).reshape(ROWS, GR * HD)
-    keyval_sum = from_rows[0][:, HD:]
+    halves_q = [
+        pick(jnp.stack([got[:, h * HD : (h + 1) * HD] for got in from_rows]), row_order) for h in range(2)
+    ]
+    both_queries = jnp.stack(halves_q).transpose(2, 0, 1, 3).reshape(ROWS, 2 * GR, HD).astype(jnp.bfloat16)
+    keyval_sum = from_rows[0][:, 2 * HD :]
     for got in from_rows[1:]:
-        keyval_sum = keyval_sum + got[:, HD:]
-    projected = jnp.concatenate([query_slots, keyval_sum], -1)
-    queries = projected[:, : GR * HD].astype(jnp.bfloat16)
-    keyval_new = projected[:, GR * HD :].astype(jnp.bfloat16)
+        keyval_sum = keyval_sum + got[:, 2 * HD :]
+    keyval_new = keyval_sum.astype(jnp.bfloat16)
     key_new = keyval_new[:, :HD]
     value_new = keyval_new[:, HD:]
-    partner_queries = from_partner(queries, "tp", 0)
-    both_queries = jnp.where(
-        my_half == 0,
-        jnp.concatenate([queries, partner_queries], 1),
-        jnp.concatenate([partner_queries, queries], 1),
-    )
-    both_queries = both_queries.reshape(ROWS, 2 * GR, HD)
     scale = 1.0 / HD**0.5
     scores = (
         jnp.einsum("bhe,bte->bht", both_queries, key_cache[0], preferred_element_type=jnp.float32)
@@ -229,7 +240,11 @@
         piece = lax.dynamic_index_in_dim(attention, grid_row ^ s, 1, keepdims=False)
         from_rows.append(swap_rows(piece, "tp", col_bits, s))
     by_row = pick(jnp.stack(from_rows), row_order)
-    every_slot = gather_rounds(by_row[None], "tp", range(col_bits))
+    if direct_cols:
+        from_cols = [by_row] + [swap_cols(by_row, "tp", s) for s in range(1, grid_cols)]
+        every_slot = pick(jnp.stack(from_cols), col_order)
+    else:
+        every_slot = gather_rounds(by_row[None], "tp", range(col_bits))
     every_slot = every_slot.transpose(1, 0, 2, 3).reshape(group_count, ROLL, ROWS, HD)
     head_ids = jnp.arange(KVH, dtype=jnp.int32)
     pair_heads = kv_assign[0::2]

time: 80.2 us -> 78.1 us (0.974)
  starting transfers between devices: 33.5 us -> 30.5 us
    ppermute x8 -> x1, starting transfers between devices: 13.7 us -> 2.06 us  [from_partner(): return lax.ppermute(value, axis, pairs)]
    ppermute x0 -> x9, starting transfers between devices: none -> 9.89 us  [swap_cols(): lax.ppermute(value, axis, [(t, t ^ s) for t in range(lax.axis_size(axis))])]
    ppermute x0 -> x9, waiting for transfers between devices: none -> 5.8 us  [swap_cols(): lax.ppermute(value, axis, [(t, t ^ s) for t in range(lax.axis_size(axis))])]
    ppermute x8 -> x1, waiting for transfers between devices: 6.81 us -> 1.17 us  [from_partner(): return lax.ppermute(value, axis, pairs)]
    ppermute x4, starting transfers between devices: 8.38 us -> 6.81 us  [local(): got = lax.ppermute(piece, 'tp', pairs)]
    select_n x7 -> x1, other arithmetic: 0.84 us -> 0.01 us  [local(): dest_head = kv_assign[dest_rank]]
    reduce_sum x6 -> x8, other arithmetic: 1.19 us -> 1.76 us  [pick(): jnp.sum(jnp.where(hit, table[None], jnp.zeros((), table.dtype)), axis=1)]
  transfers between devices with their start and end apart: 21 -> 23, of which waited for: 15 -> 13; matrix products, arithmetic and copies ran while one was open for 5% -> 5% of each run, Pallas kernels for 0% -> 0%
where the time goes in v6:
time: 78.1 us; the launch traced here: 77.7 us
  starting transfers between devices  30.5 us (39%)
  waiting for transfers between devices  19 us (24%)
  matrix products  18.4 us (24%)
  other arithmetic  5.49 us (7%)
  local copies, waits for them, and re-layouts  3.84 us (5%)
    ppermute x9, starting transfers between devices, swap_rows(): lax.ppermute(value, axis, [(t, t ^ shift) for t in range(lax.axis_size(ax...  11.8 us
    ppermute x9, starting transfers between devices, swap_cols(): lax.ppermute(value, axis, [(t, t ^ s) for t in range(lax.axis_size(axis))])  9.89 us
    ppermute x9, waiting for transfers between devices, swap_rows(): lax.ppermute(value, axis, [(t, t ^ shift) for t in range(lax.axis_size(ax...  8.4 us
    ppermute x4, starting transfers between devices, local(): got = lax.ppermute(piece, 'tp', pairs)  6.81 us
    ppermute x9, waiting for transfers between devices, swap_cols(): lax.ppermute(value, axis, [(t, t ^ s) for t in range(lax.axis_size(axis))])  5.8 us
    dot_general x1, matrix products, local(): jnp.einsum('rc,aec->rae', col_rows, q_blocks[0], preferred_element_type=j...  5.65 us
    dot_general x1, matrix products, local(): jnp.einsum('gabe,cae->gbc', chosen, o_blocks[0], preferred_element_type=j...  5.65 us
    ppermute x4, waiting for transfers between devices, local(): got = lax.ppermute(piece, 'tp', pairs)  3.67 us
  transfers between devices with their start and end apart: 23, of which 13 were waited for; matrix products, arithmetic and copies ran while one was open for 5% of the time, Pallas kernels for 0%

profile of v6, /device:TPU:1, one launch (start us, length us, event | category | flops | bytes accessed | tf_op | source)
XLA Modules:
  0.0 77.7 jit_solution(13698422916884630548)
XLA Ops:
  0.1 2.7 %collective-permute-start.1 = (bf16[8,512]{1,0:T(8,128)(2,1)}, bf16[8,512]{1,0:T(8,128)(2,1)S(1)}, u32[]{:S(2)}, u32[]{:S(2)}) collective-permute-start(bf16[8,512]{1,0:T(8,128)(2,1)} %bitcast.198), channel_id=1, source_target_pairs={{0,2},{1,3},{2,0},{3,1},{4,6},{5,7},{6,4},{7,5},{8,10},{9,11},{10,... | collective-permute-start | bytes 24584 | tf_op jit(solution)/shard_map/ppermute | solution.py:105
  3.8 1.3 %gather_fusion.1 = s32[16]{0:T(128)S(1)} fusion(s32[16]{0:T(128)} %param.14, s32[1024]{0:T(1024)S(1)} %pad_clamp_fusion), kind=kCustom, calls=%fused_computation.1 | custom fusion | bytes 192 | tf_op jit(solution)/shard_map/gather | solution.py:128
  6.8 3.8 %collective-permute-start.5 = (bf16[4,8,512]{2,1,0:T(8,128)(2,1)S(1)}, bf16[4,8,512]{2,1,0:T(8,128)(2,1)S(1)}, u32[]{:S(2)}, u32[]{:S(2)}) collective-permute-start(bf16[4,8,512]{2,1,0:T(8,128)(2,1)S(1)} %select_reduce_fusion.7), channel_id=1, source_target_pairs={{0,12},{1,13},{2,14},{3,15},{4,8},{5,9},{6,10},{7,11},{8,4},{9,5},... | collective-permute-start | bytes 98312 | tf_op jit(solution)/shard_map/ppermute | solution.py:101
  11.1 1.2 %collective-permute-done.5 = bf16[4,8,512]{2,1,0:T(8,128)(2,1)S(1)} collective-permute-done((bf16[4,8,512]{2,1,0:T(8,128)(2,1)S(1)}, bf16[4,8,512]{2,1,0:T(8,128)(2,1)S(1)}, u32[]{:S(2)}, u32[]{:S(2)}) %collective-permute-start.5) | collective-permute-done | bytes 32800 | tf_op jit(solution)/shard_map/ppermute | solution.py:101
  16.3 5.7 %fusion.14 = f32[16,8,128]{2,1,0:T(8,128)S(1)} fusion(bf16[1,16,128,2048]{3,2,1,0:T(8,128)(2,1)} %param.11, bf16[8,8192]{1,0:T(8,128)(2,1)S(1)} %multiply_convert_fusion, s32[]{:T(128)S(6)} %select_n.283), kind=kOutput, calls=%fused_computation.12 | convolution fusion | flops 67108864 | bytes 8486916 | tf_op jit(solution)/shard_map/rc,aec->rae/dot_general | solution.py:152
  23.0 1.6 %collective-permute-start.6 = (f32[4,8,512]{2,1,0:T(8,128)S(1)}, f32[4,8,512]{2,1,0:T(8,128)S(1)}, u32[]{:S(2)}, u32[]{:S(2)}) collective-permute-start(f32[4,8,512]{2,1,0:T(8,128)S(1)} %get-tuple-element.15), channel_id=1, source_target_pairs={{0,1},{1,0},{2,3},{3,2},{4,5},{5,4},{6,7},{7,6},{8,9},{9,8},{10,11... | collective-permute-start | bytes 196616 | tf_op jit(solution)/shard_map/ppermute | solution.py:105
  24.6 1.2 %collective-permute-start.7 = (f32[4,8,512]{2,1,0:T(8,128)S(1)}, f32[4,8,512]{2,1,0:T(8,128)S(1)}, u32[]{:S(2)}, u32[]{:S(2)}) collective-permute-start(f32[4,8,512]{2,1,0:T(8,128)S(1)} %get-tuple-element.17), channel_id=1, source_target_pairs={{0,2},{1,3},{2,0},{3,1},{4,6},{5,7},{6,4},{7,5},{8,10},{9,11},{10,... | collective-permute-start | bytes 196616 | tf_op jit(solution)/shard_map/ppermute | solution.py:105
  26.4 1.8 %collective-permute-done.7 = f32[4,8,512]{2,1,0:T(8,128)S(1)} collective-permute-done((f32[4,8,512]{2,1,0:T(8,128)S(1)}, f32[4,8,512]{2,1,0:T(8,128)S(1)}, u32[]{:S(2)}, u32[]{:S(2)}) %collective-permute-start.7) | collective-permute-done | bytes 65568 | tf_op jit(solution)/shard_map/ppermute | solution.py:105
  28.2 1.6 %collective-permute-done.8 = f32[4,8,512]{2,1,0:T(8,128)S(1)} collective-permute-done((f32[4,8,512]{2,1,0:T(8,128)S(1)}, f32[4,8,512]{2,1,0:T(8,128)S(1)}, u32[]{:S(2)}, u32[]{:S(2)}) %collective-permute-start.8) | collective-permute-done | bytes 65568 | tf_op jit(solution)/shard_map/ppermute | solution.py:105
  29.9 1.8 %collective-permute-start.9 = (f32[8,512]{1,0:T(8,128)S(1)}, f32[8,512]{1,0:T(8,128)S(1)}, u32[]{:S(2)}, u32[]{:S(2)}) collective-permute-start(f32[8,512]{1,0:T(8,128)S(1)} %get-tuple-element.29), channel_id=1, source_target_pairs={{0,4},{1,5},{2,6},{3,7},{4,0},{5,1},{6,2},{7,3},{8,12},{9,13},{10,... | collective-permute-start | bytes 49160 | tf_op jit(solution)/shard_map/ppermute | solution.py:101
  31.7 2.2 %collective-permute-start.11 = (f32[8,512]{1,0:T(8,128)S(1)}, f32[8,512]{1,0:T(8,128)S(1)}, u32[]{:S(2)}, u32[]{:S(2)}) collective-permute-start(f32[8,512]{1,0:T(8,128)S(1)} %get-tuple-element.27), channel_id=1, source_target_pairs={{0,12},{1,13},{2,14},{3,15},{4,8},{5,9},{6,10},{7,11},{8,4},{9,5},... | collective-permute-start | bytes 49160 | tf_op jit(solution)/shard_map/ppermute | solution.py:101
  33.8 1.3 %collective-permute-done.10 = f32[8,512]{1,0:T(8,128)S(1)} collective-permute-done((f32[8,512]{1,0:T(8,128)S(1)}, f32[8,512]{1,0:T(8,128)S(1)}, u32[]{:S(2)}, u32[]{:S(2)}) %collective-permute-start.10) | collective-permute-done | bytes 16416 | tf_op jit(solution)/shard_map/ppermute | solution.py:101
  36.4 3.5 %select_reduce_fusion.4 = (f32[8,8]{1,0:T(8,128)S(1)}, f32[8,8,2048]{2,1,0:T(8,128)S(1)}) fusion(pred[8,2048]{1,0:T(8,128)(4,1)S(1)} %iota_compare_fusion, bf16[8,8,128]{2,1,0:T(8,128)(2,1)S(1)} %bitcast.183, bf16[1,8,2048,128]{3,2,1,0:T(8,128)(2,1)} %param.15), kind=kOutput, calls=%fused_computation.20 | convolution fusion | flops 33947584 | bytes 4751616 | tf_op jit(solution)/shard_map/bhe,bte->bht/dot_general | solution.py:198
  40.2 2.9 %fusion.17 = f32[8,8,128]{2,1,0:T(8,128)S(1)} fusion(bf16[1,8,2048,128]{3,2,1,0:T(8,128)(2,1)} %param.16, f32[8,8,2048]{2,1,0:T(8,128)S(1)} %get-tuple-element.46, f32[8,8]{1,0:T(8,128)S(1)} %fusion.42, pred[8,2048]{1,0:T(8,128)(4,1)S(1)} %iota_compare_fusion, f32[8,128]{1,0:T(8,128)S(1)} %get-tuple-element.42, f32[8,8]{1,0:T(8,128)S(1)} %convert_element_type.70), kind=kOutput, calls=%fused_computation.14 | convolution fusion | flops 33964032 | bytes 4772352 | tf_op jit(solution)/shard_map/bht,bte->bhe/dot_general | solution.py:211
  43.7 2.1 %collective-permute-start.12 = (f32[8,4,130]{0,1,2:T(4,128)S(1)}, f32[8,4,130]{0,1,2:T(4,128)S(1)}, u32[]{:S(2)}, u32[]{:S(2)}) collective-permute-start(f32[8,4,130]{0,1,2:T(4,128)S(1)} %pad_maximum_fusion), channel_id=1, source_target_pairs={{0,1},{1,0},{2,3},{3,2},{4,5},{5,4},{6,7},{7,6},{8,9},{9,8},{10,11... | collective-permute-start | bytes 49928 | tf_op jit(solution)/shard_map/ppermute | solution.py:19
  47.5 2.2 %collective-permute-start.14 = (bf16[8,128]{1,0:T(8,128)(2,1)S(1)}, bf16[8,128]{1,0:T(8,128)(2,1)S(1)}, u32[]{:S(2)}, u32[]{:S(2)}) collective-permute-start(bf16[8,128]{1,0:T(8,128)(2,1)S(1)} %bitcast.207), channel_id=1, source_target_pairs={{0,8},{1,9},{2,10},{3,11},{4,12},{5,13},{6,14},{7,15},{8,0},{9,1},... | collective-permute-start | bytes 6152 | tf_op jit(solution)/shard_map/ppermute | solution.py:101
  49.8 1.4 %collective-permute-start.15 = (bf16[8,128]{1,0:T(8,128)(2,1)S(1)}, bf16[8,128]{1,0:T(8,128)(2,1)S(1)}, u32[]{:S(2)}, u32[]{:S(2)}) collective-permute-start(bf16[8,128]{1,0:T(8,128)(2,1)S(1)} %bitcast.208), channel_id=1, source_target_pairs={{0,12},{1,13},{2,14},{3,15},{4,8},{5,9},{6,10},{7,11},{8,4},{9,5},... | collective-permute-start | bytes 6152 | tf_op jit(solution)/shard_map/ppermute | solution.py:101
  51.2 2.8 %collective-permute-done.15 = bf16[8,128]{1,0:T(8,128)(2,1)S(1)} collective-permute-done((bf16[8,128]{1,0:T(8,128)(2,1)S(1)}, bf16[8,128]{1,0:T(8,128)(2,1)S(1)}, u32[]{:S(2)}, u32[]{:S(2)}) %collective-permute-start.15) | collective-permute-done | bytes 2080 | tf_op jit(solution)/shard_map/ppermute | solution.py:101
  54.2 2.1 %collective-permute-start.16 = (bf16[4,8,128]{2,1,0:T(8,128)(2,1)S(1)}, bf16[4,8,128]{2,1,0:T(8,128)(2,1)S(1)}, u32[]{:S(2)}, u32[]{:S(2)}) collective-permute-start(bf16[4,8,128]{2,1,0:T(8,128)(2,1)S(1)} %select_reduce_fusion.10), channel_id=1, source_target_pairs={{0,1},{1,0},{2,3},{3,2},{4,5},{5,4},{6,7},{7,6},{8,9},{9,8},{10,11... | collective-permute-start | bytes 24584 | tf_op jit(solution)/shard_map/ppermute | solution.py:105
  58.8 1.6 %collective-permute-done.18 = bf16[4,8,128]{2,1,0:T(8,128)(2,1)S(1)} collective-permute-done((bf16[4,8,128]{2,1,0:T(8,128)(2,1)S(1)}, bf16[4,8,128]{2,1,0:T(8,128)(2,1)S(1)}, u32[]{:S(2)}, u32[]{:S(2)}) %collective-permute-start.18) | collective-permute-done | bytes 8224 | tf_op jit(solution)/shard_map/ppermute | solution.py:105
  61.0 5.6 %fusion.11 = f32[8,4,512]{2,0,1:T(8,128)S(1)} fusion(bf16[4,512,16,128]{3,2,1,0:T(8,128)(2,1)} %bitcast.173, bf16[16,8,128]{2,1,0:T(8,128)(2,1)S(1)} %select_reduce_fusion.3), kind=kOutput, calls=%fused_computation.11 | convolution fusion | flops 67108864 | bytes 8486912 | tf_op jit(solution)/shard_map/gabe,cae->gbc/dot_general | solution.py:257
  66.6 1.9 %collective-permute-start.19 = (f32[8,512]{1,0:T(8,128)S(1)}, f32[8,512]{1,0:T(8,128)S(1)}, u32[]{:S(2)}, u32[]{:S(2)}) collective-permute-start(f32[8,512]{1,0:T(8,128)S(1)} %get-tuple-element.25), channel_id=1, source_target_pairs={{0,0},{1,4},{2,8},{3,12},{4,1},{5,5},{6,9},{7,13},{8,2},{9,6},{10,... | collective-permute-start | bytes 49160 | tf_op jit(solution)/shard_map/ppermute | solution.py:264
  68.6 4.4 %collective-permute-start.21 = (f32[8,512]{1,0:T(8,128)S(1)}, f32[8,512]{1,0:T(8,128)S(1)}, u32[]{:S(2)}, u32[]{:S(2)}) collective-permute-start(f32[8,512]{1,0:T(8,128)S(1)} %get-tuple-element.24), channel_id=1, source_target_pairs={{0,2},{1,6},{2,10},{3,14},{4,3},{5,7},{6,11},{7,15},{8,0},{9,4},{1... | collective-permute-start | bytes 49160 | tf_op jit(solution)/shard_map/ppermute | solution.py:264
  74.2 2.9 %collective-permute-done.22 = f32[8,512]{1,0:T(8,128)S(1)} collective-permute-done((f32[8,512]{1,0:T(8,128)S(1)}, f32[8,512]{1,0:T(8,128)S(1)}, u32[]{:S(2)}, u32[]{:S(2)}) %collective-permute-start.22) | collective-permute-done | bytes 16416 | tf_op jit(solution)/shard_map/ppermute | solution.py:264
  (105 shorter events, 17.7 us)
Async XLA Ops:
  0.0 15.7 %copy-start = (bf16[2,1024,512]{2,1,0:T(8,128)(2,1)S(1)}, bf16[2,1024,512]{2,1,0:T(8,128)(2,1)}, u32[]{:S(2)}) copy-start(bf16[2,1024,512]{2,1,0:T(8,128)(2,1)} %param.13) | copy-start | bytes 6291460
  0.0 6.0 %collective-permute-start = (bf16[8,512]{1,0:T(8,128)(2,1)}, bf16[8,512]{1,0:T(8,128)(2,1)S(1)}, u32[]{:S(2)}, u32[]{:S(2)}) collective-permute-start(bf16[8,512]{1,0:T(8,128)(2,1)} %bitcast.197), channel_id=1, source_target_pairs={{0,1},{1,0},{2,3},{3,2},{4,5},{5,4},{6,7},{7,6},{8,9},{9,8},{10,11... | collective-permute-start | bytes 24584 | tf_op jit(solution)/shard_map/ppermute | solution.py:105
  0.1 5.9 %collective-permute-start.1 = (bf16[8,512]{1,0:T(8,128)(2,1)}, bf16[8,512]{1,0:T(8,128)(2,1)S(1)}, u32[]{:S(2)}, u32[]{:S(2)}) collective-permute-start(bf16[8,512]{1,0:T(8,128)(2,1)} %bitcast.198), channel_id=1, source_target_pairs={{0,2},{1,3},{2,0},{3,1},{4,6},{5,7},{6,4},{7,5},{8,10},{9,11},{10,... | collective-permute-start | bytes 24584 | tf_op jit(solution)/shard_map/ppermute | solution.py:105
  2.7 3.3 %collective-permute-start.2 = (bf16[8,512]{1,0:T(8,128)(2,1)}, bf16[8,512]{1,0:T(8,128)(2,1)S(1)}, u32[]{:S(2)}, u32[]{:S(2)}) collective-permute-start(bf16[8,512]{1,0:T(8,128)(2,1)} %bitcast.199), channel_id=1, source_target_pairs={{0,3},{1,2},{2,1},{3,0},{4,7},{5,6},{6,5},{7,4},{8,11},{9,10},{10,... | collective-permute-start | bytes 24584 | tf_op jit(solution)/shard_map/ppermute | solution.py:105
  6.8 5.4 %collective-permute-start.5 = (bf16[4,8,512]{2,1,0:T(8,128)(2,1)S(1)}, bf16[4,8,512]{2,1,0:T(8,128)(2,1)S(1)}, u32[]{:S(2)}, u32[]{:S(2)}) collective-permute-start(bf16[4,8,512]{2,1,0:T(8,128)(2,1)S(1)} %select_reduce_fusion.7), channel_id=1, source_target_pairs={{0,12},{1,13},{2,14},{3,15},{4,8},{5,9},{6,10},{7,11},{8,4},{9,5},... | collective-permute-start | bytes 98312 | tf_op jit(solution)/shard_map/ppermute | solution.py:101
  10.7 2.8 %collective-permute-start.3 = (bf16[4,8,512]{2,1,0:T(8,128)(2,1)S(1)}, bf16[4,8,512]{2,1,0:T(8,128)(2,1)S(1)}, u32[]{:S(2)}, u32[]{:S(2)}) collective-permute-start(bf16[4,8,512]{2,1,0:T(8,128)(2,1)S(1)} %select_reduce_fusion.7), channel_id=1, source_target_pairs={{0,4},{1,5},{2,6},{3,7},{4,0},{5,1},{6,2},{7,3},{8,12},{9,13},{10,... | collective-permute-start | bytes 98312 | tf_op jit(solution)/shard_map/ppermute | solution.py:101
  10.7 3.8 %collective-permute-start.4 = (bf16[4,8,512]{2,1,0:T(8,128)(2,1)S(1)}, bf16[4,8,512]{2,1,0:T(8,128)(2,1)S(1)}, u32[]{:S(2)}, u32[]{:S(2)}) collective-permute-start(bf16[4,8,512]{2,1,0:T(8,128)(2,1)S(1)} %select_reduce_fusion.7), channel_id=1, source_target_pairs={{0,8},{1,9},{2,10},{3,11},{4,12},{5,13},{6,14},{7,15},{8,0},{9,1},... | collective-permute-start | bytes 98312 | tf_op jit(solution)/shard_map/ppermute | solution.py:101
  23.0 3.4 %collective-permute-start.6 = (f32[4,8,512]{2,1,0:T(8,128)S(1)}, f32[4,8,512]{2,1,0:T(8,128)S(1)}, u32[]{:S(2)}, u32[]{:S(2)}) collective-permute-start(f32[4,8,512]{2,1,0:T(8,128)S(1)} %get-tuple-element.15), channel_id=1, source_target_pairs={{0,1},{1,0},{2,3},{3,2},{4,5},{5,4},{6,7},{7,6},{8,9},{9,8},{10,11... | collective-permute-start | bytes 196616 | tf_op jit(solution)/shard_map/ppermute | solution.py:105
  24.6 3.7 %collective-permute-start.7 = (f32[4,8,512]{2,1,0:T(8,128)S(1)}, f32[4,8,512]{2,1,0:T(8,128)S(1)}, u32[]{:S(2)}, u32[]{:S(2)}) collective-permute-start(f32[4,8,512]{2,1,0:T(8,128)S(1)} %get-tuple-element.17), channel_id=1, source_target_pairs={{0,2},{1,3},{2,0},{3,1},{4,6},{5,7},{6,4},{7,5},{8,10},{9,11},{10,... | collective-permute-start | bytes 196616 | tf_op jit(solution)/shard_map/ppermute | solution.py:105
  25.8 4.0 %collective-permute-start.8 = (f32[4,8,512]{2,1,0:T(8,128)S(1)}, f32[4,8,512]{2,1,0:T(8,128)S(1)}, u32[]{:S(2)}, u32[]{:S(2)}) collective-permute-start(f32[4,8,512]{2,1,0:T(8,128)S(1)} %get-tuple-element.16), channel_id=1, source_target_pairs={{0,3},{1,2},{2,1},{3,0},{4,7},{5,6},{6,5},{7,4},{8,11},{9,10},{10,... | collective-permute-start | bytes 196616 | tf_op jit(solution)/shard_map/ppermute | solution.py:105
  29.9 4.0 %collective-permute-start.9 = (f32[8,512]{1,0:T(8,128)S(1)}, f32[8,512]{1,0:T(8,128)S(1)}, u32[]{:S(2)}, u32[]{:S(2)}) collective-permute-start(f32[8,512]{1,0:T(8,128)S(1)} %get-tuple-element.29), channel_id=1, source_target_pairs={{0,4},{1,5},{2,6},{3,7},{4,0},{5,1},{6,2},{7,3},{8,12},{9,13},{10,... | collective-permute-start | bytes 49160 | tf_op jit(solution)/shard_map/ppermute | solution.py:101
  31.7 3.5 %collective-permute-start.10 = (f32[8,512]{1,0:T(8,128)S(1)}, f32[8,512]{1,0:T(8,128)S(1)}, u32[]{:S(2)}, u32[]{:S(2)}) collective-permute-start(f32[8,512]{1,0:T(8,128)S(1)} %get-tuple-element.28), channel_id=1, source_target_pairs={{0,8},{1,9},{2,10},{3,11},{4,12},{5,13},{6,14},{7,15},{8,0},{9,1},... | collective-permute-start | bytes 49160 | tf_op jit(solution)/shard_map/ppermute | solution.py:101
  31.7 4.4 %collective-permute-start.11 = (f32[8,512]{1,0:T(8,128)S(1)}, f32[8,512]{1,0:T(8,128)S(1)}, u32[]{:S(2)}, u32[]{:S(2)}) collective-permute-start(f32[8,512]{1,0:T(8,128)S(1)} %get-tuple-element.27), channel_id=1, source_target_pairs={{0,12},{1,13},{2,14},{3,15},{4,8},{5,9},{6,10},{7,11},{8,4},{9,5},... | collective-permute-start | bytes 49160 | tf_op jit(solution)/shard_map/ppermute | solution.py:101
  43.7 3.2 %collective-permute-start.12 = (f32[8,4,130]{0,1,2:T(4,128)S(1)}, f32[8,4,130]{0,1,2:T(4,128)S(1)}, u32[]{:S(2)}, u32[]{:S(2)}) collective-permute-start(f32[8,4,130]{0,1,2:T(4,128)S(1)} %pad_maximum_fusion), channel_id=1, source_target_pairs={{0,1},{1,0},{2,3},{3,2},{4,5},{5,4},{6,7},{7,6},{8,9},{9,8},{10,11... | collective-permute-start | bytes 49928 | tf_op jit(solution)/shard_map/ppermute | solution.py:19
  47.4 3.8 %collective-permute-start.13 = (bf16[8,128]{1,0:T(8,128)(2,1)S(1)}, bf16[8,128]{1,0:T(8,128)(2,1)S(1)}, u32[]{:S(2)}, u32[]{:S(2)}) collective-permute-start(bf16[8,128]{1,0:T(8,128)(2,1)S(1)} %bitcast.206), channel_id=1, source_target_pairs={{0,4},{1,5},{2,6},{3,7},{4,0},{5,1},{6,2},{7,3},{8,12},{9,13},{10,... | collective-permute-start | bytes 6152 | tf_op jit(solution)/shard_map/ppermute | solution.py:101
  47.5 3.7 %collective-permute-start.14 = (bf16[8,128]{1,0:T(8,128)(2,1)S(1)}, bf16[8,128]{1,0:T(8,128)(2,1)S(1)}, u32[]{:S(2)}, u32[]{:S(2)}) collective-permute-start(bf16[8,128]{1,0:T(8,128)(2,1)S(1)} %bitcast.207), channel_id=1, source_target_pairs={{0,8},{1,9},{2,10},{3,11},{4,12},{5,13},{6,14},{7,15},{8,0},{9,1},... | collective-permute-start | bytes 6152 | tf_op jit(solution)/shard_map/ppermute | solution.py:101
  49.8 4.3 %collective-permute-start.15 = (bf16[8,128]{1,0:T(8,128)(2,1)S(1)}, bf16[8,128]{1,0:T(8,128)(2,1)S(1)}, u32[]{:S(2)}, u32[]{:S(2)}) collective-permute-start(bf16[8,128]{1,0:T(8,128)(2,1)S(1)} %bitcast.208), channel_id=1, source_target_pairs={{0,12},{1,13},{2,14},{3,15},{4,8},{5,9},{6,10},{7,11},{8,4},{9,5},... | collective-permute-start | bytes 6152 | tf_op jit(solution)/shard_map/ppermute | solution.py:101
  54.2 3.9 %collective-permute-start.16 = (bf16[4,8,128]{2,1,0:T(8,128)(2,1)S(1)}, bf16[4,8,128]{2,1,0:T(8,128)(2,1)S(1)}, u32[]{:S(2)}, u32[]{:S(2)}) collective-permute-start(bf16[4,8,128]{2,1,0:T(8,128)(2,1)S(1)} %select_reduce_fusion.10), channel_id=1, source_target_pairs={{0,1},{1,0},{2,3},{3,2},{4,5},{5,4},{6,7},{7,6},{8,9},{9,8},{10,11... | collective-permute-start | bytes 24584 | tf_op jit(solution)/shard_map/ppermute | solution.py:105
  56.3 2.5 %collective-permute-start.17 = (bf16[4,8,128]{2,1,0:T(8,128)(2,1)S(1)}, bf16[4,8,128]{2,1,0:T(8,128)(2,1)S(1)}, u32[]{:S(2)}, u32[]{:S(2)}) collective-permute-start(bf16[4,8,128]{2,1,0:T(8,128)(2,1)S(1)} %select_reduce_fusion.10), channel_id=1, source_target_pairs={{0,2},{1,3},{2,0},{3,1},{4,6},{5,7},{6,4},{7,5},{8,10},{9,11},{10,... | collective-permute-start | bytes 24584 | tf_op jit(solution)/shard_map/ppermute | solution.py:105
  57.4 3.1 %collective-permute-start.18 = (bf16[4,8,128]{2,1,0:T(8,128)(2,1)S(1)}, bf16[4,8,128]{2,1,0:T(8,128)(2,1)S(1)}, u32[]{:S(2)}, u32[]{:S(2)}) collective-permute-start(bf16[4,8,128]{2,1,0:T(8,128)(2,1)S(1)} %select_reduce_fusion.10), channel_id=1, source_target_pairs={{0,3},{1,2},{2,1},{3,0},{4,7},{5,6},{6,5},{7,4},{8,11},{9,10},{10,... | collective-permute-start | bytes 24584 | tf_op jit(solution)/shard_map/ppermute | solution.py:105
  66.6 6.8 %collective-permute-start.19 = (f32[8,512]{1,0:T(8,128)S(1)}, f32[8,512]{1,0:T(8,128)S(1)}, u32[]{:S(2)}, u32[]{:S(2)}) collective-permute-start(f32[8,512]{1,0:T(8,128)S(1)} %get-tuple-element.25), channel_id=1, source_target_pairs={{0,0},{1,4},{2,8},{3,12},{4,1},{5,5},{6,9},{7,13},{8,2},{9,6},{10,... | collective-permute-start | bytes 49160 | tf_op jit(solution)/shard_map/ppermute | solution.py:264
  68.6 4.9 %collective-permute-start.20 = (f32[8,512]{1,0:T(8,128)S(1)}, f32[8,512]{1,0:T(8,128)S(1)}, u32[]{:S(2)}, u32[]{:S(2)}) collective-permute-start(f32[8,512]{1,0:T(8,128)S(1)} %get-tuple-element.22), channel_id=1, source_target_pairs={{0,1},{1,5},{2,9},{3,13},{4,0},{5,4},{6,8},{7,12},{8,3},{9,7},{10,... | collective-permute-start | bytes 49160 | tf_op jit(solution)/shard_map/ppermute | solution.py:264
  68.6 5.6 %collective-permute-start.21 = (f32[8,512]{1,0:T(8,128)S(1)}, f32[8,512]{1,0:T(8,128)S(1)}, u32[]{:S(2)}, u32[]{:S(2)}) collective-permute-start(f32[8,512]{1,0:T(8,128)S(1)} %get-tuple-element.24), channel_id=1, source_target_pairs={{0,2},{1,6},{2,10},{3,14},{4,3},{5,7},{6,11},{7,15},{8,0},{9,4},{1... | collective-permute-start | bytes 49160 | tf_op jit(solution)/shard_map/ppermute | solution.py:264
  73.1 4.1 %collective-permute-start.22 = (f32[8,512]{1,0:T(8,128)S(1)}, f32[8,512]{1,0:T(8,128)S(1)}, u32[]{:S(2)}, u32[]{:S(2)}) collective-permute-start(f32[8,512]{1,0:T(8,128)S(1)} %get-tuple-element.23), channel_id=1, source_target_pairs={{0,3},{1,7},{2,11},{3,15},{4,2},{5,6},{6,10},{7,14},{8,1},{9,5},{1... | collective-permute-start | bytes 49160 | tf_op jit(solution)/shard_map/ppermute | solution.py:264
  (1 other events, 10.0 us)

commit v7 on v6

--- a/solution.py
+++ b/solution.py
@@ -216,36 +216,29 @@
     )
     new_rounded = lax.optimization_barrier(new_weight.astype(jnp.bfloat16)).astype(jnp.float32)
     summed = summed + new_rounded[..., None] * value_new.astype(jnp.float32)[:, None, :]
-    top_split = top.reshape(ROWS, 2, GR)
-    total_split = total.reshape(ROWS, 2, GR)
-    summed_split = summed.reshape(ROWS, 2, GR, HD)
-    first_half = my_half == 0
-    own_top = jnp.where(first_half, top_split[:, 0], top_split[:, 1])
-    own_total = jnp.where(first_half, total_split[:, 0], total_split[:, 1])
-    own_summed = jnp.where(first_half, summed_split[:, 0], summed_split[:, 1])
-    give_top = jnp.where(first_half, top_split[:, 1], top_split[:, 0])
-    give_total = jnp.where(first_half, total_split[:, 1], total_split[:, 0])
-    give_summed = jnp.where(first_half, summed_split[:, 1], summed_split[:, 0])
-    give = jnp.concatenate([give_summed, give_top[..., None], give_total[..., None]], -1)
-    got = from_partner(give, "tp", 0)
-    got_summed, got_top, got_total = got[..., :HD], got[..., HD], got[..., HD + 1]
-    joint = jnp.maximum(own_top, got_top)
-    factor_own = jnp.exp(own_top - joint)
-    factor_got = jnp.exp(got_top - joint)
-    numer = own_summed * factor_own[..., None] + got_summed * factor_got[..., None]
-    denom = own_total * factor_own + got_total * factor_got
-    attention = (numer / denom[..., None]).astype(jnp.bfloat16)
-    from_rows = [lax.dynamic_index_in_dim(attention, grid_row, 1, keepdims=False)]
+    parts = jnp.concatenate([summed, top[..., None], total[..., None]], -1)
+    parts = parts.reshape(ROWS, 2, GR, HD + 2).transpose(2, 0, 1, 3)
+    from_rows = [lax.dynamic_index_in_dim(parts, grid_row, 0, keepdims=False)]
     for s in range(1, GR):
-        piece = lax.dynamic_index_in_dim(attention, grid_row ^ s, 1, keepdims=False)
+        piece = lax.dynamic_index_in_dim(parts, grid_row ^ s, 0, keepdims=False)
         from_rows.append(swap_rows(piece, "tp", col_bits, s))
-    by_row = pick(jnp.stack(from_rows), row_order)
-    if direct_cols:
-        from_cols = [by_row] + [swap_cols(by_row, "tp", s) for s in range(1, grid_cols)]
-        every_slot = pick(jnp.stack(from_cols), col_order)
-    else:
-        every_slot = gather_rounds(by_row[None], "tp", range(col_bits))
-    every_slot = every_slot.transpose(1, 0, 2, 3).reshape(group_count, ROLL, ROWS, HD)
+    mine = pick(jnp.stack(from_rows), row_order)
+    theirs = swap_cols(mine, "tp", 1)
+    even_col = grid_col % 2 == 0
+    first = jnp.where(even_col, mine, theirs)
+    second = jnp.where(even_col, theirs, mine)
+    joint = jnp.maximum(first[..., HD], second[..., HD])
+    factor_first = jnp.exp(first[..., HD] - joint)
+    factor_second = jnp.exp(second[..., HD] - joint)
+    numer = first[..., :HD] * factor_first[..., None] + second[..., :HD] * factor_second[..., None]
+    denom = first[..., HD + 1] * factor_first + second[..., HD + 1] * factor_second
+    pair_attn = (numer / denom[..., None]).astype(jnp.bfloat16)
+    if grid_cols == 4:
+        every_pair = jnp.stack([pair_attn, swap_cols(pair_attn, "tp", 2)])
+        every_pair = jnp.where(grid_col // 2 == 0, every_pair, every_pair[::-1])
+    else:
+        every_pair = gather_rounds(pair_attn[None], "tp", range(1, col_bits))
+    every_slot = every_pair.transpose(1, 0, 3, 2, 4).reshape(group_count, ROLL, ROWS, HD)
     head_ids = jnp.arange(KVH, dtype=jnp.int32)
     pair_heads = kv_assign[0::2]
     inverse = jnp.sum(

time: 78.1 us -> 80.9 us (1.036)
  the two profiles are of different devices: /device:TPU:1 before, /device:TPU:3 now
where the time goes in v7:
time: 80.9 us; the launch traced here: 80.5 us
  starting transfers between devices  29.2 us (36%)
  waiting for transfers between devices  22.1 us (27%)
  matrix products  18.4 us (23%)
  other arithmetic  6.11 us (8%)
  local copies, waits for them, and re-layouts  4.27 us (5%)
    ppermute x8, waiting for transfers between devices, swap_cols(): lax.ppermute(value, axis, [(t, t ^ s) for t in range(lax.axis_size(axis))])  11.1 us
    ppermute x9, starting transfers between devices, swap_rows(): lax.ppermute(value, axis, [(t, t ^ shift) for t in range(lax.axis_size(ax...  11 us
    ppermute x8, starting transfers between devices, swap_cols(): lax.ppermute(value, axis, [(t, t ^ s) for t in range(lax.axis_size(axis))])  9.31 us
    ppermute x4, starting transfers between devices, local(): got = lax.ppermute(piece, 'tp', pairs)  8.87 us
    ppermute x9, waiting for transfers between devices, swap_rows(): lax.ppermute(value, axis, [(t, t ^ shift) for t in range(lax.axis_size(ax...  7.13 us
    dot_general x1, matrix products, local(): jnp.einsum('rc,aec->rae', col_rows, q_blocks[0], preferred_element_type=j...  5.65 us
    dot_general x1, matrix products, local(): jnp.einsum('gabe,cae->gbc', chosen, o_blocks[0], preferred_element_type=j...  5.65 us
    ppermute x4, waiting for transfers between devices, local(): got = lax.ppermute(piece, 'tp', pairs)  3.91 us
  transfers between devices with their start and end apart: 21, of which 12 were waited for; matrix products, arithmetic and copies ran while one was open for 5% of the time, Pallas kernels for 0%

profile of v7, /device:TPU:3, one launch (start us, length us, event | category | flops | bytes accessed | tf_op | source)
XLA Modules:
  0.0 80.5 jit_solution(799755886050099795)
XLA Ops:
  0.0 2.0 %collective-permute-start.1 = (bf16[8,512]{1,0:T(8,128)(2,1)}, bf16[8,512]{1,0:T(8,128)(2,1)S(1)}, u32[]{:S(2)}, u32[]{:S(2)}) collective-permute-start(bf16[8,512]{1,0:T(8,128)(2,1)} %bitcast.184), channel_id=1, source_target_pairs={{0,2},{1,3},{2,0},{3,1},{4,6},{5,7},{6,4},{7,5},{8,10},{9,11},{10,... | collective-permute-start | bytes 24584 | tf_op jit(solution)/shard_map/ppermute | solution.py:105
  3.1 1.3 %gather_fusion.1 = s32[16]{0:T(128)S(1)} fusion(s32[16]{0:T(128)} %param.14, s32[1024]{0:T(1024)S(1)} %pad_clamp_fusion), kind=kCustom, calls=%fused_computation.1 | custom fusion | bytes 192 | tf_op jit(solution)/shard_map/gather | solution.py:128
  6.2 3.4 %collective-permute-start.5 = (bf16[4,8,512]{2,1,0:T(8,128)(2,1)S(1)}, bf16[4,8,512]{2,1,0:T(8,128)(2,1)S(1)}, u32[]{:S(2)}, u32[]{:S(2)}) collective-permute-start(bf16[4,8,512]{2,1,0:T(8,128)(2,1)S(1)} %select_reduce_fusion.7), channel_id=1, source_target_pairs={{0,12},{1,13},{2,14},{3,15},{4,8},{5,9},{6,10},{7,11},{8,4},{9,5},... | collective-permute-start | bytes 98312 | tf_op jit(solution)/shard_map/ppermute | solution.py:101
  10.0 0.9 %collective-permute-done.5 = bf16[4,8,512]{2,1,0:T(8,128)(2,1)S(1)} collective-permute-done((bf16[4,8,512]{2,1,0:T(8,128)(2,1)S(1)}, bf16[4,8,512]{2,1,0:T(8,128)(2,1)S(1)}, u32[]{:S(2)}, u32[]{:S(2)}) %collective-permute-start.5) | collective-permute-done | bytes 32800 | tf_op jit(solution)/shard_map/ppermute | solution.py:101
  10.9 2.7 %collective-permute-done.4 = bf16[4,8,512]{2,1,0:T(8,128)(2,1)S(1)} collective-permute-done((bf16[4,8,512]{2,1,0:T(8,128)(2,1)S(1)}, bf16[4,8,512]{2,1,0:T(8,128)(2,1)S(1)}, u32[]{:S(2)}, u32[]{:S(2)}) %collective-permute-start.4) | collective-permute-done | bytes 32800 | tf_op jit(solution)/shard_map/ppermute | solution.py:101
  15.6 5.7 %fusion.14 = f32[16,8,128]{2,1,0:T(8,128)S(1)} fusion(bf16[1,16,128,2048]{3,2,1,0:T(8,128)(2,1)} %param.11, bf16[8,8192]{1,0:T(8,128)(2,1)S(1)} %multiply_convert_fusion, s32[]{:T(128)S(6)} %select_n.227), kind=kOutput, calls=%fused_computation.12 | convolution fusion | flops 67108864 | bytes 8486916 | tf_op jit(solution)/shard_map/rc,aec->rae/dot_general | solution.py:152
  22.2 1.5 %collective-permute-start.6 = (f32[4,8,512]{2,1,0:T(8,128)S(1)}, f32[4,8,512]{2,1,0:T(8,128)S(1)}, u32[]{:S(2)}, u32[]{:S(2)}) collective-permute-start(f32[4,8,512]{2,1,0:T(8,128)S(1)} %get-tuple-element.16), channel_id=1, source_target_pairs={{0,1},{1,0},{2,3},{3,2},{4,5},{5,4},{6,7},{7,6},{8,9},{9,8},{10,11... | collective-permute-start | bytes 196616 | tf_op jit(solution)/shard_map/ppermute | solution.py:105
  24.0 1.2 %collective-permute-start.7 = (f32[4,8,512]{2,1,0:T(8,128)S(1)}, f32[4,8,512]{2,1,0:T(8,128)S(1)}, u32[]{:S(2)}, u32[]{:S(2)}) collective-permute-start(f32[4,8,512]{2,1,0:T(8,128)S(1)} %get-tuple-element.18), channel_id=1, source_target_pairs={{0,2},{1,3},{2,0},{3,1},{4,6},{5,7},{6,4},{7,5},{8,10},{9,11},{10,... | collective-permute-start | bytes 196616 | tf_op jit(solution)/shard_map/ppermute | solution.py:105
  25.3 2.8 %collective-permute-done.8 = f32[4,8,512]{2,1,0:T(8,128)S(1)} collective-permute-done((f32[4,8,512]{2,1,0:T(8,128)S(1)}, f32[4,8,512]{2,1,0:T(8,128)S(1)}, u32[]{:S(2)}, u32[]{:S(2)}) %collective-permute-start.8) | collective-permute-done | bytes 65568 | tf_op jit(solution)/shard_map/ppermute | solution.py:105
  28.7 1.2 %collective-permute-start.11 = (f32[8,512]{1,0:T(8,128)S(1)}, f32[8,512]{1,0:T(8,128)S(1)}, u32[]{:S(2)}, u32[]{:S(2)}) collective-permute-start(f32[8,512]{1,0:T(8,128)S(1)} %get-tuple-element.28), channel_id=1, source_target_pairs={{0,12},{1,13},{2,14},{3,15},{4,8},{5,9},{6,10},{7,11},{8,4},{9,5},... | collective-permute-start | bytes 49160 | tf_op jit(solution)/shard_map/ppermute | solution.py:101
  30.6 1.7 %collective-permute-start.9 = (f32[8,512]{1,0:T(8,128)S(1)}, f32[8,512]{1,0:T(8,128)S(1)}, u32[]{:S(2)}, u32[]{:S(2)}) collective-permute-start(f32[8,512]{1,0:T(8,128)S(1)} %get-tuple-element.30), channel_id=1, source_target_pairs={{0,4},{1,5},{2,6},{3,7},{4,0},{5,1},{6,2},{7,3},{8,12},{9,13},{10,... | collective-permute-start | bytes 49160 | tf_op jit(solution)/shard_map/ppermute | solution.py:101
  33.9 3.5 %select_reduce_fusion.4 = (f32[8,8]{1,0:T(8,128)S(1)}, f32[8,8,2048]{2,1,0:T(8,128)S(1)}) fusion(pred[8,2048]{1,0:T(8,128)(4,1)S(1)} %iota_compare_fusion, bf16[8,8,128]{2,1,0:T(8,128)(2,1)S(1)} %bitcast.170, bf16[1,8,2048,128]{3,2,1,0:T(8,128)(2,1)} %param.15), kind=kOutput, calls=%fused_computation.27 | convolution fusion | flops 33947584 | bytes 4751616 | tf_op jit(solution)/shard_map/bhe,bte->bht/dot_general | solution.py:198
  37.7 2.9 %fusion.17 = f32[8,8,128]{2,1,0:T(8,128)S(1)} fusion(bf16[1,8,2048,128]{3,2,1,0:T(8,128)(2,1)} %param.16, f32[8,8,2048]{2,1,0:T(8,128)S(1)} %get-tuple-element.45, f32[8,8]{1,0:T(8,128)S(1)} %fusion.47, pred[8,2048]{1,0:T(8,128)(4,1)S(1)} %iota_compare_fusion, f32[8,128]{1,0:T(8,128)S(1)} %get-tuple-element.41, f32[8,8]{1,0:T(8,128)S(1)} %convert_element_type.66), kind=kOutput, calls=%fused_computation.14 | convolution fusion | flops 33964032 | bytes 4772352 | tf_op jit(solution)/shard_map/bht,bte->bhe/dot_general | solution.py:211
  41.1 2.4 %collective-permute-start.14 = (f32[8,2,130]{2,0,1:T(8,128)S(1)}, f32[8,2,130]{2,0,1:T(8,128)S(1)}, u32[]{:S(2)}, u32[]{:S(2)}) collective-permute-start(f32[8,2,130]{2,0,1:T(8,128)S(1)} %get-tuple-element.24), channel_id=1, source_target_pairs={{0,12},{1,13},{2,14},{3,15},{4,8},{5,9},{6,10},{7,11},{8,4},{9,5},... | collective-permute-start | bytes 24968 | tf_op jit(solution)/shard_map/ppermute | solution.py:101
  43.6 1.1 %collective-permute-start.12 = (f32[8,2,130]{2,0,1:T(8,128)S(1)}, f32[8,2,130]{2,0,1:T(8,128)S(1)}, u32[]{:S(2)}, u32[]{:S(2)}) collective-permute-start(f32[8,2,130]{2,0,1:T(8,128)S(1)} %get-tuple-element.26), channel_id=1, source_target_pairs={{0,4},{1,5},{2,6},{3,7},{4,0},{5,1},{6,2},{7,3},{8,12},{9,13},{10,... | collective-permute-start | bytes 24968 | tf_op jit(solution)/shard_map/ppermute | solution.py:101
  45.5 1.4 %collective-permute-done.13 = f32[8,2,130]{2,0,1:T(8,128)S(1)} collective-permute-done((f32[8,2,130]{2,0,1:T(8,128)S(1)}, f32[8,2,130]{2,0,1:T(8,128)S(1)}, u32[]{:S(2)}, u32[]{:S(2)}) %collective-permute-start.13) | collective-permute-done | bytes 8352 | tf_op jit(solution)/shard_map/ppermute | solution.py:101
  47.1 3.9 %collective-permute-start.15 = (f32[4,8,2,130]{3,1,2,0:T(8,128)S(1)}, f32[4,8,2,130]{3,1,2,0:T(8,128)S(1)}, u32[]{:S(2)}, u32[]{:S(2)}) collective-permute-start(f32[4,8,2,130]{3,1,2,0:T(8,128)S(1)} %select_reduce_fusion.6), channel_id=1, source_target_pairs={{0,1},{1,0},{2,3},{3,2},{4,5},{5,4},{6,7},{7,6},{8,9},{9,8},{10,11... | collective-permute-start | bytes 99848 | tf_op jit(solution)/shard_map/ppermute | solution.py:105
  52.9 7.2 %collective-permute-done.16 = bf16[4,8,2,128]{1,0,3,2:T(4,128)(2,1)S(1)} collective-permute-done((bf16[4,8,2,128]{1,0,3,2:T(4,128)(2,1)S(1)}, bf16[4,8,2,128]{1,0,3,2:T(4,128)(2,1)S(1)}, u32[]{:S(2)}, u32[]{:S(2)}) %collective-permute-start.16) | collective-permute-done | bytes 16416 | tf_op jit(solution)/shard_map/ppermute | solution.py:105
  61.4 5.6 %fusion.11 = f32[8,4,512]{2,0,1:T(8,128)S(1)} fusion(bf16[4,512,16,128]{3,2,1,0:T(8,128)(2,1)} %bitcast.153, bf16[16,8,128]{2,1,0:T(8,128)(2,1)S(1)} %select_reduce_fusion.3), kind=kOutput, calls=%fused_computation.11 | convolution fusion | flops 67108864 | bytes 8486912 | tf_op jit(solution)/shard_map/gabe,cae->gbc/dot_general | solution.py:250
  67.1 1.2 %collective-permute-start.18 = (f32[8,512]{1,0:T(8,128)S(1)}, f32[8,512]{1,0:T(8,128)S(1)}, u32[]{:S(2)}, u32[]{:S(2)}) collective-permute-start(f32[8,512]{1,0:T(8,128)S(1)} %get-tuple-element.19), channel_id=1, source_target_pairs={{0,1},{1,5},{2,9},{3,13},{4,0},{5,4},{6,8},{7,12},{8,3},{9,7},{10,... | collective-permute-start | bytes 49160 | tf_op jit(solution)/shard_map/ppermute | solution.py:257
  68.3 1.2 %collective-permute-start.20 = (f32[8,512]{1,0:T(8,128)S(1)}, f32[8,512]{1,0:T(8,128)S(1)}, u32[]{:S(2)}, u32[]{:S(2)}) collective-permute-start(f32[8,512]{1,0:T(8,128)S(1)} %get-tuple-element.20), channel_id=1, source_target_pairs={{0,3},{1,7},{2,11},{3,15},{4,2},{5,6},{6,10},{7,14},{8,1},{9,5},{1... | collective-permute-start | bytes 49160 | tf_op jit(solution)/shard_map/ppermute | solution.py:257
  69.5 2.7 %collective-permute-start.19 = (f32[8,512]{1,0:T(8,128)S(1)}, f32[8,512]{1,0:T(8,128)S(1)}, u32[]{:S(2)}, u32[]{:S(2)}) collective-permute-start(f32[8,512]{1,0:T(8,128)S(1)} %get-tuple-element.21), channel_id=1, source_target_pairs={{0,2},{1,6},{2,10},{3,14},{4,3},{5,7},{6,11},{7,15},{8,0},{9,4},{1... | collective-permute-start | bytes 49160 | tf_op jit(solution)/shard_map/ppermute | solution.py:257
  72.2 3.8 %collective-permute-start.17 = (f32[8,512]{1,0:T(8,128)S(1)}, f32[8,512]{1,0:T(8,128)S(1)}, u32[]{:S(2)}, u32[]{:S(2)}) collective-permute-start(f32[8,512]{1,0:T(8,128)S(1)} %get-tuple-element.22), channel_id=1, source_target_pairs={{0,0},{1,4},{2,8},{3,12},{4,1},{5,5},{6,9},{7,13},{8,2},{9,6},{10,... | collective-permute-start | bytes 49160 | tf_op jit(solution)/shard_map/ppermute | solution.py:257
  76.0 3.9 %collective-permute-done.17 = f32[8,512]{1,0:T(8,128)S(1)} collective-permute-done((f32[8,512]{1,0:T(8,128)S(1)}, f32[8,512]{1,0:T(8,128)S(1)}, u32[]{:S(2)}, u32[]{:S(2)}) %collective-permute-start.17) | collective-permute-done | bytes 16416 | tf_op jit(solution)/shard_map/ppermute | solution.py:257
  (96 shorter events, 14.9 us)
Async XLA Ops:
  0.0 14.9 %copy-start = (bf16[2,1024,512]{2,1,0:T(8,128)(2,1)S(1)}, bf16[2,1024,512]{2,1,0:T(8,128)(2,1)}, u32[]{:S(2)}) copy-start(bf16[2,1024,512]{2,1,0:T(8,128)(2,1)} %param.13) | copy-start | bytes 6291460
  0.0 5.4 %collective-permute-start.2 = (bf16[8,512]{1,0:T(8,128)(2,1)}, bf16[8,512]{1,0:T(8,128)(2,1)S(1)}, u32[]{:S(2)}, u32[]{:S(2)}) collective-permute-start(bf16[8,512]{1,0:T(8,128)(2,1)} %bitcast.183), channel_id=1, source_target_pairs={{0,3},{1,2},{2,1},{3,0},{4,7},{5,6},{6,5},{7,4},{8,11},{9,10},{10,... | collective-permute-start | bytes 24584 | tf_op jit(solution)/shard_map/ppermute | solution.py:105
  0.0 5.4 %collective-permute-start.1 = (bf16[8,512]{1,0:T(8,128)(2,1)}, bf16[8,512]{1,0:T(8,128)(2,1)S(1)}, u32[]{:S(2)}, u32[]{:S(2)}) collective-permute-start(bf16[8,512]{1,0:T(8,128)(2,1)} %bitcast.184), channel_id=1, source_target_pairs={{0,2},{1,3},{2,0},{3,1},{4,6},{5,7},{6,4},{7,5},{8,10},{9,11},{10,... | collective-permute-start | bytes 24584 | tf_op jit(solution)/shard_map/ppermute | solution.py:105
  2.0 3.4 %collective-permute-start = (bf16[8,512]{1,0:T(8,128)(2,1)}, bf16[8,512]{1,0:T(8,128)(2,1)S(1)}, u32[]{:S(2)}, u32[]{:S(2)}) collective-permute-start(bf16[8,512]{1,0:T(8,128)(2,1)} %bitcast.185), channel_id=1, source_target_pairs={{0,1},{1,0},{2,3},{3,2},{4,5},{5,4},{6,7},{7,6},{8,9},{9,8},{10,11... | collective-permute-start | bytes 24584 | tf_op jit(solution)/shard_map/ppermute | solution.py:105
  6.2 4.7 %collective-permute-start.5 = (bf16[4,8,512]{2,1,0:T(8,128)(2,1)S(1)}, bf16[4,8,512]{2,1,0:T(8,128)(2,1)S(1)}, u32[]{:S(2)}, u32[]{:S(2)}) collective-permute-start(bf16[4,8,512]{2,1,0:T(8,128)(2,1)S(1)} %select_reduce_fusion.7), channel_id=1, source_target_pairs={{0,12},{1,13},{2,14},{3,15},{4,8},{5,9},{6,10},{7,11},{8,4},{9,5},... | collective-permute-start | bytes 98312 | tf_op jit(solution)/shard_map/ppermute | solution.py:101
  9.6 4.0 %collective-permute-start.4 = (bf16[4,8,512]{2,1,0:T(8,128)(2,1)S(1)}, bf16[4,8,512]{2,1,0:T(8,128)(2,1)S(1)}, u32[]{:S(2)}, u32[]{:S(2)}) collective-permute-start(bf16[4,8,512]{2,1,0:T(8,128)(2,1)S(1)} %select_reduce_fusion.7), channel_id=1, source_target_pairs={{0,8},{1,9},{2,10},{3,11},{4,12},{5,13},{6,14},{7,15},{8,0},{9,1},... | collective-permute-start | bytes 98312 | tf_op jit(solution)/shard_map/ppermute | solution.py:101
  9.6 4.0 %collective-permute-start.3 = (bf16[4,8,512]{2,1,0:T(8,128)(2,1)S(1)}, bf16[4,8,512]{2,1,0:T(8,128)(2,1)S(1)}, u32[]{:S(2)}, u32[]{:S(2)}) collective-permute-start(bf16[4,8,512]{2,1,0:T(8,128)(2,1)S(1)} %select_reduce_fusion.7), channel_id=1, source_target_pairs={{0,4},{1,5},{2,6},{3,7},{4,0},{5,1},{6,2},{7,3},{8,12},{9,13},{10,... | collective-permute-start | bytes 98312 | tf_op jit(solution)/shard_map/ppermute | solution.py:101
  15.5 9.6 %copy-start.1 = (s32[1,8]{1,0:T(1,128)S(1)}, s32[1,8]{1,0:T(1,128)}, u32[]{:S(2)}) copy-start(s32[1,8]{1,0:T(1,128)} %param.17) | copy-start | bytes 100
  22.2 3.1 %collective-permute-start.6 = (f32[4,8,512]{2,1,0:T(8,128)S(1)}, f32[4,8,512]{2,1,0:T(8,128)S(1)}, u32[]{:S(2)}, u32[]{:S(2)}) collective-permute-start(f32[4,8,512]{2,1,0:T(8,128)S(1)} %get-tuple-element.16), channel_id=1, source_target_pairs={{0,1},{1,0},{2,3},{3,2},{4,5},{5,4},{6,7},{7,6},{8,9},{9,8},{10,11... | collective-permute-start | bytes 196616 | tf_op jit(solution)/shard_map/ppermute | solution.py:105
  23.7 4.3 %collective-permute-start.8 = (f32[4,8,512]{2,1,0:T(8,128)S(1)}, f32[4,8,512]{2,1,0:T(8,128)S(1)}, u32[]{:S(2)}, u32[]{:S(2)}) collective-permute-start(f32[4,8,512]{2,1,0:T(8,128)S(1)} %get-tuple-element.17), channel_id=1, source_target_pairs={{0,3},{1,2},{2,1},{3,0},{4,7},{5,6},{6,5},{7,4},{8,11},{9,10},{10,... | collective-permute-start | bytes 196616 | tf_op jit(solution)/shard_map/ppermute | solution.py:105
  24.0 4.7 %collective-permute-start.7 = (f32[4,8,512]{2,1,0:T(8,128)S(1)}, f32[4,8,512]{2,1,0:T(8,128)S(1)}, u32[]{:S(2)}, u32[]{:S(2)}) collective-permute-start(f32[4,8,512]{2,1,0:T(8,128)S(1)} %get-tuple-element.18), channel_id=1, source_target_pairs={{0,2},{1,3},{2,0},{3,1},{4,6},{5,7},{6,4},{7,5},{8,10},{9,11},{10,... | collective-permute-start | bytes 196616 | tf_op jit(solution)/shard_map/ppermute | solution.py:105
  28.7 4.5 %collective-permute-start.11 = (f32[8,512]{1,0:T(8,128)S(1)}, f32[8,512]{1,0:T(8,128)S(1)}, u32[]{:S(2)}, u32[]{:S(2)}) collective-permute-start(f32[8,512]{1,0:T(8,128)S(1)} %get-tuple-element.28), channel_id=1, source_target_pairs={{0,12},{1,13},{2,14},{3,15},{4,8},{5,9},{6,10},{7,11},{8,4},{9,5},... | collective-permute-start | bytes 49160 | tf_op jit(solution)/shard_map/ppermute | solution.py:101
  29.9 3.5 %collective-permute-start.10 = (f32[8,512]{1,0:T(8,128)S(1)}, f32[8,512]{1,0:T(8,128)S(1)}, u32[]{:S(2)}, u32[]{:S(2)}) collective-permute-start(f32[8,512]{1,0:T(8,128)S(1)} %get-tuple-element.29), channel_id=1, source_target_pairs={{0,8},{1,9},{2,10},{3,11},{4,12},{5,13},{6,14},{7,15},{8,0},{9,1},... | collective-permute-start | bytes 49160 | tf_op jit(solution)/shard_map/ppermute | solution.py:101
  30.6 3.0 %collective-permute-start.9 = (f32[8,512]{1,0:T(8,128)S(1)}, f32[8,512]{1,0:T(8,128)S(1)}, u32[]{:S(2)}, u32[]{:S(2)}) collective-permute-start(f32[8,512]{1,0:T(8,128)S(1)} %get-tuple-element.30), channel_id=1, source_target_pairs={{0,4},{1,5},{2,6},{3,7},{4,0},{5,1},{6,2},{7,3},{8,12},{9,13},{10,... | collective-permute-start | bytes 49160 | tf_op jit(solution)/shard_map/ppermute | solution.py:101
  41.1 4.5 %collective-permute-start.14 = (f32[8,2,130]{2,0,1:T(8,128)S(1)}, f32[8,2,130]{2,0,1:T(8,128)S(1)}, u32[]{:S(2)}, u32[]{:S(2)}) collective-permute-start(f32[8,2,130]{2,0,1:T(8,128)S(1)} %get-tuple-element.24), channel_id=1, source_target_pairs={{0,12},{1,13},{2,14},{3,15},{4,8},{5,9},{6,10},{7,11},{8,4},{9,5},... | collective-permute-start | bytes 24968 | tf_op jit(solution)/shard_map/ppermute | solution.py:101
  43.5 3.5 %collective-permute-start.13 = (f32[8,2,130]{2,0,1:T(8,128)S(1)}, f32[8,2,130]{2,0,1:T(8,128)S(1)}, u32[]{:S(2)}, u32[]{:S(2)}) collective-permute-start(f32[8,2,130]{2,0,1:T(8,128)S(1)} %get-tuple-element.25), channel_id=1, source_target_pairs={{0,8},{1,9},{2,10},{3,11},{4,12},{5,13},{6,14},{7,15},{8,0},{9,1},... | collective-permute-start | bytes 24968 | tf_op jit(solution)/shard_map/ppermute | solution.py:101
  43.6 3.3 %collective-permute-start.12 = (f32[8,2,130]{2,0,1:T(8,128)S(1)}, f32[8,2,130]{2,0,1:T(8,128)S(1)}, u32[]{:S(2)}, u32[]{:S(2)}) collective-permute-start(f32[8,2,130]{2,0,1:T(8,128)S(1)} %get-tuple-element.26), channel_id=1, source_target_pairs={{0,4},{1,5},{2,6},{3,7},{4,0},{5,1},{6,2},{7,3},{8,12},{9,13},{10,... | collective-permute-start | bytes 24968 | tf_op jit(solution)/shard_map/ppermute | solution.py:101
  47.1 4.8 %collective-permute-start.15 = (f32[4,8,2,130]{3,1,2,0:T(8,128)S(1)}, f32[4,8,2,130]{3,1,2,0:T(8,128)S(1)}, u32[]{:S(2)}, u32[]{:S(2)}) collective-permute-start(f32[4,8,2,130]{3,1,2,0:T(8,128)S(1)} %select_reduce_fusion.6), channel_id=1, source_target_pairs={{0,1},{1,0},{2,3},{3,2},{4,5},{5,4},{6,7},{7,6},{8,9},{9,8},{10,11... | collective-permute-start | bytes 99848 | tf_op jit(solution)/shard_map/ppermute | solution.py:105
  52.5 7.6 %collective-permute-start.16 = (bf16[4,8,2,128]{1,0,3,2:T(4,128)(2,1)S(1)}, bf16[4,8,2,128]{1,0,3,2:T(4,128)(2,1)S(1)}, u32[]{:S(2)}, u32[]{:S(2)}) collective-permute-start(bf16[4,8,2,128]{1,0,3,2:T(4,128)(2,1)S(1)} %fusion.23), channel_id=1, source_target_pairs={{0,2},{1,3},{2,0},{3,1},{4,6},{5,7},{6,4},{7,5},{8,10},{9,11},{10,... | collective-permute-start | bytes 49160 | tf_op jit(solution)/shard_map/ppermute | solution.py:105
  67.1 8.9 %collective-permute-start.18 = (f32[8,512]{1,0:T(8,128)S(1)}, f32[8,512]{1,0:T(8,128)S(1)}, u32[]{:S(2)}, u32[]{:S(2)}) collective-permute-start(f32[8,512]{1,0:T(8,128)S(1)} %get-tuple-element.19), channel_id=1, source_target_pairs={{0,1},{1,5},{2,9},{3,13},{4,0},{5,4},{6,8},{7,12},{8,3},{9,7},{10,... | collective-permute-start | bytes 49160 | tf_op jit(solution)/shard_map/ppermute | solution.py:257
  68.3 7.7 %collective-permute-start.20 = (f32[8,512]{1,0:T(8,128)S(1)}, f32[8,512]{1,0:T(8,128)S(1)}, u32[]{:S(2)}, u32[]{:S(2)}) collective-permute-start(f32[8,512]{1,0:T(8,128)S(1)} %get-tuple-element.20), channel_id=1, source_target_pairs={{0,3},{1,7},{2,11},{3,15},{4,2},{5,6},{6,10},{7,14},{8,1},{9,5},{1... | collective-permute-start | bytes 49160 | tf_op jit(solution)/shard_map/ppermute | solution.py:257
  69.5 6.5 %collective-permute-start.19 = (f32[8,512]{1,0:T(8,128)S(1)}, f32[8,512]{1,0:T(8,128)S(1)}, u32[]{:S(2)}, u32[]{:S(2)}) collective-permute-start(f32[8,512]{1,0:T(8,128)S(1)} %get-tuple-element.21), channel_id=1, source_target_pairs={{0,2},{1,6},{2,10},{3,14},{4,3},{5,7},{6,11},{7,15},{8,0},{9,4},{1... | collective-permute-start | bytes 49160 | tf_op jit(solution)/shard_map/ppermute | solution.py:257
  72.2 7.7 %collective-permute-start.17 = (f32[8,512]{1,0:T(8,128)S(1)}, f32[8,512]{1,0:T(8,128)S(1)}, u32[]{:S(2)}, u32[]{:S(2)}) collective-permute-start(f32[8,512]{1,0:T(8,128)S(1)} %get-tuple-element.22), channel_id=1, source_target_pairs={{0,0},{1,4},{2,8},{3,12},{4,1},{5,5},{6,9},{7,13},{8,2},{9,6},{10,... | collective-permute-start | bytes 49160 | tf_op jit(solution)/shard_map/ppermute | solution.py:257

commit v8 on v6

--- a/solution.py
+++ b/solution.py
@@ -125,7 +125,7 @@
     grid_col = my_index % grid_cols
     dest_ids = jnp.arange(ranks, dtype=jnp.int32)
     dest_rank = dest_ids % ROLL
-    dest_head = kv_assign[dest_rank]
+    dest_head = pick(kv_assign, dest_rank)
     dest_group = 2 * dest_head + dest_rank % 2
     dest_copy = dest_ids // ROLL
     bits = ranks.bit_length() - 1
@@ -134,21 +134,37 @@
     row_order = jnp.arange(GR, dtype=jnp.int32) ^ grid_row
     col_order = jnp.arange(grid_cols, dtype=jnp.int32) ^ grid_col
     direct_cols = grid_cols <= 4
+    fast_norm = direct_cols and group_count == 1 and GR == grid_cols and col_width == grid_cols * DS
+    fast_norm = fast_norm and key_width == DS
     if direct_cols:
         from_cols = [hidden_in[0]] + [swap_cols(hidden_in[0], "tp", s) for s in range(1, grid_cols)]
-        in_row = pick(jnp.stack(from_cols), col_order)
+        in_row = jnp.stack(from_cols)
+        if not fast_norm:
+            in_row = pick(in_row, col_order)
     else:
         in_row = gather_rounds(hidden_in, "tp", range(col_bits))
     from_rows = [in_row] + [swap_rows(in_row, "tp", col_bits, s) for s in range(1, GR)]
-    every_rows = pick(jnp.stack(from_rows), row_order).reshape(ranks, ROWS, DS)
-    rows_float = (
-        every_rows.reshape(group_count, ROLL, ROWS, DS)
-        .transpose(0, 2, 1, 3)
-        .reshape(group_count * ROWS, D)
-        .astype(jnp.float32)
-    )
-    normed_every = norm_rows(rows_float, norm_gain)
-    col_rows = lax.dynamic_slice_in_dim(normed_every, grid_col * col_width, col_width, 1)
+    if fast_norm:
+        arrived = jnp.stack(from_rows).astype(jnp.float32)
+        mean_square = jnp.sum(arrived * arrived, axis=(0, 1, 3))[:, None] / D
+        scale_rows = lax.rsqrt(mean_square + 1e-05)
+        col_x = pick(lax.dynamic_index_in_dim(arrived, grid_row ^ grid_col, 0, keepdims=False), col_order)
+        col_x = col_x.transpose(1, 0, 2).reshape(ROWS, col_width)
+        col_gain = lax.dynamic_slice_in_dim(norm_gain, grid_col * col_width, col_width)
+        col_rows = (col_x * scale_rows * col_gain[None, :]).astype(jnp.bfloat16)
+        own_gain = lax.dynamic_slice_in_dim(norm_gain, my_index * key_width, key_width)
+        key_rows = (hidden_in[0].astype(jnp.float32) * scale_rows * own_gain[None, :]).astype(jnp.bfloat16)
+    else:
+        every_rows = pick(jnp.stack(from_rows), row_order).reshape(ranks, ROWS, DS)
+        rows_float = (
+            every_rows.reshape(group_count, ROLL, ROWS, DS)
+            .transpose(0, 2, 1, 3)
+            .reshape(group_count * ROWS, D)
+            .astype(jnp.float32)
+        )
+        normed_every = norm_rows(rows_float, norm_gain)
+        col_rows = lax.dynamic_slice_in_dim(normed_every, grid_col * col_width, col_width, 1)
+        key_rows = lax.dynamic_slice_in_dim(normed_every, my_index * key_width, key_width, 1)
     query_part = jnp.einsum(
         "rc,aec->rae", col_rows, q_blocks[0], preferred_element_type=jnp.float32
     )
@@ -157,9 +173,8 @@
         .transpose(0, 2, 1, 3)
         .reshape(group_count * QG, ROWS, HD)
     )
-    pair_first = dest_copy * QG + 2 * dest_head
-    query_pick = jnp.concatenate([pick(query_part, pair_first), pick(query_part, pair_first + 1)], -1)
-    key_rows = lax.dynamic_slice_in_dim(normed_every, my_index * key_width, key_width, 1)
+    query_pairs = pick(query_part.reshape(group_count * KVH, 2, ROWS, HD), dest_copy * KVH + dest_head)
+    query_pick = query_pairs.transpose(0, 2, 1, 3).reshape(ranks, ROWS, 2 * HD)
     keyval_part = jnp.einsum("rc,kfc->rkf", key_rows, kv_blocks, preferred_element_type=jnp.float32)
     keyval_part = (
         keyval_part.reshape(group_count, ROWS, 2, KVH, HD)
@@ -247,12 +262,12 @@
         every_slot = gather_rounds(by_row[None], "tp", range(col_bits))
     every_slot = every_slot.transpose(1, 0, 2, 3).reshape(group_count, ROLL, ROWS, HD)
     head_ids = jnp.arange(KVH, dtype=jnp.int32)
-    pair_heads = kv_assign[0::2]
+    pair_heads = kv_assign.reshape(KVH, 2)[:, 0]
     inverse = jnp.sum(
         head_ids[None, :] * (pair_heads[None, :] == head_ids[:, None]).astype(jnp.int32), axis=1
     )
     slot_ids = jnp.arange(QG, dtype=jnp.int32)
-    rank_of_slot = 2 * inverse[slot_ids // 2] + slot_ids % 2
+    rank_of_slot = 2 * jnp.broadcast_to(inverse[:, None], (KVH, 2)).reshape(QG) + slot_ids % 2
     chosen = jax.vmap(lambda per_group: pick(per_group, rank_of_slot))(every_slot)
     out_part = jnp.einsum("gabe,cae->gbc", chosen, o_blocks[0], preferred_element_type=jnp.float32)
     if group_count == 1 and grid_cols == GR and col_width == GR * DS:

time: 78.1 us -> 78.4 us (level)
    gather x2 -> x0, local copies, waits for them, and re-layouts: 1.98 us -> none  [the longest x1 1.32 us: local(): dest_head = kv_assign[dest_rank]]
    dynamic_slice x0 -> x2, local copies, waits for them, and re-layouts: none -> 1.46 us  [the longest x1 0.76 us: local(): lax.dynamic_slice_in_dim(norm_gain, my_index * key_width, key_width)]
    ppermute x9, starting transfers between devices: 11.8 us -> 10.9 us  [swap_rows(): lax.ppermute(value, axis, [(t, t ^ shift) for t in range(lax.axis_size(ax...]
  transfers between devices with their start and end apart: 23 -> 23, of which waited for: 13 -> 14; matrix products, arithmetic and copies ran while one was open for 5% -> 6% of each run, Pallas kernels for 0% -> 0%
where the time goes in v8:
time: 78.4 us; the launch traced here: 78 us
  starting transfers between devices  30.3 us (39%)
  waiting for transfers between devices  19.3 us (25%)
  matrix products  19.1 us (24%)
  other arithmetic  5.4 us (7%)
  local copies, waits for them, and re-layouts  3.56 us (5%)
    ppermute x9, starting transfers between devices, swap_rows(): lax.ppermute(value, axis, [(t, t ^ shift) for t in range(lax.axis_size(ax...  10.9 us
    ppermute x9, starting transfers between devices, swap_cols(): lax.ppermute(value, axis, [(t, t ^ s) for t in range(lax.axis_size(axis))])  10.4 us
    ppermute x9, waiting for transfers between devices, swap_rows(): lax.ppermute(value, axis, [(t, t ^ shift) for t in range(lax.axis_size(ax...  8.44 us
    ppermute x4, starting transfers between devices, local(): got = lax.ppermute(piece, 'tp', pairs)  6.9 us
    ppermute x9, waiting for transfers between devices, swap_cols(): lax.ppermute(value, axis, [(t, t ^ s) for t in range(lax.axis_size(axis))])  6.08 us
    dot_general x1, matrix products, local(): jnp.einsum('gabe,cae->gbc', chosen, o_blocks[0], preferred_element_type=j...  5.65 us
    dot_general x1, matrix products, local(): jnp.einsum('rc,aec->rae', col_rows, q_blocks[0], preferred_element_type=j...  5.64 us
    ppermute x4, waiting for transfers between devices, local(): got = lax.ppermute(piece, 'tp', pairs)  3.67 us
  transfers between devices with their start and end apart: 23, of which 14 were waited for; matrix products, arithmetic and copies ran while one was open for 6% of the time, Pallas kernels for 0%

profile of v8, /device:TPU:1, one launch (start us, length us, event | category | flops | bytes accessed | tf_op | source)
XLA Modules:
  0.0 78.0 jit_solution(6897126575761216713)
XLA Ops:
  0.1 2.7 %collective-permute-start.1 = (bf16[8,512]{1,0:T(8,128)(2,1)}, bf16[8,512]{1,0:T(8,128)(2,1)S(1)}, u32[]{:S(2)}, u32[]{:S(2)}) collective-permute-start(bf16[8,512]{1,0:T(8,128)(2,1)} %bitcast.202), channel_id=1, source_target_pairs={{0,2},{1,3},{2,0},{3,1},{4,6},{5,7},{6,4},{7,5},{8,10},{9,11},{10,... | collective-permute-start | bytes 24584 | tf_op jit(solution)/shard_map/ppermute | solution.py:105
  6.7 1.4 %collective-permute-start.3 = (bf16[4,8,512]{2,1,0:T(8,128)(2,1)S(1)}, bf16[4,8,512]{2,1,0:T(8,128)(2,1)S(1)}, u32[]{:S(2)}, u32[]{:S(2)}) collective-permute-start(bf16[4,8,512]{2,1,0:T(8,128)(2,1)S(1)} %get-tuple-element.29), channel_id=1, source_target_pairs={{0,4},{1,5},{2,6},{3,7},{4,0},{5,1},{6,2},{7,3},{8,12},{9,13},{10,... | collective-permute-start | bytes 98312 | tf_op jit(solution)/shard_map/ppermute | solution.py:101
  8.1 2.3 %collective-permute-start.4 = (bf16[4,8,512]{2,1,0:T(8,128)(2,1)S(1)}, bf16[4,8,512]{2,1,0:T(8,128)(2,1)S(1)}, u32[]{:S(2)}, u32[]{:S(2)}) collective-permute-start(bf16[4,8,512]{2,1,0:T(8,128)(2,1)S(1)} %get-tuple-element.29), channel_id=1, source_target_pairs={{0,8},{1,9},{2,10},{3,11},{4,12},{5,13},{6,14},{7,15},{8,0},{9,1},... | collective-permute-start | bytes 98312 | tf_op jit(solution)/shard_map/ppermute | solution.py:101
  12.1 2.9 %collective-permute-done.5 = bf16[4,8,512]{2,1,0:T(8,128)(2,1)S(1)} collective-permute-done((bf16[4,8,512]{2,1,0:T(8,128)(2,1)S(1)}, bf16[4,8,512]{2,1,0:T(8,128)(2,1)S(1)}, u32[]{:S(2)}, u32[]{:S(2)}) %collective-permute-start.5) | collective-permute-done | bytes 32800 | tf_op jit(solution)/shard_map/ppermute | solution.py:101
  15.2 1.3 %convolution_bitcast_fusion = f32[1,8,8,2,128]{4,2,1,3,0:T(8,128)S(1)} fusion(bf16[2,8,128,512]{3,2,1,0:T(8,128)(2,1)S(1)} %bitcast.177, bf16[1,8,512]{2,1,0:T(8,128)(2,1)} %param.9, f32[512]{0:T(512)S(1)} %dynamic_slice.64, f32[8]{0:T(128)S(1)} %add_rsqrt_fusion), kind=kOutput, calls=%fused_computation.10 | convolution fusion | flops 16793600 | bytes 2172960 | tf_op jit(solution)/shard_map/rc,kfc->rkf/dot_general | solution.py:178
  16.8 5.6 %fusion = f32[8,16,128]{2,0,1:T(8,128)S(1)} fusion(bf16[8,2048,1]{1,0,2:T(8,128)(2,1)S(1)} %bitcast.186, bf16[1,16,128,2048]{3,2,1,0:T(8,128)(2,1)} %param.11), kind=kOutput, calls=%fused_computation | convolution fusion | flops 67108864 | bytes 8486912 | tf_op jit(solution)/shard_map/rc,aec->rae/dot_general | solution.py:168
  22.9 2.0 %collective-permute-start.6 = (f32[4,8,512]{2,1,0:T(8,128)S(1)}, f32[4,8,512]{2,1,0:T(8,128)S(1)}, u32[]{:S(2)}, u32[]{:S(2)}) collective-permute-start(f32[4,8,512]{2,1,0:T(8,128)S(1)} %get-tuple-element.11), channel_id=1, source_target_pairs={{0,1},{1,0},{2,3},{3,2},{4,5},{5,4},{6,7},{7,6},{8,9},{9,8},{10,11... | collective-permute-start | bytes 196616 | tf_op jit(solution)/shard_map/ppermute | solution.py:105
  24.9 1.1 %collective-permute-start.7 = (f32[4,8,512]{2,1,0:T(8,128)S(1)}, f32[4,8,512]{2,1,0:T(8,128)S(1)}, u32[]{:S(2)}, u32[]{:S(2)}) collective-permute-start(f32[4,8,512]{2,1,0:T(8,128)S(1)} %get-tuple-element.12), channel_id=1, source_target_pairs={{0,2},{1,3},{2,0},{3,1},{4,6},{5,7},{6,4},{7,5},{8,10},{9,11},{10,... | collective-permute-start | bytes 196616 | tf_op jit(solution)/shard_map/ppermute | solution.py:105
  26.7 1.9 %collective-permute-done.7 = f32[4,8,512]{2,1,0:T(8,128)S(1)} collective-permute-done((f32[4,8,512]{2,1,0:T(8,128)S(1)}, f32[4,8,512]{2,1,0:T(8,128)S(1)}, u32[]{:S(2)}, u32[]{:S(2)}) %collective-permute-start.7) | collective-permute-done | bytes 65568 | tf_op jit(solution)/shard_map/ppermute | solution.py:105
  28.6 1.6 %collective-permute-done.8 = f32[4,8,512]{2,1,0:T(8,128)S(1)} collective-permute-done((f32[4,8,512]{2,1,0:T(8,128)S(1)}, f32[4,8,512]{2,1,0:T(8,128)S(1)}, u32[]{:S(2)}, u32[]{:S(2)}) %collective-permute-start.8) | collective-permute-done | bytes 65568 | tf_op jit(solution)/shard_map/ppermute | solution.py:105
  30.6 3.1 %collective-permute-start.11 = (f32[8,512]{1,0:T(8,128)S(1)}, f32[8,512]{1,0:T(8,128)S(1)}, u32[]{:S(2)}, u32[]{:S(2)}) collective-permute-start(f32[8,512]{1,0:T(8,128)S(1)} %get-tuple-element.23), channel_id=1, source_target_pairs={{0,12},{1,13},{2,14},{3,15},{4,8},{5,9},{6,10},{7,11},{8,4},{9,5},... | collective-permute-start | bytes 49160 | tf_op jit(solution)/shard_map/ppermute | solution.py:101
  33.9 1.2 %collective-permute-done.11 = f32[8,512]{1,0:T(8,128)S(1)} collective-permute-done((f32[8,512]{1,0:T(8,128)S(1)}, f32[8,512]{1,0:T(8,128)S(1)}, u32[]{:S(2)}, u32[]{:S(2)}) %collective-permute-start.11) | collective-permute-done | bytes 16416 | tf_op jit(solution)/shard_map/ppermute | solution.py:101
  35.4 3.5 %select_reduce_fusion.3 = (f32[8,8]{1,0:T(8,128)S(1)}, f32[8,8,2048]{2,1,0:T(8,128)S(1)}) fusion(pred[8,2048]{1,0:T(8,128)(4,1)S(1)} %iota_compare_fusion, bf16[8,8,128]{2,1,0:T(8,128)(2,1)S(1)} %bitcast.196, bf16[1,8,2048,128]{3,2,1,0:T(8,128)(2,1)} %param.15), kind=kOutput, calls=%fused_computation.16 | convolution fusion | flops 33947584 | bytes 4751616 | tf_op jit(solution)/shard_map/bhe,bte->bht/dot_general | solution.py:213
  39.2 2.9 %fusion.14 = f32[8,8,128]{2,1,0:T(8,128)S(1)} fusion(bf16[1,8,2048,128]{3,2,1,0:T(8,128)(2,1)} %param.16, f32[8,8,2048]{2,1,0:T(8,128)S(1)} %get-tuple-element.43, f32[8,8]{1,0:T(8,128)S(1)} %fusion.46, pred[8,2048]{1,0:T(8,128)(4,1)S(1)} %iota_compare_fusion, f32[8,128]{1,0:T(8,128)S(1)} %get-tuple-element.40, f32[8,8]{1,0:T(8,128)S(1)} %convert_element_type.66), kind=kOutput, calls=%fused_computation.11 | convolution fusion | flops 33964032 | bytes 4772352 | tf_op jit(solution)/shard_map/bht,bte->bhe/dot_general | solution.py:226
  42.7 2.1 %collective-permute-start.12 = (f32[8,4,130]{0,1,2:T(4,128)S(1)}, f32[8,4,130]{0,1,2:T(4,128)S(1)}, u32[]{:S(2)}, u32[]{:S(2)}) collective-permute-start(f32[8,4,130]{0,1,2:T(4,128)S(1)} %pad_maximum_fusion), channel_id=1, source_target_pairs={{0,1},{1,0},{2,3},{3,2},{4,5},{5,4},{6,7},{7,6},{8,9},{9,8},{10,11... | collective-permute-start | bytes 49928 | tf_op jit(solution)/shard_map/ppermute | solution.py:19
  44.8 1.2 %collective-permute-done.12 = f32[8,4,130]{0,1,2:T(4,128)S(1)} collective-permute-done((f32[8,4,130]{0,1,2:T(4,128)S(1)}, f32[8,4,130]{0,1,2:T(4,128)S(1)}, u32[]{:S(2)}, u32[]{:S(2)}) %collective-permute-start.12) | collective-permute-done | bytes 16672 | tf_op jit(solution)/shard_map/ppermute | solution.py:19
  46.6 3.4 %collective-permute-start.14 = (bf16[8,128]{1,0:T(8,128)(2,1)S(1)}, bf16[8,128]{1,0:T(8,128)(2,1)S(1)}, u32[]{:S(2)}, u32[]{:S(2)}) collective-permute-start(bf16[8,128]{1,0:T(8,128)(2,1)S(1)} %bitcast.217), channel_id=1, source_target_pairs={{0,8},{1,9},{2,10},{3,11},{4,12},{5,13},{6,14},{7,15},{8,0},{9,1},... | collective-permute-start | bytes 6152 | tf_op jit(solution)/shard_map/ppermute | solution.py:101
  51.0 3.4 %collective-permute-done.15 = bf16[8,128]{1,0:T(8,128)(2,1)S(1)} collective-permute-done((bf16[8,128]{1,0:T(8,128)(2,1)S(1)}, bf16[8,128]{1,0:T(8,128)(2,1)S(1)}, u32[]{:S(2)}, u32[]{:S(2)}) %collective-permute-start.15) | collective-permute-done | bytes 2080 | tf_op jit(solution)/shard_map/ppermute | solution.py:101
  54.4 2.1 %collective-permute-start.16 = (bf16[4,8,128]{2,1,0:T(8,128)(2,1)S(1)}, bf16[4,8,128]{2,1,0:T(8,128)(2,1)S(1)}, u32[]{:S(2)}, u32[]{:S(2)}) collective-permute-start(bf16[4,8,128]{2,1,0:T(8,128)(2,1)S(1)} %select_reduce_fusion.8), channel_id=1, source_target_pairs={{0,1},{1,0},{2,3},{3,2},{4,5},{5,4},{6,7},{7,6},{8,9},{9,8},{10,11... | collective-permute-start | bytes 24584 | tf_op jit(solution)/shard_map/ppermute | solution.py:105
  59.1 1.6 %collective-permute-done.18 = bf16[4,8,128]{2,1,0:T(8,128)(2,1)S(1)} collective-permute-done((bf16[4,8,128]{2,1,0:T(8,128)(2,1)S(1)}, bf16[4,8,128]{2,1,0:T(8,128)(2,1)S(1)}, u32[]{:S(2)}, u32[]{:S(2)}) %collective-permute-start.18) | collective-permute-done | bytes 8224 | tf_op jit(solution)/shard_map/ppermute | solution.py:105
  61.1 5.6 %fusion.11 = f32[8,4,512]{2,0,1:T(8,128)S(1)} fusion(bf16[4,512,16,128]{3,2,1,0:T(8,128)(2,1)} %bitcast.178, bf16[16,8,128]{2,1,0:T(8,128)(2,1)S(1)} %select_reduce_fusion.2), kind=kOutput, calls=%fused_computation.9 | convolution fusion | flops 67108864 | bytes 8486912 | tf_op jit(solution)/shard_map/gabe,cae->gbc/dot_general | solution.py:272
  66.8 1.9 %collective-permute-start.19 = (f32[8,512]{1,0:T(8,128)S(1)}, f32[8,512]{1,0:T(8,128)S(1)}, u32[]{:S(2)}, u32[]{:S(2)}) collective-permute-start(f32[8,512]{1,0:T(8,128)S(1)} %get-tuple-element.21), channel_id=1, source_target_pairs={{0,0},{1,4},{2,8},{3,12},{4,1},{5,5},{6,9},{7,13},{8,2},{9,6},{10,... | collective-permute-start | bytes 49160 | tf_op jit(solution)/shard_map/ppermute | solution.py:279
  68.8 4.5 %collective-permute-start.21 = (f32[8,512]{1,0:T(8,128)S(1)}, f32[8,512]{1,0:T(8,128)S(1)}, u32[]{:S(2)}, u32[]{:S(2)}) collective-permute-start(f32[8,512]{1,0:T(8,128)S(1)} %get-tuple-element.20), channel_id=1, source_target_pairs={{0,2},{1,6},{2,10},{3,14},{4,3},{5,7},{6,11},{7,15},{8,0},{9,4},{1... | collective-permute-start | bytes 49160 | tf_op jit(solution)/shard_map/ppermute | solution.py:279
  74.4 3.0 %collective-permute-done.22 = f32[8,512]{1,0:T(8,128)S(1)} collective-permute-done((f32[8,512]{1,0:T(8,128)S(1)}, f32[8,512]{1,0:T(8,128)S(1)}, u32[]{:S(2)}, u32[]{:S(2)}) %collective-permute-start.22) | collective-permute-done | bytes 16416 | tf_op jit(solution)/shard_map/ppermute | solution.py:279
  (102 shorter events, 15.3 us)
Async XLA Ops:
  0.0 15.2 %copy-start = (bf16[2,1024,512]{2,1,0:T(8,128)(2,1)S(1)}, bf16[2,1024,512]{2,1,0:T(8,128)(2,1)}, u32[]{:S(2)}) copy-start(bf16[2,1024,512]{2,1,0:T(8,128)(2,1)} %param.13) | copy-start | bytes 6291460
  0.0 5.7 %collective-permute-start = (bf16[8,512]{1,0:T(8,128)(2,1)}, bf16[8,512]{1,0:T(8,128)(2,1)S(1)}, u32[]{:S(2)}, u32[]{:S(2)}) collective-permute-start(bf16[8,512]{1,0:T(8,128)(2,1)} %bitcast.201), channel_id=1, source_target_pairs={{0,1},{1,0},{2,3},{3,2},{4,5},{5,4},{6,7},{7,6},{8,9},{9,8},{10,11... | collective-permute-start | bytes 24584 | tf_op jit(solution)/shard_map/ppermute | solution.py:105
  0.1 5.6 %collective-permute-start.1 = (bf16[8,512]{1,0:T(8,128)(2,1)}, bf16[8,512]{1,0:T(8,128)(2,1)S(1)}, u32[]{:S(2)}, u32[]{:S(2)}) collective-permute-start(bf16[8,512]{1,0:T(8,128)(2,1)} %bitcast.202), channel_id=1, source_target_pairs={{0,2},{1,3},{2,0},{3,1},{4,6},{5,7},{6,4},{7,5},{8,10},{9,11},{10,... | collective-permute-start | bytes 24584 | tf_op jit(solution)/shard_map/ppermute | solution.py:105
  2.7 3.3 %collective-permute-start.2 = (bf16[8,512]{1,0:T(8,128)(2,1)}, bf16[8,512]{1,0:T(8,128)(2,1)S(1)}, u32[]{:S(2)}, u32[]{:S(2)}) collective-permute-start(bf16[8,512]{1,0:T(8,128)(2,1)} %bitcast.203), channel_id=1, source_target_pairs={{0,3},{1,2},{2,1},{3,0},{4,7},{5,6},{6,5},{7,4},{8,11},{9,10},{10,... | collective-permute-start | bytes 24584 | tf_op jit(solution)/shard_map/ppermute | solution.py:105
  6.7 5.2 %collective-permute-start.3 = (bf16[4,8,512]{2,1,0:T(8,128)(2,1)S(1)}, bf16[4,8,512]{2,1,0:T(8,128)(2,1)S(1)}, u32[]{:S(2)}, u32[]{:S(2)}) collective-permute-start(bf16[4,8,512]{2,1,0:T(8,128)(2,1)S(1)} %get-tuple-element.29), channel_id=1, source_target_pairs={{0,4},{1,5},{2,6},{3,7},{4,0},{5,1},{6,2},{7,3},{8,12},{9,13},{10,... | collective-permute-start | bytes 98312 | tf_op jit(solution)/shard_map/ppermute | solution.py:101
  8.1 4.0 %collective-permute-start.4 = (bf16[4,8,512]{2,1,0:T(8,128)(2,1)S(1)}, bf16[4,8,512]{2,1,0:T(8,128)(2,1)S(1)}, u32[]{:S(2)}, u32[]{:S(2)}) collective-permute-start(bf16[4,8,512]{2,1,0:T(8,128)(2,1)S(1)} %get-tuple-element.29), channel_id=1, source_target_pairs={{0,8},{1,9},{2,10},{3,11},{4,12},{5,13},{6,14},{7,15},{8,0},{9,1},... | collective-permute-start | bytes 98312 | tf_op jit(solution)/shard_map/ppermute | solution.py:101
  10.4 4.6 %collective-permute-start.5 = (bf16[4,8,512]{2,1,0:T(8,128)(2,1)S(1)}, bf16[4,8,512]{2,1,0:T(8,128)(2,1)S(1)}, u32[]{:S(2)}, u32[]{:S(2)}) collective-permute-start(bf16[4,8,512]{2,1,0:T(8,128)(2,1)S(1)} %get-tuple-element.29), channel_id=1, source_target_pairs={{0,12},{1,13},{2,14},{3,15},{4,8},{5,9},{6,10},{7,11},{8,4},{9,5},... | collective-permute-start | bytes 98312 | tf_op jit(solution)/shard_map/ppermute | solution.py:101
  22.9 3.8 %collective-permute-start.6 = (f32[4,8,512]{2,1,0:T(8,128)S(1)}, f32[4,8,512]{2,1,0:T(8,128)S(1)}, u32[]{:S(2)}, u32[]{:S(2)}) collective-permute-start(f32[4,8,512]{2,1,0:T(8,128)S(1)} %get-tuple-element.11), channel_id=1, source_target_pairs={{0,1},{1,0},{2,3},{3,2},{4,5},{5,4},{6,7},{7,6},{8,9},{9,8},{10,11... | collective-permute-start | bytes 196616 | tf_op jit(solution)/shard_map/ppermute | solution.py:105
  24.9 3.7 %collective-permute-start.7 = (f32[4,8,512]{2,1,0:T(8,128)S(1)}, f32[4,8,512]{2,1,0:T(8,128)S(1)}, u32[]{:S(2)}, u32[]{:S(2)}) collective-permute-start(f32[4,8,512]{2,1,0:T(8,128)S(1)} %get-tuple-element.12), channel_id=1, source_target_pairs={{0,2},{1,3},{2,0},{3,1},{4,6},{5,7},{6,4},{7,5},{8,10},{9,11},{10,... | collective-permute-start | bytes 196616 | tf_op jit(solution)/shard_map/ppermute | solution.py:105
  26.0 4.1 %collective-permute-start.8 = (f32[4,8,512]{2,1,0:T(8,128)S(1)}, f32[4,8,512]{2,1,0:T(8,128)S(1)}, u32[]{:S(2)}, u32[]{:S(2)}) collective-permute-start(f32[4,8,512]{2,1,0:T(8,128)S(1)} %get-tuple-element.13), channel_id=1, source_target_pairs={{0,3},{1,2},{2,1},{3,0},{4,7},{5,6},{6,5},{7,4},{8,11},{9,10},{10,... | collective-permute-start | bytes 196616 | tf_op jit(solution)/shard_map/ppermute | solution.py:105
  30.2 3.6 %collective-permute-start.9 = (f32[8,512]{1,0:T(8,128)S(1)}, f32[8,512]{1,0:T(8,128)S(1)}, u32[]{:S(2)}, u32[]{:S(2)}) collective-permute-start(f32[8,512]{1,0:T(8,128)S(1)} %get-tuple-element.25), channel_id=1, source_target_pairs={{0,4},{1,5},{2,6},{3,7},{4,0},{5,1},{6,2},{7,3},{8,12},{9,13},{10,... | collective-permute-start | bytes 49160 | tf_op jit(solution)/shard_map/ppermute | solution.py:101
  30.2 3.6 %collective-permute-start.10 = (f32[8,512]{1,0:T(8,128)S(1)}, f32[8,512]{1,0:T(8,128)S(1)}, u32[]{:S(2)}, u32[]{:S(2)}) collective-permute-start(f32[8,512]{1,0:T(8,128)S(1)} %get-tuple-element.24), channel_id=1, source_target_pairs={{0,8},{1,9},{2,10},{3,11},{4,12},{5,13},{6,14},{7,15},{8,0},{9,1},... | collective-permute-start | bytes 49160 | tf_op jit(solution)/shard_map/ppermute | solution.py:101
  30.6 4.5 %collective-permute-start.11 = (f32[8,512]{1,0:T(8,128)S(1)}, f32[8,512]{1,0:T(8,128)S(1)}, u32[]{:S(2)}, u32[]{:S(2)}) collective-permute-start(f32[8,512]{1,0:T(8,128)S(1)} %get-tuple-element.23), channel_id=1, source_target_pairs={{0,12},{1,13},{2,14},{3,15},{4,8},{5,9},{6,10},{7,11},{8,4},{9,5},... | collective-permute-start | bytes 49160 | tf_op jit(solution)/shard_map/ppermute | solution.py:101
  42.7 3.3 %collective-permute-start.12 = (f32[8,4,130]{0,1,2:T(4,128)S(1)}, f32[8,4,130]{0,1,2:T(4,128)S(1)}, u32[]{:S(2)}, u32[]{:S(2)}) collective-permute-start(f32[8,4,130]{0,1,2:T(4,128)S(1)} %pad_maximum_fusion), channel_id=1, source_target_pairs={{0,1},{1,0},{2,3},{3,2},{4,5},{5,4},{6,7},{7,6},{8,9},{9,8},{10,11... | collective-permute-start | bytes 49928 | tf_op jit(solution)/shard_map/ppermute | solution.py:19
  46.5 3.8 %collective-permute-start.13 = (bf16[8,128]{1,0:T(8,128)(2,1)S(1)}, bf16[8,128]{1,0:T(8,128)(2,1)S(1)}, u32[]{:S(2)}, u32[]{:S(2)}) collective-permute-start(bf16[8,128]{1,0:T(8,128)(2,1)S(1)} %bitcast.216), channel_id=1, source_target_pairs={{0,4},{1,5},{2,6},{3,7},{4,0},{5,1},{6,2},{7,3},{8,12},{9,13},{10,... | collective-permute-start | bytes 6152 | tf_op jit(solution)/shard_map/ppermute | solution.py:101
  46.6 4.4 %collective-permute-start.14 = (bf16[8,128]{1,0:T(8,128)(2,1)S(1)}, bf16[8,128]{1,0:T(8,128)(2,1)S(1)}, u32[]{:S(2)}, u32[]{:S(2)}) collective-permute-start(bf16[8,128]{1,0:T(8,128)(2,1)S(1)} %bitcast.217), channel_id=1, source_target_pairs={{0,8},{1,9},{2,10},{3,11},{4,12},{5,13},{6,14},{7,15},{8,0},{9,1},... | collective-permute-start | bytes 6152 | tf_op jit(solution)/shard_map/ppermute | solution.py:101
  50.1 4.3 %collective-permute-start.15 = (bf16[8,128]{1,0:T(8,128)(2,1)S(1)}, bf16[8,128]{1,0:T(8,128)(2,1)S(1)}, u32[]{:S(2)}, u32[]{:S(2)}) collective-permute-start(bf16[8,128]{1,0:T(8,128)(2,1)S(1)} %bitcast.218), channel_id=1, source_target_pairs={{0,12},{1,13},{2,14},{3,15},{4,8},{5,9},{6,10},{7,11},{8,4},{9,5},... | collective-permute-start | bytes 6152 | tf_op jit(solution)/shard_map/ppermute | solution.py:101
  54.4 3.9 %collective-permute-start.16 = (bf16[4,8,128]{2,1,0:T(8,128)(2,1)S(1)}, bf16[4,8,128]{2,1,0:T(8,128)(2,1)S(1)}, u32[]{:S(2)}, u32[]{:S(2)}) collective-permute-start(bf16[4,8,128]{2,1,0:T(8,128)(2,1)S(1)} %select_reduce_fusion.8), channel_id=1, source_target_pairs={{0,1},{1,0},{2,3},{3,2},{4,5},{5,4},{6,7},{7,6},{8,9},{9,8},{10,11... | collective-permute-start | bytes 24584 | tf_op jit(solution)/shard_map/ppermute | solution.py:105
  56.6 2.5 %collective-permute-start.17 = (bf16[4,8,128]{2,1,0:T(8,128)(2,1)S(1)}, bf16[4,8,128]{2,1,0:T(8,128)(2,1)S(1)}, u32[]{:S(2)}, u32[]{:S(2)}) collective-permute-start(bf16[4,8,128]{2,1,0:T(8,128)(2,1)S(1)} %select_reduce_fusion.8), channel_id=1, source_target_pairs={{0,2},{1,3},{2,0},{3,1},{4,6},{5,7},{6,4},{7,5},{8,10},{9,11},{10,... | collective-permute-start | bytes 24584 | tf_op jit(solution)/shard_map/ppermute | solution.py:105
  57.6 3.1 %collective-permute-start.18 = (bf16[4,8,128]{2,1,0:T(8,128)(2,1)S(1)}, bf16[4,8,128]{2,1,0:T(8,128)(2,1)S(1)}, u32[]{:S(2)}, u32[]{:S(2)}) collective-permute-start(bf16[4,8,128]{2,1,0:T(8,128)(2,1)S(1)} %select_reduce_fusion.8), channel_id=1, source_target_pairs={{0,3},{1,2},{2,1},{3,0},{4,7},{5,6},{6,5},{7,4},{8,11},{9,10},{10,... | collective-permute-start | bytes 24584 | tf_op jit(solution)/shard_map/ppermute | solution.py:105
  66.8 6.9 %collective-permute-start.19 = (f32[8,512]{1,0:T(8,128)S(1)}, f32[8,512]{1,0:T(8,128)S(1)}, u32[]{:S(2)}, u32[]{:S(2)}) collective-permute-start(f32[8,512]{1,0:T(8,128)S(1)} %get-tuple-element.21), channel_id=1, source_target_pairs={{0,0},{1,4},{2,8},{3,12},{4,1},{5,5},{6,9},{7,13},{8,2},{9,6},{10,... | collective-permute-start | bytes 49160 | tf_op jit(solution)/shard_map/ppermute | solution.py:279
  68.7 5.0 %collective-permute-start.20 = (f32[8,512]{1,0:T(8,128)S(1)}, f32[8,512]{1,0:T(8,128)S(1)}, u32[]{:S(2)}, u32[]{:S(2)}) collective-permute-start(f32[8,512]{1,0:T(8,128)S(1)} %get-tuple-element.18), channel_id=1, source_target_pairs={{0,1},{1,5},{2,9},{3,13},{4,0},{5,4},{6,8},{7,12},{8,3},{9,7},{10,... | collective-permute-start | bytes 49160 | tf_op jit(solution)/shard_map/ppermute | solution.py:279
  68.8 5.6 %collective-permute-start.21 = (f32[8,512]{1,0:T(8,128)S(1)}, f32[8,512]{1,0:T(8,128)S(1)}, u32[]{:S(2)}, u32[]{:S(2)}) collective-permute-start(f32[8,512]{1,0:T(8,128)S(1)} %get-tuple-element.20), channel_id=1, source_target_pairs={{0,2},{1,6},{2,10},{3,14},{4,3},{5,7},{6,11},{7,15},{8,0},{9,4},{1... | collective-permute-start | bytes 49160 | tf_op jit(solution)/shard_map/ppermute | solution.py:279
  73.3 4.1 %collective-permute-start.22 = (f32[8,512]{1,0:T(8,128)S(1)}, f32[8,512]{1,0:T(8,128)S(1)}, u32[]{:S(2)}, u32[]{:S(2)}) collective-permute-start(f32[8,512]{1,0:T(8,128)S(1)} %get-tuple-element.19), channel_id=1, source_target_pairs={{0,3},{1,7},{2,11},{3,15},{4,2},{5,6},{6,10},{7,14},{8,1},{9,5},{1... | collective-permute-start | bytes 49160 | tf_op jit(solution)/shard_map/ppermute | solution.py:279

commit v9 on v8

--- a/solution.py
+++ b/solution.py
@@ -133,8 +133,8 @@
     row_bits = GR.bit_length() - 1
     row_order = jnp.arange(GR, dtype=jnp.int32) ^ grid_row
     col_order = jnp.arange(grid_cols, dtype=jnp.int32) ^ grid_col
-    direct_cols = grid_cols <= 4
-    fast_norm = direct_cols and group_count == 1 and GR == grid_cols and col_width == grid_cols * DS
+    direct_cols = False
+    fast_norm = group_count == 1 and GR == grid_cols and col_width == grid_cols * DS
     fast_norm = fast_norm and key_width == DS
     if direct_cols:
         from_cols = [hidden_in[0]] + [swap_cols(hidden_in[0], "tp", s) for s in range(1, grid_cols)]
@@ -148,7 +148,9 @@
         arrived = jnp.stack(from_rows).astype(jnp.float32)
         mean_square = jnp.sum(arrived * arrived, axis=(0, 1, 3))[:, None] / D
         scale_rows = lax.rsqrt(mean_square + 1e-05)
-        col_x = pick(lax.dynamic_index_in_dim(arrived, grid_row ^ grid_col, 0, keepdims=False), col_order)
+        col_x = lax.dynamic_index_in_dim(arrived, grid_row ^ grid_col, 0, keepdims=False)
+        if direct_cols:
+            col_x = pick(col_x, col_order)
         col_x = col_x.transpose(1, 0, 2).reshape(ROWS, col_width)
         col_gain = lax.dynamic_slice_in_dim(norm_gain, grid_col * col_width, col_width)
         col_rows = (col_x * scale_rows * col_gain[None, :]).astype(jnp.bfloat16)

time: 78.4 us -> 80.8 us (1.031)
  starting transfers between devices: 30.3 us -> 33 us
  matrix products: 19.1 us -> 17.1 us
    ppermute x1 -> x7, starting transfers between devices: 2.09 us -> 13.5 us  [from_partner(): return lax.ppermute(value, axis, pairs)]
    ppermute x9 -> x0, starting transfers between devices: 10.4 us -> none  [swap_cols(): lax.ppermute(value, axis, [(t, t ^ s) for t in range(lax.axis_size(axis))])]
    ppermute x9 -> x0, waiting for transfers between devices: 6.08 us -> none  [swap_cols(): lax.ppermute(value, axis, [(t, t ^ s) for t in range(lax.axis_size(axis))])]
    ppermute x1 -> x7, waiting for transfers between devices: 1.17 us -> 6.23 us  [from_partner(): return lax.ppermute(value, axis, pairs)]
    dot_general x1, matrix products: 3.46 us -> 1.27 us  [local(): jnp.einsum('bhe,bte->bht', both_queries, key_cache[0], preferred_element_...]
    ppermute x4, starting transfers between devices: 6.9 us -> 8.38 us  [local(): got = lax.ppermute(piece, 'tp', pairs)]
    ppermute x9, waiting for transfers between devices: 8.44 us -> 9.76 us  [swap_rows(): lax.ppermute(value, axis, [(t, t ^ shift) for t in range(lax.axis_size(ax...]
    select_n x0 -> x6, other arithmetic: none -> 0.83 us  [the longest x4 0.8 us: gather_rounds(): jnp.where(low, jnp.concatenate([held, other], 0), jnp.concatenate([other,...]
  transfers between devices with their start and end apart: 23 -> 20, of which waited for: 14 -> 13; matrix products, arithmetic and copies ran while one was open for 6% -> 7% of each run, Pallas kernels for 0% -> 0%
where the time goes in v9:
time: 80.8 us; the launch traced here: 80.3 us
  starting transfers between devices  33 us (41%)
  waiting for transfers between devices  20.1 us (25%)
  matrix products  17.1 us (21%)
  other arithmetic  6.17 us (8%)
  local copies, waits for them, and re-layouts  3.56 us (4%)
    ppermute x7, starting transfers between devices, from_partner(): return lax.ppermute(value, axis, pairs)  13.5 us
    ppermute x9, starting transfers between devices, swap_rows(): lax.ppermute(value, axis, [(t, t ^ shift) for t in range(lax.axis_size(ax...  11.1 us
    ppermute x9, waiting for transfers between devices, swap_rows(): lax.ppermute(value, axis, [(t, t ^ shift) for t in range(lax.axis_size(ax...  9.76 us
    ppermute x4, starting transfers between devices, local(): got = lax.ppermute(piece, 'tp', pairs)  8.38 us
    ppermute x7, waiting for transfers between devices, from_partner(): return lax.ppermute(value, axis, pairs)  6.23 us
    dot_general x1, matrix products, local(): jnp.einsum('rc,aec->rae', col_rows, q_blocks[0], preferred_element_type=j...  5.79 us
    dot_general x1, matrix products, local(): jnp.einsum('gabe,cae->gbc', chosen, o_blocks[0], preferred_element_type=j...  5.65 us
    ppermute x4, waiting for transfers between devices, local(): got = lax.ppermute(piece, 'tp', pairs)  4.06 us
  transfers between devices with their start and end apart: 20, of which 13 were waited for; matrix products, arithmetic and copies ran while one was open for 7% of the time, Pallas kernels for 0%

profile of v9, /device:TPU:1, one launch (start us, length us, event | category | flops | bytes accessed | tf_op | source)
XLA Modules:
  0.0 80.3 jit_solution(10028922275764155096)
XLA Ops:
  4.9 2.5 %collective-permute-start.1 = (bf16[2,8,512]{2,1,0:T(8,128)(2,1)S(1)}, bf16[2,8,512]{2,1,0:T(8,128)(2,1)S(1)}, u32[]{:S(2)}, u32[]{:S(2)}) collective-permute-start(bf16[2,8,512]{2,1,0:T(8,128)(2,1)S(1)} %maximum_select_fusion.3), channel_id=1, source_target_pairs={{0,2},{1,3},{2,0},{3,1},{4,6},{5,7},{6,4},{7,5},{8,10},{9,11},{10,... | collective-permute-start | bytes 49160 | tf_op jit(solution)/shard_map/ppermute | solution.py:19
  8.6 1.6 %collective-permute-start.2 = (bf16[4,8,512]{2,1,0:T(8,128)(2,1)S(1)}, bf16[4,8,512]{2,1,0:T(8,128)(2,1)S(1)}, u32[]{:S(2)}, u32[]{:S(2)}) collective-permute-start(bf16[4,8,512]{2,1,0:T(8,128)(2,1)S(1)} %maximum_select_fusion.1), channel_id=1, source_target_pairs={{0,4},{1,5},{2,6},{3,7},{4,0},{5,1},{6,2},{7,3},{8,12},{9,13},{10,... | collective-permute-start | bytes 98312 | tf_op jit(solution)/shard_map/ppermute | solution.py:101
  10.2 2.3 %collective-permute-start.3 = (bf16[4,8,512]{2,1,0:T(8,128)(2,1)S(1)}, bf16[4,8,512]{2,1,0:T(8,128)(2,1)S(1)}, u32[]{:S(2)}, u32[]{:S(2)}) collective-permute-start(bf16[4,8,512]{2,1,0:T(8,128)(2,1)S(1)} %maximum_select_fusion.1), channel_id=1, source_target_pairs={{0,8},{1,9},{2,10},{3,11},{4,12},{5,13},{6,14},{7,15},{8,0},{9,1},... | collective-permute-start | bytes 98312 | tf_op jit(solution)/shard_map/ppermute | solution.py:101
  12.5 1.7 %collective-permute-done.3 = bf16[4,8,512]{2,1,0:T(8,128)(2,1)S(1)} collective-permute-done((bf16[4,8,512]{2,1,0:T(8,128)(2,1)S(1)}, bf16[4,8,512]{2,1,0:T(8,128)(2,1)S(1)}, u32[]{:S(2)}, u32[]{:S(2)}) %collective-permute-start.3) | collective-permute-done | bytes 32800 | tf_op jit(solution)/shard_map/ppermute | solution.py:101
  14.2 2.9 %collective-permute-done.4 = bf16[4,8,512]{2,1,0:T(8,128)(2,1)S(1)} collective-permute-done((bf16[4,8,512]{2,1,0:T(8,128)(2,1)S(1)}, bf16[4,8,512]{2,1,0:T(8,128)(2,1)S(1)}, u32[]{:S(2)}, u32[]{:S(2)}) %collective-permute-start.4) | collective-permute-done | bytes 32800 | tf_op jit(solution)/shard_map/ppermute | solution.py:101
  17.3 1.3 %convolution_bitcast_fusion = f32[1,8,8,2,128]{4,2,1,3,0:T(8,128)S(1)} fusion(bf16[2,8,128,512]{3,2,1,0:T(8,128)(2,1)S(1)} %bitcast.199, bf16[1,8,512]{2,1,0:T(8,128)(2,1)} %param.9, f32[512]{0:T(512)S(1)} %dynamic_slice.51, f32[8]{0:T(128)S(1)} %add_rsqrt_fusion), kind=kOutput, calls=%fused_computation.10 | convolution fusion | flops 16793600 | bytes 2172960 | tf_op jit(solution)/shard_map/rc,kfc->rkf/dot_general | solution.py:180
  18.8 5.8 %fusion = f32[8,16,128]{2,0,1:T(8,128)S(1)} fusion(bf16[8,2048,1]{1,0,2:T(8,128)(2,1)S(1)} %bitcast.209, bf16[1,16,128,2048]{3,2,1,0:T(8,128)(2,1)} %param.11), kind=kOutput, calls=%fused_computation | convolution fusion | flops 67108864 | bytes 8486912 | tf_op jit(solution)/shard_map/rc,aec->rae/dot_general | solution.py:170
  25.0 3.1 %collective-permute-start.5 = (f32[2,2,2,8,512]{4,3,2,1,0:T(8,128)S(1)}, f32[2,2,2,8,512]{4,3,2,1,0:T(8,128)S(1)}, u32[]{:S(2)}, u32[]{:S(2)}) collective-permute-start(f32[2,2,2,8,512]{4,3,2,1,0:T(8,128)S(1)} %select_bitcast_fusion.1), channel_id=1, source_target_pairs={{0,1},{1,0},{2,3},{3,2},{4,5},{5,4},{6,7},{7,6},{8,9},{9,8},{10,11... | collective-permute-start | bytes 393224 | tf_op jit(solution)/shard_map/ppermute | solution.py:19
  29.1 1.3 %collective-permute-start.6 = (f32[2,2,8,512]{3,2,1,0:T(8,128)S(1)}, f32[2,2,8,512]{3,2,1,0:T(8,128)S(1)}, u32[]{:S(2)}, u32[]{:S(2)}) collective-permute-start(f32[2,2,8,512]{3,2,1,0:T(8,128)S(1)} %select_bitcast_fusion.2), channel_id=1, source_target_pairs={{0,2},{1,3},{2,0},{3,1},{4,6},{5,7},{6,4},{7,5},{8,10},{9,11},{10,... | collective-permute-start | bytes 196616 | tf_op jit(solution)/shard_map/ppermute | solution.py:19
  30.5 1.8 %collective-permute-done.6 = f32[2,2,8,512]{3,2,1,0:T(8,128)S(1)} collective-permute-done((f32[2,2,8,512]{3,2,1,0:T(8,128)S(1)}, f32[2,2,8,512]{3,2,1,0:T(8,128)S(1)}, u32[]{:S(2)}, u32[]{:S(2)}) %collective-permute-start.6) | collective-permute-done | bytes 65568 | tf_op jit(solution)/shard_map/ppermute | solution.py:19
  32.8 3.2 %collective-permute-start.9 = (f32[8,512]{1,0:T(8,128)S(1)}, f32[8,512]{1,0:T(8,128)S(1)}, u32[]{:S(2)}, u32[]{:S(2)}) collective-permute-start(f32[8,512]{1,0:T(8,128)S(1)} %get-tuple-element.20), channel_id=1, source_target_pairs={{0,12},{1,13},{2,14},{3,15},{4,8},{5,9},{6,10},{7,11},{8,4},{9,5},... | collective-permute-start | bytes 49160 | tf_op jit(solution)/shard_map/ppermute | solution.py:101
  36.0 1.3 %collective-permute-done.9 = f32[8,512]{1,0:T(8,128)S(1)} collective-permute-done((f32[8,512]{1,0:T(8,128)S(1)}, f32[8,512]{1,0:T(8,128)S(1)}, u32[]{:S(2)}, u32[]{:S(2)}) %collective-permute-start.9) | collective-permute-done | bytes 16416 | tf_op jit(solution)/shard_map/ppermute | solution.py:101
  37.6 1.3 %select_reduce_fusion.3 = (f32[8,8]{1,0:T(8,128)S(1)}, f32[8,8,2048]{2,1,0:T(8,128)S(1)}) fusion(pred[8,2048]{1,0:T(8,128)(4,1)S(1)} %iota_compare_fusion, bf16[8,8,128]{2,1,0:T(8,128)(2,1)S(1)} %bitcast.218, bf16[1,8,2048,128]{3,2,1,0:T(8,128)(2,1)S(1)} %copy-done.1), kind=kOutput, calls=%fused_computation.16 | convolution fusion | flops 33947584 | bytes 4751616 | tf_op jit(solution)/shard_map/bhe,bte->bht/dot_general | solution.py:215
  39.2 2.9 %fusion.14 = f32[8,8,128]{2,1,0:T(8,128)S(1)} fusion(bf16[1,8,2048,128]{3,2,1,0:T(8,128)(2,1)} %param.16, f32[8,8,2048]{2,1,0:T(8,128)S(1)} %get-tuple-element.38, f32[8,8]{1,0:T(8,128)S(1)} %fusion.43, pred[8,2048]{1,0:T(8,128)(4,1)S(1)} %iota_compare_fusion, f32[8,128]{1,0:T(8,128)S(1)} %get-tuple-element.35, f32[8,8]{1,0:T(8,128)S(1)} %convert_element_type.64), kind=kOutput, calls=%fused_computation.11 | convolution fusion | flops 33964032 | bytes 4772352 | tf_op jit(solution)/shard_map/bht,bte->bhe/dot_general | solution.py:228
  42.7 3.2 %collective-permute-start.10 = (f32[8,4,130]{0,1,2:T(4,128)S(1)}, f32[8,4,130]{0,1,2:T(4,128)S(1)}, u32[]{:S(2)}, u32[]{:S(2)}) collective-permute-start(f32[8,4,130]{0,1,2:T(4,128)S(1)} %pad_maximum_fusion), channel_id=1, source_target_pairs={{0,1},{1,0},{2,3},{3,2},{4,5},{5,4},{6,7},{7,6},{8,9},{9,8},{10,11... | collective-permute-start | bytes 49928 | tf_op jit(solution)/shard_map/ppermute | solution.py:19
  47.7 3.5 %collective-permute-start.12 = (bf16[8,128]{1,0:T(8,128)(2,1)S(1)}, bf16[8,128]{1,0:T(8,128)(2,1)S(1)}, u32[]{:S(2)}, u32[]{:S(2)}) collective-permute-start(bf16[8,128]{1,0:T(8,128)(2,1)S(1)} %bitcast.232), channel_id=1, source_target_pairs={{0,8},{1,9},{2,10},{3,11},{4,12},{5,13},{6,14},{7,15},{8,0},{9,1},... | collective-permute-start | bytes 6152 | tf_op jit(solution)/shard_map/ppermute | solution.py:101
  52.1 3.4 %collective-permute-done.13 = bf16[8,128]{1,0:T(8,128)(2,1)S(1)} collective-permute-done((bf16[8,128]{1,0:T(8,128)(2,1)S(1)}, bf16[8,128]{1,0:T(8,128)(2,1)S(1)}, u32[]{:S(2)}, u32[]{:S(2)}) %collective-permute-start.13) | collective-permute-done | bytes 2080 | tf_op jit(solution)/shard_map/ppermute | solution.py:101
  55.6 2.1 %collective-permute-start.14 = (bf16[1,4,8,128]{3,2,1,0:T(8,128)(2,1)S(1)}, bf16[1,4,8,128]{3,2,1,0:T(8,128)(2,1)S(1)}, u32[]{:S(2)}, u32[]{:S(2)}) collective-permute-start(bf16[1,4,8,128]{3,2,1,0:T(8,128)(2,1)S(1)} %bitcast.226), channel_id=1, source_target_pairs={{0,1},{1,0},{2,3},{3,2},{4,5},{5,4},{6,7},{7,6},{8,9},{9,8},{10,11... | collective-permute-start | bytes 24584 | tf_op jit(solution)/shard_map/ppermute | solution.py:19
  58.6 1.2 %collective-permute-start.15 = (bf16[2,4,8,128]{3,2,1,0:T(8,128)(2,1)S(1)}, bf16[2,4,8,128]{3,2,1,0:T(8,128)(2,1)S(1)}, u32[]{:S(2)}, u32[]{:S(2)}) collective-permute-start(bf16[2,4,8,128]{3,2,1,0:T(8,128)(2,1)S(1)} %maximum_select_fusion.4), channel_id=1, source_target_pairs={{0,2},{1,3},{2,0},{3,1},{4,6},{5,7},{6,4},{7,5},{8,10},{9,11},{10,... | collective-permute-start | bytes 49160 | tf_op jit(solution)/shard_map/ppermute | solution.py:19
  59.8 1.3 %collective-permute-done.15 = bf16[2,4,8,128]{3,2,1,0:T(8,128)(2,1)S(1)} collective-permute-done((bf16[2,4,8,128]{3,2,1,0:T(8,128)(2,1)S(1)}, bf16[2,4,8,128]{3,2,1,0:T(8,128)(2,1)S(1)}, u32[]{:S(2)}, u32[]{:S(2)}) %collective-permute-start.15) | collective-permute-done | bytes 16416 | tf_op jit(solution)/shard_map/ppermute | solution.py:19
  61.5 5.6 %fusion.11 = f32[8,4,512]{2,0,1:T(8,128)S(1)} fusion(bf16[4,512,16,128]{3,2,1,0:T(8,128)(2,1)} %bitcast.200, bf16[16,8,128]{2,1,0:T(8,128)(2,1)S(1)} %select_reduce_fusion.2), kind=kOutput, calls=%fused_computation.9 | convolution fusion | flops 67108864 | bytes 8486912 | tf_op jit(solution)/shard_map/gabe,cae->gbc/dot_general | solution.py:274
  67.2 1.9 %collective-permute-start.16 = (f32[8,512]{1,0:T(8,128)S(1)}, f32[8,512]{1,0:T(8,128)S(1)}, u32[]{:S(2)}, u32[]{:S(2)}) collective-permute-start(f32[8,512]{1,0:T(8,128)S(1)} %get-tuple-element.18), channel_id=1, source_target_pairs={{0,0},{1,4},{2,8},{3,12},{4,1},{5,5},{6,9},{7,13},{8,2},{9,6},{10,... | collective-permute-start | bytes 49160 | tf_op jit(solution)/shard_map/ppermute | solution.py:281
  69.2 6.4 %collective-permute-start.18 = (f32[8,512]{1,0:T(8,128)S(1)}, f32[8,512]{1,0:T(8,128)S(1)}, u32[]{:S(2)}, u32[]{:S(2)}) collective-permute-start(f32[8,512]{1,0:T(8,128)S(1)} %get-tuple-element.17), channel_id=1, source_target_pairs={{0,2},{1,6},{2,10},{3,14},{4,3},{5,7},{6,11},{7,15},{8,0},{9,4},{1... | collective-permute-start | bytes 49160 | tf_op jit(solution)/shard_map/ppermute | solution.py:281
  76.8 2.8 %collective-permute-done.19 = f32[8,512]{1,0:T(8,128)S(1)} collective-permute-done((f32[8,512]{1,0:T(8,128)S(1)}, f32[8,512]{1,0:T(8,128)S(1)}, u32[]{:S(2)}, u32[]{:S(2)}) %collective-permute-start.19) | collective-permute-done | bytes 16416 | tf_op jit(solution)/shard_map/ppermute | solution.py:281
  (99 shorter events, 15.5 us)
Async XLA Ops:
  0.0 17.3 %copy-start = (bf16[2,1024,512]{2,1,0:T(8,128)(2,1)S(1)}, bf16[2,1024,512]{2,1,0:T(8,128)(2,1)}, u32[]{:S(2)}) copy-start(bf16[2,1024,512]{2,1,0:T(8,128)(2,1)} %param.13) | copy-start | bytes 6291460
  0.0 4.2 %collective-permute-start = (bf16[1,8,512]{2,1,0:T(8,128)(2,1)}, bf16[1,8,512]{2,1,0:T(8,128)(2,1)S(1)}, u32[]{:S(2)}, u32[]{:S(2)}) collective-permute-start(bf16[1,8,512]{2,1,0:T(8,128)(2,1)} %param.9), channel_id=1, source_target_pairs={{0,1},{1,0},{2,3},{3,2},{4,5},{5,4},{6,7},{7,6},{8,9},{9,8},{10,11... | collective-permute-start | bytes 24584 | tf_op jit(solution)/shard_map/ppermute | solution.py:19
  4.9 3.6 %collective-permute-start.1 = (bf16[2,8,512]{2,1,0:T(8,128)(2,1)S(1)}, bf16[2,8,512]{2,1,0:T(8,128)(2,1)S(1)}, u32[]{:S(2)}, u32[]{:S(2)}) collective-permute-start(bf16[2,8,512]{2,1,0:T(8,128)(2,1)S(1)} %maximum_select_fusion.3), channel_id=1, source_target_pairs={{0,2},{1,3},{2,0},{3,1},{4,6},{5,7},{6,4},{7,5},{8,10},{9,11},{10,... | collective-permute-start | bytes 49160 | tf_op jit(solution)/shard_map/ppermute | solution.py:19
  8.6 3.9 %collective-permute-start.2 = (bf16[4,8,512]{2,1,0:T(8,128)(2,1)S(1)}, bf16[4,8,512]{2,1,0:T(8,128)(2,1)S(1)}, u32[]{:S(2)}, u32[]{:S(2)}) collective-permute-start(bf16[4,8,512]{2,1,0:T(8,128)(2,1)S(1)} %maximum_select_fusion.1), channel_id=1, source_target_pairs={{0,4},{1,5},{2,6},{3,7},{4,0},{5,1},{6,2},{7,3},{8,12},{9,13},{10,... | collective-permute-start | bytes 98312 | tf_op jit(solution)/shard_map/ppermute | solution.py:101
  10.2 4.0 %collective-permute-start.3 = (bf16[4,8,512]{2,1,0:T(8,128)(2,1)S(1)}, bf16[4,8,512]{2,1,0:T(8,128)(2,1)S(1)}, u32[]{:S(2)}, u32[]{:S(2)}) collective-permute-start(bf16[4,8,512]{2,1,0:T(8,128)(2,1)S(1)} %maximum_select_fusion.1), channel_id=1, source_target_pairs={{0,8},{1,9},{2,10},{3,11},{4,12},{5,13},{6,14},{7,15},{8,0},{9,1},... | collective-permute-start | bytes 98312 | tf_op jit(solution)/shard_map/ppermute | solution.py:101
  12.5 4.6 %collective-permute-start.4 = (bf16[4,8,512]{2,1,0:T(8,128)(2,1)S(1)}, bf16[4,8,512]{2,1,0:T(8,128)(2,1)S(1)}, u32[]{:S(2)}, u32[]{:S(2)}) collective-permute-start(bf16[4,8,512]{2,1,0:T(8,128)(2,1)S(1)} %maximum_select_fusion.1), channel_id=1, source_target_pairs={{0,12},{1,13},{2,14},{3,15},{4,8},{5,9},{6,10},{7,11},{8,4},{9,5},... | collective-permute-start | bytes 98312 | tf_op jit(solution)/shard_map/ppermute | solution.py:101
  18.8 18.8 %copy-start.1 = (bf16[1,8,2048,128]{3,2,1,0:T(8,128)(2,1)S(1)}, bf16[1,8,2048,128]{3,2,1,0:T(8,128)(2,1)}, u32[]{:S(2)}) copy-start(bf16[1,8,2048,128]{3,2,1,0:T(8,128)(2,1)} %param.15) | copy-start | bytes 12582916
  25.0 4.1 %collective-permute-start.5 = (f32[2,2,2,8,512]{4,3,2,1,0:T(8,128)S(1)}, f32[2,2,2,8,512]{4,3,2,1,0:T(8,128)S(1)}, u32[]{:S(2)}, u32[]{:S(2)}) collective-permute-start(f32[2,2,2,8,512]{4,3,2,1,0:T(8,128)S(1)} %select_bitcast_fusion.1), channel_id=1, source_target_pairs={{0,1},{1,0},{2,3},{3,2},{4,5},{5,4},{6,7},{7,6},{8,9},{9,8},{10,11... | collective-permute-start | bytes 393224 | tf_op jit(solution)/shard_map/ppermute | solution.py:19
  29.1 3.2 %collective-permute-start.6 = (f32[2,2,8,512]{3,2,1,0:T(8,128)S(1)}, f32[2,2,8,512]{3,2,1,0:T(8,128)S(1)}, u32[]{:S(2)}, u32[]{:S(2)}) collective-permute-start(f32[2,2,8,512]{3,2,1,0:T(8,128)S(1)} %select_bitcast_fusion.2), channel_id=1, source_target_pairs={{0,2},{1,3},{2,0},{3,1},{4,6},{5,7},{6,4},{7,5},{8,10},{9,11},{10,... | collective-permute-start | bytes 196616 | tf_op jit(solution)/shard_map/ppermute | solution.py:19
  32.4 3.6 %collective-permute-start.7 = (f32[8,512]{1,0:T(8,128)S(1)}, f32[8,512]{1,0:T(8,128)S(1)}, u32[]{:S(2)}, u32[]{:S(2)}) collective-permute-start(f32[8,512]{1,0:T(8,128)S(1)} %get-tuple-element.22), channel_id=1, source_target_pairs={{0,4},{1,5},{2,6},{3,7},{4,0},{5,1},{6,2},{7,3},{8,12},{9,13},{10,... | collective-permute-start | bytes 49160 | tf_op jit(solution)/shard_map/ppermute | solution.py:101
  32.4 3.6 %collective-permute-start.8 = (f32[8,512]{1,0:T(8,128)S(1)}, f32[8,512]{1,0:T(8,128)S(1)}, u32[]{:S(2)}, u32[]{:S(2)}) collective-permute-start(f32[8,512]{1,0:T(8,128)S(1)} %get-tuple-element.21), channel_id=1, source_target_pairs={{0,8},{1,9},{2,10},{3,11},{4,12},{5,13},{6,14},{7,15},{8,0},{9,1},... | collective-permute-start | bytes 49160 | tf_op jit(solution)/shard_map/ppermute | solution.py:101
  32.8 4.5 %collective-permute-start.9 = (f32[8,512]{1,0:T(8,128)S(1)}, f32[8,512]{1,0:T(8,128)S(1)}, u32[]{:S(2)}, u32[]{:S(2)}) collective-permute-start(f32[8,512]{1,0:T(8,128)S(1)} %get-tuple-element.20), channel_id=1, source_target_pairs={{0,12},{1,13},{2,14},{3,15},{4,8},{5,9},{6,10},{7,11},{8,4},{9,5},... | collective-permute-start | bytes 49160 | tf_op jit(solution)/shard_map/ppermute | solution.py:101
  42.7 4.4 %collective-permute-start.10 = (f32[8,4,130]{0,1,2:T(4,128)S(1)}, f32[8,4,130]{0,1,2:T(4,128)S(1)}, u32[]{:S(2)}, u32[]{:S(2)}) collective-permute-start(f32[8,4,130]{0,1,2:T(4,128)S(1)} %pad_maximum_fusion), channel_id=1, source_target_pairs={{0,1},{1,0},{2,3},{3,2},{4,5},{5,4},{6,7},{7,6},{8,9},{9,8},{10,11... | collective-permute-start | bytes 49928 | tf_op jit(solution)/shard_map/ppermute | solution.py:19
  47.5 4.0 %collective-permute-start.11 = (bf16[8,128]{1,0:T(8,128)(2,1)S(1)}, bf16[8,128]{1,0:T(8,128)(2,1)S(1)}, u32[]{:S(2)}, u32[]{:S(2)}) collective-permute-start(bf16[8,128]{1,0:T(8,128)(2,1)S(1)} %bitcast.231), channel_id=1, source_target_pairs={{0,4},{1,5},{2,6},{3,7},{4,0},{5,1},{6,2},{7,3},{8,12},{9,13},{10,... | collective-permute-start | bytes 6152 | tf_op jit(solution)/shard_map/ppermute | solution.py:101
  47.7 4.5 %collective-permute-start.12 = (bf16[8,128]{1,0:T(8,128)(2,1)S(1)}, bf16[8,128]{1,0:T(8,128)(2,1)S(1)}, u32[]{:S(2)}, u32[]{:S(2)}) collective-permute-start(bf16[8,128]{1,0:T(8,128)(2,1)S(1)} %bitcast.232), channel_id=1, source_target_pairs={{0,8},{1,9},{2,10},{3,11},{4,12},{5,13},{6,14},{7,15},{8,0},{9,1},... | collective-permute-start | bytes 6152 | tf_op jit(solution)/shard_map/ppermute | solution.py:101
  51.2 4.3 %collective-permute-start.13 = (bf16[8,128]{1,0:T(8,128)(2,1)S(1)}, bf16[8,128]{1,0:T(8,128)(2,1)S(1)}, u32[]{:S(2)}, u32[]{:S(2)}) collective-permute-start(bf16[8,128]{1,0:T(8,128)(2,1)S(1)} %bitcast.233), channel_id=1, source_target_pairs={{0,12},{1,13},{2,14},{3,15},{4,8},{5,9},{6,10},{7,11},{8,4},{9,5},... | collective-permute-start | bytes 6152 | tf_op jit(solution)/shard_map/ppermute | solution.py:101
  55.6 3.0 %collective-permute-start.14 = (bf16[1,4,8,128]{3,2,1,0:T(8,128)(2,1)S(1)}, bf16[1,4,8,128]{3,2,1,0:T(8,128)(2,1)S(1)}, u32[]{:S(2)}, u32[]{:S(2)}) collective-permute-start(bf16[1,4,8,128]{3,2,1,0:T(8,128)(2,1)S(1)} %bitcast.226), channel_id=1, source_target_pairs={{0,1},{1,0},{2,3},{3,2},{4,5},{5,4},{6,7},{7,6},{8,9},{9,8},{10,11... | collective-permute-start | bytes 24584 | tf_op jit(solution)/shard_map/ppermute | solution.py:19
  58.6 2.6 %collective-permute-start.15 = (bf16[2,4,8,128]{3,2,1,0:T(8,128)(2,1)S(1)}, bf16[2,4,8,128]{3,2,1,0:T(8,128)(2,1)S(1)}, u32[]{:S(2)}, u32[]{:S(2)}) collective-permute-start(bf16[2,4,8,128]{3,2,1,0:T(8,128)(2,1)S(1)} %maximum_select_fusion.4), channel_id=1, source_target_pairs={{0,2},{1,3},{2,0},{3,1},{4,6},{5,7},{6,4},{7,5},{8,10},{9,11},{10,... | collective-permute-start | bytes 49160 | tf_op jit(solution)/shard_map/ppermute | solution.py:19
  67.2 8.4 %collective-permute-start.16 = (f32[8,512]{1,0:T(8,128)S(1)}, f32[8,512]{1,0:T(8,128)S(1)}, u32[]{:S(2)}, u32[]{:S(2)}) collective-permute-start(f32[8,512]{1,0:T(8,128)S(1)} %get-tuple-element.18), channel_id=1, source_target_pairs={{0,0},{1,4},{2,8},{3,12},{4,1},{5,5},{6,9},{7,13},{8,2},{9,6},{10,... | collective-permute-start | bytes 49160 | tf_op jit(solution)/shard_map/ppermute | solution.py:281
  69.1 6.5 %collective-permute-start.17 = (f32[8,512]{1,0:T(8,128)S(1)}, f32[8,512]{1,0:T(8,128)S(1)}, u32[]{:S(2)}, u32[]{:S(2)}) collective-permute-start(f32[8,512]{1,0:T(8,128)S(1)} %get-tuple-element.15), channel_id=1, source_target_pairs={{0,1},{1,5},{2,9},{3,13},{4,0},{5,4},{6,8},{7,12},{8,3},{9,7},{10,... | collective-permute-start | bytes 49160 | tf_op jit(solution)/shard_map/ppermute | solution.py:281
  69.2 7.6 %collective-permute-start.18 = (f32[8,512]{1,0:T(8,128)S(1)}, f32[8,512]{1,0:T(8,128)S(1)}, u32[]{:S(2)}, u32[]{:S(2)}) collective-permute-start(f32[8,512]{1,0:T(8,128)S(1)} %get-tuple-element.17), channel_id=1, source_target_pairs={{0,2},{1,6},{2,10},{3,14},{4,3},{5,7},{6,11},{7,15},{8,0},{9,4},{1... | collective-permute-start | bytes 49160 | tf_op jit(solution)/shard_map/ppermute | solution.py:281
  75.6 4.1 %collective-permute-start.19 = (f32[8,512]{1,0:T(8,128)S(1)}, f32[8,512]{1,0:T(8,128)S(1)}, u32[]{:S(2)}, u32[]{:S(2)}) collective-permute-start(f32[8,512]{1,0:T(8,128)S(1)} %get-tuple-element.16), channel_id=1, source_target_pairs={{0,3},{1,7},{2,11},{3,15},{4,2},{5,6},{6,10},{7,14},{8,1},{9,5},{1... | collective-permute-start | bytes 49160 | tf_op jit(solution)/shard_map/ppermute | solution.py:281

commit v10 on v8

--- a/solution.py
+++ b/solution.py
@@ -231,36 +231,56 @@
     )
     new_rounded = lax.optimization_barrier(new_weight.astype(jnp.bfloat16)).astype(jnp.float32)
     summed = summed + new_rounded[..., None] * value_new.astype(jnp.float32)[:, None, :]
-    top_split = top.reshape(ROWS, 2, GR)
-    total_split = total.reshape(ROWS, 2, GR)
-    summed_split = summed.reshape(ROWS, 2, GR, HD)
-    first_half = my_half == 0
-    own_top = jnp.where(first_half, top_split[:, 0], top_split[:, 1])
-    own_total = jnp.where(first_half, total_split[:, 0], total_split[:, 1])
-    own_summed = jnp.where(first_half, summed_split[:, 0], summed_split[:, 1])
-    give_top = jnp.where(first_half, top_split[:, 1], top_split[:, 0])
-    give_total = jnp.where(first_half, total_split[:, 1], total_split[:, 0])
-    give_summed = jnp.where(first_half, summed_split[:, 1], summed_split[:, 0])
-    give = jnp.concatenate([give_summed, give_top[..., None], give_total[..., None]], -1)
-    got = from_partner(give, "tp", 0)
-    got_summed, got_top, got_total = got[..., :HD], got[..., HD], got[..., HD + 1]
-    joint = jnp.maximum(own_top, got_top)
-    factor_own = jnp.exp(own_top - joint)
-    factor_got = jnp.exp(got_top - joint)
-    numer = own_summed * factor_own[..., None] + got_summed * factor_got[..., None]
-    denom = own_total * factor_own + got_total * factor_got
-    attention = (numer / denom[..., None]).astype(jnp.bfloat16)
-    from_rows = [lax.dynamic_index_in_dim(attention, grid_row, 1, keepdims=False)]
-    for s in range(1, GR):
-        piece = lax.dynamic_index_in_dim(attention, grid_row ^ s, 1, keepdims=False)
-        from_rows.append(swap_rows(piece, "tp", col_bits, s))
-    by_row = pick(jnp.stack(from_rows), row_order)
     if direct_cols:
+        parts = jnp.concatenate([summed, top[..., None], total[..., None]], -1)
+        parts = parts.reshape(ROWS, 2, GR, HD + 2).transpose(2, 0, 1, 3)
+        from_rows = [lax.dynamic_index_in_dim(parts, grid_row, 0, keepdims=False)]
+        for s in range(1, GR):
+            piece = lax.dynamic_index_in_dim(parts, grid_row ^ s, 0, keepdims=False)
+            from_rows.append(swap_rows(piece, "tp", col_bits, s))
+        by_row = pick(jnp.stack(from_rows), row_order)
         from_cols = [by_row] + [swap_cols(by_row, "tp", s) for s in range(1, grid_cols)]
-        every_slot = pick(jnp.stack(from_cols), col_order)
-    else:
-        every_slot = gather_rounds(by_row[None], "tp", range(col_bits))
-    every_slot = every_slot.transpose(1, 0, 2, 3).reshape(group_count, ROLL, ROWS, HD)
+        every_part = pick(jnp.stack(from_cols), col_order).reshape(grid_cols // 2, 2, GR, ROWS, 2, HD + 2)
+        first = every_part[:, 0]
+        second = every_part[:, 1]
+        joint = jnp.maximum(first[..., HD], second[..., HD])
+        factor_first = jnp.exp(first[..., HD] - joint)
+        factor_second = jnp.exp(second[..., HD] - joint)
+        numer = first[..., :HD] * factor_first[..., None] + second[..., :HD] * factor_second[..., None]
+        denom = first[..., HD + 1] * factor_first + second[..., HD + 1] * factor_second
+        pair_attn = (numer / denom[..., None]).astype(jnp.bfloat16)
+        every_slot = pair_attn.transpose(1, 0, 3, 2, 4).reshape(group_count, ROLL, ROWS, HD)
+    else:
+        top_split = top.reshape(ROWS, 2, GR)
+        total_split = total.reshape(ROWS, 2, GR)
+        summed_split = summed.reshape(ROWS, 2, GR, HD)
+        first_half = my_half == 0
+        own_top = jnp.where(first_half, top_split[:, 0], top_split[:, 1])
+        own_total = jnp.where(first_half, total_split[:, 0], total_split[:, 1])
+        own_summed = jnp.where(first_half, summed_split[:, 0], summed_split[:, 1])
+        give_top = jnp.where(first_half, top_split[:, 1], top_split[:, 0])
+        give_total = jnp.where(first_half, total_split[:, 1], total_split[:, 0])
+        give_summed = jnp.where(first_half, summed_split[:, 1], summed_split[:, 0])
+        give = jnp.concatenate([give_summed, give_top[..., None], give_total[..., None]], -1)
+        got = from_partner(give, "tp", 0)
+        got_summed, got_top, got_total = got[..., :HD], got[..., HD], got[..., HD + 1]
+        joint = jnp.maximum(own_top, got_top)
+        factor_own = jnp.exp(own_top - joint)
+        factor_got = jnp.exp(got_top - joint)
+        numer = own_summed * factor_own[..., None] + got_summed * factor_got[..., None]
+        denom = own_total * factor_own + got_total * factor_got
+        attention = (numer / denom[..., None]).astype(jnp.bfloat16)
+        from_rows = [lax.dynamic_index_in_dim(attention, grid_row, 1, keepdims=False)]
+        for s in range(1, GR):
+            piece = lax.dynamic_index_in_dim(attention, grid_row ^ s, 1, keepdims=False)
+            from_rows.append(swap_rows(piece, "tp", col_bits, s))
+        by_row = pick(jnp.stack(from_rows), row_order)
+        if direct_cols:
+            from_cols = [by_row] + [swap_cols(by_row, "tp", s) for s in range(1, grid_cols)]
+            every_slot = pick(jnp.stack(from_cols), col_order)
+        else:
+            every_slot = gather_rounds(by_row[None], "tp", range(col_bits))
+        every_slot = every_slot.transpose(1, 0, 2, 3).reshape(group_count, ROLL, ROWS, HD)
     head_ids = jnp.arange(KVH, dtype=jnp.int32)
     pair_heads = kv_assign.reshape(KVH, 2)[:, 0]
     inverse = jnp.sum(

time: 78.4 us -> 84.7 us (1.080)
  other arithmetic: 5.4 us -> 8.41 us
  local copies, waits for them, and re-layouts: 3.56 us -> 6.56 us
    transpose x0 -> x1, other arithmetic: none -> 2.39 us  [local(): pair_attn.transpose(1, 0, 3, 2, 4).reshape(group_count, ROLL, ROWS, HD)]
    ppermute x1 -> x0, starting transfers between devices: 2.09 us -> none  [from_partner(): return lax.ppermute(value, axis, pairs)]
    unnamed x4, local copies, waits for them, and re-layouts: 0.31 us -> 2.32 us
    ppermute x9, starting transfers between devices: 10.4 us -> 12.1 us  [swap_cols(): lax.ppermute(value, axis, [(t, t ^ s) for t in range(lax.axis_size(axis))])]
    transpose x1, local copies, waits for them, and re-layouts: 0.01 us -> 1.27 us  [local(): pair_attn.transpose(1, 0, 3, 2, 4).reshape(group_count, ROLL, ROWS, HD)]
    ppermute x9, waiting for transfers between devices: 6.08 us -> 7.29 us  [swap_cols(): lax.ppermute(value, axis, [(t, t ^ s) for t in range(lax.axis_size(axis))])]
    ppermute x1 -> x0, waiting for transfers between devices: 1.17 us -> none  [from_partner(): return lax.ppermute(value, axis, pairs)]
  transfers between devices with their start and end apart: 23 -> 22, of which waited for: 14 -> 13; matrix products, arithmetic and copies ran while one was open for 6% -> 5% of each run, Pallas kernels for 0% -> 0%
where the time goes in v10:
time: 84.7 us; the launch traced here: 84.1 us
  starting transfers between devices  30.4 us (36%)
  waiting for transfers between devices  19.4 us (23%)
  matrix products  19.1 us (23%)
  other arithmetic  8.41 us (10%)
  local copies, waits for them, and re-layouts  6.56 us (8%)
    ppermute x9, starting transfers between devices, swap_cols(): lax.ppermute(value, axis, [(t, t ^ s) for t in range(lax.axis_size(axis))])  12.1 us
    ppermute x9, starting transfers between devices, swap_rows(): lax.ppermute(value, axis, [(t, t ^ shift) for t in range(lax.axis_size(ax...  10.9 us
    ppermute x9, waiting for transfers between devices, swap_rows(): lax.ppermute(value, axis, [(t, t ^ shift) for t in range(lax.axis_size(ax...  8.59 us
    ppermute x4, starting transfers between devices, local(): got = lax.ppermute(piece, 'tp', pairs)  7.34 us
    ppermute x9, waiting for transfers between devices, swap_cols(): lax.ppermute(value, axis, [(t, t ^ s) for t in range(lax.axis_size(axis))])  7.29 us
    dot_general x1, matrix products, local(): jnp.einsum('gabe,cae->gbc', chosen, o_blocks[0], preferred_element_type=j...  5.65 us
    dot_general x1, matrix products, local(): jnp.einsum('rc,aec->rae', col_rows, q_blocks[0], preferred_element_type=j...  5.64 us
    ppermute x4, waiting for transfers between devices, local(): got = lax.ppermute(piece, 'tp', pairs)  3.56 us
  transfers between devices with their start and end apart: 22, of which 13 were waited for; matrix products, arithmetic and copies ran while one was open for 5% of the time, Pallas kernels for 0%

profile of v10, /device:TPU:1, one launch (start us, length us, event | category | flops | bytes accessed | tf_op | source)
XLA Modules:
  0.0 84.1 jit_solution(15886880986299514677)
XLA Ops:
  0.1 2.7 %collective-permute-start.1 = (bf16[8,512]{1,0:T(8,128)(2,1)}, bf16[8,512]{1,0:T(8,128)(2,1)S(1)}, u32[]{:S(2)}, u32[]{:S(2)}) collective-permute-start(bf16[8,512]{1,0:T(8,128)(2,1)} %bitcast.187), channel_id=1, source_target_pairs={{0,2},{1,3},{2,0},{3,1},{4,6},{5,7},{6,4},{7,5},{8,10},{9,11},{10,... | collective-permute-start | bytes 24584 | tf_op jit(solution)/shard_map/ppermute | solution.py:105
  6.7 1.4 %collective-permute-start.3 = (bf16[4,8,512]{2,1,0:T(8,128)(2,1)S(1)}, bf16[4,8,512]{2,1,0:T(8,128)(2,1)S(1)}, u32[]{:S(2)}, u32[]{:S(2)}) collective-permute-start(bf16[4,8,512]{2,1,0:T(8,128)(2,1)S(1)} %get-tuple-element.28), channel_id=1, source_target_pairs={{0,4},{1,5},{2,6},{3,7},{4,0},{5,1},{6,2},{7,3},{8,12},{9,13},{10,... | collective-permute-start | bytes 98312 | tf_op jit(solution)/shard_map/ppermute | solution.py:101
  8.1 2.3 %collective-permute-start.4 = (bf16[4,8,512]{2,1,0:T(8,128)(2,1)S(1)}, bf16[4,8,512]{2,1,0:T(8,128)(2,1)S(1)}, u32[]{:S(2)}, u32[]{:S(2)}) collective-permute-start(bf16[4,8,512]{2,1,0:T(8,128)(2,1)S(1)} %get-tuple-element.28), channel_id=1, source_target_pairs={{0,8},{1,9},{2,10},{3,11},{4,12},{5,13},{6,14},{7,15},{8,0},{9,1},... | collective-permute-start | bytes 98312 | tf_op jit(solution)/shard_map/ppermute | solution.py:101
  12.1 2.9 %collective-permute-done.5 = bf16[4,8,512]{2,1,0:T(8,128)(2,1)S(1)} collective-permute-done((bf16[4,8,512]{2,1,0:T(8,128)(2,1)S(1)}, bf16[4,8,512]{2,1,0:T(8,128)(2,1)S(1)}, u32[]{:S(2)}, u32[]{:S(2)}) %collective-permute-start.5) | collective-permute-done | bytes 32800 | tf_op jit(solution)/shard_map/ppermute | solution.py:101
  15.2 1.3 %convolution_bitcast_fusion = f32[1,8,8,2,128]{4,2,1,3,0:T(8,128)S(1)} fusion(bf16[2,8,128,512]{3,2,1,0:T(8,128)(2,1)S(1)} %bitcast.158, bf16[1,8,512]{2,1,0:T(8,128)(2,1)} %param.9, f32[512]{0:T(512)S(1)} %dynamic_slice.58, f32[8]{0:T(128)S(1)} %add_rsqrt_fusion), kind=kOutput, calls=%fused_computation.10 | convolution fusion | flops 16793600 | bytes 2172960 | tf_op jit(solution)/shard_map/rc,kfc->rkf/dot_general | solution.py:178
  16.8 5.6 %fusion = f32[8,16,128]{2,0,1:T(8,128)S(1)} fusion(bf16[8,2048,1]{1,0,2:T(8,128)(2,1)S(1)} %bitcast.173, bf16[1,16,128,2048]{3,2,1,0:T(8,128)(2,1)} %param.11), kind=kOutput, calls=%fused_computation | convolution fusion | flops 67108864 | bytes 8486912 | tf_op jit(solution)/shard_map/rc,aec->rae/dot_general | solution.py:168
  22.9 2.0 %collective-permute-start.6 = (f32[4,8,512]{2,1,0:T(8,128)S(1)}, f32[4,8,512]{2,1,0:T(8,128)S(1)}, u32[]{:S(2)}, u32[]{:S(2)}) collective-permute-start(f32[4,8,512]{2,1,0:T(8,128)S(1)} %get-tuple-element.12), channel_id=1, source_target_pairs={{0,1},{1,0},{2,3},{3,2},{4,5},{5,4},{6,7},{7,6},{8,9},{9,8},{10,11... | collective-permute-start | bytes 196616 | tf_op jit(solution)/shard_map/ppermute | solution.py:105
  26.7 1.9 %collective-permute-done.7 = f32[4,8,512]{2,1,0:T(8,128)S(1)} collective-permute-done((f32[4,8,512]{2,1,0:T(8,128)S(1)}, f32[4,8,512]{2,1,0:T(8,128)S(1)}, u32[]{:S(2)}, u32[]{:S(2)}) %collective-permute-start.7) | collective-permute-done | bytes 65568 | tf_op jit(solution)/shard_map/ppermute | solution.py:105
  28.6 1.6 %collective-permute-done.8 = f32[4,8,512]{2,1,0:T(8,128)S(1)} collective-permute-done((f32[4,8,512]{2,1,0:T(8,128)S(1)}, f32[4,8,512]{2,1,0:T(8,128)S(1)}, u32[]{:S(2)}, u32[]{:S(2)}) %collective-permute-start.8) | collective-permute-done | bytes 65568 | tf_op jit(solution)/shard_map/ppermute | solution.py:105
  30.6 3.1 %collective-permute-start.11 = (f32[8,512]{1,0:T(8,128)S(1)}, f32[8,512]{1,0:T(8,128)S(1)}, u32[]{:S(2)}, u32[]{:S(2)}) collective-permute-start(f32[8,512]{1,0:T(8,128)S(1)} %get-tuple-element.24), channel_id=1, source_target_pairs={{0,12},{1,13},{2,14},{3,15},{4,8},{5,9},{6,10},{7,11},{8,4},{9,5},... | collective-permute-start | bytes 49160 | tf_op jit(solution)/shard_map/ppermute | solution.py:101
  35.4 3.5 %select_reduce_fusion.4 = (f32[8,8]{1,0:T(8,128)S(1)}, f32[8,8,2048]{2,1,0:T(8,128)S(1)}) fusion(pred[8,2048]{1,0:T(8,128)(4,1)S(1)} %iota_compare_fusion, bf16[8,8,128]{2,1,0:T(8,128)(2,1)S(1)} %bitcast.182, bf16[1,8,2048,128]{3,2,1,0:T(8,128)(2,1)} %param.15), kind=kOutput, calls=%fused_computation.22 | convolution fusion | flops 33947584 | bytes 4751616 | tf_op jit(solution)/shard_map/bhe,bte->bht/dot_general | solution.py:213
  39.2 2.9 %fusion.14 = f32[8,8,128]{2,1,0:T(8,128)S(1)} fusion(bf16[1,8,2048,128]{3,2,1,0:T(8,128)(2,1)} %param.16, f32[8,8,2048]{2,1,0:T(8,128)S(1)} %get-tuple-element.42, f32[8,8]{1,0:T(8,128)S(1)} %fusion.51, pred[8,2048]{1,0:T(8,128)(4,1)S(1)} %iota_compare_fusion, f32[8,128]{1,0:T(8,128)S(1)} %get-tuple-element.39, f32[8,8]{1,0:T(8,128)S(1)} %convert_element_type.62), kind=kOutput, calls=%fused_computation.11 | convolution fusion | flops 33964032 | bytes 4772352 | tf_op jit(solution)/shard_map/bht,bte->bhe/dot_general | solution.py:226
  42.7 3.2 %collective-permute-start.13 = (f32[8,2,130]{2,0,1:T(8,128)S(1)}, f32[8,2,130]{2,0,1:T(8,128)S(1)}, u32[]{:S(2)}, u32[]{:S(2)}) collective-permute-start(f32[8,2,130]{2,0,1:T(8,128)S(1)} %get-tuple-element.21), channel_id=1, source_target_pairs={{0,8},{1,9},{2,10},{3,11},{4,12},{5,13},{6,14},{7,15},{8,0},{9,1},... | collective-permute-start | bytes 24968 | tf_op jit(solution)/shard_map/ppermute | solution.py:101
  47.1 3.3 %collective-permute-done.14 = f32[8,2,130]{2,0,1:T(8,128)S(1)} collective-permute-done((f32[8,2,130]{2,0,1:T(8,128)S(1)}, f32[8,2,130]{2,0,1:T(8,128)S(1)}, u32[]{:S(2)}, u32[]{:S(2)}) %collective-permute-start.14) | collective-permute-done | bytes 8352 | tf_op jit(solution)/shard_map/ppermute | solution.py:101
  50.5 3.9 %collective-permute-start.15 = (f32[4,8,2,130]{3,1,2,0:T(8,128)S(1)}, f32[4,8,2,130]{3,1,2,0:T(8,128)S(1)}, u32[]{:S(2)}, u32[]{:S(2)}) collective-permute-start(f32[4,8,2,130]{3,1,2,0:T(8,128)S(1)} %select_reduce_fusion.5), channel_id=1, source_target_pairs={{0,1},{1,0},{2,3},{3,2},{4,5},{5,4},{6,7},{7,6},{8,9},{9,8},{10,11... | collective-permute-start | bytes 99848 | tf_op jit(solution)/shard_map/ppermute | solution.py:105
  56.1 1.9 %collective-permute-done.16 = f32[4,8,2,130]{3,1,2,0:T(8,128)S(1)} collective-permute-done((f32[4,8,2,130]{3,1,2,0:T(8,128)S(1)}, f32[4,8,2,130]{3,1,2,0:T(8,128)S(1)}, u32[]{:S(2)}, u32[]{:S(2)}) %collective-permute-start.16) | collective-permute-done | bytes 33312 | tf_op jit(solution)/shard_map/ppermute | solution.py:105
  58.0 1.6 %collective-permute-done.17 = f32[4,8,2,130]{3,1,2,0:T(8,128)S(1)} collective-permute-done((f32[4,8,2,130]{3,1,2,0:T(8,128)S(1)}, f32[4,8,2,130]{3,1,2,0:T(8,128)S(1)}, u32[]{:S(2)}, u32[]{:S(2)}) %collective-permute-start.17) | collective-permute-done | bytes 33312 | tf_op jit(solution)/shard_map/ppermute | solution.py:105
  60.5 1.6 %copy.90 = f32[2,1,4,8,2,130]{3,2,5,4,0,1:T(4,128)} copy(f32[2,1,4,8,2,130]{5,3,4,2,1,0:T(8,128)S(1)} %get-tuple-element.11) | data formatting | bytes 133120
  62.9 2.4 %fusion.20 = bf16[4,2,2,8,128]{3,0,4,2,1:T(4,128)(2,1)} fusion(f32[2,4,8,2]{2,1,3,0:T(4,128)S(1)} %get-tuple-element.9, f32[2,4,8,2]{2,1,3,0:T(4,128)S(1)} %get-tuple-element.8, f32[2,4,8,2,130]{2,1,4,3,0:T(4,128)} %bitcast.163, f32[2,4,8,2]{2,1,3,0:T(4,128)S(1)} %get-tuple-element.7, f32[2,4,8,2,130]{2,1,4,3,0:T(4,128)S(1)} %bitcast.161), kind=kLoop, calls=%fused_computation.23 | loop fusion | flops 81920 | bytes 165376 | tf_op jit(solution)/shard_map/transpose | solution.py:252
  65.3 1.3 %copy.83 = bf16[4,2,2,8,128]{4,3,2,1,0:T(8,128)(2,1)S(1)} copy(bf16[4,2,2,8,128]{3,0,4,2,1:T(4,128)(2,1)} %fusion.20) | data formatting | bytes 65536 | tf_op jit(solution)/shard_map/transpose | solution.py:252
  66.9 5.6 %fusion.11 = f32[8,4,512]{2,0,1:T(8,128)S(1)} fusion(bf16[4,512,16,128]{3,2,1,0:T(8,128)(2,1)} %bitcast.159, bf16[16,8,128]{2,1,0:T(8,128)(2,1)S(1)} %select_reduce_fusion.3), kind=kOutput, calls=%fused_computation.9 | convolution fusion | flops 67108864 | bytes 8486912 | tf_op jit(solution)/shard_map/gabe,cae->gbc/dot_general | solution.py:292
  72.6 1.9 %collective-permute-start.18 = (f32[8,512]{1,0:T(8,128)S(1)}, f32[8,512]{1,0:T(8,128)S(1)}, u32[]{:S(2)}, u32[]{:S(2)}) collective-permute-start(f32[8,512]{1,0:T(8,128)S(1)} %get-tuple-element.18), channel_id=1, source_target_pairs={{0,0},{1,4},{2,8},{3,12},{4,1},{5,5},{6,9},{7,13},{8,2},{9,6},{10,... | collective-permute-start | bytes 49160 | tf_op jit(solution)/shard_map/ppermute | solution.py:299
  74.6 4.9 %collective-permute-start.20 = (f32[8,512]{1,0:T(8,128)S(1)}, f32[8,512]{1,0:T(8,128)S(1)}, u32[]{:S(2)}, u32[]{:S(2)}) collective-permute-start(f32[8,512]{1,0:T(8,128)S(1)} %get-tuple-element.17), channel_id=1, source_target_pairs={{0,2},{1,6},{2,10},{3,14},{4,3},{5,7},{6,11},{7,15},{8,0},{9,4},{1... | collective-permute-start | bytes 49160 | tf_op jit(solution)/shard_map/ppermute | solution.py:299
  80.5 3.0 %collective-permute-done.21 = f32[8,512]{1,0:T(8,128)S(1)} collective-permute-done((f32[8,512]{1,0:T(8,128)S(1)}, f32[8,512]{1,0:T(8,128)S(1)}, u32[]{:S(2)}, u32[]{:S(2)}) %collective-permute-start.21) | collective-permute-done | bytes 16416 | tf_op jit(solution)/shard_map/ppermute | solution.py:299
  (95 shorter events, 18.1 us)
Async XLA Ops:
  0.0 15.2 %copy-start = (bf16[2,1024,512]{2,1,0:T(8,128)(2,1)S(1)}, bf16[2,1024,512]{2,1,0:T(8,128)(2,1)}, u32[]{:S(2)}) copy-start(bf16[2,1024,512]{2,1,0:T(8,128)(2,1)} %param.13) | copy-start | bytes 6291460
  0.0 5.7 %collective-permute-start = (bf16[8,512]{1,0:T(8,128)(2,1)}, bf16[8,512]{1,0:T(8,128)(2,1)S(1)}, u32[]{:S(2)}, u32[]{:S(2)}) collective-permute-start(bf16[8,512]{1,0:T(8,128)(2,1)} %bitcast.186), channel_id=1, source_target_pairs={{0,1},{1,0},{2,3},{3,2},{4,5},{5,4},{6,7},{7,6},{8,9},{9,8},{10,11... | collective-permute-start | bytes 24584 | tf_op jit(solution)/shard_map/ppermute | solution.py:105
  0.1 5.6 %collective-permute-start.1 = (bf16[8,512]{1,0:T(8,128)(2,1)}, bf16[8,512]{1,0:T(8,128)(2,1)S(1)}, u32[]{:S(2)}, u32[]{:S(2)}) collective-permute-start(bf16[8,512]{1,0:T(8,128)(2,1)} %bitcast.187), channel_id=1, source_target_pairs={{0,2},{1,3},{2,0},{3,1},{4,6},{5,7},{6,4},{7,5},{8,10},{9,11},{10,... | collective-permute-start | bytes 24584 | tf_op jit(solution)/shard_map/ppermute | solution.py:105
  2.7 3.3 %collective-permute-start.2 = (bf16[8,512]{1,0:T(8,128)(2,1)}, bf16[8,512]{1,0:T(8,128)(2,1)S(1)}, u32[]{:S(2)}, u32[]{:S(2)}) collective-permute-start(bf16[8,512]{1,0:T(8,128)(2,1)} %bitcast.188), channel_id=1, source_target_pairs={{0,3},{1,2},{2,1},{3,0},{4,7},{5,6},{6,5},{7,4},{8,11},{9,10},{10,... | collective-permute-start | bytes 24584 | tf_op jit(solution)/shard_map/ppermute | solution.py:105
  6.7 5.2 %collective-permute-start.3 = (bf16[4,8,512]{2,1,0:T(8,128)(2,1)S(1)}, bf16[4,8,512]{2,1,0:T(8,128)(2,1)S(1)}, u32[]{:S(2)}, u32[]{:S(2)}) collective-permute-start(bf16[4,8,512]{2,1,0:T(8,128)(2,1)S(1)} %get-tuple-element.28), channel_id=1, source_target_pairs={{0,4},{1,5},{2,6},{3,7},{4,0},{5,1},{6,2},{7,3},{8,12},{9,13},{10,... | collective-permute-start | bytes 98312 | tf_op jit(solution)/shard_map/ppermute | solution.py:101
  8.1 4.0 %collective-permute-start.4 = (bf16[4,8,512]{2,1,0:T(8,128)(2,1)S(1)}, bf16[4,8,512]{2,1,0:T(8,128)(2,1)S(1)}, u32[]{:S(2)}, u32[]{:S(2)}) collective-permute-start(bf16[4,8,512]{2,1,0:T(8,128)(2,1)S(1)} %get-tuple-element.28), channel_id=1, source_target_pairs={{0,8},{1,9},{2,10},{3,11},{4,12},{5,13},{6,14},{7,15},{8,0},{9,1},... | collective-permute-start | bytes 98312 | tf_op jit(solution)/shard_map/ppermute | solution.py:101
  10.4 4.6 %collective-permute-start.5 = (bf16[4,8,512]{2,1,0:T(8,128)(2,1)S(1)}, bf16[4,8,512]{2,1,0:T(8,128)(2,1)S(1)}, u32[]{:S(2)}, u32[]{:S(2)}) collective-permute-start(bf16[4,8,512]{2,1,0:T(8,128)(2,1)S(1)} %get-tuple-element.28), channel_id=1, source_target_pairs={{0,12},{1,13},{2,14},{3,15},{4,8},{5,9},{6,10},{7,11},{8,4},{9,5},... | collective-permute-start | bytes 98312 | tf_op jit(solution)/shard_map/ppermute | solution.py:101
  22.9 3.8 %collective-permute-start.6 = (f32[4,8,512]{2,1,0:T(8,128)S(1)}, f32[4,8,512]{2,1,0:T(8,128)S(1)}, u32[]{:S(2)}, u32[]{:S(2)}) collective-permute-start(f32[4,8,512]{2,1,0:T(8,128)S(1)} %get-tuple-element.12), channel_id=1, source_target_pairs={{0,1},{1,0},{2,3},{3,2},{4,5},{5,4},{6,7},{7,6},{8,9},{9,8},{10,11... | collective-permute-start | bytes 196616 | tf_op jit(solution)/shard_map/ppermute | solution.py:105
  24.9 3.7 %collective-permute-start.7 = (f32[4,8,512]{2,1,0:T(8,128)S(1)}, f32[4,8,512]{2,1,0:T(8,128)S(1)}, u32[]{:S(2)}, u32[]{:S(2)}) collective-permute-start(f32[4,8,512]{2,1,0:T(8,128)S(1)} %get-tuple-element.13), channel_id=1, source_target_pairs={{0,2},{1,3},{2,0},{3,1},{4,6},{5,7},{6,4},{7,5},{8,10},{9,11},{10,... | collective-permute-start | bytes 196616 | tf_op jit(solution)/shard_map/ppermute | solution.py:105
  26.0 4.1 %collective-permute-start.8 = (f32[4,8,512]{2,1,0:T(8,128)S(1)}, f32[4,8,512]{2,1,0:T(8,128)S(1)}, u32[]{:S(2)}, u32[]{:S(2)}) collective-permute-start(f32[4,8,512]{2,1,0:T(8,128)S(1)} %get-tuple-element.14), channel_id=1, source_target_pairs={{0,3},{1,2},{2,1},{3,0},{4,7},{5,6},{6,5},{7,4},{8,11},{9,10},{10,... | collective-permute-start | bytes 196616 | tf_op jit(solution)/shard_map/ppermute | solution.py:105
  30.2 3.6 %collective-permute-start.9 = (f32[8,512]{1,0:T(8,128)S(1)}, f32[8,512]{1,0:T(8,128)S(1)}, u32[]{:S(2)}, u32[]{:S(2)}) collective-permute-start(f32[8,512]{1,0:T(8,128)S(1)} %get-tuple-element.26), channel_id=1, source_target_pairs={{0,4},{1,5},{2,6},{3,7},{4,0},{5,1},{6,2},{7,3},{8,12},{9,13},{10,... | collective-permute-start | bytes 49160 | tf_op jit(solution)/shard_map/ppermute | solution.py:101
  30.2 3.6 %collective-permute-start.10 = (f32[8,512]{1,0:T(8,128)S(1)}, f32[8,512]{1,0:T(8,128)S(1)}, u32[]{:S(2)}, u32[]{:S(2)}) collective-permute-start(f32[8,512]{1,0:T(8,128)S(1)} %get-tuple-element.25), channel_id=1, source_target_pairs={{0,8},{1,9},{2,10},{3,11},{4,12},{5,13},{6,14},{7,15},{8,0},{9,1},... | collective-permute-start | bytes 49160 | tf_op jit(solution)/shard_map/ppermute | solution.py:101
  30.6 4.5 %collective-permute-start.11 = (f32[8,512]{1,0:T(8,128)S(1)}, f32[8,512]{1,0:T(8,128)S(1)}, u32[]{:S(2)}, u32[]{:S(2)}) collective-permute-start(f32[8,512]{1,0:T(8,128)S(1)} %get-tuple-element.24), channel_id=1, source_target_pairs={{0,12},{1,13},{2,14},{3,15},{4,8},{5,9},{6,10},{7,11},{8,4},{9,5},... | collective-permute-start | bytes 49160 | tf_op jit(solution)/shard_map/ppermute | solution.py:101
  42.5 3.6 %collective-permute-start.12 = (f32[8,2,130]{2,0,1:T(8,128)S(1)}, f32[8,2,130]{2,0,1:T(8,128)S(1)}, u32[]{:S(2)}, u32[]{:S(2)}) collective-permute-start(f32[8,2,130]{2,0,1:T(8,128)S(1)} %get-tuple-element.22), channel_id=1, source_target_pairs={{0,4},{1,5},{2,6},{3,7},{4,0},{5,1},{6,2},{7,3},{8,12},{9,13},{10,... | collective-permute-start | bytes 24968 | tf_op jit(solution)/shard_map/ppermute | solution.py:101
  42.7 4.4 %collective-permute-start.13 = (f32[8,2,130]{2,0,1:T(8,128)S(1)}, f32[8,2,130]{2,0,1:T(8,128)S(1)}, u32[]{:S(2)}, u32[]{:S(2)}) collective-permute-start(f32[8,2,130]{2,0,1:T(8,128)S(1)} %get-tuple-element.21), channel_id=1, source_target_pairs={{0,8},{1,9},{2,10},{3,11},{4,12},{5,13},{6,14},{7,15},{8,0},{9,1},... | collective-permute-start | bytes 24968 | tf_op jit(solution)/shard_map/ppermute | solution.py:101
  46.0 4.4 %collective-permute-start.14 = (f32[8,2,130]{2,0,1:T(8,128)S(1)}, f32[8,2,130]{2,0,1:T(8,128)S(1)}, u32[]{:S(2)}, u32[]{:S(2)}) collective-permute-start(f32[8,2,130]{2,0,1:T(8,128)S(1)} %get-tuple-element.20), channel_id=1, source_target_pairs={{0,12},{1,13},{2,14},{3,15},{4,8},{5,9},{6,10},{7,11},{8,4},{9,5},... | collective-permute-start | bytes 24968 | tf_op jit(solution)/shard_map/ppermute | solution.py:101
  50.5 5.7 %collective-permute-start.15 = (f32[4,8,2,130]{3,1,2,0:T(8,128)S(1)}, f32[4,8,2,130]{3,1,2,0:T(8,128)S(1)}, u32[]{:S(2)}, u32[]{:S(2)}) collective-permute-start(f32[4,8,2,130]{3,1,2,0:T(8,128)S(1)} %select_reduce_fusion.5), channel_id=1, source_target_pairs={{0,1},{1,0},{2,3},{3,2},{4,5},{5,4},{6,7},{7,6},{8,9},{9,8},{10,11... | collective-permute-start | bytes 99848 | tf_op jit(solution)/shard_map/ppermute | solution.py:105
  54.3 3.7 %collective-permute-start.16 = (f32[4,8,2,130]{3,1,2,0:T(8,128)S(1)}, f32[4,8,2,130]{3,1,2,0:T(8,128)S(1)}, u32[]{:S(2)}, u32[]{:S(2)}) collective-permute-start(f32[4,8,2,130]{3,1,2,0:T(8,128)S(1)} %select_reduce_fusion.5), channel_id=1, source_target_pairs={{0,2},{1,3},{2,0},{3,1},{4,6},{5,7},{6,4},{7,5},{8,10},{9,11},{10,... | collective-permute-start | bytes 99848 | tf_op jit(solution)/shard_map/ppermute | solution.py:105
  55.3 4.3 %collective-permute-start.17 = (f32[4,8,2,130]{3,1,2,0:T(8,128)S(1)}, f32[4,8,2,130]{3,1,2,0:T(8,128)S(1)}, u32[]{:S(2)}, u32[]{:S(2)}) collective-permute-start(f32[4,8,2,130]{3,1,2,0:T(8,128)S(1)} %select_reduce_fusion.5), channel_id=1, source_target_pairs={{0,3},{1,2},{2,1},{3,0},{4,7},{5,6},{6,5},{7,4},{8,11},{9,10},{10,... | collective-permute-start | bytes 99848 | tf_op jit(solution)/shard_map/ppermute | solution.py:105
  72.6 7.4 %collective-permute-start.18 = (f32[8,512]{1,0:T(8,128)S(1)}, f32[8,512]{1,0:T(8,128)S(1)}, u32[]{:S(2)}, u32[]{:S(2)}) collective-permute-start(f32[8,512]{1,0:T(8,128)S(1)} %get-tuple-element.18), channel_id=1, source_target_pairs={{0,0},{1,4},{2,8},{3,12},{4,1},{5,5},{6,9},{7,13},{8,2},{9,6},{10,... | collective-permute-start | bytes 49160 | tf_op jit(solution)/shard_map/ppermute | solution.py:299
  74.5 5.4 %collective-permute-start.19 = (f32[8,512]{1,0:T(8,128)S(1)}, f32[8,512]{1,0:T(8,128)S(1)}, u32[]{:S(2)}, u32[]{:S(2)}) collective-permute-start(f32[8,512]{1,0:T(8,128)S(1)} %get-tuple-element.15), channel_id=1, source_target_pairs={{0,1},{1,5},{2,9},{3,13},{4,0},{5,4},{6,8},{7,12},{8,3},{9,7},{10,... | collective-permute-start | bytes 49160 | tf_op jit(solution)/shard_map/ppermute | solution.py:299
  74.6 6.0 %collective-permute-start.20 = (f32[8,512]{1,0:T(8,128)S(1)}, f32[8,512]{1,0:T(8,128)S(1)}, u32[]{:S(2)}, u32[]{:S(2)}) collective-permute-start(f32[8,512]{1,0:T(8,128)S(1)} %get-tuple-element.17), channel_id=1, source_target_pairs={{0,2},{1,6},{2,10},{3,14},{4,3},{5,7},{6,11},{7,15},{8,0},{9,4},{1... | collective-permute-start | bytes 49160 | tf_op jit(solution)/shard_map/ppermute | solution.py:299
  79.4 4.1 %collective-permute-start.21 = (f32[8,512]{1,0:T(8,128)S(1)}, f32[8,512]{1,0:T(8,128)S(1)}, u32[]{:S(2)}, u32[]{:S(2)}) collective-permute-start(f32[8,512]{1,0:T(8,128)S(1)} %get-tuple-element.16), channel_id=1, source_target_pairs={{0,3},{1,7},{2,11},{3,15},{4,2},{5,6},{6,10},{7,14},{8,1},{9,5},{1... | collective-permute-start | bytes 49160 | tf_op jit(solution)/shard_map/ppermute | solution.py:299

commit v11 on v6

--- a/solution.py
+++ b/solution.py
@@ -134,6 +134,7 @@
     row_order = jnp.arange(GR, dtype=jnp.int32) ^ grid_row
     col_order = jnp.arange(grid_cols, dtype=jnp.int32) ^ grid_col
     direct_cols = grid_cols <= 4
+    direct_sums = False
     if direct_cols:
         from_cols = [hidden_in[0]] + [swap_cols(hidden_in[0], "tp", s) for s in range(1, grid_cols)]
         in_row = pick(jnp.stack(from_cols), col_order)
@@ -169,7 +170,7 @@
     keyval_term = pick(keyval_part, dest_copy * KVH + dest_head)
     width = 4 * HD
     compact = jnp.concatenate([query_pick, keyval_term], -1)
-    if direct_cols:
+    if direct_sums:
         by_col = compact.reshape(GR, grid_cols, ROWS, width)
         held = lax.dynamic_index_in_dim(by_col, grid_col, 1, keepdims=False)
         for s in range(1, grid_cols):

time: 78.1 us -> 78.3 us (level)
    ppermute x1 -> x3, starting transfers between devices: 2.06 us -> 6.06 us  [from_partner(): return lax.ppermute(value, axis, pairs)]
    ppermute x9 -> x6, starting transfers between devices: 9.89 us -> 6.63 us  [swap_cols(): lax.ppermute(value, axis, [(t, t ^ s) for t in range(lax.axis_size(axis))])]
    ppermute x9 -> x6, waiting for transfers between devices: 5.8 us -> 2.53 us  [swap_cols(): lax.ppermute(value, axis, [(t, t ^ s) for t in range(lax.axis_size(axis))])]
    ppermute x1 -> x3, waiting for transfers between devices: 1.17 us -> 3.92 us  [from_partner(): return lax.ppermute(value, axis, pairs)]
  transfers between devices with their start and end apart: 23 -> 22, of which waited for: 13 -> 13; matrix products, arithmetic and copies ran while one was open for 5% -> 5% of each run, Pallas kernels for 0% -> 0%
where the time goes in v11:
time: 78.3 us; the launch traced here: 77.9 us
  starting transfers between devices  31.2 us (40%)
  waiting for transfers between devices  18.6 us (24%)
  matrix products  18.4 us (23%)
  other arithmetic  5.55 us (7%)
  local copies, waits for them, and re-layouts  3.82 us (5%)
    ppermute x9, starting transfers between devices, swap_rows(): lax.ppermute(value, axis, [(t, t ^ shift) for t in range(lax.axis_size(ax...  11.8 us
    ppermute x9, waiting for transfers between devices, swap_rows(): lax.ppermute(value, axis, [(t, t ^ shift) for t in range(lax.axis_size(ax...  8.4 us
    ppermute x4, starting transfers between devices, local(): got = lax.ppermute(piece, 'tp', pairs)  6.7 us
    ppermute x6, starting transfers between devices, swap_cols(): lax.ppermute(value, axis, [(t, t ^ s) for t in range(lax.axis_size(axis))])  6.63 us
    ppermute x3, starting transfers between devices, from_partner(): return lax.ppermute(value, axis, pairs)  6.06 us
    dot_general x1, matrix products, local(): jnp.einsum('rc,aec->rae', col_rows, q_blocks[0], preferred_element_type=j...  5.65 us
    dot_general x1, matrix products, local(): jnp.einsum('gabe,cae->gbc', chosen, o_blocks[0], preferred_element_type=j...  5.65 us
    ppermute x3, waiting for transfers between devices, from_partner(): return lax.ppermute(value, axis, pairs)  3.92 us
  transfers between devices with their start and end apart: 22, of which 13 were waited for; matrix products, arithmetic and copies ran while one was open for 5% of the time, Pallas kernels for 0%

profile of v11, /device:TPU:1, one launch (start us, length us, event | category | flops | bytes accessed | tf_op | source)
XLA Modules:
  0.0 77.9 jit_solution(265067678342380081)
XLA Ops:
  0.1 2.7 %collective-permute-start.1 = (bf16[8,512]{1,0:T(8,128)(2,1)}, bf16[8,512]{1,0:T(8,128)(2,1)S(1)}, u32[]{:S(2)}, u32[]{:S(2)}) collective-permute-start(bf16[8,512]{1,0:T(8,128)(2,1)} %bitcast.224), channel_id=1, source_target_pairs={{0,2},{1,3},{2,0},{3,1},{4,6},{5,7},{6,4},{7,5},{8,10},{9,11},{10,... | collective-permute-start | bytes 24584 | tf_op jit(solution)/shard_map/ppermute | solution.py:105
  3.8 1.3 %gather_fusion.1 = s32[16]{0:T(128)S(1)} fusion(s32[16]{0:T(128)} %param.14, s32[1024]{0:T(1024)S(1)} %pad_clamp_fusion), kind=kCustom, calls=%fused_computation.1 | custom fusion | bytes 192 | tf_op jit(solution)/shard_map/gather | solution.py:128
  6.8 3.8 %collective-permute-start.5 = (bf16[4,8,512]{2,1,0:T(8,128)(2,1)S(1)}, bf16[4,8,512]{2,1,0:T(8,128)(2,1)S(1)}, u32[]{:S(2)}, u32[]{:S(2)}) collective-permute-start(bf16[4,8,512]{2,1,0:T(8,128)(2,1)S(1)} %select_reduce_fusion.7), channel_id=1, source_target_pairs={{0,12},{1,13},{2,14},{3,15},{4,8},{5,9},{6,10},{7,11},{8,4},{9,5},... | collective-permute-start | bytes 98312 | tf_op jit(solution)/shard_map/ppermute | solution.py:101
  11.1 1.2 %collective-permute-done.5 = bf16[4,8,512]{2,1,0:T(8,128)(2,1)S(1)} collective-permute-done((bf16[4,8,512]{2,1,0:T(8,128)(2,1)S(1)}, bf16[4,8,512]{2,1,0:T(8,128)(2,1)S(1)}, u32[]{:S(2)}, u32[]{:S(2)}) %collective-permute-start.5) | collective-permute-done | bytes 32800 | tf_op jit(solution)/shard_map/ppermute | solution.py:101
  16.3 5.7 %fusion.14 = f32[16,8,128]{2,1,0:T(8,128)S(1)} fusion(bf16[1,16,128,2048]{3,2,1,0:T(8,128)(2,1)} %param.11, bf16[8,8192]{1,0:T(8,128)(2,1)S(1)} %multiply_convert_fusion, s32[]{:T(128)S(6)} %select_n.308), kind=kOutput, calls=%fused_computation.12 | convolution fusion | flops 67108864 | bytes 8486916 | tf_op jit(solution)/shard_map/rc,aec->rae/dot_general | solution.py:153
  23.0 1.6 %collective-permute-start.6 = (f32[2,2,2,8,512]{4,3,2,1,0:T(8,128)S(1)}, f32[2,2,2,8,512]{4,3,2,1,0:T(8,128)S(1)}, u32[]{:S(2)}, u32[]{:S(2)}) collective-permute-start(f32[2,2,2,8,512]{4,3,2,1,0:T(8,128)S(1)} %select_bitcast_fusion.1), channel_id=1, source_target_pairs={{0,1},{1,0},{2,3},{3,2},{4,5},{5,4},{6,7},{7,6},{8,9},{9,8},{10,11... | collective-permute-start | bytes 393224 | tf_op jit(solution)/shard_map/ppermute | solution.py:19
  25.6 1.3 %collective-permute-start.7 = (f32[2,2,8,512]{3,2,1,0:T(8,128)S(1)}, f32[2,2,8,512]{3,2,1,0:T(8,128)S(1)}, u32[]{:S(2)}, u32[]{:S(2)}) collective-permute-start(f32[2,2,8,512]{3,2,1,0:T(8,128)S(1)} %select_bitcast_fusion.2), channel_id=1, source_target_pairs={{0,2},{1,3},{2,0},{3,1},{4,6},{5,7},{6,4},{7,5},{8,10},{9,11},{10,... | collective-permute-start | bytes 196616 | tf_op jit(solution)/shard_map/ppermute | solution.py:19
  27.0 1.8 %collective-permute-done.7 = f32[2,2,8,512]{3,2,1,0:T(8,128)S(1)} collective-permute-done((f32[2,2,8,512]{3,2,1,0:T(8,128)S(1)}, f32[2,2,8,512]{3,2,1,0:T(8,128)S(1)}, u32[]{:S(2)}, u32[]{:S(2)}) %collective-permute-start.7) | collective-permute-done | bytes 65568 | tf_op jit(solution)/shard_map/ppermute | solution.py:19
  28.8 1.8 %collective-permute-start.8 = (f32[8,512]{1,0:T(8,128)S(1)}, f32[8,512]{1,0:T(8,128)S(1)}, u32[]{:S(2)}, u32[]{:S(2)}) collective-permute-start(f32[8,512]{1,0:T(8,128)S(1)} %get-tuple-element.26), channel_id=1, source_target_pairs={{0,4},{1,5},{2,6},{3,7},{4,0},{5,1},{6,2},{7,3},{8,12},{9,13},{10,... | collective-permute-start | bytes 49160 | tf_op jit(solution)/shard_map/ppermute | solution.py:101
  30.6 2.2 %collective-permute-start.10 = (f32[8,512]{1,0:T(8,128)S(1)}, f32[8,512]{1,0:T(8,128)S(1)}, u32[]{:S(2)}, u32[]{:S(2)}) collective-permute-start(f32[8,512]{1,0:T(8,128)S(1)} %get-tuple-element.24), channel_id=1, source_target_pairs={{0,12},{1,13},{2,14},{3,15},{4,8},{5,9},{6,10},{7,11},{8,4},{9,5},... | collective-permute-start | bytes 49160 | tf_op jit(solution)/shard_map/ppermute | solution.py:101
  32.8 1.3 %collective-permute-done.9 = f32[8,512]{1,0:T(8,128)S(1)} collective-permute-done((f32[8,512]{1,0:T(8,128)S(1)}, f32[8,512]{1,0:T(8,128)S(1)}, u32[]{:S(2)}, u32[]{:S(2)}) %collective-permute-start.9) | collective-permute-done | bytes 16416 | tf_op jit(solution)/shard_map/ppermute | solution.py:101
  35.3 3.5 %select_reduce_fusion.4 = (f32[8,8]{1,0:T(8,128)S(1)}, f32[8,8,2048]{2,1,0:T(8,128)S(1)}) fusion(pred[8,2048]{1,0:T(8,128)(4,1)S(1)} %iota_compare_fusion, bf16[8,8,128]{2,1,0:T(8,128)(2,1)S(1)} %bitcast.209, bf16[1,8,2048,128]{3,2,1,0:T(8,128)(2,1)} %param.15), kind=kOutput, calls=%fused_computation.20 | convolution fusion | flops 33947584 | bytes 4751616 | tf_op jit(solution)/shard_map/bhe,bte->bht/dot_general | solution.py:199
  39.1 2.9 %fusion.17 = f32[8,8,128]{2,1,0:T(8,128)S(1)} fusion(bf16[1,8,2048,128]{3,2,1,0:T(8,128)(2,1)} %param.16, f32[8,8,2048]{2,1,0:T(8,128)S(1)} %get-tuple-element.43, f32[8,8]{1,0:T(8,128)S(1)} %fusion.42, pred[8,2048]{1,0:T(8,128)(4,1)S(1)} %iota_compare_fusion, f32[8,128]{1,0:T(8,128)S(1)} %get-tuple-element.39, f32[8,8]{1,0:T(8,128)S(1)} %convert_element_type.70), kind=kOutput, calls=%fused_computation.14 | convolution fusion | flops 33964032 | bytes 4772352 | tf_op jit(solution)/shard_map/bht,bte->bhe/dot_general | solution.py:212
  42.6 3.2 %collective-permute-start.11 = (f32[8,4,130]{0,1,2:T(4,128)S(1)}, f32[8,4,130]{0,1,2:T(4,128)S(1)}, u32[]{:S(2)}, u32[]{:S(2)}) collective-permute-start(f32[8,4,130]{0,1,2:T(4,128)S(1)} %pad_maximum_fusion), channel_id=1, source_target_pairs={{0,1},{1,0},{2,3},{3,2},{4,5},{5,4},{6,7},{7,6},{8,9},{9,8},{10,11... | collective-permute-start | bytes 49928 | tf_op jit(solution)/shard_map/ppermute | solution.py:19
  47.6 2.2 %collective-permute-start.13 = (bf16[8,128]{1,0:T(8,128)(2,1)S(1)}, bf16[8,128]{1,0:T(8,128)(2,1)S(1)}, u32[]{:S(2)}, u32[]{:S(2)}) collective-permute-start(bf16[8,128]{1,0:T(8,128)(2,1)S(1)} %bitcast.233), channel_id=1, source_target_pairs={{0,8},{1,9},{2,10},{3,11},{4,12},{5,13},{6,14},{7,15},{8,0},{9,1},... | collective-permute-start | bytes 6152 | tf_op jit(solution)/shard_map/ppermute | solution.py:101
  49.9 1.4 %collective-permute-start.14 = (bf16[8,128]{1,0:T(8,128)(2,1)S(1)}, bf16[8,128]{1,0:T(8,128)(2,1)S(1)}, u32[]{:S(2)}, u32[]{:S(2)}) collective-permute-start(bf16[8,128]{1,0:T(8,128)(2,1)S(1)} %bitcast.234), channel_id=1, source_target_pairs={{0,12},{1,13},{2,14},{3,15},{4,8},{5,9},{6,10},{7,11},{8,4},{9,5},... | collective-permute-start | bytes 6152 | tf_op jit(solution)/shard_map/ppermute | solution.py:101
  51.3 2.8 %collective-permute-done.14 = bf16[8,128]{1,0:T(8,128)(2,1)S(1)} collective-permute-done((bf16[8,128]{1,0:T(8,128)(2,1)S(1)}, bf16[8,128]{1,0:T(8,128)(2,1)S(1)}, u32[]{:S(2)}, u32[]{:S(2)}) %collective-permute-start.14) | collective-permute-done | bytes 2080 | tf_op jit(solution)/shard_map/ppermute | solution.py:101
  54.3 2.1 %collective-permute-start.15 = (bf16[4,8,128]{2,1,0:T(8,128)(2,1)S(1)}, bf16[4,8,128]{2,1,0:T(8,128)(2,1)S(1)}, u32[]{:S(2)}, u32[]{:S(2)}) collective-permute-start(bf16[4,8,128]{2,1,0:T(8,128)(2,1)S(1)} %select_reduce_fusion.10), channel_id=1, source_target_pairs={{0,1},{1,0},{2,3},{3,2},{4,5},{5,4},{6,7},{7,6},{8,9},{9,8},{10,11... | collective-permute-start | bytes 24584 | tf_op jit(solution)/shard_map/ppermute | solution.py:105
  56.4 1.2 %collective-permute-start.16 = (bf16[4,8,128]{2,1,0:T(8,128)(2,1)S(1)}, bf16[4,8,128]{2,1,0:T(8,128)(2,1)S(1)}, u32[]{:S(2)}, u32[]{:S(2)}) collective-permute-start(bf16[4,8,128]{2,1,0:T(8,128)(2,1)S(1)} %select_reduce_fusion.10), channel_id=1, source_target_pairs={{0,2},{1,3},{2,0},{3,1},{4,6},{5,7},{6,4},{7,5},{8,10},{9,11},{10,... | collective-permute-start | bytes 24584 | tf_op jit(solution)/shard_map/ppermute | solution.py:105
  59.0 1.8 %collective-permute-done.17 = bf16[4,8,128]{2,1,0:T(8,128)(2,1)S(1)} collective-permute-done((bf16[4,8,128]{2,1,0:T(8,128)(2,1)S(1)}, bf16[4,8,128]{2,1,0:T(8,128)(2,1)S(1)}, u32[]{:S(2)}, u32[]{:S(2)}) %collective-permute-start.17) | collective-permute-done | bytes 8224 | tf_op jit(solution)/shard_map/ppermute | solution.py:105
  61.2 5.6 %fusion.11 = f32[8,4,512]{2,0,1:T(8,128)S(1)} fusion(bf16[4,512,16,128]{3,2,1,0:T(8,128)(2,1)} %bitcast.198, bf16[16,8,128]{2,1,0:T(8,128)(2,1)S(1)} %select_reduce_fusion.3), kind=kOutput, calls=%fused_computation.11 | convolution fusion | flops 67108864 | bytes 8486912 | tf_op jit(solution)/shard_map/gabe,cae->gbc/dot_general | solution.py:258
  66.9 1.9 %collective-permute-start.18 = (f32[8,512]{1,0:T(8,128)S(1)}, f32[8,512]{1,0:T(8,128)S(1)}, u32[]{:S(2)}, u32[]{:S(2)}) collective-permute-start(f32[8,512]{1,0:T(8,128)S(1)} %get-tuple-element.22), channel_id=1, source_target_pairs={{0,0},{1,4},{2,8},{3,12},{4,1},{5,5},{6,9},{7,13},{8,2},{9,6},{10,... | collective-permute-start | bytes 49160 | tf_op jit(solution)/shard_map/ppermute | solution.py:265
  68.9 4.4 %collective-permute-start.20 = (f32[8,512]{1,0:T(8,128)S(1)}, f32[8,512]{1,0:T(8,128)S(1)}, u32[]{:S(2)}, u32[]{:S(2)}) collective-permute-start(f32[8,512]{1,0:T(8,128)S(1)} %get-tuple-element.21), channel_id=1, source_target_pairs={{0,2},{1,6},{2,10},{3,14},{4,3},{5,7},{6,11},{7,15},{8,0},{9,4},{1... | collective-permute-start | bytes 49160 | tf_op jit(solution)/shard_map/ppermute | solution.py:265
  74.4 2.9 %collective-permute-done.21 = f32[8,512]{1,0:T(8,128)S(1)} collective-permute-done((f32[8,512]{1,0:T(8,128)S(1)}, f32[8,512]{1,0:T(8,128)S(1)}, u32[]{:S(2)}, u32[]{:S(2)}) %collective-permute-start.21) | collective-permute-done | bytes 16416 | tf_op jit(solution)/shard_map/ppermute | solution.py:265
  (105 shorter events, 16.9 us)
Async XLA Ops:
  0.0 15.7 %copy-start = (bf16[2,1024,512]{2,1,0:T(8,128)(2,1)S(1)}, bf16[2,1024,512]{2,1,0:T(8,128)(2,1)}, u32[]{:S(2)}) copy-start(bf16[2,1024,512]{2,1,0:T(8,128)(2,1)} %param.13) | copy-start | bytes 6291460
  0.0 6.0 %collective-permute-start = (bf16[8,512]{1,0:T(8,128)(2,1)}, bf16[8,512]{1,0:T(8,128)(2,1)S(1)}, u32[]{:S(2)}, u32[]{:S(2)}) collective-permute-start(bf16[8,512]{1,0:T(8,128)(2,1)} %bitcast.223), channel_id=1, source_target_pairs={{0,1},{1,0},{2,3},{3,2},{4,5},{5,4},{6,7},{7,6},{8,9},{9,8},{10,11... | collective-permute-start | bytes 24584 | tf_op jit(solution)/shard_map/ppermute | solution.py:105
  0.1 5.9 %collective-permute-start.1 = (bf16[8,512]{1,0:T(8,128)(2,1)}, bf16[8,512]{1,0:T(8,128)(2,1)S(1)}, u32[]{:S(2)}, u32[]{:S(2)}) collective-permute-start(bf16[8,512]{1,0:T(8,128)(2,1)} %bitcast.224), channel_id=1, source_target_pairs={{0,2},{1,3},{2,0},{3,1},{4,6},{5,7},{6,4},{7,5},{8,10},{9,11},{10,... | collective-permute-start | bytes 24584 | tf_op jit(solution)/shard_map/ppermute | solution.py:105
  2.7 3.3 %collective-permute-start.2 = (bf16[8,512]{1,0:T(8,128)(2,1)}, bf16[8,512]{1,0:T(8,128)(2,1)S(1)}, u32[]{:S(2)}, u32[]{:S(2)}) collective-permute-start(bf16[8,512]{1,0:T(8,128)(2,1)} %bitcast.225), channel_id=1, source_target_pairs={{0,3},{1,2},{2,1},{3,0},{4,7},{5,6},{6,5},{7,4},{8,11},{9,10},{10,... | collective-permute-start | bytes 24584 | tf_op jit(solution)/shard_map/ppermute | solution.py:105
  6.8 5.4 %collective-permute-start.5 = (bf16[4,8,512]{2,1,0:T(8,128)(2,1)S(1)}, bf16[4,8,512]{2,1,0:T(8,128)(2,1)S(1)}, u32[]{:S(2)}, u32[]{:S(2)}) collective-permute-start(bf16[4,8,512]{2,1,0:T(8,128)(2,1)S(1)} %select_reduce_fusion.7), channel_id=1, source_target_pairs={{0,12},{1,13},{2,14},{3,15},{4,8},{5,9},{6,10},{7,11},{8,4},{9,5},... | collective-permute-start | bytes 98312 | tf_op jit(solution)/shard_map/ppermute | solution.py:101
  10.7 2.8 %collective-permute-start.3 = (bf16[4,8,512]{2,1,0:T(8,128)(2,1)S(1)}, bf16[4,8,512]{2,1,0:T(8,128)(2,1)S(1)}, u32[]{:S(2)}, u32[]{:S(2)}) collective-permute-start(bf16[4,8,512]{2,1,0:T(8,128)(2,1)S(1)} %select_reduce_fusion.7), channel_id=1, source_target_pairs={{0,4},{1,5},{2,6},{3,7},{4,0},{5,1},{6,2},{7,3},{8,12},{9,13},{10,... | collective-permute-start | bytes 98312 | tf_op jit(solution)/shard_map/ppermute | solution.py:101
  10.7 3.8 %collective-permute-start.4 = (bf16[4,8,512]{2,1,0:T(8,128)(2,1)S(1)}, bf16[4,8,512]{2,1,0:T(8,128)(2,1)S(1)}, u32[]{:S(2)}, u32[]{:S(2)}) collective-permute-start(bf16[4,8,512]{2,1,0:T(8,128)(2,1)S(1)} %select_reduce_fusion.7), channel_id=1, source_target_pairs={{0,8},{1,9},{2,10},{3,11},{4,12},{5,13},{6,14},{7,15},{8,0},{9,1},... | collective-permute-start | bytes 98312 | tf_op jit(solution)/shard_map/ppermute | solution.py:101
  16.3 10.6 %copy-start.1 = (s32[1,8]{1,0:T(1,128)S(1)}, s32[1,8]{1,0:T(1,128)}, u32[]{:S(2)}) copy-start(s32[1,8]{1,0:T(1,128)} %param.17) | copy-start | bytes 100
  23.0 2.5 %collective-permute-start.6 = (f32[2,2,2,8,512]{4,3,2,1,0:T(8,128)S(1)}, f32[2,2,2,8,512]{4,3,2,1,0:T(8,128)S(1)}, u32[]{:S(2)}, u32[]{:S(2)}) collective-permute-start(f32[2,2,2,8,512]{4,3,2,1,0:T(8,128)S(1)} %select_bitcast_fusion.1), channel_id=1, source_target_pairs={{0,1},{1,0},{2,3},{3,2},{4,5},{5,4},{6,7},{7,6},{8,9},{9,8},{10,11... | collective-permute-start | bytes 393224 | tf_op jit(solution)/shard_map/ppermute | solution.py:19
  25.6 3.2 %collective-permute-start.7 = (f32[2,2,8,512]{3,2,1,0:T(8,128)S(1)}, f32[2,2,8,512]{3,2,1,0:T(8,128)S(1)}, u32[]{:S(2)}, u32[]{:S(2)}) collective-permute-start(f32[2,2,8,512]{3,2,1,0:T(8,128)S(1)} %select_bitcast_fusion.2), channel_id=1, source_target_pairs={{0,2},{1,3},{2,0},{3,1},{4,6},{5,7},{6,4},{7,5},{8,10},{9,11},{10,... | collective-permute-start | bytes 196616 | tf_op jit(solution)/shard_map/ppermute | solution.py:19
  28.8 4.0 %collective-permute-start.8 = (f32[8,512]{1,0:T(8,128)S(1)}, f32[8,512]{1,0:T(8,128)S(1)}, u32[]{:S(2)}, u32[]{:S(2)}) collective-permute-start(f32[8,512]{1,0:T(8,128)S(1)} %get-tuple-element.26), channel_id=1, source_target_pairs={{0,4},{1,5},{2,6},{3,7},{4,0},{5,1},{6,2},{7,3},{8,12},{9,13},{10,... | collective-permute-start | bytes 49160 | tf_op jit(solution)/shard_map/ppermute | solution.py:101
  30.6 3.5 %collective-permute-start.9 = (f32[8,512]{1,0:T(8,128)S(1)}, f32[8,512]{1,0:T(8,128)S(1)}, u32[]{:S(2)}, u32[]{:S(2)}) collective-permute-start(f32[8,512]{1,0:T(8,128)S(1)} %get-tuple-element.25), channel_id=1, source_target_pairs={{0,8},{1,9},{2,10},{3,11},{4,12},{5,13},{6,14},{7,15},{8,0},{9,1},... | collective-permute-start | bytes 49160 | tf_op jit(solution)/shard_map/ppermute | solution.py:101
  30.6 4.4 %collective-permute-start.10 = (f32[8,512]{1,0:T(8,128)S(1)}, f32[8,512]{1,0:T(8,128)S(1)}, u32[]{:S(2)}, u32[]{:S(2)}) collective-permute-start(f32[8,512]{1,0:T(8,128)S(1)} %get-tuple-element.24), channel_id=1, source_target_pairs={{0,12},{1,13},{2,14},{3,15},{4,8},{5,9},{6,10},{7,11},{8,4},{9,5},... | collective-permute-start | bytes 49160 | tf_op jit(solution)/shard_map/ppermute | solution.py:101
  42.6 4.4 %collective-permute-start.11 = (f32[8,4,130]{0,1,2:T(4,128)S(1)}, f32[8,4,130]{0,1,2:T(4,128)S(1)}, u32[]{:S(2)}, u32[]{:S(2)}) collective-permute-start(f32[8,4,130]{0,1,2:T(4,128)S(1)} %pad_maximum_fusion), channel_id=1, source_target_pairs={{0,1},{1,0},{2,3},{3,2},{4,5},{5,4},{6,7},{7,6},{8,9},{9,8},{10,11... | collective-permute-start | bytes 49928 | tf_op jit(solution)/shard_map/ppermute | solution.py:19
  47.5 3.8 %collective-permute-start.12 = (bf16[8,128]{1,0:T(8,128)(2,1)S(1)}, bf16[8,128]{1,0:T(8,128)(2,1)S(1)}, u32[]{:S(2)}, u32[]{:S(2)}) collective-permute-start(bf16[8,128]{1,0:T(8,128)(2,1)S(1)} %bitcast.232), channel_id=1, source_target_pairs={{0,4},{1,5},{2,6},{3,7},{4,0},{5,1},{6,2},{7,3},{8,12},{9,13},{10,... | collective-permute-start | bytes 6152 | tf_op jit(solution)/shard_map/ppermute | solution.py:101
  47.6 3.7 %collective-permute-start.13 = (bf16[8,128]{1,0:T(8,128)(2,1)S(1)}, bf16[8,128]{1,0:T(8,128)(2,1)S(1)}, u32[]{:S(2)}, u32[]{:S(2)}) collective-permute-start(bf16[8,128]{1,0:T(8,128)(2,1)S(1)} %bitcast.233), channel_id=1, source_target_pairs={{0,8},{1,9},{2,10},{3,11},{4,12},{5,13},{6,14},{7,15},{8,0},{9,1},... | collective-permute-start | bytes 6152 | tf_op jit(solution)/shard_map/ppermute | solution.py:101
  49.9 4.3 %collective-permute-start.14 = (bf16[8,128]{1,0:T(8,128)(2,1)S(1)}, bf16[8,128]{1,0:T(8,128)(2,1)S(1)}, u32[]{:S(2)}, u32[]{:S(2)}) collective-permute-start(bf16[8,128]{1,0:T(8,128)(2,1)S(1)} %bitcast.234), channel_id=1, source_target_pairs={{0,12},{1,13},{2,14},{3,15},{4,8},{5,9},{6,10},{7,11},{8,4},{9,5},... | collective-permute-start | bytes 6152 | tf_op jit(solution)/shard_map/ppermute | solution.py:101
  54.3 3.9 %collective-permute-start.15 = (bf16[4,8,128]{2,1,0:T(8,128)(2,1)S(1)}, bf16[4,8,128]{2,1,0:T(8,128)(2,1)S(1)}, u32[]{:S(2)}, u32[]{:S(2)}) collective-permute-start(bf16[4,8,128]{2,1,0:T(8,128)(2,1)S(1)} %select_reduce_fusion.10), channel_id=1, source_target_pairs={{0,1},{1,0},{2,3},{3,2},{4,5},{5,4},{6,7},{7,6},{8,9},{9,8},{10,11... | collective-permute-start | bytes 24584 | tf_op jit(solution)/shard_map/ppermute | solution.py:105
  56.4 2.5 %collective-permute-start.16 = (bf16[4,8,128]{2,1,0:T(8,128)(2,1)S(1)}, bf16[4,8,128]{2,1,0:T(8,128)(2,1)S(1)}, u32[]{:S(2)}, u32[]{:S(2)}) collective-permute-start(bf16[4,8,128]{2,1,0:T(8,128)(2,1)S(1)} %select_reduce_fusion.10), channel_id=1, source_target_pairs={{0,2},{1,3},{2,0},{3,1},{4,6},{5,7},{6,4},{7,5},{8,10},{9,11},{10,... | collective-permute-start | bytes 24584 | tf_op jit(solution)/shard_map/ppermute | solution.py:105
  57.7 3.1 %collective-permute-start.17 = (bf16[4,8,128]{2,1,0:T(8,128)(2,1)S(1)}, bf16[4,8,128]{2,1,0:T(8,128)(2,1)S(1)}, u32[]{:S(2)}, u32[]{:S(2)}) collective-permute-start(bf16[4,8,128]{2,1,0:T(8,128)(2,1)S(1)} %select_reduce_fusion.10), channel_id=1, source_target_pairs={{0,3},{1,2},{2,1},{3,0},{4,7},{5,6},{6,5},{7,4},{8,11},{9,10},{10,... | collective-permute-start | bytes 24584 | tf_op jit(solution)/shard_map/ppermute | solution.py:105
  66.9 6.7 %collective-permute-start.18 = (f32[8,512]{1,0:T(8,128)S(1)}, f32[8,512]{1,0:T(8,128)S(1)}, u32[]{:S(2)}, u32[]{:S(2)}) collective-permute-start(f32[8,512]{1,0:T(8,128)S(1)} %get-tuple-element.22), channel_id=1, source_target_pairs={{0,0},{1,4},{2,8},{3,12},{4,1},{5,5},{6,9},{7,13},{8,2},{9,6},{10,... | collective-permute-start | bytes 49160 | tf_op jit(solution)/shard_map/ppermute | solution.py:265
  68.8 4.8 %collective-permute-start.19 = (f32[8,512]{1,0:T(8,128)S(1)}, f32[8,512]{1,0:T(8,128)S(1)}, u32[]{:S(2)}, u32[]{:S(2)}) collective-permute-start(f32[8,512]{1,0:T(8,128)S(1)} %get-tuple-element.19), channel_id=1, source_target_pairs={{0,1},{1,5},{2,9},{3,13},{4,0},{5,4},{6,8},{7,12},{8,3},{9,7},{10,... | collective-permute-start | bytes 49160 | tf_op jit(solution)/shard_map/ppermute | solution.py:265
  68.9 5.5 %collective-permute-start.20 = (f32[8,512]{1,0:T(8,128)S(1)}, f32[8,512]{1,0:T(8,128)S(1)}, u32[]{:S(2)}, u32[]{:S(2)}) collective-permute-start(f32[8,512]{1,0:T(8,128)S(1)} %get-tuple-element.21), channel_id=1, source_target_pairs={{0,2},{1,6},{2,10},{3,14},{4,3},{5,7},{6,11},{7,15},{8,0},{9,4},{1... | collective-permute-start | bytes 49160 | tf_op jit(solution)/shard_map/ppermute | solution.py:265
  73.3 4.1 %collective-permute-start.21 = (f32[8,512]{1,0:T(8,128)S(1)}, f32[8,512]{1,0:T(8,128)S(1)}, u32[]{:S(2)}, u32[]{:S(2)}) collective-permute-start(f32[8,512]{1,0:T(8,128)S(1)} %get-tuple-element.20), channel_id=1, source_target_pairs={{0,3},{1,7},{2,11},{3,15},{4,2},{5,6},{6,10},{7,14},{8,1},{9,5},{1... | collective-permute-start | bytes 49160 | tf_op jit(solution)/shard_map/ppermute | solution.py:265

commit v12 on v6

--- a/solution.py
+++ b/solution.py
@@ -193,48 +193,53 @@
     keyval_new = keyval_sum.astype(jnp.bfloat16)
     key_new = keyval_new[:, :HD]
     value_new = keyval_new[:, HD:]
-    scale = 1.0 / HD**0.5
-    scores = (
-        jnp.einsum("bhe,bte->bht", both_queries, key_cache[0], preferred_element_type=jnp.float32)
-        * scale
-    )
-    positions = jnp.arange(scores.shape[2], dtype=jnp.int32)
-    masked = positions[None, None, :] < lengths[0][:, None, None]
-    new_score = (
-        jnp.einsum("bhe,be->bh", both_queries, key_new, preferred_element_type=jnp.float32) * scale
-    )
-    new_score = jnp.where(my_half == 0, new_score, jnp.float32(-1e30))
-    top = jnp.maximum(jnp.max(jnp.where(masked, scores, jnp.float32(-1e30)), axis=-1), new_score)
-    weights = jnp.where(masked, jnp.exp(scores - top[..., None]), jnp.float32(0.0))
-    new_weight = jnp.exp(new_score - top)
-    total = jnp.sum(weights, axis=-1) + new_weight
-    summed = jnp.einsum(
-        "bht,bte->bhe",
-        weights.astype(jnp.bfloat16),
-        value_cache[0],
-        preferred_element_type=jnp.float32,
-    )
-    new_rounded = lax.optimization_barrier(new_weight.astype(jnp.bfloat16)).astype(jnp.float32)
-    summed = summed + new_rounded[..., None] * value_new.astype(jnp.float32)[:, None, :]
-    top_split = top.reshape(ROWS, 2, GR)
-    total_split = total.reshape(ROWS, 2, GR)
-    summed_split = summed.reshape(ROWS, 2, GR, HD)
-    first_half = my_half == 0
-    own_top = jnp.where(first_half, top_split[:, 0], top_split[:, 1])
-    own_total = jnp.where(first_half, total_split[:, 0], total_split[:, 1])
-    own_summed = jnp.where(first_half, summed_split[:, 0], summed_split[:, 1])
-    give_top = jnp.where(first_half, top_split[:, 1], top_split[:, 0])
-    give_total = jnp.where(first_half, total_split[:, 1], total_split[:, 0])
-    give_summed = jnp.where(first_half, summed_split[:, 1], summed_split[:, 0])
-    give = jnp.concatenate([give_summed, give_top[..., None], give_total[..., None]], -1)
-    got = from_partner(give, "tp", 0)
-    got_summed, got_top, got_total = got[..., :HD], got[..., HD], got[..., HD + 1]
-    joint = jnp.maximum(own_top, got_top)
-    factor_own = jnp.exp(own_top - joint)
-    factor_got = jnp.exp(got_top - joint)
-    numer = own_summed * factor_own[..., None] + got_summed * factor_got[..., None]
-    denom = own_total * factor_own + got_total * factor_got
-    attention = (numer / denom[..., None]).astype(jnp.bfloat16)
+    def attend(lo, hi):
+        queries_c, keys_c, values_c = both_queries[lo:hi], key_cache[0, lo:hi], value_cache[0, lo:hi]
+        lengths_c, key_new_c, value_new_c = lengths[0, lo:hi], key_new[lo:hi], value_new[lo:hi]
+        scale = 1.0 / HD**0.5
+        scores = (
+            jnp.einsum("bhe,bte->bht", queries_c, keys_c, preferred_element_type=jnp.float32)
+            * scale
+        )
+        positions = jnp.arange(scores.shape[2], dtype=jnp.int32)
+        masked = positions[None, None, :] < lengths_c[:, None, None]
+        new_score = (
+            jnp.einsum("bhe,be->bh", queries_c, key_new_c, preferred_element_type=jnp.float32) * scale
+        )
+        new_score = jnp.where(my_half == 0, new_score, jnp.float32(-1e30))
+        top = jnp.maximum(jnp.max(jnp.where(masked, scores, jnp.float32(-1e30)), axis=-1), new_score)
+        weights = jnp.where(masked, jnp.exp(scores - top[..., None]), jnp.float32(0.0))
+        new_weight = jnp.exp(new_score - top)
+        total = jnp.sum(weights, axis=-1) + new_weight
+        summed = jnp.einsum(
+            "bht,bte->bhe",
+            weights.astype(jnp.bfloat16),
+            values_c,
+            preferred_element_type=jnp.float32,
+        )
+        new_rounded = lax.optimization_barrier(new_weight.astype(jnp.bfloat16)).astype(jnp.float32)
+        summed = summed + new_rounded[..., None] * value_new_c.astype(jnp.float32)[:, None, :]
+        top_split = top.reshape(-1, 2, GR)
+        total_split = total.reshape(-1, 2, GR)
+        summed_split = summed.reshape(-1, 2, GR, HD)
+        first_half = my_half == 0
+        own_top = jnp.where(first_half, top_split[:, 0], top_split[:, 1])
+        own_total = jnp.where(first_half, total_split[:, 0], total_split[:, 1])
+        own_summed = jnp.where(first_half, summed_split[:, 0], summed_split[:, 1])
+        give_top = jnp.where(first_half, top_split[:, 1], top_split[:, 0])
+        give_total = jnp.where(first_half, total_split[:, 1], total_split[:, 0])
+        give_summed = jnp.where(first_half, summed_split[:, 1], summed_split[:, 0])
+        give = jnp.concatenate([give_summed, give_top[..., None], give_total[..., None]], -1)
+        got = from_partner(give, "tp", 0)
+        got_summed, got_top, got_total = got[..., :HD], got[..., HD], got[..., HD + 1]
+        joint = jnp.maximum(own_top, got_top)
+        factor_own = jnp.exp(own_top - joint)
+        factor_got = jnp.exp(got_top - joint)
+        numer = own_summed * factor_own[..., None] + got_summed * factor_got[..., None]
+        denom = own_total * factor_own + got_total * factor_got
+        return (numer / denom[..., None]).astype(jnp.bfloat16)
+
+    attention = jnp.concatenate([attend(0, ROWS // 2), attend(ROWS // 2, ROWS)], 0)
     from_rows = [lax.dynamic_index_in_dim(attention, grid_row, 1, keepdims=False)]
     for s in range(1, GR):
         piece = lax.dynamic_index_in_dim(attention, grid_row ^ s, 1, keepdims=False)

time: 78.1 us -> 85.6 us (1.096)
  other arithmetic: 5.49 us -> 10.1 us
  matrix products: 18.4 us -> 20.9 us
  local copies, waits for them, and re-layouts: 3.84 us -> 5.08 us
  waiting for transfers between devices: 19 us -> 18.1 us
    dot_general x3 -> x6, matrix products: 6.48 us -> 8.94 us  [the longest x2 4.64 us: attend(): jnp.einsum('bhe,bte->bht', queries_c, keys_c, preferred_element_type=jnp....]
    add x0 -> x2, other arithmetic: none -> 2.1 us  [attend(): own_summed * factor_own[..., None] + got_summed * factor_got[..., None]]
    div x0 -> x2, other arithmetic: none -> 1.4 us  [attend(): return (numer / denom[..., None]).astype(jnp.bfloat16)]
    ppermute x1 -> x2, waiting for transfers between devices: 1.17 us -> 0.01 us  [from_partner(): return lax.ppermute(value, axis, pairs)]
    ppermute x1 -> x2, starting transfers between devices: 2.06 us -> 1.94 us  [from_partner(): return lax.ppermute(value, axis, pairs)]
  transfers between devices with their start and end apart: 23 -> 24, of which waited for: 13 -> 12; matrix products, arithmetic and copies ran while one was open for 5% -> 14% of each run, Pallas kernels for 0% -> 0%
where the time goes in v12:
time: 85.6 us; the launch traced here: 85 us
  starting transfers between devices  30.4 us (36%)
  matrix products  20.9 us (24%)
  waiting for transfers between devices  18.1 us (21%)
  other arithmetic  10.1 us (12%)
  local copies, waits for them, and re-layouts  5.08 us (6%)
    ppermute x9, starting transfers between devices, swap_rows(): lax.ppermute(value, axis, [(t, t ^ shift) for t in range(lax.axis_size(ax...  11.7 us
    ppermute x9, starting transfers between devices, swap_cols(): lax.ppermute(value, axis, [(t, t ^ s) for t in range(lax.axis_size(axis))])  10 us
    ppermute x9, waiting for transfers between devices, swap_rows(): lax.ppermute(value, axis, [(t, t ^ shift) for t in range(lax.axis_size(ax...  8.62 us
    ppermute x4, starting transfers between devices, local(): got = lax.ppermute(piece, 'tp', pairs)  6.81 us
    ppermute x9, waiting for transfers between devices, swap_cols(): lax.ppermute(value, axis, [(t, t ^ s) for t in range(lax.axis_size(axis))])  5.78 us
    dot_general x1, matrix products, local(): jnp.einsum('rc,aec->rae', col_rows, q_blocks[0], preferred_element_type=j...  5.66 us
    dot_general x1, matrix products, local(): jnp.einsum('gabe,cae->gbc', chosen, o_blocks[0], preferred_element_type=j...  5.65 us
    dot_general x2, matrix products, attend(): jnp.einsum('bhe,bte->bht', queries_c, keys_c, preferred_element_type=jnp....  4.64 us
  transfers between devices with their start and end apart: 24, of which 12 were waited for; matrix products, arithmetic and copies ran while one was open for 14% of the time, Pallas kernels for 0%

profile of v12, /device:TPU:1, one launch (start us, length us, event | category | flops | bytes accessed | tf_op | source)
XLA Modules:
  0.0 85.0 jit_solution(6295729644627420373)
XLA Ops:
  0.1 2.7 %collective-permute-start.1 = (bf16[8,512]{1,0:T(8,128)(2,1)}, bf16[8,512]{1,0:T(8,128)(2,1)S(1)}, u32[]{:S(2)}, u32[]{:S(2)}) collective-permute-start(bf16[8,512]{1,0:T(8,128)(2,1)} %bitcast.226), channel_id=1, source_target_pairs={{0,2},{1,3},{2,0},{3,1},{4,6},{5,7},{6,4},{7,5},{8,10},{9,11},{10,... | collective-permute-start | bytes 24584 | tf_op jit(solution)/shard_map/ppermute | solution.py:105
  3.8 1.3 %gather_fusion.1 = s32[16]{0:T(128)S(1)} fusion(s32[16]{0:T(128)} %param.14, s32[1024]{0:T(1024)S(1)} %pad_clamp_fusion), kind=kCustom, calls=%fused_computation.1 | custom fusion | bytes 192 | tf_op jit(solution)/shard_map/gather | solution.py:128
  7.6 3.8 %collective-permute-start.5 = (bf16[4,8,512]{2,1,0:T(8,128)(2,1)S(1)}, bf16[4,8,512]{2,1,0:T(8,128)(2,1)S(1)}, u32[]{:S(2)}, u32[]{:S(2)}) collective-permute-start(bf16[4,8,512]{2,1,0:T(8,128)(2,1)S(1)} %select_reduce_fusion.8), channel_id=1, source_target_pairs={{0,12},{1,13},{2,14},{3,15},{4,8},{5,9},{6,10},{7,11},{8,4},{9,5},... | collective-permute-start | bytes 98312 | tf_op jit(solution)/shard_map/ppermute | solution.py:101
  17.1 5.7 %fusion.17 = f32[16,8,128]{2,1,0:T(8,128)S(1)} fusion(bf16[1,16,128,2048]{3,2,1,0:T(8,128)(2,1)} %param.11, bf16[8,8192]{1,0:T(8,128)(2,1)S(1)} %multiply_convert_fusion, s32[]{:T(128)S(6)} %select_n.365), kind=kOutput, calls=%fused_computation.19 | convolution fusion | flops 67108864 | bytes 8486916 | tf_op jit(solution)/shard_map/rc,aec->rae/dot_general | solution.py:152
  23.8 1.6 %collective-permute-start.6 = (f32[4,8,512]{2,1,0:T(8,128)S(1)}, f32[4,8,512]{2,1,0:T(8,128)S(1)}, u32[]{:S(2)}, u32[]{:S(2)}) collective-permute-start(f32[4,8,512]{2,1,0:T(8,128)S(1)} %get-tuple-element.17), channel_id=1, source_target_pairs={{0,1},{1,0},{2,3},{3,2},{4,5},{5,4},{6,7},{7,6},{8,9},{9,8},{10,11... | collective-permute-start | bytes 196616 | tf_op jit(solution)/shard_map/ppermute | solution.py:105
  27.2 1.8 %collective-permute-done.7 = f32[4,8,512]{2,1,0:T(8,128)S(1)} collective-permute-done((f32[4,8,512]{2,1,0:T(8,128)S(1)}, f32[4,8,512]{2,1,0:T(8,128)S(1)}, u32[]{:S(2)}, u32[]{:S(2)}) %collective-permute-start.7) | collective-permute-done | bytes 65568 | tf_op jit(solution)/shard_map/ppermute | solution.py:105
  29.0 1.6 %collective-permute-done.8 = f32[4,8,512]{2,1,0:T(8,128)S(1)} collective-permute-done((f32[4,8,512]{2,1,0:T(8,128)S(1)}, f32[4,8,512]{2,1,0:T(8,128)S(1)}, u32[]{:S(2)}, u32[]{:S(2)}) %collective-permute-start.8) | collective-permute-done | bytes 65568 | tf_op jit(solution)/shard_map/ppermute | solution.py:105
  31.6 3.0 %collective-permute-start.11 = (f32[8,512]{1,0:T(8,128)S(1)}, f32[8,512]{1,0:T(8,128)S(1)}, u32[]{:S(2)}, u32[]{:S(2)}) collective-permute-start(f32[8,512]{1,0:T(8,128)S(1)} %get-tuple-element.25), channel_id=1, source_target_pairs={{0,12},{1,13},{2,14},{3,15},{4,8},{5,9},{6,10},{7,11},{8,4},{9,5},... | collective-permute-start | bytes 49160 | tf_op jit(solution)/shard_map/ppermute | solution.py:101
  34.6 1.4 %collective-permute-done.11 = f32[8,512]{1,0:T(8,128)S(1)} collective-permute-done((f32[8,512]{1,0:T(8,128)S(1)}, f32[8,512]{1,0:T(8,128)S(1)}, u32[]{:S(2)}, u32[]{:S(2)}) %collective-permute-start.11) | collective-permute-done | bytes 16416 | tf_op jit(solution)/shard_map/ppermute | solution.py:101
  36.0 1.4 %collective-permute-done.9 = f32[8,512]{1,0:T(8,128)S(1)} collective-permute-done((f32[8,512]{1,0:T(8,128)S(1)}, f32[8,512]{1,0:T(8,128)S(1)}, u32[]{:S(2)}, u32[]{:S(2)}) %collective-permute-start.9) | collective-permute-done | bytes 16416 | tf_op jit(solution)/shard_map/ppermute | solution.py:101
  37.7 2.3 %select_reduce_fusion.5 = (f32[4,8]{1,0:T(4,128)S(1)}, f32[4,8,2048]{2,1,0:T(8,128)S(1)}) fusion(pred[4,2048]{1,0:T(4,128)(4,1)S(1)} %get-tuple-element.70, bf16[4,8,128]{2,1,0:T(8,128)(2,1)S(1)} %bitcast.206, bf16[1,8,2048,128]{3,2,1,0:T(8,128)(2,1)} %param.15), kind=kOutput, calls=%fused_computation.39 | convolution fusion | flops 16973792 | bytes 2375808 | tf_op jit(solution)/shard_map/bhe,bte->bht/dot_general | solution.py:201
  40.3 2.0 %fusion.23 = f32[4,8,128]{2,1,0:T(8,128)S(1)} fusion(bf16[1,8,2048,128]{3,2,1,0:T(8,128)(2,1)} %param.16, f32[4,8,2048]{2,1,0:T(8,128)S(1)} %get-tuple-element.68, f32[4,8]{1,0:T(4,128)S(1)} %fusion.72, pred[4,2048]{1,0:T(4,128)(4,1)S(1)} %get-tuple-element.70, f32[4,128]{1,0:T(4,128)S(1)} %get-tuple-element.52, f32[4,8]{1,0:T(4,128)S(1)} %convert_element_type.87), kind=kOutput, calls=%fused_computation.22 | convolution fusion | flops 16982016 | bytes 2386176 | tf_op jit(solution)/shard_map/bht,bte->bhe/dot_general | solution.py:214
  43.0 1.9 %collective-permute-start.13 = (f32[4,4,130]{1,0,2:T(4,128)S(1)}, f32[4,4,130]{1,0,2:T(4,128)}, u32[]{:S(2)}, u32[]{:S(2)}) collective-permute-start(f32[4,4,130]{1,0,2:T(4,128)S(1)} %pad_maximum_fusion.1), channel_id=1, source_target_pairs={{0,1},{1,0},{2,3},{3,2},{4,5},{5,4},{6,7},{7,6},{8,9},{9,8},{10,11... | collective-permute-start | bytes 24968 | tf_op jit(solution)/shard_map/ppermute | solution.py:19
  44.9 2.3 %select_reduce_fusion.6 = (f32[4,8]{1,0:T(4,128)S(1)}, f32[4,8,2048]{2,1,0:T(8,128)S(1)}) fusion(pred[4,2048]{1,0:T(4,128)(4,1)S(1)} %get-tuple-element.71, bf16[4,8,128]{2,1,0:T(8,128)(2,1)S(1)} %bitcast.203, bf16[1,8,2048,128]{3,2,1,0:T(8,128)(2,1)} %param.15), kind=kOutput, calls=%fused_computation.42 | convolution fusion | flops 16973792 | bytes 2375808 | tf_op jit(solution)/shard_map/bhe,bte->bht/dot_general | solution.py:201
  47.7 2.0 %fusion.20 = f32[4,8,128]{2,1,0:T(8,128)S(1)} fusion(bf16[1,8,2048,128]{3,2,1,0:T(8,128)(2,1)} %param.16, f32[4,8,2048]{2,1,0:T(8,128)S(1)} %get-tuple-element.66, f32[4,8]{1,0:T(4,128)S(1)} %fusion.71, pred[4,2048]{1,0:T(4,128)(4,1)S(1)} %get-tuple-element.71, f32[4,128]{1,0:T(4,128)S(1)} %get-tuple-element.54, f32[4,8]{1,0:T(4,128)S(1)} %convert_element_type.82), kind=kOutput, calls=%fused_computation.21 | convolution fusion | flops 16982016 | bytes 2386176 | tf_op jit(solution)/shard_map/bht,bte->bhe/dot_general | solution.py:214
  55.2 1.8 %collective-permute-start.15 = (bf16[8,128]{1,0:T(8,128)(2,1)S(1)}, bf16[8,128]{1,0:T(8,128)(2,1)S(1)}, u32[]{:S(2)}, u32[]{:S(2)}) collective-permute-start(bf16[8,128]{1,0:T(8,128)(2,1)S(1)} %get-tuple-element.44), channel_id=1, source_target_pairs={{0,8},{1,9},{2,10},{3,11},{4,12},{5,13},{6,14},{7,15},{8,0},{9,1},... | collective-permute-start | bytes 6152 | tf_op jit(solution)/shard_map/ppermute | solution.py:101
  57.0 1.7 %collective-permute-start.16 = (bf16[8,128]{1,0:T(8,128)(2,1)S(1)}, bf16[8,128]{1,0:T(8,128)(2,1)S(1)}, u32[]{:S(2)}, u32[]{:S(2)}) collective-permute-start(bf16[8,128]{1,0:T(8,128)(2,1)S(1)} %get-tuple-element.45), channel_id=1, source_target_pairs={{0,12},{1,13},{2,14},{3,15},{4,8},{5,9},{6,10},{7,11},{8,4},{9,5},... | collective-permute-start | bytes 6152 | tf_op jit(solution)/shard_map/ppermute | solution.py:101
  58.8 2.5 %collective-permute-done.16 = bf16[8,128]{1,0:T(8,128)(2,1)S(1)} collective-permute-done((bf16[8,128]{1,0:T(8,128)(2,1)S(1)}, bf16[8,128]{1,0:T(8,128)(2,1)S(1)}, u32[]{:S(2)}, u32[]{:S(2)}) %collective-permute-start.16) | collective-permute-done | bytes 2080 | tf_op jit(solution)/shard_map/ppermute | solution.py:101
  61.4 2.3 %collective-permute-start.17 = (bf16[4,8,128]{2,1,0:T(8,128)(2,1)S(1)}, bf16[4,8,128]{2,1,0:T(8,128)(2,1)S(1)}, u32[]{:S(2)}, u32[]{:S(2)}) collective-permute-start(bf16[4,8,128]{2,1,0:T(8,128)(2,1)S(1)} %select_reduce_fusion.11), channel_id=1, source_target_pairs={{0,1},{1,0},{2,3},{3,2},{4,5},{5,4},{6,7},{7,6},{8,9},{9,8},{10,11... | collective-permute-start | bytes 24584 | tf_op jit(solution)/shard_map/ppermute | solution.py:105
  66.2 1.6 %collective-permute-done.19 = bf16[4,8,128]{2,1,0:T(8,128)(2,1)S(1)} collective-permute-done((bf16[4,8,128]{2,1,0:T(8,128)(2,1)S(1)}, bf16[4,8,128]{2,1,0:T(8,128)(2,1)S(1)}, u32[]{:S(2)}, u32[]{:S(2)}) %collective-permute-start.19) | collective-permute-done | bytes 8224 | tf_op jit(solution)/shard_map/ppermute | solution.py:105
  68.3 5.6 %fusion.14 = f32[8,4,512]{2,0,1:T(8,128)S(1)} fusion(bf16[4,512,16,128]{3,2,1,0:T(8,128)(2,1)} %bitcast.193, bf16[16,8,128]{2,1,0:T(8,128)(2,1)S(1)} %select_reduce_fusion.3), kind=kOutput, calls=%fused_computation.18 | convolution fusion | flops 67108864 | bytes 8486912 | tf_op jit(solution)/shard_map/gabe,cae->gbc/dot_general | solution.py:262
  73.9 1.9 %collective-permute-start.20 = (f32[8,512]{1,0:T(8,128)S(1)}, f32[8,512]{1,0:T(8,128)S(1)}, u32[]{:S(2)}, u32[]{:S(2)}) collective-permute-start(f32[8,512]{1,0:T(8,128)S(1)} %get-tuple-element.23), channel_id=1, source_target_pairs={{0,0},{1,4},{2,8},{3,12},{4,1},{5,5},{6,9},{7,13},{8,2},{9,6},{10,... | collective-permute-start | bytes 49160 | tf_op jit(solution)/shard_map/ppermute | solution.py:269
  75.9 4.4 %collective-permute-start.22 = (f32[8,512]{1,0:T(8,128)S(1)}, f32[8,512]{1,0:T(8,128)S(1)}, u32[]{:S(2)}, u32[]{:S(2)}) collective-permute-start(f32[8,512]{1,0:T(8,128)S(1)} %get-tuple-element.22), channel_id=1, source_target_pairs={{0,2},{1,6},{2,10},{3,14},{4,3},{5,7},{6,11},{7,15},{8,0},{9,4},{1... | collective-permute-start | bytes 49160 | tf_op jit(solution)/shard_map/ppermute | solution.py:269
  81.5 2.9 %collective-permute-done.23 = f32[8,512]{1,0:T(8,128)S(1)} collective-permute-done((f32[8,512]{1,0:T(8,128)S(1)}, f32[8,512]{1,0:T(8,128)S(1)}, u32[]{:S(2)}, u32[]{:S(2)}) %collective-permute-start.23) | collective-permute-done | bytes 16416 | tf_op jit(solution)/shard_map/ppermute | solution.py:269
  (127 shorter events, 24.9 us)
Async XLA Ops:
  0.0 6.8 %collective-permute-start = (bf16[8,512]{1,0:T(8,128)(2,1)}, bf16[8,512]{1,0:T(8,128)(2,1)S(1)}, u32[]{:S(2)}, u32[]{:S(2)}) collective-permute-start(bf16[8,512]{1,0:T(8,128)(2,1)} %bitcast.225), channel_id=1, source_target_pairs={{0,1},{1,0},{2,3},{3,2},{4,5},{5,4},{6,7},{7,6},{8,9},{9,8},{10,11... | collective-permute-start | bytes 24584 | tf_op jit(solution)/shard_map/ppermute | solution.py:105
  0.1 6.7 %collective-permute-start.1 = (bf16[8,512]{1,0:T(8,128)(2,1)}, bf16[8,512]{1,0:T(8,128)(2,1)S(1)}, u32[]{:S(2)}, u32[]{:S(2)}) collective-permute-start(bf16[8,512]{1,0:T(8,128)(2,1)} %bitcast.226), channel_id=1, source_target_pairs={{0,2},{1,3},{2,0},{3,1},{4,6},{5,7},{6,4},{7,5},{8,10},{9,11},{10,... | collective-permute-start | bytes 24584 | tf_op jit(solution)/shard_map/ppermute | solution.py:105
  2.7 4.1 %collective-permute-start.2 = (bf16[8,512]{1,0:T(8,128)(2,1)}, bf16[8,512]{1,0:T(8,128)(2,1)S(1)}, u32[]{:S(2)}, u32[]{:S(2)}) collective-permute-start(bf16[8,512]{1,0:T(8,128)(2,1)} %bitcast.227), channel_id=1, source_target_pairs={{0,3},{1,2},{2,1},{3,0},{4,7},{5,6},{6,5},{7,4},{8,11},{9,10},{10,... | collective-permute-start | bytes 24584 | tf_op jit(solution)/shard_map/ppermute | solution.py:105
  7.6 5.4 %collective-permute-start.5 = (bf16[4,8,512]{2,1,0:T(8,128)(2,1)S(1)}, bf16[4,8,512]{2,1,0:T(8,128)(2,1)S(1)}, u32[]{:S(2)}, u32[]{:S(2)}) collective-permute-start(bf16[4,8,512]{2,1,0:T(8,128)(2,1)S(1)} %select_reduce_fusion.8), channel_id=1, source_target_pairs={{0,12},{1,13},{2,14},{3,15},{4,8},{5,9},{6,10},{7,11},{8,4},{9,5},... | collective-permute-start | bytes 98312 | tf_op jit(solution)/shard_map/ppermute | solution.py:101
  11.4 2.8 %collective-permute-start.3 = (bf16[4,8,512]{2,1,0:T(8,128)(2,1)S(1)}, bf16[4,8,512]{2,1,0:T(8,128)(2,1)S(1)}, u32[]{:S(2)}, u32[]{:S(2)}) collective-permute-start(bf16[4,8,512]{2,1,0:T(8,128)(2,1)S(1)} %select_reduce_fusion.8), channel_id=1, source_target_pairs={{0,4},{1,5},{2,6},{3,7},{4,0},{5,1},{6,2},{7,3},{8,12},{9,13},{10,... | collective-permute-start | bytes 98312 | tf_op jit(solution)/shard_map/ppermute | solution.py:101
  11.4 3.8 %collective-permute-start.4 = (bf16[4,8,512]{2,1,0:T(8,128)(2,1)S(1)}, bf16[4,8,512]{2,1,0:T(8,128)(2,1)S(1)}, u32[]{:S(2)}, u32[]{:S(2)}) collective-permute-start(bf16[4,8,512]{2,1,0:T(8,128)(2,1)S(1)} %select_reduce_fusion.8), channel_id=1, source_target_pairs={{0,8},{1,9},{2,10},{3,11},{4,12},{5,13},{6,14},{7,15},{8,0},{9,1},... | collective-permute-start | bytes 98312 | tf_op jit(solution)/shard_map/ppermute | solution.py:101
  23.8 3.4 %collective-permute-start.6 = (f32[4,8,512]{2,1,0:T(8,128)S(1)}, f32[4,8,512]{2,1,0:T(8,128)S(1)}, u32[]{:S(2)}, u32[]{:S(2)}) collective-permute-start(f32[4,8,512]{2,1,0:T(8,128)S(1)} %get-tuple-element.17), channel_id=1, source_target_pairs={{0,1},{1,0},{2,3},{3,2},{4,5},{5,4},{6,7},{7,6},{8,9},{9,8},{10,11... | collective-permute-start | bytes 196616 | tf_op jit(solution)/shard_map/ppermute | solution.py:105
  25.3 3.7 %collective-permute-start.7 = (f32[4,8,512]{2,1,0:T(8,128)S(1)}, f32[4,8,512]{2,1,0:T(8,128)S(1)}, u32[]{:S(2)}, u32[]{:S(2)}) collective-permute-start(f32[4,8,512]{2,1,0:T(8,128)S(1)} %get-tuple-element.19), channel_id=1, source_target_pairs={{0,2},{1,3},{2,0},{3,1},{4,6},{5,7},{6,4},{7,5},{8,10},{9,11},{10,... | collective-permute-start | bytes 196616 | tf_op jit(solution)/shard_map/ppermute | solution.py:105
  26.6 4.0 %collective-permute-start.8 = (f32[4,8,512]{2,1,0:T(8,128)S(1)}, f32[4,8,512]{2,1,0:T(8,128)S(1)}, u32[]{:S(2)}, u32[]{:S(2)}) collective-permute-start(f32[4,8,512]{2,1,0:T(8,128)S(1)} %get-tuple-element.18), channel_id=1, source_target_pairs={{0,3},{1,2},{2,1},{3,0},{4,7},{5,6},{6,5},{7,4},{8,11},{9,10},{10,... | collective-permute-start | bytes 196616 | tf_op jit(solution)/shard_map/ppermute | solution.py:105
  30.7 3.9 %collective-permute-start.10 = (f32[8,512]{1,0:T(8,128)S(1)}, f32[8,512]{1,0:T(8,128)S(1)}, u32[]{:S(2)}, u32[]{:S(2)}) collective-permute-start(f32[8,512]{1,0:T(8,128)S(1)} %get-tuple-element.26), channel_id=1, source_target_pairs={{0,8},{1,9},{2,10},{3,11},{4,12},{5,13},{6,14},{7,15},{8,0},{9,1},... | collective-permute-start | bytes 49160 | tf_op jit(solution)/shard_map/ppermute | solution.py:101
  31.6 4.4 %collective-permute-start.11 = (f32[8,512]{1,0:T(8,128)S(1)}, f32[8,512]{1,0:T(8,128)S(1)}, u32[]{:S(2)}, u32[]{:S(2)}) collective-permute-start(f32[8,512]{1,0:T(8,128)S(1)} %get-tuple-element.25), channel_id=1, source_target_pairs={{0,12},{1,13},{2,14},{3,15},{4,8},{5,9},{6,10},{7,11},{8,4},{9,5},... | collective-permute-start | bytes 49160 | tf_op jit(solution)/shard_map/ppermute | solution.py:101
  34.5 2.8 %collective-permute-start.9 = (f32[8,512]{1,0:T(8,128)S(1)}, f32[8,512]{1,0:T(8,128)S(1)}, u32[]{:S(2)}, u32[]{:S(2)}) collective-permute-start(f32[8,512]{1,0:T(8,128)S(1)} %get-tuple-element.27), channel_id=1, source_target_pairs={{0,4},{1,5},{2,6},{3,7},{4,0},{5,1},{6,2},{7,3},{8,12},{9,13},{10,... | collective-permute-start | bytes 49160 | tf_op jit(solution)/shard_map/ppermute | solution.py:101
  43.0 8.1 %collective-permute-start.13 = (f32[4,4,130]{1,0,2:T(4,128)S(1)}, f32[4,4,130]{1,0,2:T(4,128)}, u32[]{:S(2)}, u32[]{:S(2)}) collective-permute-start(f32[4,4,130]{1,0,2:T(4,128)S(1)} %pad_maximum_fusion.1), channel_id=1, source_target_pairs={{0,1},{1,0},{2,3},{3,2},{4,5},{5,4},{6,7},{7,6},{8,9},{9,8},{10,11... | collective-permute-start | bytes 24968 | tf_op jit(solution)/shard_map/ppermute | solution.py:19
  51.0 2.0 %collective-permute-start.12 = (f32[4,4,130]{1,0,2:T(4,128)}, f32[4,4,130]{1,0,2:T(4,128)}, u32[]{:S(2)}, u32[]{:S(2)}) collective-permute-start(f32[4,4,130]{1,0,2:T(4,128)} %pad_maximum_fusion), channel_id=1, source_target_pairs={{0,1},{1,0},{2,3},{3,2},{4,5},{5,4},{6,7},{7,6},{8,9},{9,8},{10,11... | collective-permute-start | bytes 24968 | tf_op jit(solution)/shard_map/ppermute | solution.py:19
  55.2 3.6 %collective-permute-start.14 = (bf16[8,128]{1,0:T(8,128)(2,1)S(1)}, bf16[8,128]{1,0:T(8,128)(2,1)S(1)}, u32[]{:S(2)}, u32[]{:S(2)}) collective-permute-start(bf16[8,128]{1,0:T(8,128)(2,1)S(1)} %get-tuple-element.43), channel_id=1, source_target_pairs={{0,4},{1,5},{2,6},{3,7},{4,0},{5,1},{6,2},{7,3},{8,12},{9,13},{10,... | collective-permute-start | bytes 6152 | tf_op jit(solution)/shard_map/ppermute | solution.py:101
  55.2 3.5 %collective-permute-start.15 = (bf16[8,128]{1,0:T(8,128)(2,1)S(1)}, bf16[8,128]{1,0:T(8,128)(2,1)S(1)}, u32[]{:S(2)}, u32[]{:S(2)}) collective-permute-start(bf16[8,128]{1,0:T(8,128)(2,1)S(1)} %get-tuple-element.44), channel_id=1, source_target_pairs={{0,8},{1,9},{2,10},{3,11},{4,12},{5,13},{6,14},{7,15},{8,0},{9,1},... | collective-permute-start | bytes 6152 | tf_op jit(solution)/shard_map/ppermute | solution.py:101
  57.0 4.2 %collective-permute-start.16 = (bf16[8,128]{1,0:T(8,128)(2,1)S(1)}, bf16[8,128]{1,0:T(8,128)(2,1)S(1)}, u32[]{:S(2)}, u32[]{:S(2)}) collective-permute-start(bf16[8,128]{1,0:T(8,128)(2,1)S(1)} %get-tuple-element.45), channel_id=1, source_target_pairs={{0,12},{1,13},{2,14},{3,15},{4,8},{5,9},{6,10},{7,11},{8,4},{9,5},... | collective-permute-start | bytes 6152 | tf_op jit(solution)/shard_map/ppermute | solution.py:101
  61.4 4.0 %collective-permute-start.17 = (bf16[4,8,128]{2,1,0:T(8,128)(2,1)S(1)}, bf16[4,8,128]{2,1,0:T(8,128)(2,1)S(1)}, u32[]{:S(2)}, u32[]{:S(2)}) collective-permute-start(bf16[4,8,128]{2,1,0:T(8,128)(2,1)S(1)} %select_reduce_fusion.11), channel_id=1, source_target_pairs={{0,1},{1,0},{2,3},{3,2},{4,5},{5,4},{6,7},{7,6},{8,9},{9,8},{10,11... | collective-permute-start | bytes 24584 | tf_op jit(solution)/shard_map/ppermute | solution.py:105
  63.6 2.5 %collective-permute-start.18 = (bf16[4,8,128]{2,1,0:T(8,128)(2,1)S(1)}, bf16[4,8,128]{2,1,0:T(8,128)(2,1)S(1)}, u32[]{:S(2)}, u32[]{:S(2)}) collective-permute-start(bf16[4,8,128]{2,1,0:T(8,128)(2,1)S(1)} %select_reduce_fusion.11), channel_id=1, source_target_pairs={{0,2},{1,3},{2,0},{3,1},{4,6},{5,7},{6,4},{7,5},{8,10},{9,11},{10,... | collective-permute-start | bytes 24584 | tf_op jit(solution)/shard_map/ppermute | solution.py:105
  64.7 3.1 %collective-permute-start.19 = (bf16[4,8,128]{2,1,0:T(8,128)(2,1)S(1)}, bf16[4,8,128]{2,1,0:T(8,128)(2,1)S(1)}, u32[]{:S(2)}, u32[]{:S(2)}) collective-permute-start(bf16[4,8,128]{2,1,0:T(8,128)(2,1)S(1)} %select_reduce_fusion.11), channel_id=1, source_target_pairs={{0,3},{1,2},{2,1},{3,0},{4,7},{5,6},{6,5},{7,4},{8,11},{9,10},{10,... | collective-permute-start | bytes 24584 | tf_op jit(solution)/shard_map/ppermute | solution.py:105
  73.9 6.8 %collective-permute-start.20 = (f32[8,512]{1,0:T(8,128)S(1)}, f32[8,512]{1,0:T(8,128)S(1)}, u32[]{:S(2)}, u32[]{:S(2)}) collective-permute-start(f32[8,512]{1,0:T(8,128)S(1)} %get-tuple-element.23), channel_id=1, source_target_pairs={{0,0},{1,4},{2,8},{3,12},{4,1},{5,5},{6,9},{7,13},{8,2},{9,6},{10,... | collective-permute-start | bytes 49160 | tf_op jit(solution)/shard_map/ppermute | solution.py:269
  75.9 4.9 %collective-permute-start.21 = (f32[8,512]{1,0:T(8,128)S(1)}, f32[8,512]{1,0:T(8,128)S(1)}, u32[]{:S(2)}, u32[]{:S(2)}) collective-permute-start(f32[8,512]{1,0:T(8,128)S(1)} %get-tuple-element.20), channel_id=1, source_target_pairs={{0,1},{1,5},{2,9},{3,13},{4,0},{5,4},{6,8},{7,12},{8,3},{9,7},{10,... | collective-permute-start | bytes 49160 | tf_op jit(solution)/shard_map/ppermute | solution.py:269
  75.9 5.5 %collective-permute-start.22 = (f32[8,512]{1,0:T(8,128)S(1)}, f32[8,512]{1,0:T(8,128)S(1)}, u32[]{:S(2)}, u32[]{:S(2)}) collective-permute-start(f32[8,512]{1,0:T(8,128)S(1)} %get-tuple-element.22), channel_id=1, source_target_pairs={{0,2},{1,6},{2,10},{3,14},{4,3},{5,7},{6,11},{7,15},{8,0},{9,4},{1... | collective-permute-start | bytes 49160 | tf_op jit(solution)/shard_map/ppermute | solution.py:269
  80.4 4.1 %collective-permute-start.23 = (f32[8,512]{1,0:T(8,128)S(1)}, f32[8,512]{1,0:T(8,128)S(1)}, u32[]{:S(2)}, u32[]{:S(2)}) collective-permute-start(f32[8,512]{1,0:T(8,128)S(1)} %get-tuple-element.21), channel_id=1, source_target_pairs={{0,3},{1,7},{2,11},{3,15},{4,2},{5,6},{6,10},{7,14},{8,1},{9,5},{1... | collective-permute-start | bytes 49160 | tf_op jit(solution)/shard_map/ppermute | solution.py:269
  (1 other events, 16.5 us)

commit v13 on v6

--- a/solution.py
+++ b/solution.py
@@ -135,12 +135,14 @@
     col_order = jnp.arange(grid_cols, dtype=jnp.int32) ^ grid_col
     direct_cols = grid_cols <= 4
     if direct_cols:
-        from_cols = [hidden_in[0]] + [swap_cols(hidden_in[0], "tp", s) for s in range(1, grid_cols)]
-        in_row = pick(jnp.stack(from_cols), col_order)
+        from_rows = [hidden_in[0]] + [swap_rows(hidden_in[0], "tp", col_bits, s) for s in range(1, GR)]
+        by_rows = pick(jnp.stack(from_rows), row_order)
+        from_cols = [by_rows] + [swap_cols(by_rows, "tp", s) for s in range(1, grid_cols)]
+        every_rows = pick(jnp.stack(from_cols), col_order).transpose(1, 0, 2, 3).reshape(ranks, ROWS, DS)
     else:
         in_row = gather_rounds(hidden_in, "tp", range(col_bits))
-    from_rows = [in_row] + [swap_rows(in_row, "tp", col_bits, s) for s in range(1, GR)]
-    every_rows = pick(jnp.stack(from_rows), row_order).reshape(ranks, ROWS, DS)
+        from_rows = [in_row] + [swap_rows(in_row, "tp", col_bits, s) for s in range(1, GR)]
+        every_rows = pick(jnp.stack(from_rows), row_order).reshape(ranks, ROWS, DS)
     rows_float = (
         every_rows.reshape(group_count, ROLL, ROWS, DS)
         .transpose(0, 2, 1, 3)

time: 78.1 us -> 79.7 us (1.020)
  starting transfers between devices: 30.5 us -> 32.2 us
    ppermute x9, waiting for transfers between devices: 8.4 us -> 6.56 us  [swap_rows(): lax.ppermute(value, axis, [(t, t ^ shift) for t in range(lax.axis_size(ax...]
    ppermute x9, waiting for transfers between devices: 5.8 us -> 7.52 us  [swap_cols(): lax.ppermute(value, axis, [(t, t ^ s) for t in range(lax.axis_size(axis))])]
    ppermute x9, starting transfers between devices: 9.89 us -> 11.1 us  [swap_cols(): lax.ppermute(value, axis, [(t, t ^ s) for t in range(lax.axis_size(axis))])]
  transfers between devices with their start and end apart: 23 -> 23, of which waited for: 13 -> 12; matrix products, arithmetic and copies ran while one was open for 5% -> 5% of each run, Pallas kernels for 0% -> 0%
where the time goes in v13:
time: 79.7 us; the launch traced here: 79.3 us
  starting transfers between devices  32.2 us (40%)
  waiting for transfers between devices  18.9 us (24%)
  matrix products  18.4 us (23%)
  other arithmetic  5.48 us (7%)
  local copies, waits for them, and re-layouts  3.86 us (5%)
    ppermute x9, starting transfers between devices, swap_rows(): lax.ppermute(value, axis, [(t, t ^ shift) for t in range(lax.axis_size(ax...  11.7 us
    ppermute x9, starting transfers between devices, swap_cols(): lax.ppermute(value, axis, [(t, t ^ s) for t in range(lax.axis_size(axis))])  11.1 us
    ppermute x9, waiting for transfers between devices, swap_cols(): lax.ppermute(value, axis, [(t, t ^ s) for t in range(lax.axis_size(axis))])  7.52 us
    ppermute x4, starting transfers between devices, local(): got = lax.ppermute(piece, 'tp', pairs)  7.47 us
    ppermute x9, waiting for transfers between devices, swap_rows(): lax.ppermute(value, axis, [(t, t ^ shift) for t in range(lax.axis_size(ax...  6.56 us
    dot_general x1, matrix products, local(): jnp.einsum('rc,aec->rae', col_rows, q_blocks[0], preferred_element_type=j...  5.65 us
    dot_general x1, matrix products, local(): jnp.einsum('gabe,cae->gbc', chosen, o_blocks[0], preferred_element_type=j...  5.65 us
    ppermute x4, waiting for transfers between devices, local(): got = lax.ppermute(piece, 'tp', pairs)  3.67 us
  transfers between devices with their start and end apart: 23, of which 12 were waited for; matrix products, arithmetic and copies ran while one was open for 5% of the time, Pallas kernels for 0%

profile of v13, /device:TPU:1, one launch (start us, length us, event | category | flops | bytes accessed | tf_op | source)
XLA Modules:
  0.0 79.3 jit_solution(16014762659442619057)
XLA Ops:
  0.0 2.1 %collective-permute-start = (bf16[8,512]{1,0:T(8,128)(2,1)}, bf16[8,512]{1,0:T(8,128)(2,1)S(1)}, u32[]{:S(2)}, u32[]{:S(2)}) collective-permute-start(bf16[8,512]{1,0:T(8,128)(2,1)} %bitcast.199), channel_id=1, source_target_pairs={{0,4},{1,5},{2,6},{3,7},{4,0},{5,1},{6,2},{7,3},{8,12},{9,13},{10,... | collective-permute-start | bytes 24584 | tf_op jit(solution)/shard_map/ppermute | solution.py:101
  2.1 2.3 %collective-permute-start.1 = (bf16[8,512]{1,0:T(8,128)(2,1)}, bf16[8,512]{1,0:T(8,128)(2,1)S(1)}, u32[]{:S(2)}, u32[]{:S(2)}) collective-permute-start(bf16[8,512]{1,0:T(8,128)(2,1)} %bitcast.200), channel_id=1, source_target_pairs={{0,8},{1,9},{2,10},{3,11},{4,12},{5,13},{6,14},{7,15},{8,0},{9,1},... | collective-permute-start | bytes 24584 | tf_op jit(solution)/shard_map/ppermute | solution.py:101
  5.4 1.3 %gather_fusion.1 = s32[16]{0:T(128)S(1)} fusion(s32[16]{0:T(128)} %param.14, s32[1024]{0:T(1024)S(1)} %pad_clamp_fusion), kind=kCustom, calls=%fused_computation.1 | custom fusion | bytes 192 | tf_op jit(solution)/shard_map/gather | solution.py:128
  9.8 3.5 %collective-permute-start.5 = (bf16[4,8,512]{2,1,0:T(8,128)(2,1)S(1)}, bf16[4,8,512]{2,1,0:T(8,128)(2,1)S(1)}, u32[]{:S(2)}, u32[]{:S(2)}) collective-permute-start(bf16[4,8,512]{2,1,0:T(8,128)(2,1)S(1)} %select_reduce_fusion.7), channel_id=1, source_target_pairs={{0,3},{1,2},{2,1},{3,0},{4,7},{5,6},{6,5},{7,4},{8,11},{9,10},{10,... | collective-permute-start | bytes 98312 | tf_op jit(solution)/shard_map/ppermute | solution.py:105
  13.6 1.8 %collective-permute-done.5 = bf16[4,8,512]{2,1,0:T(8,128)(2,1)S(1)} collective-permute-done((bf16[4,8,512]{2,1,0:T(8,128)(2,1)S(1)}, bf16[4,8,512]{2,1,0:T(8,128)(2,1)S(1)}, u32[]{:S(2)}, u32[]{:S(2)}) %collective-permute-start.5) | collective-permute-done | bytes 32800 | tf_op jit(solution)/shard_map/ppermute | solution.py:105
  18.0 5.7 %fusion.14 = f32[16,8,128]{2,1,0:T(8,128)S(1)} fusion(bf16[1,16,128,2048]{3,2,1,0:T(8,128)(2,1)} %param.11, bf16[8,8192]{1,0:T(8,128)(2,1)S(1)} %multiply_convert_fusion, s32[]{:T(128)S(6)} %select_n.283), kind=kOutput, calls=%fused_computation.12 | convolution fusion | flops 67108864 | bytes 8486916 | tf_op jit(solution)/shard_map/rc,aec->rae/dot_general | solution.py:154
  24.7 1.7 %collective-permute-start.6 = (f32[4,8,512]{2,1,0:T(8,128)S(1)}, f32[4,8,512]{2,1,0:T(8,128)S(1)}, u32[]{:S(2)}, u32[]{:S(2)}) collective-permute-start(f32[4,8,512]{2,1,0:T(8,128)S(1)} %get-tuple-element.15), channel_id=1, source_target_pairs={{0,1},{1,0},{2,3},{3,2},{4,5},{5,4},{6,7},{7,6},{8,9},{9,8},{10,11... | collective-permute-start | bytes 196616 | tf_op jit(solution)/shard_map/ppermute | solution.py:105
  26.7 1.4 %collective-permute-start.8 = (f32[4,8,512]{2,1,0:T(8,128)S(1)}, f32[4,8,512]{2,1,0:T(8,128)S(1)}, u32[]{:S(2)}, u32[]{:S(2)}) collective-permute-start(f32[4,8,512]{2,1,0:T(8,128)S(1)} %get-tuple-element.16), channel_id=1, source_target_pairs={{0,3},{1,2},{2,1},{3,0},{4,7},{5,6},{6,5},{7,4},{8,11},{9,10},{10,... | collective-permute-start | bytes 196616 | tf_op jit(solution)/shard_map/ppermute | solution.py:105
  28.3 1.8 %collective-permute-done.7 = f32[4,8,512]{2,1,0:T(8,128)S(1)} collective-permute-done((f32[4,8,512]{2,1,0:T(8,128)S(1)}, f32[4,8,512]{2,1,0:T(8,128)S(1)}, u32[]{:S(2)}, u32[]{:S(2)}) %collective-permute-start.7) | collective-permute-done | bytes 65568 | tf_op jit(solution)/shard_map/ppermute | solution.py:105
  30.1 1.6 %collective-permute-done.8 = f32[4,8,512]{2,1,0:T(8,128)S(1)} collective-permute-done((f32[4,8,512]{2,1,0:T(8,128)S(1)}, f32[4,8,512]{2,1,0:T(8,128)S(1)}, u32[]{:S(2)}, u32[]{:S(2)}) %collective-permute-start.8) | collective-permute-done | bytes 65568 | tf_op jit(solution)/shard_map/ppermute | solution.py:105
  31.8 1.4 %collective-permute-start.10 = (f32[8,512]{1,0:T(8,128)S(1)}, f32[8,512]{1,0:T(8,128)S(1)}, u32[]{:S(2)}, u32[]{:S(2)}) collective-permute-start(f32[8,512]{1,0:T(8,128)S(1)} %get-tuple-element.28), channel_id=1, source_target_pairs={{0,8},{1,9},{2,10},{3,11},{4,12},{5,13},{6,14},{7,15},{8,0},{9,1},... | collective-permute-start | bytes 49160 | tf_op jit(solution)/shard_map/ppermute | solution.py:101
  33.2 2.1 %collective-permute-start.11 = (f32[8,512]{1,0:T(8,128)S(1)}, f32[8,512]{1,0:T(8,128)S(1)}, u32[]{:S(2)}, u32[]{:S(2)}) collective-permute-start(f32[8,512]{1,0:T(8,128)S(1)} %get-tuple-element.27), channel_id=1, source_target_pairs={{0,12},{1,13},{2,14},{3,15},{4,8},{5,9},{6,10},{7,11},{8,4},{9,5},... | collective-permute-start | bytes 49160 | tf_op jit(solution)/shard_map/ppermute | solution.py:101
  35.3 2.2 %collective-permute-done.11 = f32[8,512]{1,0:T(8,128)S(1)} collective-permute-done((f32[8,512]{1,0:T(8,128)S(1)}, f32[8,512]{1,0:T(8,128)S(1)}, u32[]{:S(2)}, u32[]{:S(2)}) %collective-permute-start.11) | collective-permute-done | bytes 16416 | tf_op jit(solution)/shard_map/ppermute | solution.py:101
  37.8 3.5 %select_reduce_fusion.4 = (f32[8,8]{1,0:T(8,128)S(1)}, f32[8,8,2048]{2,1,0:T(8,128)S(1)}) fusion(pred[8,2048]{1,0:T(8,128)(4,1)S(1)} %iota_compare_fusion, bf16[8,8,128]{2,1,0:T(8,128)(2,1)S(1)} %bitcast.185, bf16[1,8,2048,128]{3,2,1,0:T(8,128)(2,1)} %param.15), kind=kOutput, calls=%fused_computation.20 | convolution fusion | flops 33947584 | bytes 4751616 | tf_op jit(solution)/shard_map/bhe,bte->bht/dot_general | solution.py:200
  41.7 2.9 %fusion.17 = f32[8,8,128]{2,1,0:T(8,128)S(1)} fusion(bf16[1,8,2048,128]{3,2,1,0:T(8,128)(2,1)} %param.16, f32[8,8,2048]{2,1,0:T(8,128)S(1)} %get-tuple-element.46, f32[8,8]{1,0:T(8,128)S(1)} %fusion.43, pred[8,2048]{1,0:T(8,128)(4,1)S(1)} %iota_compare_fusion, f32[8,128]{1,0:T(8,128)S(1)} %get-tuple-element.42, f32[8,8]{1,0:T(8,128)S(1)} %convert_element_type.75), kind=kOutput, calls=%fused_computation.14 | convolution fusion | flops 33964032 | bytes 4772352 | tf_op jit(solution)/shard_map/bht,bte->bhe/dot_general | solution.py:213
  45.2 2.0 %collective-permute-start.12 = (f32[8,4,130]{0,1,2:T(4,128)S(1)}, f32[8,4,130]{0,1,2:T(4,128)S(1)}, u32[]{:S(2)}, u32[]{:S(2)}) collective-permute-start(f32[8,4,130]{0,1,2:T(4,128)S(1)} %pad_maximum_fusion), channel_id=1, source_target_pairs={{0,1},{1,0},{2,3},{3,2},{4,5},{5,4},{6,7},{7,6},{8,9},{9,8},{10,11... | collective-permute-start | bytes 49928 | tf_op jit(solution)/shard_map/ppermute | solution.py:19
  48.9 2.4 %collective-permute-start.14 = (bf16[8,128]{1,0:T(8,128)(2,1)S(1)}, bf16[8,128]{1,0:T(8,128)(2,1)S(1)}, u32[]{:S(2)}, u32[]{:S(2)}) collective-permute-start(bf16[8,128]{1,0:T(8,128)(2,1)S(1)} %bitcast.209), channel_id=1, source_target_pairs={{0,8},{1,9},{2,10},{3,11},{4,12},{5,13},{6,14},{7,15},{8,0},{9,1},... | collective-permute-start | bytes 6152 | tf_op jit(solution)/shard_map/ppermute | solution.py:101
  52.7 3.0 %collective-permute-done.15 = bf16[8,128]{1,0:T(8,128)(2,1)S(1)} collective-permute-done((bf16[8,128]{1,0:T(8,128)(2,1)S(1)}, bf16[8,128]{1,0:T(8,128)(2,1)S(1)}, u32[]{:S(2)}, u32[]{:S(2)}) %collective-permute-start.15) | collective-permute-done | bytes 2080 | tf_op jit(solution)/shard_map/ppermute | solution.py:101
  55.8 2.1 %collective-permute-start.16 = (bf16[4,8,128]{2,1,0:T(8,128)(2,1)S(1)}, bf16[4,8,128]{2,1,0:T(8,128)(2,1)S(1)}, u32[]{:S(2)}, u32[]{:S(2)}) collective-permute-start(bf16[4,8,128]{2,1,0:T(8,128)(2,1)S(1)} %select_reduce_fusion.10), channel_id=1, source_target_pairs={{0,1},{1,0},{2,3},{3,2},{4,5},{5,4},{6,7},{7,6},{8,9},{9,8},{10,11... | collective-permute-start | bytes 24584 | tf_op jit(solution)/shard_map/ppermute | solution.py:105
  58.4 1.3 %collective-permute-start.18 = (bf16[4,8,128]{2,1,0:T(8,128)(2,1)S(1)}, bf16[4,8,128]{2,1,0:T(8,128)(2,1)S(1)}, u32[]{:S(2)}, u32[]{:S(2)}) collective-permute-start(bf16[4,8,128]{2,1,0:T(8,128)(2,1)S(1)} %select_reduce_fusion.10), channel_id=1, source_target_pairs={{0,3},{1,2},{2,1},{3,0},{4,7},{5,6},{6,5},{7,4},{8,11},{9,10},{10,... | collective-permute-start | bytes 24584 | tf_op jit(solution)/shard_map/ppermute | solution.py:105
  61.9 5.6 %fusion.11 = f32[8,4,512]{2,0,1:T(8,128)S(1)} fusion(bf16[4,512,16,128]{3,2,1,0:T(8,128)(2,1)} %bitcast.175, bf16[16,8,128]{2,1,0:T(8,128)(2,1)S(1)} %select_reduce_fusion.3), kind=kOutput, calls=%fused_computation.11 | convolution fusion | flops 67108864 | bytes 8486912 | tf_op jit(solution)/shard_map/gabe,cae->gbc/dot_general | solution.py:259
  67.6 1.9 %collective-permute-start.19 = (f32[8,512]{1,0:T(8,128)S(1)}, f32[8,512]{1,0:T(8,128)S(1)}, u32[]{:S(2)}, u32[]{:S(2)}) collective-permute-start(f32[8,512]{1,0:T(8,128)S(1)} %get-tuple-element.25), channel_id=1, source_target_pairs={{0,0},{1,4},{2,8},{3,12},{4,1},{5,5},{6,9},{7,13},{8,2},{9,6},{10,... | collective-permute-start | bytes 49160 | tf_op jit(solution)/shard_map/ppermute | solution.py:266
  69.6 5.1 %collective-permute-start.21 = (f32[8,512]{1,0:T(8,128)S(1)}, f32[8,512]{1,0:T(8,128)S(1)}, u32[]{:S(2)}, u32[]{:S(2)}) collective-permute-start(f32[8,512]{1,0:T(8,128)S(1)} %get-tuple-element.24), channel_id=1, source_target_pairs={{0,2},{1,6},{2,10},{3,14},{4,3},{5,7},{6,11},{7,15},{8,0},{9,4},{1... | collective-permute-start | bytes 49160 | tf_op jit(solution)/shard_map/ppermute | solution.py:266
  75.7 3.0 %collective-permute-done.22 = f32[8,512]{1,0:T(8,128)S(1)} collective-permute-done((f32[8,512]{1,0:T(8,128)S(1)}, f32[8,512]{1,0:T(8,128)S(1)}, u32[]{:S(2)}, u32[]{:S(2)}) %collective-permute-start.22) | collective-permute-done | bytes 16416 | tf_op jit(solution)/shard_map/ppermute | solution.py:266
  (106 shorter events, 16.9 us)
Async XLA Ops:
  0.0 17.3 %copy-start = (bf16[2,1024,512]{2,1,0:T(8,128)(2,1)S(1)}, bf16[2,1024,512]{2,1,0:T(8,128)(2,1)}, u32[]{:S(2)}) copy-start(bf16[2,1024,512]{2,1,0:T(8,128)(2,1)} %param.13) | copy-start | bytes 6291460
  0.0 7.7 %collective-permute-start = (bf16[8,512]{1,0:T(8,128)(2,1)}, bf16[8,512]{1,0:T(8,128)(2,1)S(1)}, u32[]{:S(2)}, u32[]{:S(2)}) collective-permute-start(bf16[8,512]{1,0:T(8,128)(2,1)} %bitcast.199), channel_id=1, source_target_pairs={{0,4},{1,5},{2,6},{3,7},{4,0},{5,1},{6,2},{7,3},{8,12},{9,13},{10,... | collective-permute-start | bytes 24584 | tf_op jit(solution)/shard_map/ppermute | solution.py:101
  2.1 5.6 %collective-permute-start.1 = (bf16[8,512]{1,0:T(8,128)(2,1)}, bf16[8,512]{1,0:T(8,128)(2,1)S(1)}, u32[]{:S(2)}, u32[]{:S(2)}) collective-permute-start(bf16[8,512]{1,0:T(8,128)(2,1)} %bitcast.200), channel_id=1, source_target_pairs={{0,8},{1,9},{2,10},{3,11},{4,12},{5,13},{6,14},{7,15},{8,0},{9,1},... | collective-permute-start | bytes 24584 | tf_op jit(solution)/shard_map/ppermute | solution.py:101
  4.4 4.5 %collective-permute-start.2 = (bf16[8,512]{1,0:T(8,128)(2,1)}, bf16[8,512]{1,0:T(8,128)(2,1)S(1)}, u32[]{:S(2)}, u32[]{:S(2)}) collective-permute-start(bf16[8,512]{1,0:T(8,128)(2,1)} %bitcast.201), channel_id=1, source_target_pairs={{0,12},{1,13},{2,14},{3,15},{4,8},{5,9},{6,10},{7,11},{8,4},{9,5},... | collective-permute-start | bytes 24584 | tf_op jit(solution)/shard_map/ppermute | solution.py:101
  9.8 5.7 %collective-permute-start.5 = (bf16[4,8,512]{2,1,0:T(8,128)(2,1)S(1)}, bf16[4,8,512]{2,1,0:T(8,128)(2,1)S(1)}, u32[]{:S(2)}, u32[]{:S(2)}) collective-permute-start(bf16[4,8,512]{2,1,0:T(8,128)(2,1)S(1)} %select_reduce_fusion.7), channel_id=1, source_target_pairs={{0,3},{1,2},{2,1},{3,0},{4,7},{5,6},{6,5},{7,4},{8,11},{9,10},{10,... | collective-permute-start | bytes 98312 | tf_op jit(solution)/shard_map/ppermute | solution.py:105
  13.3 2.2 %collective-permute-start.3 = (bf16[4,8,512]{2,1,0:T(8,128)(2,1)S(1)}, bf16[4,8,512]{2,1,0:T(8,128)(2,1)S(1)}, u32[]{:S(2)}, u32[]{:S(2)}) collective-permute-start(bf16[4,8,512]{2,1,0:T(8,128)(2,1)S(1)} %select_reduce_fusion.7), channel_id=1, source_target_pairs={{0,1},{1,0},{2,3},{3,2},{4,5},{5,4},{6,7},{7,6},{8,9},{9,8},{10,11... | collective-permute-start | bytes 98312 | tf_op jit(solution)/shard_map/ppermute | solution.py:105
  13.3 2.8 %collective-permute-start.4 = (bf16[4,8,512]{2,1,0:T(8,128)(2,1)S(1)}, bf16[4,8,512]{2,1,0:T(8,128)(2,1)S(1)}, u32[]{:S(2)}, u32[]{:S(2)}) collective-permute-start(bf16[4,8,512]{2,1,0:T(8,128)(2,1)S(1)} %select_reduce_fusion.7), channel_id=1, source_target_pairs={{0,2},{1,3},{2,0},{3,1},{4,6},{5,7},{6,4},{7,5},{8,10},{9,11},{10,... | collective-permute-start | bytes 98312 | tf_op jit(solution)/shard_map/ppermute | solution.py:105
  24.7 3.6 %collective-permute-start.6 = (f32[4,8,512]{2,1,0:T(8,128)S(1)}, f32[4,8,512]{2,1,0:T(8,128)S(1)}, u32[]{:S(2)}, u32[]{:S(2)}) collective-permute-start(f32[4,8,512]{2,1,0:T(8,128)S(1)} %get-tuple-element.15), channel_id=1, source_target_pairs={{0,1},{1,0},{2,3},{3,2},{4,5},{5,4},{6,7},{7,6},{8,9},{9,8},{10,11... | collective-permute-start | bytes 196616 | tf_op jit(solution)/shard_map/ppermute | solution.py:105
  26.4 3.7 %collective-permute-start.7 = (f32[4,8,512]{2,1,0:T(8,128)S(1)}, f32[4,8,512]{2,1,0:T(8,128)S(1)}, u32[]{:S(2)}, u32[]{:S(2)}) collective-permute-start(f32[4,8,512]{2,1,0:T(8,128)S(1)} %get-tuple-element.17), channel_id=1, source_target_pairs={{0,2},{1,3},{2,0},{3,1},{4,6},{5,7},{6,4},{7,5},{8,10},{9,11},{10,... | collective-permute-start | bytes 196616 | tf_op jit(solution)/shard_map/ppermute | solution.py:105
  26.7 5.0 %collective-permute-start.8 = (f32[4,8,512]{2,1,0:T(8,128)S(1)}, f32[4,8,512]{2,1,0:T(8,128)S(1)}, u32[]{:S(2)}, u32[]{:S(2)}) collective-permute-start(f32[4,8,512]{2,1,0:T(8,128)S(1)} %get-tuple-element.16), channel_id=1, source_target_pairs={{0,3},{1,2},{2,1},{3,0},{4,7},{5,6},{6,5},{7,4},{8,11},{9,10},{10,... | collective-permute-start | bytes 196616 | tf_op jit(solution)/shard_map/ppermute | solution.py:105
  31.7 3.6 %collective-permute-start.9 = (f32[8,512]{1,0:T(8,128)S(1)}, f32[8,512]{1,0:T(8,128)S(1)}, u32[]{:S(2)}, u32[]{:S(2)}) collective-permute-start(f32[8,512]{1,0:T(8,128)S(1)} %get-tuple-element.29), channel_id=1, source_target_pairs={{0,4},{1,5},{2,6},{3,7},{4,0},{5,1},{6,2},{7,3},{8,12},{9,13},{10,... | collective-permute-start | bytes 49160 | tf_op jit(solution)/shard_map/ppermute | solution.py:101
  31.8 3.6 %collective-permute-start.10 = (f32[8,512]{1,0:T(8,128)S(1)}, f32[8,512]{1,0:T(8,128)S(1)}, u32[]{:S(2)}, u32[]{:S(2)}) collective-permute-start(f32[8,512]{1,0:T(8,128)S(1)} %get-tuple-element.28), channel_id=1, source_target_pairs={{0,8},{1,9},{2,10},{3,11},{4,12},{5,13},{6,14},{7,15},{8,0},{9,1},... | collective-permute-start | bytes 49160 | tf_op jit(solution)/shard_map/ppermute | solution.py:101
  33.2 4.4 %collective-permute-start.11 = (f32[8,512]{1,0:T(8,128)S(1)}, f32[8,512]{1,0:T(8,128)S(1)}, u32[]{:S(2)}, u32[]{:S(2)}) collective-permute-start(f32[8,512]{1,0:T(8,128)S(1)} %get-tuple-element.27), channel_id=1, source_target_pairs={{0,12},{1,13},{2,14},{3,15},{4,8},{5,9},{6,10},{7,11},{8,4},{9,5},... | collective-permute-start | bytes 49160 | tf_op jit(solution)/shard_map/ppermute | solution.py:101
  45.2 3.2 %collective-permute-start.12 = (f32[8,4,130]{0,1,2:T(4,128)S(1)}, f32[8,4,130]{0,1,2:T(4,128)S(1)}, u32[]{:S(2)}, u32[]{:S(2)}) collective-permute-start(f32[8,4,130]{0,1,2:T(4,128)S(1)} %pad_maximum_fusion), channel_id=1, source_target_pairs={{0,1},{1,0},{2,3},{3,2},{4,5},{5,4},{6,7},{7,6},{8,9},{9,8},{10,11... | collective-permute-start | bytes 49928 | tf_op jit(solution)/shard_map/ppermute | solution.py:19
  48.8 3.8 %collective-permute-start.13 = (bf16[8,128]{1,0:T(8,128)(2,1)S(1)}, bf16[8,128]{1,0:T(8,128)(2,1)S(1)}, u32[]{:S(2)}, u32[]{:S(2)}) collective-permute-start(bf16[8,128]{1,0:T(8,128)(2,1)S(1)} %bitcast.208), channel_id=1, source_target_pairs={{0,4},{1,5},{2,6},{3,7},{4,0},{5,1},{6,2},{7,3},{8,12},{9,13},{10,... | collective-permute-start | bytes 6152 | tf_op jit(solution)/shard_map/ppermute | solution.py:101
  48.9 3.7 %collective-permute-start.14 = (bf16[8,128]{1,0:T(8,128)(2,1)S(1)}, bf16[8,128]{1,0:T(8,128)(2,1)S(1)}, u32[]{:S(2)}, u32[]{:S(2)}) collective-permute-start(bf16[8,128]{1,0:T(8,128)(2,1)S(1)} %bitcast.209), channel_id=1, source_target_pairs={{0,8},{1,9},{2,10},{3,11},{4,12},{5,13},{6,14},{7,15},{8,0},{9,1},... | collective-permute-start | bytes 6152 | tf_op jit(solution)/shard_map/ppermute | solution.py:101
  51.4 4.3 %collective-permute-start.15 = (bf16[8,128]{1,0:T(8,128)(2,1)S(1)}, bf16[8,128]{1,0:T(8,128)(2,1)S(1)}, u32[]{:S(2)}, u32[]{:S(2)}) collective-permute-start(bf16[8,128]{1,0:T(8,128)(2,1)S(1)} %bitcast.210), channel_id=1, source_target_pairs={{0,12},{1,13},{2,14},{3,15},{4,8},{5,9},{6,10},{7,11},{8,4},{9,5},... | collective-permute-start | bytes 6152 | tf_op jit(solution)/shard_map/ppermute | solution.py:101
  55.8 3.9 %collective-permute-start.16 = (bf16[4,8,128]{2,1,0:T(8,128)(2,1)S(1)}, bf16[4,8,128]{2,1,0:T(8,128)(2,1)S(1)}, u32[]{:S(2)}, u32[]{:S(2)}) collective-permute-start(bf16[4,8,128]{2,1,0:T(8,128)(2,1)S(1)} %select_reduce_fusion.10), channel_id=1, source_target_pairs={{0,1},{1,0},{2,3},{3,2},{4,5},{5,4},{6,7},{7,6},{8,9},{9,8},{10,11... | collective-permute-start | bytes 24584 | tf_op jit(solution)/shard_map/ppermute | solution.py:105
  58.0 2.5 %collective-permute-start.17 = (bf16[4,8,128]{2,1,0:T(8,128)(2,1)S(1)}, bf16[4,8,128]{2,1,0:T(8,128)(2,1)S(1)}, u32[]{:S(2)}, u32[]{:S(2)}) collective-permute-start(bf16[4,8,128]{2,1,0:T(8,128)(2,1)S(1)} %select_reduce_fusion.10), channel_id=1, source_target_pairs={{0,2},{1,3},{2,0},{3,1},{4,6},{5,7},{6,4},{7,5},{8,10},{9,11},{10,... | collective-permute-start | bytes 24584 | tf_op jit(solution)/shard_map/ppermute | solution.py:105
  58.4 3.1 %collective-permute-start.18 = (bf16[4,8,128]{2,1,0:T(8,128)(2,1)S(1)}, bf16[4,8,128]{2,1,0:T(8,128)(2,1)S(1)}, u32[]{:S(2)}, u32[]{:S(2)}) collective-permute-start(bf16[4,8,128]{2,1,0:T(8,128)(2,1)S(1)} %select_reduce_fusion.10), channel_id=1, source_target_pairs={{0,3},{1,2},{2,1},{3,0},{4,7},{5,6},{6,5},{7,4},{8,11},{9,10},{10,... | collective-permute-start | bytes 24584 | tf_op jit(solution)/shard_map/ppermute | solution.py:105
  67.6 7.5 %collective-permute-start.19 = (f32[8,512]{1,0:T(8,128)S(1)}, f32[8,512]{1,0:T(8,128)S(1)}, u32[]{:S(2)}, u32[]{:S(2)}) collective-permute-start(f32[8,512]{1,0:T(8,128)S(1)} %get-tuple-element.25), channel_id=1, source_target_pairs={{0,0},{1,4},{2,8},{3,12},{4,1},{5,5},{6,9},{7,13},{8,2},{9,6},{10,... | collective-permute-start | bytes 49160 | tf_op jit(solution)/shard_map/ppermute | solution.py:266
  69.5 5.6 %collective-permute-start.20 = (f32[8,512]{1,0:T(8,128)S(1)}, f32[8,512]{1,0:T(8,128)S(1)}, u32[]{:S(2)}, u32[]{:S(2)}) collective-permute-start(f32[8,512]{1,0:T(8,128)S(1)} %get-tuple-element.22), channel_id=1, source_target_pairs={{0,1},{1,5},{2,9},{3,13},{4,0},{5,4},{6,8},{7,12},{8,3},{9,7},{10,... | collective-permute-start | bytes 49160 | tf_op jit(solution)/shard_map/ppermute | solution.py:266
  69.6 6.1 %collective-permute-start.21 = (f32[8,512]{1,0:T(8,128)S(1)}, f32[8,512]{1,0:T(8,128)S(1)}, u32[]{:S(2)}, u32[]{:S(2)}) collective-permute-start(f32[8,512]{1,0:T(8,128)S(1)} %get-tuple-element.24), channel_id=1, source_target_pairs={{0,2},{1,6},{2,10},{3,14},{4,3},{5,7},{6,11},{7,15},{8,0},{9,4},{1... | collective-permute-start | bytes 49160 | tf_op jit(solution)/shard_map/ppermute | solution.py:266
  74.7 4.1 %collective-permute-start.22 = (f32[8,512]{1,0:T(8,128)S(1)}, f32[8,512]{1,0:T(8,128)S(1)}, u32[]{:S(2)}, u32[]{:S(2)}) collective-permute-start(f32[8,512]{1,0:T(8,128)S(1)} %get-tuple-element.23), channel_id=1, source_target_pairs={{0,3},{1,7},{2,11},{3,15},{4,2},{5,6},{6,10},{7,14},{8,1},{9,5},{1... | collective-permute-start | bytes 49160 | tf_op jit(solution)/shard_map/ppermute | solution.py:266
  (1 other events, 10.1 us)

commit v14 on v6

--- a/solution.py
+++ b/solution.py
@@ -235,17 +235,22 @@
     numer = own_summed * factor_own[..., None] + got_summed * factor_got[..., None]
     denom = own_total * factor_own + got_total * factor_got
     attention = (numer / denom[..., None]).astype(jnp.bfloat16)
-    from_rows = [lax.dynamic_index_in_dim(attention, grid_row, 1, keepdims=False)]
-    for s in range(1, GR):
-        piece = lax.dynamic_index_in_dim(attention, grid_row ^ s, 1, keepdims=False)
-        from_rows.append(swap_rows(piece, "tp", col_bits, s))
-    by_row = pick(jnp.stack(from_rows), row_order)
     if direct_cols:
-        from_cols = [by_row] + [swap_cols(by_row, "tp", s) for s in range(1, grid_cols)]
-        every_slot = pick(jnp.stack(from_cols), col_order)
-    else:
+        from_cols = [attention] + [swap_cols(attention, "tp", s) for s in range(1, grid_cols)]
+        in_row_attn = pick(jnp.stack(from_cols), col_order)
+        from_rows = [lax.dynamic_index_in_dim(in_row_attn, grid_row, 2, keepdims=False)]
+        for s in range(1, GR):
+            piece = lax.dynamic_index_in_dim(in_row_attn, grid_row ^ s, 2, keepdims=False)
+            from_rows.append(swap_rows(piece, "tp", col_bits, s))
+        every_slot = pick(jnp.stack(from_rows), row_order).reshape(group_count, ROLL, ROWS, HD)
+    else:
+        from_rows = [lax.dynamic_index_in_dim(attention, grid_row, 1, keepdims=False)]
+        for s in range(1, GR):
+            piece = lax.dynamic_index_in_dim(attention, grid_row ^ s, 1, keepdims=False)
+            from_rows.append(swap_rows(piece, "tp", col_bits, s))
+        by_row = pick(jnp.stack(from_rows), row_order)
         every_slot = gather_rounds(by_row[None], "tp", range(col_bits))
-    every_slot = every_slot.transpose(1, 0, 2, 3).reshape(group_count, ROLL, ROWS, HD)
+        every_slot = every_slot.transpose(1, 0, 2, 3).reshape(group_count, ROLL, ROWS, HD)
     head_ids = jnp.arange(KVH, dtype=jnp.int32)
     pair_heads = kv_assign[0::2]
     inverse = jnp.sum(

time: 78.1 us -> 82.8 us (1.060)
  waiting for transfers between devices: 19 us -> 23.4 us
    ppermute x9, waiting for transfers between devices: 5.8 us -> 9.67 us  [swap_cols(): lax.ppermute(value, axis, [(t, t ^ s) for t in range(lax.axis_size(axis))])]
    ppermute x4, starting transfers between devices: 6.81 us -> 8.6 us  [local(): got = lax.ppermute(piece, 'tp', pairs)]
    ppermute x9, starting transfers between devices: 9.89 us -> 8.26 us  [swap_cols(): lax.ppermute(value, axis, [(t, t ^ s) for t in range(lax.axis_size(axis))])]
  transfers between devices with their start and end apart: 23 -> 23, of which waited for: 13 -> 13; matrix products, arithmetic and copies ran while one was open for 5% -> 4% of each run, Pallas kernels for 0% -> 0%
where the time goes in v14:
time: 82.8 us; the launch traced here: 82.4 us
  starting transfers between devices  30.7 us (37%)
  waiting for transfers between devices  23.4 us (28%)
  matrix products  18.4 us (22%)
  other arithmetic  6.05 us (7%)
  local copies, waits for them, and re-layouts  3.51 us (4%)
    ppermute x9, starting transfers between devices, swap_rows(): lax.ppermute(value, axis, [(t, t ^ shift) for t in range(lax.axis_size(ax...  11.7 us
    ppermute x9, waiting for transfers between devices, swap_cols(): lax.ppermute(value, axis, [(t, t ^ s) for t in range(lax.axis_size(axis))])  9.67 us
    ppermute x4, starting transfers between devices, local(): got = lax.ppermute(piece, 'tp', pairs)  8.6 us
    ppermute x9, waiting for transfers between devices, swap_rows(): lax.ppermute(value, axis, [(t, t ^ shift) for t in range(lax.axis_size(ax...  8.46 us
    ppermute x9, starting transfers between devices, swap_cols(): lax.ppermute(value, axis, [(t, t ^ s) for t in range(lax.axis_size(axis))])  8.26 us
    dot_general x1, matrix products, local(): jnp.einsum('rc,aec->rae', col_rows, q_blocks[0], preferred_element_type=j...  5.65 us
    dot_general x1, matrix products, local(): jnp.einsum('gabe,cae->gbc', chosen, o_blocks[0], preferred_element_type=j...  5.65 us
    ppermute x4, waiting for transfers between devices, local(): got = lax.ppermute(piece, 'tp', pairs)  4.06 us
  transfers between devices with their start and end apart: 23, of which 13 were waited for; matrix products, arithmetic and copies ran while one was open for 4% of the time, Pallas kernels for 0%

profile of v14, /device:TPU:1, one launch (start us, length us, event | category | flops | bytes accessed | tf_op | source)
XLA Modules:
  0.0 82.4 jit_solution(10708013504053743491)
XLA Ops:
  0.1 2.7 %collective-permute-start.1 = (bf16[8,512]{1,0:T(8,128)(2,1)}, bf16[8,512]{1,0:T(8,128)(2,1)S(1)}, u32[]{:S(2)}, u32[]{:S(2)}) collective-permute-start(bf16[8,512]{1,0:T(8,128)(2,1)} %bitcast.202), channel_id=1, source_target_pairs={{0,2},{1,3},{2,0},{3,1},{4,6},{5,7},{6,4},{7,5},{8,10},{9,11},{10,... | collective-permute-start | bytes 24584 | tf_op jit(solution)/shard_map/ppermute | solution.py:105
  3.8 1.3 %gather_fusion.1 = s32[16]{0:T(128)S(1)} fusion(s32[16]{0:T(128)} %param.14, s32[1024]{0:T(1024)S(1)} %pad_clamp_fusion), kind=kCustom, calls=%fused_computation.1 | custom fusion | bytes 192 | tf_op jit(solution)/shard_map/gather | solution.py:128
  6.8 3.8 %collective-permute-start.5 = (bf16[4,8,512]{2,1,0:T(8,128)(2,1)S(1)}, bf16[4,8,512]{2,1,0:T(8,128)(2,1)S(1)}, u32[]{:S(2)}, u32[]{:S(2)}) collective-permute-start(bf16[4,8,512]{2,1,0:T(8,128)(2,1)S(1)} %select_reduce_fusion.8), channel_id=1, source_target_pairs={{0,12},{1,13},{2,14},{3,15},{4,8},{5,9},{6,10},{7,11},{8,4},{9,5},... | collective-permute-start | bytes 98312 | tf_op jit(solution)/shard_map/ppermute | solution.py:101
  11.1 1.2 %collective-permute-done.5 = bf16[4,8,512]{2,1,0:T(8,128)(2,1)S(1)} collective-permute-done((bf16[4,8,512]{2,1,0:T(8,128)(2,1)S(1)}, bf16[4,8,512]{2,1,0:T(8,128)(2,1)S(1)}, u32[]{:S(2)}, u32[]{:S(2)}) %collective-permute-start.5) | collective-permute-done | bytes 32800 | tf_op jit(solution)/shard_map/ppermute | solution.py:101
  16.3 5.7 %fusion.14 = f32[16,8,128]{2,1,0:T(8,128)S(1)} fusion(bf16[1,16,128,2048]{3,2,1,0:T(8,128)(2,1)} %param.11, bf16[8,8192]{1,0:T(8,128)(2,1)S(1)} %multiply_convert_fusion, s32[]{:T(128)S(6)} %select_n.283), kind=kOutput, calls=%fused_computation.12 | convolution fusion | flops 67108864 | bytes 8486916 | tf_op jit(solution)/shard_map/rc,aec->rae/dot_general | solution.py:152
  23.0 1.6 %collective-permute-start.6 = (f32[4,8,512]{2,1,0:T(8,128)S(1)}, f32[4,8,512]{2,1,0:T(8,128)S(1)}, u32[]{:S(2)}, u32[]{:S(2)}) collective-permute-start(f32[4,8,512]{2,1,0:T(8,128)S(1)} %get-tuple-element.15), channel_id=1, source_target_pairs={{0,1},{1,0},{2,3},{3,2},{4,5},{5,4},{6,7},{7,6},{8,9},{9,8},{10,11... | collective-permute-start | bytes 196616 | tf_op jit(solution)/shard_map/ppermute | solution.py:105
  24.6 1.2 %collective-permute-start.7 = (f32[4,8,512]{2,1,0:T(8,128)S(1)}, f32[4,8,512]{2,1,0:T(8,128)S(1)}, u32[]{:S(2)}, u32[]{:S(2)}) collective-permute-start(f32[4,8,512]{2,1,0:T(8,128)S(1)} %get-tuple-element.17), channel_id=1, source_target_pairs={{0,2},{1,3},{2,0},{3,1},{4,6},{5,7},{6,4},{7,5},{8,10},{9,11},{10,... | collective-permute-start | bytes 196616 | tf_op jit(solution)/shard_map/ppermute | solution.py:105
  26.4 1.8 %collective-permute-done.7 = f32[4,8,512]{2,1,0:T(8,128)S(1)} collective-permute-done((f32[4,8,512]{2,1,0:T(8,128)S(1)}, f32[4,8,512]{2,1,0:T(8,128)S(1)}, u32[]{:S(2)}, u32[]{:S(2)}) %collective-permute-start.7) | collective-permute-done | bytes 65568 | tf_op jit(solution)/shard_map/ppermute | solution.py:105
  28.2 1.6 %collective-permute-done.8 = f32[4,8,512]{2,1,0:T(8,128)S(1)} collective-permute-done((f32[4,8,512]{2,1,0:T(8,128)S(1)}, f32[4,8,512]{2,1,0:T(8,128)S(1)}, u32[]{:S(2)}, u32[]{:S(2)}) %collective-permute-start.8) | collective-permute-done | bytes 65568 | tf_op jit(solution)/shard_map/ppermute | solution.py:105
  29.9 1.8 %collective-permute-start.9 = (f32[8,512]{1,0:T(8,128)S(1)}, f32[8,512]{1,0:T(8,128)S(1)}, u32[]{:S(2)}, u32[]{:S(2)}) collective-permute-start(f32[8,512]{1,0:T(8,128)S(1)} %get-tuple-element.25), channel_id=1, source_target_pairs={{0,4},{1,5},{2,6},{3,7},{4,0},{5,1},{6,2},{7,3},{8,12},{9,13},{10,... | collective-permute-start | bytes 49160 | tf_op jit(solution)/shard_map/ppermute | solution.py:101
  31.7 2.2 %collective-permute-start.11 = (f32[8,512]{1,0:T(8,128)S(1)}, f32[8,512]{1,0:T(8,128)S(1)}, u32[]{:S(2)}, u32[]{:S(2)}) collective-permute-start(f32[8,512]{1,0:T(8,128)S(1)} %get-tuple-element.23), channel_id=1, source_target_pairs={{0,12},{1,13},{2,14},{3,15},{4,8},{5,9},{6,10},{7,11},{8,4},{9,5},... | collective-permute-start | bytes 49160 | tf_op jit(solution)/shard_map/ppermute | solution.py:101
  33.8 1.3 %collective-permute-done.10 = f32[8,512]{1,0:T(8,128)S(1)} collective-permute-done((f32[8,512]{1,0:T(8,128)S(1)}, f32[8,512]{1,0:T(8,128)S(1)}, u32[]{:S(2)}, u32[]{:S(2)}) %collective-permute-start.10) | collective-permute-done | bytes 16416 | tf_op jit(solution)/shard_map/ppermute | solution.py:101
  36.4 3.5 %select_reduce_fusion.4 = (f32[8,8]{1,0:T(8,128)S(1)}, f32[8,8,2048]{2,1,0:T(8,128)S(1)}) fusion(pred[8,2048]{1,0:T(8,128)(4,1)S(1)} %iota_compare_fusion, bf16[8,8,128]{2,1,0:T(8,128)(2,1)S(1)} %bitcast.189, bf16[1,8,2048,128]{3,2,1,0:T(8,128)(2,1)} %param.15), kind=kOutput, calls=%fused_computation.21 | convolution fusion | flops 33947584 | bytes 4751616 | tf_op jit(solution)/shard_map/bhe,bte->bht/dot_general | solution.py:198
  40.2 2.9 %fusion.17 = f32[8,8,128]{2,1,0:T(8,128)S(1)} fusion(bf16[1,8,2048,128]{3,2,1,0:T(8,128)(2,1)} %param.16, f32[8,8,2048]{2,1,0:T(8,128)S(1)} %get-tuple-element.46, f32[8,8]{1,0:T(8,128)S(1)} %fusion.42, pred[8,2048]{1,0:T(8,128)(4,1)S(1)} %iota_compare_fusion, f32[8,128]{1,0:T(8,128)S(1)} %get-tuple-element.42, f32[8,8]{1,0:T(8,128)S(1)} %convert_element_type.70), kind=kOutput, calls=%fused_computation.14 | convolution fusion | flops 33964032 | bytes 4772352 | tf_op jit(solution)/shard_map/bht,bte->bhe/dot_general | solution.py:211
  43.7 2.1 %collective-permute-start.12 = (f32[8,4,130]{0,1,2:T(4,128)S(1)}, f32[8,4,130]{0,1,2:T(4,128)S(1)}, u32[]{:S(2)}, u32[]{:S(2)}) collective-permute-start(f32[8,4,130]{0,1,2:T(4,128)S(1)} %pad_maximum_fusion.1), channel_id=1, source_target_pairs={{0,1},{1,0},{2,3},{3,2},{4,5},{5,4},{6,7},{7,6},{8,9},{9,8},{10,11... | collective-permute-start | bytes 49928 | tf_op jit(solution)/shard_map/ppermute | solution.py:19
  49.3 3.2 %collective-permute-done.14 = bf16[8,4,128]{0,1,2:T(4,128)(2,1)S(1)} collective-permute-done((bf16[8,4,128]{0,1,2:T(4,128)(2,1)S(1)}, bf16[8,4,128]{0,1,2:T(4,128)(2,1)S(1)}, u32[]{:S(2)}, u32[]{:S(2)}) %collective-permute-start.14) | collective-permute-done | bytes 8224 | tf_op jit(solution)/shard_map/ppermute | solution.py:105
  52.4 3.1 %collective-permute-done.15 = bf16[8,4,128]{0,1,2:T(4,128)(2,1)S(1)} collective-permute-done((bf16[8,4,128]{0,1,2:T(4,128)(2,1)S(1)}, bf16[8,4,128]{0,1,2:T(4,128)(2,1)S(1)}, u32[]{:S(2)}, u32[]{:S(2)}) %collective-permute-start.15) | collective-permute-done | bytes 8224 | tf_op jit(solution)/shard_map/ppermute | solution.py:105
  56.5 2.2 %collective-permute-start.17 = (bf16[4,8,128]{2,1,0:T(8,128)(2,1)S(1)}, bf16[4,8,128]{2,1,0:T(8,128)(2,1)S(1)}, u32[]{:S(2)}, u32[]{:S(2)}) collective-permute-start(bf16[4,8,128]{2,1,0:T(8,128)(2,1)S(1)} %get-tuple-element.28), channel_id=1, source_target_pairs={{0,8},{1,9},{2,10},{3,11},{4,12},{5,13},{6,14},{7,15},{8,0},{9,1},... | collective-permute-start | bytes 24584 | tf_op jit(solution)/shard_map/ppermute | solution.py:101
  58.7 1.3 %collective-permute-start.18 = (bf16[4,8,128]{2,1,0:T(8,128)(2,1)S(1)}, bf16[4,8,128]{2,1,0:T(8,128)(2,1)S(1)}, u32[]{:S(2)}, u32[]{:S(2)}) collective-permute-start(bf16[4,8,128]{2,1,0:T(8,128)(2,1)S(1)} %get-tuple-element.27), channel_id=1, source_target_pairs={{0,12},{1,13},{2,14},{3,15},{4,8},{5,9},{6,10},{7,11},{8,4},{9,5},... | collective-permute-start | bytes 24584 | tf_op jit(solution)/shard_map/ppermute | solution.py:101
  60.1 2.9 %collective-permute-done.18 = bf16[4,8,128]{2,1,0:T(8,128)(2,1)S(1)} collective-permute-done((bf16[4,8,128]{2,1,0:T(8,128)(2,1)S(1)}, bf16[4,8,128]{2,1,0:T(8,128)(2,1)S(1)}, u32[]{:S(2)}, u32[]{:S(2)}) %collective-permute-start.18) | collective-permute-done | bytes 8224 | tf_op jit(solution)/shard_map/ppermute | solution.py:101
  63.5 5.6 %fusion.11 = f32[8,4,512]{2,0,1:T(8,128)S(1)} fusion(bf16[4,512,16,128]{3,2,1,0:T(8,128)(2,1)} %bitcast.176, bf16[16,8,128]{2,1,0:T(8,128)(2,1)S(1)} %select_reduce_fusion.3), kind=kOutput, calls=%fused_computation.11 | convolution fusion | flops 67108864 | bytes 8486912 | tf_op jit(solution)/shard_map/gabe,cae->gbc/dot_general | solution.py:262
  69.1 1.9 %collective-permute-start.19 = (f32[8,512]{1,0:T(8,128)S(1)}, f32[8,512]{1,0:T(8,128)S(1)}, u32[]{:S(2)}, u32[]{:S(2)}) collective-permute-start(f32[8,512]{1,0:T(8,128)S(1)} %get-tuple-element.21), channel_id=1, source_target_pairs={{0,0},{1,4},{2,8},{3,12},{4,1},{5,5},{6,9},{7,13},{8,2},{9,6},{10,... | collective-permute-start | bytes 49160 | tf_op jit(solution)/shard_map/ppermute | solution.py:269
  71.1 6.6 %collective-permute-start.21 = (f32[8,512]{1,0:T(8,128)S(1)}, f32[8,512]{1,0:T(8,128)S(1)}, u32[]{:S(2)}, u32[]{:S(2)}) collective-permute-start(f32[8,512]{1,0:T(8,128)S(1)} %get-tuple-element.20), channel_id=1, source_target_pairs={{0,2},{1,6},{2,10},{3,14},{4,3},{5,7},{6,11},{7,15},{8,0},{9,4},{1... | collective-permute-start | bytes 49160 | tf_op jit(solution)/shard_map/ppermute | solution.py:269
  78.8 3.0 %collective-permute-done.22 = f32[8,512]{1,0:T(8,128)S(1)} collective-permute-done((f32[8,512]{1,0:T(8,128)S(1)}, f32[8,512]{1,0:T(8,128)S(1)}, u32[]{:S(2)}, u32[]{:S(2)}) %collective-permute-start.22) | collective-permute-done | bytes 16416 | tf_op jit(solution)/shard_map/ppermute | solution.py:269
  (101 shorter events, 17.6 us)
Async XLA Ops:
  0.0 15.7 %copy-start = (bf16[2,1024,512]{2,1,0:T(8,128)(2,1)S(1)}, bf16[2,1024,512]{2,1,0:T(8,128)(2,1)}, u32[]{:S(2)}) copy-start(bf16[2,1024,512]{2,1,0:T(8,128)(2,1)} %param.13) | copy-start | bytes 6291460
  0.0 6.0 %collective-permute-start = (bf16[8,512]{1,0:T(8,128)(2,1)}, bf16[8,512]{1,0:T(8,128)(2,1)S(1)}, u32[]{:S(2)}, u32[]{:S(2)}) collective-permute-start(bf16[8,512]{1,0:T(8,128)(2,1)} %bitcast.201), channel_id=1, source_target_pairs={{0,1},{1,0},{2,3},{3,2},{4,5},{5,4},{6,7},{7,6},{8,9},{9,8},{10,11... | collective-permute-start | bytes 24584 | tf_op jit(solution)/shard_map/ppermute | solution.py:105
  0.1 5.9 %collective-permute-start.1 = (bf16[8,512]{1,0:T(8,128)(2,1)}, bf16[8,512]{1,0:T(8,128)(2,1)S(1)}, u32[]{:S(2)}, u32[]{:S(2)}) collective-permute-start(bf16[8,512]{1,0:T(8,128)(2,1)} %bitcast.202), channel_id=1, source_target_pairs={{0,2},{1,3},{2,0},{3,1},{4,6},{5,7},{6,4},{7,5},{8,10},{9,11},{10,... | collective-permute-start | bytes 24584 | tf_op jit(solution)/shard_map/ppermute | solution.py:105
  2.7 3.3 %collective-permute-start.2 = (bf16[8,512]{1,0:T(8,128)(2,1)}, bf16[8,512]{1,0:T(8,128)(2,1)S(1)}, u32[]{:S(2)}, u32[]{:S(2)}) collective-permute-start(bf16[8,512]{1,0:T(8,128)(2,1)} %bitcast.203), channel_id=1, source_target_pairs={{0,3},{1,2},{2,1},{3,0},{4,7},{5,6},{6,5},{7,4},{8,11},{9,10},{10,... | collective-permute-start | bytes 24584 | tf_op jit(solution)/shard_map/ppermute | solution.py:105
  6.8 5.4 %collective-permute-start.5 = (bf16[4,8,512]{2,1,0:T(8,128)(2,1)S(1)}, bf16[4,8,512]{2,1,0:T(8,128)(2,1)S(1)}, u32[]{:S(2)}, u32[]{:S(2)}) collective-permute-start(bf16[4,8,512]{2,1,0:T(8,128)(2,1)S(1)} %select_reduce_fusion.8), channel_id=1, source_target_pairs={{0,12},{1,13},{2,14},{3,15},{4,8},{5,9},{6,10},{7,11},{8,4},{9,5},... | collective-permute-start | bytes 98312 | tf_op jit(solution)/shard_map/ppermute | solution.py:101
  10.7 2.8 %collective-permute-start.3 = (bf16[4,8,512]{2,1,0:T(8,128)(2,1)S(1)}, bf16[4,8,512]{2,1,0:T(8,128)(2,1)S(1)}, u32[]{:S(2)}, u32[]{:S(2)}) collective-permute-start(bf16[4,8,512]{2,1,0:T(8,128)(2,1)S(1)} %select_reduce_fusion.8), channel_id=1, source_target_pairs={{0,4},{1,5},{2,6},{3,7},{4,0},{5,1},{6,2},{7,3},{8,12},{9,13},{10,... | collective-permute-start | bytes 98312 | tf_op jit(solution)/shard_map/ppermute | solution.py:101
  10.7 3.8 %collective-permute-start.4 = (bf16[4,8,512]{2,1,0:T(8,128)(2,1)S(1)}, bf16[4,8,512]{2,1,0:T(8,128)(2,1)S(1)}, u32[]{:S(2)}, u32[]{:S(2)}) collective-permute-start(bf16[4,8,512]{2,1,0:T(8,128)(2,1)S(1)} %select_reduce_fusion.8), channel_id=1, source_target_pairs={{0,8},{1,9},{2,10},{3,11},{4,12},{5,13},{6,14},{7,15},{8,0},{9,1},... | collective-permute-start | bytes 98312 | tf_op jit(solution)/shard_map/ppermute | solution.py:101
  23.0 3.4 %collective-permute-start.6 = (f32[4,8,512]{2,1,0:T(8,128)S(1)}, f32[4,8,512]{2,1,0:T(8,128)S(1)}, u32[]{:S(2)}, u32[]{:S(2)}) collective-permute-start(f32[4,8,512]{2,1,0:T(8,128)S(1)} %get-tuple-element.15), channel_id=1, source_target_pairs={{0,1},{1,0},{2,3},{3,2},{4,5},{5,4},{6,7},{7,6},{8,9},{9,8},{10,11... | collective-permute-start | bytes 196616 | tf_op jit(solution)/shard_map/ppermute | solution.py:105
  24.6 3.7 %collective-permute-start.7 = (f32[4,8,512]{2,1,0:T(8,128)S(1)}, f32[4,8,512]{2,1,0:T(8,128)S(1)}, u32[]{:S(2)}, u32[]{:S(2)}) collective-permute-start(f32[4,8,512]{2,1,0:T(8,128)S(1)} %get-tuple-element.17), channel_id=1, source_target_pairs={{0,2},{1,3},{2,0},{3,1},{4,6},{5,7},{6,4},{7,5},{8,10},{9,11},{10,... | collective-permute-start | bytes 196616 | tf_op jit(solution)/shard_map/ppermute | solution.py:105
  25.8 4.0 %collective-permute-start.8 = (f32[4,8,512]{2,1,0:T(8,128)S(1)}, f32[4,8,512]{2,1,0:T(8,128)S(1)}, u32[]{:S(2)}, u32[]{:S(2)}) collective-permute-start(f32[4,8,512]{2,1,0:T(8,128)S(1)} %get-tuple-element.16), channel_id=1, source_target_pairs={{0,3},{1,2},{2,1},{3,0},{4,7},{5,6},{6,5},{7,4},{8,11},{9,10},{10,... | collective-permute-start | bytes 196616 | tf_op jit(solution)/shard_map/ppermute | solution.py:105
  29.9 4.0 %collective-permute-start.9 = (f32[8,512]{1,0:T(8,128)S(1)}, f32[8,512]{1,0:T(8,128)S(1)}, u32[]{:S(2)}, u32[]{:S(2)}) collective-permute-start(f32[8,512]{1,0:T(8,128)S(1)} %get-tuple-element.25), channel_id=1, source_target_pairs={{0,4},{1,5},{2,6},{3,7},{4,0},{5,1},{6,2},{7,3},{8,12},{9,13},{10,... | collective-permute-start | bytes 49160 | tf_op jit(solution)/shard_map/ppermute | solution.py:101
  31.7 3.5 %collective-permute-start.10 = (f32[8,512]{1,0:T(8,128)S(1)}, f32[8,512]{1,0:T(8,128)S(1)}, u32[]{:S(2)}, u32[]{:S(2)}) collective-permute-start(f32[8,512]{1,0:T(8,128)S(1)} %get-tuple-element.24), channel_id=1, source_target_pairs={{0,8},{1,9},{2,10},{3,11},{4,12},{5,13},{6,14},{7,15},{8,0},{9,1},... | collective-permute-start | bytes 49160 | tf_op jit(solution)/shard_map/ppermute | solution.py:101
  31.7 4.4 %collective-permute-start.11 = (f32[8,512]{1,0:T(8,128)S(1)}, f32[8,512]{1,0:T(8,128)S(1)}, u32[]{:S(2)}, u32[]{:S(2)}) collective-permute-start(f32[8,512]{1,0:T(8,128)S(1)} %get-tuple-element.23), channel_id=1, source_target_pairs={{0,12},{1,13},{2,14},{3,15},{4,8},{5,9},{6,10},{7,11},{8,4},{9,5},... | collective-permute-start | bytes 49160 | tf_op jit(solution)/shard_map/ppermute | solution.py:101
  43.7 3.2 %collective-permute-start.12 = (f32[8,4,130]{0,1,2:T(4,128)S(1)}, f32[8,4,130]{0,1,2:T(4,128)S(1)}, u32[]{:S(2)}, u32[]{:S(2)}) collective-permute-start(f32[8,4,130]{0,1,2:T(4,128)S(1)} %pad_maximum_fusion.1), channel_id=1, source_target_pairs={{0,1},{1,0},{2,3},{3,2},{4,5},{5,4},{6,7},{7,6},{8,9},{9,8},{10,11... | collective-permute-start | bytes 49928 | tf_op jit(solution)/shard_map/ppermute | solution.py:19
  47.0 2.2 %collective-permute-start.13 = (bf16[8,4,128]{0,1,2:T(4,128)(2,1)S(1)}, bf16[8,4,128]{0,1,2:T(4,128)(2,1)S(1)}, u32[]{:S(2)}, u32[]{:S(2)}) collective-permute-start(bf16[8,4,128]{0,1,2:T(4,128)(2,1)S(1)} %fusion.28), channel_id=1, source_target_pairs={{0,1},{1,0},{2,3},{3,2},{4,5},{5,4},{6,7},{7,6},{8,9},{9,8},{10,11... | collective-permute-start | bytes 24584 | tf_op jit(solution)/shard_map/ppermute | solution.py:105
  47.5 5.0 %collective-permute-start.14 = (bf16[8,4,128]{0,1,2:T(4,128)(2,1)S(1)}, bf16[8,4,128]{0,1,2:T(4,128)(2,1)S(1)}, u32[]{:S(2)}, u32[]{:S(2)}) collective-permute-start(bf16[8,4,128]{0,1,2:T(4,128)(2,1)S(1)} %fusion.28), channel_id=1, source_target_pairs={{0,2},{1,3},{2,0},{3,1},{4,6},{5,7},{6,4},{7,5},{8,10},{9,11},{10,... | collective-permute-start | bytes 24584 | tf_op jit(solution)/shard_map/ppermute | solution.py:105
  48.5 7.0 %collective-permute-start.15 = (bf16[8,4,128]{0,1,2:T(4,128)(2,1)S(1)}, bf16[8,4,128]{0,1,2:T(4,128)(2,1)S(1)}, u32[]{:S(2)}, u32[]{:S(2)}) collective-permute-start(bf16[8,4,128]{0,1,2:T(4,128)(2,1)S(1)} %fusion.28), channel_id=1, source_target_pairs={{0,3},{1,2},{2,1},{3,0},{4,7},{5,6},{6,5},{7,4},{8,11},{9,10},{10,... | collective-permute-start | bytes 24584 | tf_op jit(solution)/shard_map/ppermute | solution.py:105
  56.4 3.7 %collective-permute-start.16 = (bf16[4,8,128]{2,1,0:T(8,128)(2,1)S(1)}, bf16[4,8,128]{2,1,0:T(8,128)(2,1)S(1)}, u32[]{:S(2)}, u32[]{:S(2)}) collective-permute-start(bf16[4,8,128]{2,1,0:T(8,128)(2,1)S(1)} %get-tuple-element.29), channel_id=1, source_target_pairs={{0,4},{1,5},{2,6},{3,7},{4,0},{5,1},{6,2},{7,3},{8,12},{9,13},{10,... | collective-permute-start | bytes 24584 | tf_op jit(solution)/shard_map/ppermute | solution.py:101
  56.5 3.6 %collective-permute-start.17 = (bf16[4,8,128]{2,1,0:T(8,128)(2,1)S(1)}, bf16[4,8,128]{2,1,0:T(8,128)(2,1)S(1)}, u32[]{:S(2)}, u32[]{:S(2)}) collective-permute-start(bf16[4,8,128]{2,1,0:T(8,128)(2,1)S(1)} %get-tuple-element.28), channel_id=1, source_target_pairs={{0,8},{1,9},{2,10},{3,11},{4,12},{5,13},{6,14},{7,15},{8,0},{9,1},... | collective-permute-start | bytes 24584 | tf_op jit(solution)/shard_map/ppermute | solution.py:101
  58.7 4.3 %collective-permute-start.18 = (bf16[4,8,128]{2,1,0:T(8,128)(2,1)S(1)}, bf16[4,8,128]{2,1,0:T(8,128)(2,1)S(1)}, u32[]{:S(2)}, u32[]{:S(2)}) collective-permute-start(bf16[4,8,128]{2,1,0:T(8,128)(2,1)S(1)} %get-tuple-element.27), channel_id=1, source_target_pairs={{0,12},{1,13},{2,14},{3,15},{4,8},{5,9},{6,10},{7,11},{8,4},{9,5},... | collective-permute-start | bytes 24584 | tf_op jit(solution)/shard_map/ppermute | solution.py:101
  69.1 8.6 %collective-permute-start.19 = (f32[8,512]{1,0:T(8,128)S(1)}, f32[8,512]{1,0:T(8,128)S(1)}, u32[]{:S(2)}, u32[]{:S(2)}) collective-permute-start(f32[8,512]{1,0:T(8,128)S(1)} %get-tuple-element.21), channel_id=1, source_target_pairs={{0,0},{1,4},{2,8},{3,12},{4,1},{5,5},{6,9},{7,13},{8,2},{9,6},{10,... | collective-permute-start | bytes 49160 | tf_op jit(solution)/shard_map/ppermute | solution.py:269
  71.1 6.7 %collective-permute-start.20 = (f32[8,512]{1,0:T(8,128)S(1)}, f32[8,512]{1,0:T(8,128)S(1)}, u32[]{:S(2)}, u32[]{:S(2)}) collective-permute-start(f32[8,512]{1,0:T(8,128)S(1)} %get-tuple-element.18), channel_id=1, source_target_pairs={{0,1},{1,5},{2,9},{3,13},{4,0},{5,4},{6,8},{7,12},{8,3},{9,7},{10,... | collective-permute-start | bytes 49160 | tf_op jit(solution)/shard_map/ppermute | solution.py:269
  71.1 7.6 %collective-permute-start.21 = (f32[8,512]{1,0:T(8,128)S(1)}, f32[8,512]{1,0:T(8,128)S(1)}, u32[]{:S(2)}, u32[]{:S(2)}) collective-permute-start(f32[8,512]{1,0:T(8,128)S(1)} %get-tuple-element.20), channel_id=1, source_target_pairs={{0,2},{1,6},{2,10},{3,14},{4,3},{5,7},{6,11},{7,15},{8,0},{9,4},{1... | collective-permute-start | bytes 49160 | tf_op jit(solution)/shard_map/ppermute | solution.py:269
  77.7 4.1 %collective-permute-start.22 = (f32[8,512]{1,0:T(8,128)S(1)}, f32[8,512]{1,0:T(8,128)S(1)}, u32[]{:S(2)}, u32[]{:S(2)}) collective-permute-start(f32[8,512]{1,0:T(8,128)S(1)} %get-tuple-element.19), channel_id=1, source_target_pairs={{0,3},{1,7},{2,11},{3,15},{4,2},{5,6},{6,10},{7,14},{8,1},{9,5},{1... | collective-permute-start | bytes 49160 | tf_op jit(solution)/shard_map/ppermute | solution.py:269
  (1 other events, 10.0 us)

commit v15 on v6

--- a/solution.py
+++ b/solution.py
@@ -226,9 +226,11 @@
     give_top = jnp.where(first_half, top_split[:, 1], top_split[:, 0])
     give_total = jnp.where(first_half, total_split[:, 1], total_split[:, 0])
     give_summed = jnp.where(first_half, summed_split[:, 1], summed_split[:, 0])
-    give = jnp.concatenate([give_summed, give_top[..., None], give_total[..., None]], -1)
-    got = from_partner(give, "tp", 0)
-    got_summed, got_top, got_total = got[..., :HD], got[..., HD], got[..., HD + 1]
+    stats = jnp.concatenate([give_top, give_total], -1)
+    stats = jnp.pad(stats, ((0, 0), (0, HD - stats.shape[-1])))[:, None, :]
+    got = from_partner(jnp.concatenate([give_summed, stats], 1), "tp", 0)
+    got_summed = got[:, :GR]
+    got_top, got_total = got[:, GR, :GR], got[:, GR, GR : 2 * GR]
     joint = jnp.maximum(own_top, got_top)
     factor_own = jnp.exp(own_top - joint)
     factor_got = jnp.exp(got_top - joint)

time: 78.1 us -> 74.6 us (0.955)
  the two profiles are of different devices: /device:TPU:1 before, /device:TPU:3 now
where the time goes in v15:
time: 74.6 us; the launch traced here: 74.3 us
  starting transfers between devices  30.5 us (41%)
  matrix products  18.4 us (25%)
  waiting for transfers between devices  16.2 us (22%)
  other arithmetic  5.33 us (7%)
  local copies, waits for them, and re-layouts  3.29 us (4%)
    ppermute x9, starting transfers between devices, swap_rows(): lax.ppermute(value, axis, [(t, t ^ shift) for t in range(lax.axis_size(ax...  11 us
    ppermute x4, starting transfers between devices, local(): got = lax.ppermute(piece, 'tp', pairs)  8.8 us
    ppermute x9, starting transfers between devices, swap_cols(): lax.ppermute(value, axis, [(t, t ^ s) for t in range(lax.axis_size(axis))])  8.3 us
    ppermute x9, waiting for transfers between devices, swap_rows(): lax.ppermute(value, axis, [(t, t ^ shift) for t in range(lax.axis_size(ax...  6.81 us
    dot_general x1, matrix products, local(): jnp.einsum('rc,aec->rae', col_rows, q_blocks[0], preferred_element_type=j...  5.65 us
    dot_general x1, matrix products, local(): jnp.einsum('gabe,cae->gbc', chosen, o_blocks[0], preferred_element_type=j...  5.65 us
    ppermute x9, waiting for transfers between devices, swap_cols(): lax.ppermute(value, axis, [(t, t ^ s) for t in range(lax.axis_size(axis))])  4.6 us
    ppermute x4, waiting for transfers between devices, local(): got = lax.ppermute(piece, 'tp', pairs)  3.98 us
  transfers between devices with their start and end apart: 23, of which 13 were waited for; matrix products, arithmetic and copies ran while one was open for 5% of the time, Pallas kernels for 0%

profile of v15, /device:TPU:3, one launch (start us, length us, event | category | flops | bytes accessed | tf_op | source)
XLA Modules:
  0.0 74.3 jit_solution(14928682105352944803)
XLA Ops:
  0.0 2.0 %collective-permute-start.1 = (bf16[8,512]{1,0:T(8,128)(2,1)}, bf16[8,512]{1,0:T(8,128)(2,1)S(1)}, u32[]{:S(2)}, u32[]{:S(2)}) collective-permute-start(bf16[8,512]{1,0:T(8,128)(2,1)} %bitcast.200), channel_id=1, source_target_pairs={{0,2},{1,3},{2,0},{3,1},{4,6},{5,7},{6,4},{7,5},{8,10},{9,11},{10,... | collective-permute-start | bytes 24584 | tf_op jit(solution)/shard_map/ppermute | solution.py:105
  3.1 1.3 %gather_fusion.1 = s32[16]{0:T(128)S(1)} fusion(s32[16]{0:T(128)} %param.14, s32[1024]{0:T(1024)S(1)} %pad_clamp_fusion), kind=kCustom, calls=%fused_computation.1 | custom fusion | bytes 192 | tf_op jit(solution)/shard_map/gather | solution.py:128
  6.2 3.4 %collective-permute-start.5 = (bf16[4,8,512]{2,1,0:T(8,128)(2,1)S(1)}, bf16[4,8,512]{2,1,0:T(8,128)(2,1)S(1)}, u32[]{:S(2)}, u32[]{:S(2)}) collective-permute-start(bf16[4,8,512]{2,1,0:T(8,128)(2,1)S(1)} %select_reduce_fusion.7), channel_id=1, source_target_pairs={{0,12},{1,13},{2,14},{3,15},{4,8},{5,9},{6,10},{7,11},{8,4},{9,5},... | collective-permute-start | bytes 98312 | tf_op jit(solution)/shard_map/ppermute | solution.py:101
  10.0 0.9 %collective-permute-done.5 = bf16[4,8,512]{2,1,0:T(8,128)(2,1)S(1)} collective-permute-done((bf16[4,8,512]{2,1,0:T(8,128)(2,1)S(1)}, bf16[4,8,512]{2,1,0:T(8,128)(2,1)S(1)}, u32[]{:S(2)}, u32[]{:S(2)}) %collective-permute-start.5) | collective-permute-done | bytes 32800 | tf_op jit(solution)/shard_map/ppermute | solution.py:101
  10.9 2.7 %collective-permute-done.4 = bf16[4,8,512]{2,1,0:T(8,128)(2,1)S(1)} collective-permute-done((bf16[4,8,512]{2,1,0:T(8,128)(2,1)S(1)}, bf16[4,8,512]{2,1,0:T(8,128)(2,1)S(1)}, u32[]{:S(2)}, u32[]{:S(2)}) %collective-permute-start.4) | collective-permute-done | bytes 32800 | tf_op jit(solution)/shard_map/ppermute | solution.py:101
  15.6 5.7 %fusion.14 = f32[16,8,128]{2,1,0:T(8,128)S(1)} fusion(bf16[1,16,128,2048]{3,2,1,0:T(8,128)(2,1)} %param.11, bf16[8,8192]{1,0:T(8,128)(2,1)S(1)} %multiply_convert_fusion, s32[]{:T(128)S(6)} %select_n.267), kind=kOutput, calls=%fused_computation.12 | convolution fusion | flops 67108864 | bytes 8486916 | tf_op jit(solution)/shard_map/rc,aec->rae/dot_general | solution.py:152
  22.2 1.5 %collective-permute-start.6 = (f32[4,8,512]{2,1,0:T(8,128)S(1)}, f32[4,8,512]{2,1,0:T(8,128)S(1)}, u32[]{:S(2)}, u32[]{:S(2)}) collective-permute-start(f32[4,8,512]{2,1,0:T(8,128)S(1)} %get-tuple-element.14), channel_id=1, source_target_pairs={{0,1},{1,0},{2,3},{3,2},{4,5},{5,4},{6,7},{7,6},{8,9},{9,8},{10,11... | collective-permute-start | bytes 196616 | tf_op jit(solution)/shard_map/ppermute | solution.py:105
  24.0 1.2 %collective-permute-start.7 = (f32[4,8,512]{2,1,0:T(8,128)S(1)}, f32[4,8,512]{2,1,0:T(8,128)S(1)}, u32[]{:S(2)}, u32[]{:S(2)}) collective-permute-start(f32[4,8,512]{2,1,0:T(8,128)S(1)} %get-tuple-element.16), channel_id=1, source_target_pairs={{0,2},{1,3},{2,0},{3,1},{4,6},{5,7},{6,4},{7,5},{8,10},{9,11},{10,... | collective-permute-start | bytes 196616 | tf_op jit(solution)/shard_map/ppermute | solution.py:105
  25.3 2.8 %collective-permute-done.8 = f32[4,8,512]{2,1,0:T(8,128)S(1)} collective-permute-done((f32[4,8,512]{2,1,0:T(8,128)S(1)}, f32[4,8,512]{2,1,0:T(8,128)S(1)}, u32[]{:S(2)}, u32[]{:S(2)}) %collective-permute-start.8) | collective-permute-done | bytes 65568 | tf_op jit(solution)/shard_map/ppermute | solution.py:105
  28.7 1.2 %collective-permute-start.11 = (f32[8,512]{1,0:T(8,128)S(1)}, f32[8,512]{1,0:T(8,128)S(1)}, u32[]{:S(2)}, u32[]{:S(2)}) collective-permute-start(f32[8,512]{1,0:T(8,128)S(1)} %get-tuple-element.22), channel_id=1, source_target_pairs={{0,12},{1,13},{2,14},{3,15},{4,8},{5,9},{6,10},{7,11},{8,4},{9,5},... | collective-permute-start | bytes 49160 | tf_op jit(solution)/shard_map/ppermute | solution.py:101
  30.6 1.7 %collective-permute-start.9 = (f32[8,512]{1,0:T(8,128)S(1)}, f32[8,512]{1,0:T(8,128)S(1)}, u32[]{:S(2)}, u32[]{:S(2)}) collective-permute-start(f32[8,512]{1,0:T(8,128)S(1)} %get-tuple-element.24), channel_id=1, source_target_pairs={{0,4},{1,5},{2,6},{3,7},{4,0},{5,1},{6,2},{7,3},{8,12},{9,13},{10,... | collective-permute-start | bytes 49160 | tf_op jit(solution)/shard_map/ppermute | solution.py:101
  33.9 3.5 %select_reduce_fusion.4 = (f32[8,8]{1,0:T(8,128)S(1)}, f32[8,8,2048]{2,1,0:T(8,128)S(1)}) fusion(pred[8,2048]{1,0:T(8,128)(4,1)S(1)} %iota_compare_fusion.1, bf16[8,8,128]{2,1,0:T(8,128)(2,1)S(1)} %bitcast.186, bf16[1,8,2048,128]{3,2,1,0:T(8,128)(2,1)} %param.15), kind=kOutput, calls=%fused_computation.20 | convolution fusion | flops 33947584 | bytes 4751616 | tf_op jit(solution)/shard_map/bhe,bte->bht/dot_general | solution.py:198
  37.8 2.9 %fusion.17 = f32[8,8,128]{2,1,0:T(8,128)S(1)} fusion(bf16[1,8,2048,128]{3,2,1,0:T(8,128)(2,1)} %param.16, f32[8,8,2048]{2,1,0:T(8,128)S(1)} %get-tuple-element.47, f32[8,8]{1,0:T(8,128)S(1)} %fusion.43, pred[8,2048]{1,0:T(8,128)(4,1)S(1)} %iota_compare_fusion.1, f32[8,128]{1,0:T(8,128)S(1)} %get-tuple-element.43, f32[8,8]{1,0:T(8,128)S(1)} %convert_element_type.72), kind=kOutput, calls=%fused_computation.14 | convolution fusion | flops 33964032 | bytes 4772352 | tf_op jit(solution)/shard_map/bht,bte->bhe/dot_general | solution.py:211
  40.8 2.5 %collective-permute-start.12 = (f32[8,5,128]{2,0,1:T(8,128)S(1)}, f32[8,5,128]{2,0,1:T(8,128)S(1)}, u32[]{:S(2)}, u32[]{:S(2)}) collective-permute-start(f32[8,5,128]{2,0,1:T(8,128)S(1)} %pad_maximum_fusion.4), channel_id=1, source_target_pairs={{0,1},{1,0},{2,3},{3,2},{4,5},{5,4},{6,7},{7,6},{8,9},{9,8},{10,11... | collective-permute-start | bytes 61448 | tf_op jit(solution)/shard_map/ppermute | solution.py:19
  44.5 2.2 %collective-permute-start.15 = (bf16[8,128]{1,0:T(8,128)(2,1)S(1)}, bf16[8,128]{1,0:T(8,128)(2,1)S(1)}, u32[]{:S(2)}, u32[]{:S(2)}) collective-permute-start(bf16[8,128]{1,0:T(8,128)(2,1)S(1)} %get-tuple-element.38), channel_id=1, source_target_pairs={{0,12},{1,13},{2,14},{3,15},{4,8},{5,9},{6,10},{7,11},{8,4},{9,5},... | collective-permute-start | bytes 6152 | tf_op jit(solution)/shard_map/ppermute | solution.py:101
  48.8 1.2 %collective-permute-done.14 = bf16[8,128]{1,0:T(8,128)(2,1)S(1)} collective-permute-done((bf16[8,128]{1,0:T(8,128)(2,1)S(1)}, bf16[8,128]{1,0:T(8,128)(2,1)S(1)}, u32[]{:S(2)}, u32[]{:S(2)}) %collective-permute-start.14) | collective-permute-done | bytes 2080 | tf_op jit(solution)/shard_map/ppermute | solution.py:101
  50.2 2.0 %collective-permute-start.18 = (bf16[4,8,128]{2,1,0:T(8,128)(2,1)S(1)}, bf16[4,8,128]{2,1,0:T(8,128)(2,1)S(1)}, u32[]{:S(2)}, u32[]{:S(2)}) collective-permute-start(bf16[4,8,128]{2,1,0:T(8,128)(2,1)S(1)} %select_reduce_fusion.10), channel_id=1, source_target_pairs={{0,3},{1,2},{2,1},{3,0},{4,7},{5,6},{6,5},{7,4},{8,11},{9,10},{10,... | collective-permute-start | bytes 24584 | tf_op jit(solution)/shard_map/ppermute | solution.py:105
  52.2 1.2 %collective-permute-start.17 = (bf16[4,8,128]{2,1,0:T(8,128)(2,1)S(1)}, bf16[4,8,128]{2,1,0:T(8,128)(2,1)S(1)}, u32[]{:S(2)}, u32[]{:S(2)}) collective-permute-start(bf16[4,8,128]{2,1,0:T(8,128)(2,1)S(1)} %select_reduce_fusion.10), channel_id=1, source_target_pairs={{0,2},{1,3},{2,0},{3,1},{4,6},{5,7},{6,4},{7,5},{8,10},{9,11},{10,... | collective-permute-start | bytes 24584 | tf_op jit(solution)/shard_map/ppermute | solution.py:105
  53.5 1.2 %collective-permute-done.17 = bf16[4,8,128]{2,1,0:T(8,128)(2,1)S(1)} collective-permute-done((bf16[4,8,128]{2,1,0:T(8,128)(2,1)S(1)}, bf16[4,8,128]{2,1,0:T(8,128)(2,1)S(1)}, u32[]{:S(2)}, u32[]{:S(2)}) %collective-permute-start.17) | collective-permute-done | bytes 8224 | tf_op jit(solution)/shard_map/ppermute | solution.py:105
  55.2 5.6 %fusion.11 = f32[8,4,512]{2,0,1:T(8,128)S(1)} fusion(bf16[4,512,16,128]{3,2,1,0:T(8,128)(2,1)} %bitcast.176, bf16[16,8,128]{2,1,0:T(8,128)(2,1)S(1)} %select_reduce_fusion.3), kind=kOutput, calls=%fused_computation.11 | convolution fusion | flops 67108864 | bytes 8486912 | tf_op jit(solution)/shard_map/gabe,cae->gbc/dot_general | solution.py:259
  60.8 2.1 %collective-permute-start.20 = (f32[8,512]{1,0:T(8,128)S(1)}, f32[8,512]{1,0:T(8,128)S(1)}, u32[]{:S(2)}, u32[]{:S(2)}) collective-permute-start(f32[8,512]{1,0:T(8,128)S(1)} %get-tuple-element.17), channel_id=1, source_target_pairs={{0,1},{1,5},{2,9},{3,13},{4,0},{5,4},{6,8},{7,12},{8,3},{9,7},{10,... | collective-permute-start | bytes 49160 | tf_op jit(solution)/shard_map/ppermute | solution.py:266
  63.1 2.8 %collective-permute-start.21 = (f32[8,512]{1,0:T(8,128)S(1)}, f32[8,512]{1,0:T(8,128)S(1)}, u32[]{:S(2)}, u32[]{:S(2)}) collective-permute-start(f32[8,512]{1,0:T(8,128)S(1)} %get-tuple-element.19), channel_id=1, source_target_pairs={{0,2},{1,6},{2,10},{3,14},{4,3},{5,7},{6,11},{7,15},{8,0},{9,4},{1... | collective-permute-start | bytes 49160 | tf_op jit(solution)/shard_map/ppermute | solution.py:266
  65.9 3.7 %collective-permute-start.19 = (f32[8,512]{1,0:T(8,128)S(1)}, f32[8,512]{1,0:T(8,128)S(1)}, u32[]{:S(2)}, u32[]{:S(2)}) collective-permute-start(f32[8,512]{1,0:T(8,128)S(1)} %get-tuple-element.20), channel_id=1, source_target_pairs={{0,0},{1,4},{2,8},{3,12},{4,1},{5,5},{6,9},{7,13},{8,2},{9,6},{10,... | collective-permute-start | bytes 49160 | tf_op jit(solution)/shard_map/ppermute | solution.py:266
  69.7 4.0 %collective-permute-done.19 = f32[8,512]{1,0:T(8,128)S(1)} collective-permute-done((f32[8,512]{1,0:T(8,128)S(1)}, f32[8,512]{1,0:T(8,128)S(1)}, u32[]{:S(2)}, u32[]{:S(2)}) %collective-permute-start.19) | collective-permute-done | bytes 16416 | tf_op jit(solution)/shard_map/ppermute | solution.py:266
  (103 shorter events, 14.5 us)
Async XLA Ops:
  0.0 14.9 %copy-start = (bf16[2,1024,512]{2,1,0:T(8,128)(2,1)S(1)}, bf16[2,1024,512]{2,1,0:T(8,128)(2,1)}, u32[]{:S(2)}) copy-start(bf16[2,1024,512]{2,1,0:T(8,128)(2,1)} %param.13) | copy-start | bytes 6291460
  0.0 5.4 %collective-permute-start.2 = (bf16[8,512]{1,0:T(8,128)(2,1)}, bf16[8,512]{1,0:T(8,128)(2,1)S(1)}, u32[]{:S(2)}, u32[]{:S(2)}) collective-permute-start(bf16[8,512]{1,0:T(8,128)(2,1)} %bitcast.199), channel_id=1, source_target_pairs={{0,3},{1,2},{2,1},{3,0},{4,7},{5,6},{6,5},{7,4},{8,11},{9,10},{10,... | collective-permute-start | bytes 24584 | tf_op jit(solution)/shard_map/ppermute | solution.py:105
  0.0 5.4 %collective-permute-start.1 = (bf16[8,512]{1,0:T(8,128)(2,1)}, bf16[8,512]{1,0:T(8,128)(2,1)S(1)}, u32[]{:S(2)}, u32[]{:S(2)}) collective-permute-start(bf16[8,512]{1,0:T(8,128)(2,1)} %bitcast.200), channel_id=1, source_target_pairs={{0,2},{1,3},{2,0},{3,1},{4,6},{5,7},{6,4},{7,5},{8,10},{9,11},{10,... | collective-permute-start | bytes 24584 | tf_op jit(solution)/shard_map/ppermute | solution.py:105
  2.0 3.4 %collective-permute-start = (bf16[8,512]{1,0:T(8,128)(2,1)}, bf16[8,512]{1,0:T(8,128)(2,1)S(1)}, u32[]{:S(2)}, u32[]{:S(2)}) collective-permute-start(bf16[8,512]{1,0:T(8,128)(2,1)} %bitcast.201), channel_id=1, source_target_pairs={{0,1},{1,0},{2,3},{3,2},{4,5},{5,4},{6,7},{7,6},{8,9},{9,8},{10,11... | collective-permute-start | bytes 24584 | tf_op jit(solution)/shard_map/ppermute | solution.py:105
  6.2 4.7 %collective-permute-start.5 = (bf16[4,8,512]{2,1,0:T(8,128)(2,1)S(1)}, bf16[4,8,512]{2,1,0:T(8,128)(2,1)S(1)}, u32[]{:S(2)}, u32[]{:S(2)}) collective-permute-start(bf16[4,8,512]{2,1,0:T(8,128)(2,1)S(1)} %select_reduce_fusion.7), channel_id=1, source_target_pairs={{0,12},{1,13},{2,14},{3,15},{4,8},{5,9},{6,10},{7,11},{8,4},{9,5},... | collective-permute-start | bytes 98312 | tf_op jit(solution)/shard_map/ppermute | solution.py:101
  9.6 4.0 %collective-permute-start.4 = (bf16[4,8,512]{2,1,0:T(8,128)(2,1)S(1)}, bf16[4,8,512]{2,1,0:T(8,128)(2,1)S(1)}, u32[]{:S(2)}, u32[]{:S(2)}) collective-permute-start(bf16[4,8,512]{2,1,0:T(8,128)(2,1)S(1)} %select_reduce_fusion.7), channel_id=1, source_target_pairs={{0,8},{1,9},{2,10},{3,11},{4,12},{5,13},{6,14},{7,15},{8,0},{9,1},... | collective-permute-start | bytes 98312 | tf_op jit(solution)/shard_map/ppermute | solution.py:101
  9.6 4.0 %collective-permute-start.3 = (bf16[4,8,512]{2,1,0:T(8,128)(2,1)S(1)}, bf16[4,8,512]{2,1,0:T(8,128)(2,1)S(1)}, u32[]{:S(2)}, u32[]{:S(2)}) collective-permute-start(bf16[4,8,512]{2,1,0:T(8,128)(2,1)S(1)} %select_reduce_fusion.7), channel_id=1, source_target_pairs={{0,4},{1,5},{2,6},{3,7},{4,0},{5,1},{6,2},{7,3},{8,12},{9,13},{10,... | collective-permute-start | bytes 98312 | tf_op jit(solution)/shard_map/ppermute | solution.py:101
  22.2 3.1 %collective-permute-start.6 = (f32[4,8,512]{2,1,0:T(8,128)S(1)}, f32[4,8,512]{2,1,0:T(8,128)S(1)}, u32[]{:S(2)}, u32[]{:S(2)}) collective-permute-start(f32[4,8,512]{2,1,0:T(8,128)S(1)} %get-tuple-element.14), channel_id=1, source_target_pairs={{0,1},{1,0},{2,3},{3,2},{4,5},{5,4},{6,7},{7,6},{8,9},{9,8},{10,11... | collective-permute-start | bytes 196616 | tf_op jit(solution)/shard_map/ppermute | solution.py:105
  23.7 4.3 %collective-permute-start.8 = (f32[4,8,512]{2,1,0:T(8,128)S(1)}, f32[4,8,512]{2,1,0:T(8,128)S(1)}, u32[]{:S(2)}, u32[]{:S(2)}) collective-permute-start(f32[4,8,512]{2,1,0:T(8,128)S(1)} %get-tuple-element.15), channel_id=1, source_target_pairs={{0,3},{1,2},{2,1},{3,0},{4,7},{5,6},{6,5},{7,4},{8,11},{9,10},{10,... | collective-permute-start | bytes 196616 | tf_op jit(solution)/shard_map/ppermute | solution.py:105
  24.0 4.7 %collective-permute-start.7 = (f32[4,8,512]{2,1,0:T(8,128)S(1)}, f32[4,8,512]{2,1,0:T(8,128)S(1)}, u32[]{:S(2)}, u32[]{:S(2)}) collective-permute-start(f32[4,8,512]{2,1,0:T(8,128)S(1)} %get-tuple-element.16), channel_id=1, source_target_pairs={{0,2},{1,3},{2,0},{3,1},{4,6},{5,7},{6,4},{7,5},{8,10},{9,11},{10,... | collective-permute-start | bytes 196616 | tf_op jit(solution)/shard_map/ppermute | solution.py:105
  28.7 4.5 %collective-permute-start.11 = (f32[8,512]{1,0:T(8,128)S(1)}, f32[8,512]{1,0:T(8,128)S(1)}, u32[]{:S(2)}, u32[]{:S(2)}) collective-permute-start(f32[8,512]{1,0:T(8,128)S(1)} %get-tuple-element.22), channel_id=1, source_target_pairs={{0,12},{1,13},{2,14},{3,15},{4,8},{5,9},{6,10},{7,11},{8,4},{9,5},... | collective-permute-start | bytes 49160 | tf_op jit(solution)/shard_map/ppermute | solution.py:101
  29.9 3.5 %collective-permute-start.10 = (f32[8,512]{1,0:T(8,128)S(1)}, f32[8,512]{1,0:T(8,128)S(1)}, u32[]{:S(2)}, u32[]{:S(2)}) collective-permute-start(f32[8,512]{1,0:T(8,128)S(1)} %get-tuple-element.23), channel_id=1, source_target_pairs={{0,8},{1,9},{2,10},{3,11},{4,12},{5,13},{6,14},{7,15},{8,0},{9,1},... | collective-permute-start | bytes 49160 | tf_op jit(solution)/shard_map/ppermute | solution.py:101
  30.6 3.0 %collective-permute-start.9 = (f32[8,512]{1,0:T(8,128)S(1)}, f32[8,512]{1,0:T(8,128)S(1)}, u32[]{:S(2)}, u32[]{:S(2)}) collective-permute-start(f32[8,512]{1,0:T(8,128)S(1)} %get-tuple-element.24), channel_id=1, source_target_pairs={{0,4},{1,5},{2,6},{3,7},{4,0},{5,1},{6,2},{7,3},{8,12},{9,13},{10,... | collective-permute-start | bytes 49160 | tf_op jit(solution)/shard_map/ppermute | solution.py:101
  40.8 3.3 %collective-permute-start.12 = (f32[8,5,128]{2,0,1:T(8,128)S(1)}, f32[8,5,128]{2,0,1:T(8,128)S(1)}, u32[]{:S(2)}, u32[]{:S(2)}) collective-permute-start(f32[8,5,128]{2,0,1:T(8,128)S(1)} %pad_maximum_fusion.4), channel_id=1, source_target_pairs={{0,1},{1,0},{2,3},{3,2},{4,5},{5,4},{6,7},{7,6},{8,9},{9,8},{10,11... | collective-permute-start | bytes 61448 | tf_op jit(solution)/shard_map/ppermute | solution.py:19
  44.5 4.3 %collective-permute-start.15 = (bf16[8,128]{1,0:T(8,128)(2,1)S(1)}, bf16[8,128]{1,0:T(8,128)(2,1)S(1)}, u32[]{:S(2)}, u32[]{:S(2)}) collective-permute-start(bf16[8,128]{1,0:T(8,128)(2,1)S(1)} %get-tuple-element.38), channel_id=1, source_target_pairs={{0,12},{1,13},{2,14},{3,15},{4,8},{5,9},{6,10},{7,11},{8,4},{9,5},... | collective-permute-start | bytes 6152 | tf_op jit(solution)/shard_map/ppermute | solution.py:101
  46.7 3.3 %collective-permute-start.14 = (bf16[8,128]{1,0:T(8,128)(2,1)S(1)}, bf16[8,128]{1,0:T(8,128)(2,1)S(1)}, u32[]{:S(2)}, u32[]{:S(2)}) collective-permute-start(bf16[8,128]{1,0:T(8,128)(2,1)S(1)} %get-tuple-element.39), channel_id=1, source_target_pairs={{0,8},{1,9},{2,10},{3,11},{4,12},{5,13},{6,14},{7,15},{8,0},{9,1},... | collective-permute-start | bytes 6152 | tf_op jit(solution)/shard_map/ppermute | solution.py:101
  47.3 2.7 %collective-permute-start.13 = (bf16[8,128]{1,0:T(8,128)(2,1)S(1)}, bf16[8,128]{1,0:T(8,128)(2,1)S(1)}, u32[]{:S(2)}, u32[]{:S(2)}) collective-permute-start(bf16[8,128]{1,0:T(8,128)(2,1)S(1)} %get-tuple-element.40), channel_id=1, source_target_pairs={{0,4},{1,5},{2,6},{3,7},{4,0},{5,1},{6,2},{7,3},{8,12},{9,13},{10,... | collective-permute-start | bytes 6152 | tf_op jit(solution)/shard_map/ppermute | solution.py:101
  50.2 3.3 %collective-permute-start.18 = (bf16[4,8,128]{2,1,0:T(8,128)(2,1)S(1)}, bf16[4,8,128]{2,1,0:T(8,128)(2,1)S(1)}, u32[]{:S(2)}, u32[]{:S(2)}) collective-permute-start(bf16[4,8,128]{2,1,0:T(8,128)(2,1)S(1)} %select_reduce_fusion.10), channel_id=1, source_target_pairs={{0,3},{1,2},{2,1},{3,0},{4,7},{5,6},{6,5},{7,4},{8,11},{9,10},{10,... | collective-permute-start | bytes 24584 | tf_op jit(solution)/shard_map/ppermute | solution.py:105
  52.2 2.5 %collective-permute-start.17 = (bf16[4,8,128]{2,1,0:T(8,128)(2,1)S(1)}, bf16[4,8,128]{2,1,0:T(8,128)(2,1)S(1)}, u32[]{:S(2)}, u32[]{:S(2)}) collective-permute-start(bf16[4,8,128]{2,1,0:T(8,128)(2,1)S(1)} %select_reduce_fusion.10), channel_id=1, source_target_pairs={{0,2},{1,3},{2,0},{3,1},{4,6},{5,7},{6,4},{7,5},{8,10},{9,11},{10,... | collective-permute-start | bytes 24584 | tf_op jit(solution)/shard_map/ppermute | solution.py:105
  53.4 1.3 %collective-permute-start.16 = (bf16[4,8,128]{2,1,0:T(8,128)(2,1)S(1)}, bf16[4,8,128]{2,1,0:T(8,128)(2,1)S(1)}, u32[]{:S(2)}, u32[]{:S(2)}) collective-permute-start(bf16[4,8,128]{2,1,0:T(8,128)(2,1)S(1)} %select_reduce_fusion.10), channel_id=1, source_target_pairs={{0,1},{1,0},{2,3},{3,2},{4,5},{5,4},{6,7},{7,6},{8,9},{9,8},{10,11... | collective-permute-start | bytes 24584 | tf_op jit(solution)/shard_map/ppermute | solution.py:105
  60.8 8.8 %collective-permute-start.20 = (f32[8,512]{1,0:T(8,128)S(1)}, f32[8,512]{1,0:T(8,128)S(1)}, u32[]{:S(2)}, u32[]{:S(2)}) collective-permute-start(f32[8,512]{1,0:T(8,128)S(1)} %get-tuple-element.17), channel_id=1, source_target_pairs={{0,1},{1,5},{2,9},{3,13},{4,0},{5,4},{6,8},{7,12},{8,3},{9,7},{10,... | collective-permute-start | bytes 49160 | tf_op jit(solution)/shard_map/ppermute | solution.py:266
  63.0 6.7 %collective-permute-start.22 = (f32[8,512]{1,0:T(8,128)S(1)}, f32[8,512]{1,0:T(8,128)S(1)}, u32[]{:S(2)}, u32[]{:S(2)}) collective-permute-start(f32[8,512]{1,0:T(8,128)S(1)} %get-tuple-element.18), channel_id=1, source_target_pairs={{0,3},{1,7},{2,11},{3,15},{4,2},{5,6},{6,10},{7,14},{8,1},{9,5},{1... | collective-permute-start | bytes 49160 | tf_op jit(solution)/shard_map/ppermute | solution.py:266
  63.1 6.6 %collective-permute-start.21 = (f32[8,512]{1,0:T(8,128)S(1)}, f32[8,512]{1,0:T(8,128)S(1)}, u32[]{:S(2)}, u32[]{:S(2)}) collective-permute-start(f32[8,512]{1,0:T(8,128)S(1)} %get-tuple-element.19), channel_id=1, source_target_pairs={{0,2},{1,6},{2,10},{3,14},{4,3},{5,7},{6,11},{7,15},{8,0},{9,4},{1... | collective-permute-start | bytes 49160 | tf_op jit(solution)/shard_map/ppermute | solution.py:266
  65.9 7.7 %collective-permute-start.19 = (f32[8,512]{1,0:T(8,128)S(1)}, f32[8,512]{1,0:T(8,128)S(1)}, u32[]{:S(2)}, u32[]{:S(2)}) collective-permute-start(f32[8,512]{1,0:T(8,128)S(1)} %get-tuple-element.20), channel_id=1, source_target_pairs={{0,0},{1,4},{2,8},{3,12},{4,1},{5,5},{6,9},{7,13},{8,2},{9,6},{10,... | collective-permute-start | bytes 49160 | tf_op jit(solution)/shard_map/ppermute | solution.py:266
  (1 other events, 9.6 us)

commit v16 on v8

--- a/solution.py
+++ b/solution.py
@@ -241,9 +241,11 @@
     give_top = jnp.where(first_half, top_split[:, 1], top_split[:, 0])
     give_total = jnp.where(first_half, total_split[:, 1], total_split[:, 0])
     give_summed = jnp.where(first_half, summed_split[:, 1], summed_split[:, 0])
-    give = jnp.concatenate([give_summed, give_top[..., None], give_total[..., None]], -1)
-    got = from_partner(give, "tp", 0)
-    got_summed, got_top, got_total = got[..., :HD], got[..., HD], got[..., HD + 1]
+    stats = jnp.concatenate([give_top, give_total], -1)
+    stats = jnp.pad(stats, ((0, 0), (0, HD - stats.shape[-1])))[:, None, :]
+    got = from_partner(jnp.concatenate([give_summed, stats], 1), "tp", 0)
+    got_summed = got[:, :GR]
+    got_top, got_total = got[:, GR, :GR], got[:, GR, GR : 2 * GR]
     joint = jnp.maximum(own_top, got_top)
     factor_own = jnp.exp(own_top - joint)
     factor_got = jnp.exp(got_top - joint)

time: 78.4 us -> 74.6 us (0.952)
  the two profiles are of different devices: /device:TPU:1 before, /device:TPU:3 now
where the time goes in v16:
time: 74.6 us; the launch traced here: 74.2 us
  starting transfers between devices  30.3 us (41%)
  matrix products  19.1 us (26%)
  waiting for transfers between devices  16.2 us (22%)
  other arithmetic  5.26 us (7%)
  local copies, waits for them, and re-layouts  3 us (4%)
    ppermute x9, starting transfers between devices, swap_rows(): lax.ppermute(value, axis, [(t, t ^ shift) for t in range(lax.axis_size(ax...  10.8 us
    ppermute x9, starting transfers between devices, swap_cols(): lax.ppermute(value, axis, [(t, t ^ s) for t in range(lax.axis_size(axis))])  9.42 us
    ppermute x4, starting transfers between devices, local(): got = lax.ppermute(piece, 'tp', pairs)  8.61 us
    ppermute x9, waiting for transfers between devices, swap_rows(): lax.ppermute(value, axis, [(t, t ^ shift) for t in range(lax.axis_size(ax...  6.4 us
    dot_general x1, matrix products, local(): jnp.einsum('gabe,cae->gbc', chosen, o_blocks[0], preferred_element_type=j...  5.65 us
    dot_general x1, matrix products, local(): jnp.einsum('rc,aec->rae', col_rows, q_blocks[0], preferred_element_type=j...  5.64 us
    ppermute x9, waiting for transfers between devices, swap_cols(): lax.ppermute(value, axis, [(t, t ^ s) for t in range(lax.axis_size(axis))])  4.82 us
    ppermute x4, waiting for transfers between devices, local(): got = lax.ppermute(piece, 'tp', pairs)  4.17 us
  transfers between devices with their start and end apart: 23, of which 12 were waited for; matrix products, arithmetic and copies ran while one was open for 6% of the time, Pallas kernels for 0%

profile of v16, /device:TPU:3, one launch (start us, length us, event | category | flops | bytes accessed | tf_op | source)
XLA Modules:
  0.0 74.2 jit_solution(5029988581829370536)
XLA Ops:
  0.0 2.0 %collective-permute-start.1 = (bf16[8,512]{1,0:T(8,128)(2,1)}, bf16[8,512]{1,0:T(8,128)(2,1)S(1)}, u32[]{:S(2)}, u32[]{:S(2)}) collective-permute-start(bf16[8,512]{1,0:T(8,128)(2,1)} %bitcast.205), channel_id=1, source_target_pairs={{0,2},{1,3},{2,0},{3,1},{4,6},{5,7},{6,4},{7,5},{8,10},{9,11},{10,... | collective-permute-start | bytes 24584 | tf_op jit(solution)/shard_map/ppermute | solution.py:105
  5.8 2.3 %collective-permute-start.4 = (bf16[4,8,512]{2,1,0:T(8,128)(2,1)S(1)}, bf16[4,8,512]{2,1,0:T(8,128)(2,1)S(1)}, u32[]{:S(2)}, u32[]{:S(2)}) collective-permute-start(bf16[4,8,512]{2,1,0:T(8,128)(2,1)S(1)} %get-tuple-element.24), channel_id=1, source_target_pairs={{0,8},{1,9},{2,10},{3,11},{4,12},{5,13},{6,14},{7,15},{8,0},{9,1},... | collective-permute-start | bytes 98312 | tf_op jit(solution)/shard_map/ppermute | solution.py:101
  8.1 1.3 %collective-permute-start.3 = (bf16[4,8,512]{2,1,0:T(8,128)(2,1)S(1)}, bf16[4,8,512]{2,1,0:T(8,128)(2,1)S(1)}, u32[]{:S(2)}, u32[]{:S(2)}) collective-permute-start(bf16[4,8,512]{2,1,0:T(8,128)(2,1)S(1)} %get-tuple-element.24), channel_id=1, source_target_pairs={{0,4},{1,5},{2,6},{3,7},{4,0},{5,1},{6,2},{7,3},{8,12},{9,13},{10,... | collective-permute-start | bytes 98312 | tf_op jit(solution)/shard_map/ppermute | solution.py:101
  10.9 3.0 %collective-permute-done.5 = bf16[4,8,512]{2,1,0:T(8,128)(2,1)S(1)} collective-permute-done((bf16[4,8,512]{2,1,0:T(8,128)(2,1)S(1)}, bf16[4,8,512]{2,1,0:T(8,128)(2,1)S(1)}, u32[]{:S(2)}, u32[]{:S(2)}) %collective-permute-start.5) | collective-permute-done | bytes 32800 | tf_op jit(solution)/shard_map/ppermute | solution.py:101
  14.2 1.3 %convolution_bitcast_fusion = f32[1,8,8,2,128]{4,2,1,3,0:T(8,128)S(1)} fusion(bf16[2,8,128,512]{3,2,1,0:T(8,128)(2,1)S(1)} %bitcast.180, bf16[1,8,512]{2,1,0:T(8,128)(2,1)} %param.9, f32[512]{0:T(512)S(1)} %dynamic_slice.64, f32[8]{0:T(128)S(1)} %add_rsqrt_fusion), kind=kOutput, calls=%fused_computation.10 | convolution fusion | flops 16793600 | bytes 2172960 | tf_op jit(solution)/shard_map/rc,kfc->rkf/dot_general | solution.py:178
  15.9 5.6 %fusion = f32[8,16,128]{2,0,1:T(8,128)S(1)} fusion(bf16[8,2048,1]{1,0,2:T(8,128)(2,1)S(1)} %bitcast.189, bf16[1,16,128,2048]{3,2,1,0:T(8,128)(2,1)} %param.11), kind=kOutput, calls=%fused_computation | convolution fusion | flops 67108864 | bytes 8486912 | tf_op jit(solution)/shard_map/rc,aec->rae/dot_general | solution.py:168
  21.8 2.2 %collective-permute-start.6 = (f32[4,8,512]{2,1,0:T(8,128)S(1)}, f32[4,8,512]{2,1,0:T(8,128)S(1)}, u32[]{:S(2)}, u32[]{:S(2)}) collective-permute-start(f32[4,8,512]{2,1,0:T(8,128)S(1)} %get-tuple-element.10), channel_id=1, source_target_pairs={{0,1},{1,0},{2,3},{3,2},{4,5},{5,4},{6,7},{7,6},{8,9},{9,8},{10,11... | collective-permute-start | bytes 196616 | tf_op jit(solution)/shard_map/ppermute | solution.py:105
  24.3 1.4 %collective-permute-start.8 = (f32[4,8,512]{2,1,0:T(8,128)S(1)}, f32[4,8,512]{2,1,0:T(8,128)S(1)}, u32[]{:S(2)}, u32[]{:S(2)}) collective-permute-start(f32[4,8,512]{2,1,0:T(8,128)S(1)} %get-tuple-element.12), channel_id=1, source_target_pairs={{0,3},{1,2},{2,1},{3,0},{4,7},{5,6},{6,5},{7,4},{8,11},{9,10},{10,... | collective-permute-start | bytes 196616 | tf_op jit(solution)/shard_map/ppermute | solution.py:105
  25.8 1.9 %collective-permute-done.7 = f32[4,8,512]{2,1,0:T(8,128)S(1)} collective-permute-done((f32[4,8,512]{2,1,0:T(8,128)S(1)}, f32[4,8,512]{2,1,0:T(8,128)S(1)}, u32[]{:S(2)}, u32[]{:S(2)}) %collective-permute-start.7) | collective-permute-done | bytes 65568 | tf_op jit(solution)/shard_map/ppermute | solution.py:105
  27.7 1.6 %collective-permute-done.8 = f32[4,8,512]{2,1,0:T(8,128)S(1)} collective-permute-done((f32[4,8,512]{2,1,0:T(8,128)S(1)}, f32[4,8,512]{2,1,0:T(8,128)S(1)}, u32[]{:S(2)}, u32[]{:S(2)}) %collective-permute-start.8) | collective-permute-done | bytes 65568 | tf_op jit(solution)/shard_map/ppermute | solution.py:105
  29.4 3.5 %collective-permute-start.9 = (f32[8,512]{1,0:T(8,128)S(1)}, f32[8,512]{1,0:T(8,128)S(1)}, u32[]{:S(2)}, u32[]{:S(2)}) collective-permute-start(f32[8,512]{1,0:T(8,128)S(1)} %get-tuple-element.20), channel_id=1, source_target_pairs={{0,4},{1,5},{2,6},{3,7},{4,0},{5,1},{6,2},{7,3},{8,12},{9,13},{10,... | collective-permute-start | bytes 49160 | tf_op jit(solution)/shard_map/ppermute | solution.py:101
  34.6 3.5 %select_reduce_fusion.3 = (f32[8,8]{1,0:T(8,128)S(1)}, f32[8,8,2048]{2,1,0:T(8,128)S(1)}) fusion(pred[8,2048]{1,0:T(8,128)(4,1)S(1)} %iota_compare_fusion.1, bf16[8,8,128]{2,1,0:T(8,128)(2,1)S(1)} %bitcast.199, bf16[1,8,2048,128]{3,2,1,0:T(8,128)(2,1)} %param.15), kind=kOutput, calls=%fused_computation.16 | convolution fusion | flops 33947584 | bytes 4751616 | tf_op jit(solution)/shard_map/bhe,bte->bht/dot_general | solution.py:213
  38.5 2.9 %fusion.14 = f32[8,8,128]{2,1,0:T(8,128)S(1)} fusion(bf16[1,8,2048,128]{3,2,1,0:T(8,128)(2,1)} %param.16, f32[8,8,2048]{2,1,0:T(8,128)S(1)} %get-tuple-element.44, f32[8,8]{1,0:T(8,128)S(1)} %fusion.47, pred[8,2048]{1,0:T(8,128)(4,1)S(1)} %iota_compare_fusion.1, f32[8,128]{1,0:T(8,128)S(1)} %get-tuple-element.41, f32[8,8]{1,0:T(8,128)S(1)} %convert_element_type.68), kind=kOutput, calls=%fused_computation.11 | convolution fusion | flops 33964032 | bytes 4772352 | tf_op jit(solution)/shard_map/bht,bte->bhe/dot_general | solution.py:226
  41.6 1.4 %collective-permute-start.12 = (f32[8,5,128]{2,0,1:T(8,128)S(1)}, f32[8,5,128]{2,0,1:T(8,128)S(1)}, u32[]{:S(2)}, u32[]{:S(2)}) collective-permute-start(f32[8,5,128]{2,0,1:T(8,128)S(1)} %pad_maximum_fusion.2), channel_id=1, source_target_pairs={{0,1},{1,0},{2,3},{3,2},{4,5},{5,4},{6,7},{7,6},{8,9},{9,8},{10,11... | collective-permute-start | bytes 61448 | tf_op jit(solution)/shard_map/ppermute | solution.py:19
  44.2 2.2 %collective-permute-start.15 = (bf16[8,128]{1,0:T(8,128)(2,1)S(1)}, bf16[8,128]{1,0:T(8,128)(2,1)S(1)}, u32[]{:S(2)}, u32[]{:S(2)}) collective-permute-start(bf16[8,128]{1,0:T(8,128)(2,1)S(1)} %get-tuple-element.36), channel_id=1, source_target_pairs={{0,12},{1,13},{2,14},{3,15},{4,8},{5,9},{6,10},{7,11},{8,4},{9,5},... | collective-permute-start | bytes 6152 | tf_op jit(solution)/shard_map/ppermute | solution.py:101
  48.5 1.2 %collective-permute-done.14 = bf16[8,128]{1,0:T(8,128)(2,1)S(1)} collective-permute-done((bf16[8,128]{1,0:T(8,128)(2,1)S(1)}, bf16[8,128]{1,0:T(8,128)(2,1)S(1)}, u32[]{:S(2)}, u32[]{:S(2)}) %collective-permute-start.14) | collective-permute-done | bytes 2080 | tf_op jit(solution)/shard_map/ppermute | solution.py:101
  49.8 2.3 %collective-permute-start.18 = (bf16[4,8,128]{2,1,0:T(8,128)(2,1)S(1)}, bf16[4,8,128]{2,1,0:T(8,128)(2,1)S(1)}, u32[]{:S(2)}, u32[]{:S(2)}) collective-permute-start(bf16[4,8,128]{2,1,0:T(8,128)(2,1)S(1)} %select_reduce_fusion.8), channel_id=1, source_target_pairs={{0,3},{1,2},{2,1},{3,0},{4,7},{5,6},{6,5},{7,4},{8,11},{9,10},{10,... | collective-permute-start | bytes 24584 | tf_op jit(solution)/shard_map/ppermute | solution.py:105
  52.1 1.1 %collective-permute-start.17 = (bf16[4,8,128]{2,1,0:T(8,128)(2,1)S(1)}, bf16[4,8,128]{2,1,0:T(8,128)(2,1)S(1)}, u32[]{:S(2)}, u32[]{:S(2)}) collective-permute-start(bf16[4,8,128]{2,1,0:T(8,128)(2,1)S(1)} %select_reduce_fusion.8), channel_id=1, source_target_pairs={{0,2},{1,3},{2,0},{3,1},{4,6},{5,7},{6,4},{7,5},{8,10},{9,11},{10,... | collective-permute-start | bytes 24584 | tf_op jit(solution)/shard_map/ppermute | solution.py:105
  53.5 1.2 %collective-permute-done.17 = bf16[4,8,128]{2,1,0:T(8,128)(2,1)S(1)} collective-permute-done((bf16[4,8,128]{2,1,0:T(8,128)(2,1)S(1)}, bf16[4,8,128]{2,1,0:T(8,128)(2,1)S(1)}, u32[]{:S(2)}, u32[]{:S(2)}) %collective-permute-start.17) | collective-permute-done | bytes 8224 | tf_op jit(solution)/shard_map/ppermute | solution.py:105
  55.1 5.6 %fusion.11 = f32[8,4,512]{2,0,1:T(8,128)S(1)} fusion(bf16[4,512,16,128]{3,2,1,0:T(8,128)(2,1)} %bitcast.181, bf16[16,8,128]{2,1,0:T(8,128)(2,1)S(1)} %select_reduce_fusion.2), kind=kOutput, calls=%fused_computation.9 | convolution fusion | flops 67108864 | bytes 8486912 | tf_op jit(solution)/shard_map/gabe,cae->gbc/dot_general | solution.py:274
  60.8 1.8 %collective-permute-start.20 = (f32[8,512]{1,0:T(8,128)S(1)}, f32[8,512]{1,0:T(8,128)S(1)}, u32[]{:S(2)}, u32[]{:S(2)}) collective-permute-start(f32[8,512]{1,0:T(8,128)S(1)} %get-tuple-element.13), channel_id=1, source_target_pairs={{0,1},{1,5},{2,9},{3,13},{4,0},{5,4},{6,8},{7,12},{8,3},{9,7},{10,... | collective-permute-start | bytes 49160 | tf_op jit(solution)/shard_map/ppermute | solution.py:281
  62.8 3.1 %collective-permute-start.21 = (f32[8,512]{1,0:T(8,128)S(1)}, f32[8,512]{1,0:T(8,128)S(1)}, u32[]{:S(2)}, u32[]{:S(2)}) collective-permute-start(f32[8,512]{1,0:T(8,128)S(1)} %get-tuple-element.15), channel_id=1, source_target_pairs={{0,2},{1,6},{2,10},{3,14},{4,3},{5,7},{6,11},{7,15},{8,0},{9,4},{1... | collective-permute-start | bytes 49160 | tf_op jit(solution)/shard_map/ppermute | solution.py:281
  65.8 3.5 %collective-permute-start.19 = (f32[8,512]{1,0:T(8,128)S(1)}, f32[8,512]{1,0:T(8,128)S(1)}, u32[]{:S(2)}, u32[]{:S(2)}) collective-permute-start(f32[8,512]{1,0:T(8,128)S(1)} %get-tuple-element.16), channel_id=1, source_target_pairs={{0,0},{1,4},{2,8},{3,12},{4,1},{5,5},{6,9},{7,13},{8,2},{9,6},{10,... | collective-permute-start | bytes 49160 | tf_op jit(solution)/shard_map/ppermute | solution.py:281
  69.4 4.2 %collective-permute-done.19 = f32[8,512]{1,0:T(8,128)S(1)} collective-permute-done((f32[8,512]{1,0:T(8,128)S(1)}, f32[8,512]{1,0:T(8,128)S(1)}, u32[]{:S(2)}, u32[]{:S(2)}) %collective-permute-start.19) | collective-permute-done | bytes 16416 | tf_op jit(solution)/shard_map/ppermute | solution.py:281
  (100 shorter events, 13.8 us)
Async XLA Ops:
  0.0 14.2 %copy-start = (bf16[2,1024,512]{2,1,0:T(8,128)(2,1)S(1)}, bf16[2,1024,512]{2,1,0:T(8,128)(2,1)}, u32[]{:S(2)}) copy-start(bf16[2,1024,512]{2,1,0:T(8,128)(2,1)} %param.13) | copy-start | bytes 6291460
  0.0 5.0 %collective-permute-start.2 = (bf16[8,512]{1,0:T(8,128)(2,1)}, bf16[8,512]{1,0:T(8,128)(2,1)S(1)}, u32[]{:S(2)}, u32[]{:S(2)}) collective-permute-start(bf16[8,512]{1,0:T(8,128)(2,1)} %bitcast.204), channel_id=1, source_target_pairs={{0,3},{1,2},{2,1},{3,0},{4,7},{5,6},{6,5},{7,4},{8,11},{9,10},{10,... | collective-permute-start | bytes 24584 | tf_op jit(solution)/shard_map/ppermute | solution.py:105
  0.0 5.0 %collective-permute-start.1 = (bf16[8,512]{1,0:T(8,128)(2,1)}, bf16[8,512]{1,0:T(8,128)(2,1)S(1)}, u32[]{:S(2)}, u32[]{:S(2)}) collective-permute-start(bf16[8,512]{1,0:T(8,128)(2,1)} %bitcast.205), channel_id=1, source_target_pairs={{0,2},{1,3},{2,0},{3,1},{4,6},{5,7},{6,4},{7,5},{8,10},{9,11},{10,... | collective-permute-start | bytes 24584 | tf_op jit(solution)/shard_map/ppermute | solution.py:105
  2.0 3.0 %collective-permute-start = (bf16[8,512]{1,0:T(8,128)(2,1)}, bf16[8,512]{1,0:T(8,128)(2,1)S(1)}, u32[]{:S(2)}, u32[]{:S(2)}) collective-permute-start(bf16[8,512]{1,0:T(8,128)(2,1)} %bitcast.206), channel_id=1, source_target_pairs={{0,1},{1,0},{2,3},{3,2},{4,5},{5,4},{6,7},{7,6},{8,9},{9,8},{10,11... | collective-permute-start | bytes 24584 | tf_op jit(solution)/shard_map/ppermute | solution.py:105
  5.8 5.1 %collective-permute-start.4 = (bf16[4,8,512]{2,1,0:T(8,128)(2,1)S(1)}, bf16[4,8,512]{2,1,0:T(8,128)(2,1)S(1)}, u32[]{:S(2)}, u32[]{:S(2)}) collective-permute-start(bf16[4,8,512]{2,1,0:T(8,128)(2,1)S(1)} %get-tuple-element.24), channel_id=1, source_target_pairs={{0,8},{1,9},{2,10},{3,11},{4,12},{5,13},{6,14},{7,15},{8,0},{9,1},... | collective-permute-start | bytes 98312 | tf_op jit(solution)/shard_map/ppermute | solution.py:101
  8.1 2.9 %collective-permute-start.3 = (bf16[4,8,512]{2,1,0:T(8,128)(2,1)S(1)}, bf16[4,8,512]{2,1,0:T(8,128)(2,1)S(1)}, u32[]{:S(2)}, u32[]{:S(2)}) collective-permute-start(bf16[4,8,512]{2,1,0:T(8,128)(2,1)S(1)} %get-tuple-element.24), channel_id=1, source_target_pairs={{0,4},{1,5},{2,6},{3,7},{4,0},{5,1},{6,2},{7,3},{8,12},{9,13},{10,... | collective-permute-start | bytes 98312 | tf_op jit(solution)/shard_map/ppermute | solution.py:101
  9.4 4.6 %collective-permute-start.5 = (bf16[4,8,512]{2,1,0:T(8,128)(2,1)S(1)}, bf16[4,8,512]{2,1,0:T(8,128)(2,1)S(1)}, u32[]{:S(2)}, u32[]{:S(2)}) collective-permute-start(bf16[4,8,512]{2,1,0:T(8,128)(2,1)S(1)} %get-tuple-element.24), channel_id=1, source_target_pairs={{0,12},{1,13},{2,14},{3,15},{4,8},{5,9},{6,10},{7,11},{8,4},{9,5},... | collective-permute-start | bytes 98312 | tf_op jit(solution)/shard_map/ppermute | solution.py:101
  21.8 4.0 %collective-permute-start.6 = (f32[4,8,512]{2,1,0:T(8,128)S(1)}, f32[4,8,512]{2,1,0:T(8,128)S(1)}, u32[]{:S(2)}, u32[]{:S(2)}) collective-permute-start(f32[4,8,512]{2,1,0:T(8,128)S(1)} %get-tuple-element.10), channel_id=1, source_target_pairs={{0,1},{1,0},{2,3},{3,2},{4,5},{5,4},{6,7},{7,6},{8,9},{9,8},{10,11... | collective-permute-start | bytes 196616 | tf_op jit(solution)/shard_map/ppermute | solution.py:105
  24.0 3.7 %collective-permute-start.7 = (f32[4,8,512]{2,1,0:T(8,128)S(1)}, f32[4,8,512]{2,1,0:T(8,128)S(1)}, u32[]{:S(2)}, u32[]{:S(2)}) collective-permute-start(f32[4,8,512]{2,1,0:T(8,128)S(1)} %get-tuple-element.11), channel_id=1, source_target_pairs={{0,2},{1,3},{2,0},{3,1},{4,6},{5,7},{6,4},{7,5},{8,10},{9,11},{10,... | collective-permute-start | bytes 196616 | tf_op jit(solution)/shard_map/ppermute | solution.py:105
  24.3 4.9 %collective-permute-start.8 = (f32[4,8,512]{2,1,0:T(8,128)S(1)}, f32[4,8,512]{2,1,0:T(8,128)S(1)}, u32[]{:S(2)}, u32[]{:S(2)}) collective-permute-start(f32[4,8,512]{2,1,0:T(8,128)S(1)} %get-tuple-element.12), channel_id=1, source_target_pairs={{0,3},{1,2},{2,1},{3,0},{4,7},{5,6},{6,5},{7,4},{8,11},{9,10},{10,... | collective-permute-start | bytes 196616 | tf_op jit(solution)/shard_map/ppermute | solution.py:105
  29.3 4.5 %collective-permute-start.11 = (f32[8,512]{1,0:T(8,128)S(1)}, f32[8,512]{1,0:T(8,128)S(1)}, u32[]{:S(2)}, u32[]{:S(2)}) collective-permute-start(f32[8,512]{1,0:T(8,128)S(1)} %get-tuple-element.18), channel_id=1, source_target_pairs={{0,12},{1,13},{2,14},{3,15},{4,8},{5,9},{6,10},{7,11},{8,4},{9,5},... | collective-permute-start | bytes 49160 | tf_op jit(solution)/shard_map/ppermute | solution.py:101
  29.4 4.3 %collective-permute-start.10 = (f32[8,512]{1,0:T(8,128)S(1)}, f32[8,512]{1,0:T(8,128)S(1)}, u32[]{:S(2)}, u32[]{:S(2)}) collective-permute-start(f32[8,512]{1,0:T(8,128)S(1)} %get-tuple-element.19), channel_id=1, source_target_pairs={{0,8},{1,9},{2,10},{3,11},{4,12},{5,13},{6,14},{7,15},{8,0},{9,1},... | collective-permute-start | bytes 49160 | tf_op jit(solution)/shard_map/ppermute | solution.py:101
  29.4 4.9 %collective-permute-start.9 = (f32[8,512]{1,0:T(8,128)S(1)}, f32[8,512]{1,0:T(8,128)S(1)}, u32[]{:S(2)}, u32[]{:S(2)}) collective-permute-start(f32[8,512]{1,0:T(8,128)S(1)} %get-tuple-element.20), channel_id=1, source_target_pairs={{0,4},{1,5},{2,6},{3,7},{4,0},{5,1},{6,2},{7,3},{8,12},{9,13},{10,... | collective-permute-start | bytes 49160 | tf_op jit(solution)/shard_map/ppermute | solution.py:101
  41.6 2.3 %collective-permute-start.12 = (f32[8,5,128]{2,0,1:T(8,128)S(1)}, f32[8,5,128]{2,0,1:T(8,128)S(1)}, u32[]{:S(2)}, u32[]{:S(2)}) collective-permute-start(f32[8,5,128]{2,0,1:T(8,128)S(1)} %pad_maximum_fusion.2), channel_id=1, source_target_pairs={{0,1},{1,0},{2,3},{3,2},{4,5},{5,4},{6,7},{7,6},{8,9},{9,8},{10,11... | collective-permute-start | bytes 61448 | tf_op jit(solution)/shard_map/ppermute | solution.py:19
  44.2 4.3 %collective-permute-start.15 = (bf16[8,128]{1,0:T(8,128)(2,1)S(1)}, bf16[8,128]{1,0:T(8,128)(2,1)S(1)}, u32[]{:S(2)}, u32[]{:S(2)}) collective-permute-start(bf16[8,128]{1,0:T(8,128)(2,1)S(1)} %get-tuple-element.36), channel_id=1, source_target_pairs={{0,12},{1,13},{2,14},{3,15},{4,8},{5,9},{6,10},{7,11},{8,4},{9,5},... | collective-permute-start | bytes 6152 | tf_op jit(solution)/shard_map/ppermute | solution.py:101
  46.3 3.3 %collective-permute-start.14 = (bf16[8,128]{1,0:T(8,128)(2,1)S(1)}, bf16[8,128]{1,0:T(8,128)(2,1)S(1)}, u32[]{:S(2)}, u32[]{:S(2)}) collective-permute-start(bf16[8,128]{1,0:T(8,128)(2,1)S(1)} %get-tuple-element.37), channel_id=1, source_target_pairs={{0,8},{1,9},{2,10},{3,11},{4,12},{5,13},{6,14},{7,15},{8,0},{9,1},... | collective-permute-start | bytes 6152 | tf_op jit(solution)/shard_map/ppermute | solution.py:101
  47.2 2.5 %collective-permute-start.13 = (bf16[8,128]{1,0:T(8,128)(2,1)S(1)}, bf16[8,128]{1,0:T(8,128)(2,1)S(1)}, u32[]{:S(2)}, u32[]{:S(2)}) collective-permute-start(bf16[8,128]{1,0:T(8,128)(2,1)S(1)} %get-tuple-element.38), channel_id=1, source_target_pairs={{0,4},{1,5},{2,6},{3,7},{4,0},{5,1},{6,2},{7,3},{8,12},{9,13},{10,... | collective-permute-start | bytes 6152 | tf_op jit(solution)/shard_map/ppermute | solution.py:101
  49.8 3.7 %collective-permute-start.18 = (bf16[4,8,128]{2,1,0:T(8,128)(2,1)S(1)}, bf16[4,8,128]{2,1,0:T(8,128)(2,1)S(1)}, u32[]{:S(2)}, u32[]{:S(2)}) collective-permute-start(bf16[4,8,128]{2,1,0:T(8,128)(2,1)S(1)} %select_reduce_fusion.8), channel_id=1, source_target_pairs={{0,3},{1,2},{2,1},{3,0},{4,7},{5,6},{6,5},{7,4},{8,11},{9,10},{10,... | collective-permute-start | bytes 24584 | tf_op jit(solution)/shard_map/ppermute | solution.py:105
  52.1 2.5 %collective-permute-start.17 = (bf16[4,8,128]{2,1,0:T(8,128)(2,1)S(1)}, bf16[4,8,128]{2,1,0:T(8,128)(2,1)S(1)}, u32[]{:S(2)}, u32[]{:S(2)}) collective-permute-start(bf16[4,8,128]{2,1,0:T(8,128)(2,1)S(1)} %select_reduce_fusion.8), channel_id=1, source_target_pairs={{0,2},{1,3},{2,0},{3,1},{4,6},{5,7},{6,4},{7,5},{8,10},{9,11},{10,... | collective-permute-start | bytes 24584 | tf_op jit(solution)/shard_map/ppermute | solution.py:105
  53.2 1.4 %collective-permute-start.16 = (bf16[4,8,128]{2,1,0:T(8,128)(2,1)S(1)}, bf16[4,8,128]{2,1,0:T(8,128)(2,1)S(1)}, u32[]{:S(2)}, u32[]{:S(2)}) collective-permute-start(bf16[4,8,128]{2,1,0:T(8,128)(2,1)S(1)} %select_reduce_fusion.8), channel_id=1, source_target_pairs={{0,1},{1,0},{2,3},{3,2},{4,5},{5,4},{6,7},{7,6},{8,9},{9,8},{10,11... | collective-permute-start | bytes 24584 | tf_op jit(solution)/shard_map/ppermute | solution.py:105
  60.8 8.6 %collective-permute-start.20 = (f32[8,512]{1,0:T(8,128)S(1)}, f32[8,512]{1,0:T(8,128)S(1)}, u32[]{:S(2)}, u32[]{:S(2)}) collective-permute-start(f32[8,512]{1,0:T(8,128)S(1)} %get-tuple-element.13), channel_id=1, source_target_pairs={{0,1},{1,5},{2,9},{3,13},{4,0},{5,4},{6,8},{7,12},{8,3},{9,7},{10,... | collective-permute-start | bytes 49160 | tf_op jit(solution)/shard_map/ppermute | solution.py:281
  62.6 6.8 %collective-permute-start.22 = (f32[8,512]{1,0:T(8,128)S(1)}, f32[8,512]{1,0:T(8,128)S(1)}, u32[]{:S(2)}, u32[]{:S(2)}) collective-permute-start(f32[8,512]{1,0:T(8,128)S(1)} %get-tuple-element.14), channel_id=1, source_target_pairs={{0,3},{1,7},{2,11},{3,15},{4,2},{5,6},{6,10},{7,14},{8,1},{9,5},{1... | collective-permute-start | bytes 49160 | tf_op jit(solution)/shard_map/ppermute | solution.py:281
  62.8 6.7 %collective-permute-start.21 = (f32[8,512]{1,0:T(8,128)S(1)}, f32[8,512]{1,0:T(8,128)S(1)}, u32[]{:S(2)}, u32[]{:S(2)}) collective-permute-start(f32[8,512]{1,0:T(8,128)S(1)} %get-tuple-element.15), channel_id=1, source_target_pairs={{0,2},{1,6},{2,10},{3,14},{4,3},{5,7},{6,11},{7,15},{8,0},{9,4},{1... | collective-permute-start | bytes 49160 | tf_op jit(solution)/shard_map/ppermute | solution.py:281
  65.8 7.7 %collective-permute-start.19 = (f32[8,512]{1,0:T(8,128)S(1)}, f32[8,512]{1,0:T(8,128)S(1)}, u32[]{:S(2)}, u32[]{:S(2)}) collective-permute-start(f32[8,512]{1,0:T(8,128)S(1)} %get-tuple-element.16), channel_id=1, source_target_pairs={{0,0},{1,4},{2,8},{3,12},{4,1},{5,5},{6,9},{7,13},{8,2},{9,6},{10,... | collective-permute-start | bytes 49160 | tf_op jit(solution)/shard_map/ppermute | solution.py:281

commit v17 on v15

--- a/solution.py
+++ b/solution.py
@@ -237,6 +237,7 @@
     numer = own_summed * factor_own[..., None] + got_summed * factor_got[..., None]
     denom = own_total * factor_own + got_total * factor_got
     attention = (numer / denom[..., None]).astype(jnp.bfloat16)
+    attention = attention.astype(jnp.float32)
     from_rows = [lax.dynamic_index_in_dim(attention, grid_row, 1, keepdims=False)]
     for s in range(1, GR):
         piece = lax.dynamic_index_in_dim(attention, grid_row ^ s, 1, keepdims=False)
@@ -255,7 +256,7 @@
     )
     slot_ids = jnp.arange(QG, dtype=jnp.int32)
     rank_of_slot = 2 * inverse[slot_ids // 2] + slot_ids % 2
-    chosen = jax.vmap(lambda per_group: pick(per_group, rank_of_slot))(every_slot)
+    chosen = jax.vmap(lambda per_group: pick(per_group, rank_of_slot))(every_slot).astype(jnp.bfloat16)
     out_part = jnp.einsum("gabe,cae->gbc", chosen, o_blocks[0], preferred_element_type=jnp.float32)
     if group_count == 1 and grid_cols == GR and col_width == GR * DS:
         pieces = out_part[0].reshape(ROWS, GR, DS)

time: 74.6 us -> 74.8 us (level)
  no operation moved by 1% of the time
where the time goes in v17:
time: 74.8 us; the launch traced here: 74.4 us
  starting transfers between devices  30.5 us (41%)
  matrix products  18.4 us (25%)
  waiting for transfers between devices  16.4 us (22%)
  other arithmetic  5.32 us (7%)
  local copies, waits for them, and re-layouts  3.29 us (4%)
    ppermute x9, starting transfers between devices, swap_rows(): lax.ppermute(value, axis, [(t, t ^ shift) for t in range(lax.axis_size(ax...  11 us
    ppermute x4, starting transfers between devices, local(): got = lax.ppermute(piece, 'tp', pairs)  8.78 us
    ppermute x9, starting transfers between devices, swap_cols(): lax.ppermute(value, axis, [(t, t ^ s) for t in range(lax.axis_size(axis))])  8.33 us
    ppermute x9, waiting for transfers between devices, swap_rows(): lax.ppermute(value, axis, [(t, t ^ shift) for t in range(lax.axis_size(ax...  6.83 us
    dot_general x1, matrix products, local(): jnp.einsum('rc,aec->rae', col_rows, q_blocks[0], preferred_element_type=j...  5.65 us
    dot_general x1, matrix products, local(): jnp.einsum('gabe,cae->gbc', chosen, o_blocks[0], preferred_element_type=j...  5.65 us
    ppermute x9, waiting for transfers between devices, swap_cols(): lax.ppermute(value, axis, [(t, t ^ s) for t in range(lax.axis_size(axis))])  4.69 us
    ppermute x4, waiting for transfers between devices, local(): got = lax.ppermute(piece, 'tp', pairs)  4 us
  transfers between devices with their start and end apart: 23, of which 13 were waited for; matrix products, arithmetic and copies ran while one was open for 5% of the time, Pallas kernels for 0%

profile of v17, /device:TPU:3, one launch (start us, length us, event | category | flops | bytes accessed | tf_op | source)
XLA Modules:
  0.0 74.4 jit_solution(13031279077991770311)
XLA Ops:
  0.0 2.0 %collective-permute-start.1 = (bf16[8,512]{1,0:T(8,128)(2,1)}, bf16[8,512]{1,0:T(8,128)(2,1)S(1)}, u32[]{:S(2)}, u32[]{:S(2)}) collective-permute-start(bf16[8,512]{1,0:T(8,128)(2,1)} %bitcast.205), channel_id=1, source_target_pairs={{0,2},{1,3},{2,0},{3,1},{4,6},{5,7},{6,4},{7,5},{8,10},{9,11},{10,... | collective-permute-start | bytes 24584 | tf_op jit(solution)/shard_map/ppermute | solution.py:105
  3.1 1.3 %gather_fusion.1 = s32[16]{0:T(128)S(1)} fusion(s32[16]{0:T(128)} %param.14, s32[1024]{0:T(1024)S(1)} %pad_clamp_fusion), kind=kCustom, calls=%fused_computation.1 | custom fusion | bytes 192 | tf_op jit(solution)/shard_map/gather | solution.py:128
  6.2 3.4 %collective-permute-start.5 = (bf16[4,8,512]{2,1,0:T(8,128)(2,1)S(1)}, bf16[4,8,512]{2,1,0:T(8,128)(2,1)S(1)}, u32[]{:S(2)}, u32[]{:S(2)}) collective-permute-start(bf16[4,8,512]{2,1,0:T(8,128)(2,1)S(1)} %select_reduce_fusion.7), channel_id=1, source_target_pairs={{0,12},{1,13},{2,14},{3,15},{4,8},{5,9},{6,10},{7,11},{8,4},{9,5},... | collective-permute-start | bytes 98312 | tf_op jit(solution)/shard_map/ppermute | solution.py:101
  10.0 0.9 %collective-permute-done.5 = bf16[4,8,512]{2,1,0:T(8,128)(2,1)S(1)} collective-permute-done((bf16[4,8,512]{2,1,0:T(8,128)(2,1)S(1)}, bf16[4,8,512]{2,1,0:T(8,128)(2,1)S(1)}, u32[]{:S(2)}, u32[]{:S(2)}) %collective-permute-start.5) | collective-permute-done | bytes 32800 | tf_op jit(solution)/shard_map/ppermute | solution.py:101
  10.9 2.7 %collective-permute-done.4 = bf16[4,8,512]{2,1,0:T(8,128)(2,1)S(1)} collective-permute-done((bf16[4,8,512]{2,1,0:T(8,128)(2,1)S(1)}, bf16[4,8,512]{2,1,0:T(8,128)(2,1)S(1)}, u32[]{:S(2)}, u32[]{:S(2)}) %collective-permute-start.4) | collective-permute-done | bytes 32800 | tf_op jit(solution)/shard_map/ppermute | solution.py:101
  15.6 5.7 %fusion.14 = f32[16,8,128]{2,1,0:T(8,128)S(1)} fusion(bf16[1,16,128,2048]{3,2,1,0:T(8,128)(2,1)} %param.11, bf16[8,8192]{1,0:T(8,128)(2,1)S(1)} %multiply_convert_fusion, s32[]{:T(128)S(6)} %select_n.266), kind=kOutput, calls=%fused_computation.12 | convolution fusion | flops 67108864 | bytes 8486916 | tf_op jit(solution)/shard_map/rc,aec->rae/dot_general | solution.py:152
  22.2 1.5 %collective-permute-start.6 = (f32[4,8,512]{2,1,0:T(8,128)S(1)}, f32[4,8,512]{2,1,0:T(8,128)S(1)}, u32[]{:S(2)}, u32[]{:S(2)}) collective-permute-start(f32[4,8,512]{2,1,0:T(8,128)S(1)} %get-tuple-element.14), channel_id=1, source_target_pairs={{0,1},{1,0},{2,3},{3,2},{4,5},{5,4},{6,7},{7,6},{8,9},{9,8},{10,11... | collective-permute-start | bytes 196616 | tf_op jit(solution)/shard_map/ppermute | solution.py:105
  24.0 1.2 %collective-permute-start.7 = (f32[4,8,512]{2,1,0:T(8,128)S(1)}, f32[4,8,512]{2,1,0:T(8,128)S(1)}, u32[]{:S(2)}, u32[]{:S(2)}) collective-permute-start(f32[4,8,512]{2,1,0:T(8,128)S(1)} %get-tuple-element.16), channel_id=1, source_target_pairs={{0,2},{1,3},{2,0},{3,1},{4,6},{5,7},{6,4},{7,5},{8,10},{9,11},{10,... | collective-permute-start | bytes 196616 | tf_op jit(solution)/shard_map/ppermute | solution.py:105
  25.3 2.8 %collective-permute-done.8 = f32[4,8,512]{2,1,0:T(8,128)S(1)} collective-permute-done((f32[4,8,512]{2,1,0:T(8,128)S(1)}, f32[4,8,512]{2,1,0:T(8,128)S(1)}, u32[]{:S(2)}, u32[]{:S(2)}) %collective-permute-start.8) | collective-permute-done | bytes 65568 | tf_op jit(solution)/shard_map/ppermute | solution.py:105
  28.7 1.2 %collective-permute-start.11 = (f32[8,512]{1,0:T(8,128)S(1)}, f32[8,512]{1,0:T(8,128)S(1)}, u32[]{:S(2)}, u32[]{:S(2)}) collective-permute-start(f32[8,512]{1,0:T(8,128)S(1)} %get-tuple-element.22), channel_id=1, source_target_pairs={{0,12},{1,13},{2,14},{3,15},{4,8},{5,9},{6,10},{7,11},{8,4},{9,5},... | collective-permute-start | bytes 49160 | tf_op jit(solution)/shard_map/ppermute | solution.py:101
  30.6 1.7 %collective-permute-start.9 = (f32[8,512]{1,0:T(8,128)S(1)}, f32[8,512]{1,0:T(8,128)S(1)}, u32[]{:S(2)}, u32[]{:S(2)}) collective-permute-start(f32[8,512]{1,0:T(8,128)S(1)} %get-tuple-element.24), channel_id=1, source_target_pairs={{0,4},{1,5},{2,6},{3,7},{4,0},{5,1},{6,2},{7,3},{8,12},{9,13},{10,... | collective-permute-start | bytes 49160 | tf_op jit(solution)/shard_map/ppermute | solution.py:101
  33.9 3.5 %select_reduce_fusion.4 = (f32[8,8]{1,0:T(8,128)S(1)}, f32[8,8,2048]{2,1,0:T(8,128)S(1)}) fusion(pred[8,2048]{1,0:T(8,128)(4,1)S(1)} %iota_compare_fusion.1, bf16[8,8,128]{2,1,0:T(8,128)(2,1)S(1)} %bitcast.188, bf16[1,8,2048,128]{3,2,1,0:T(8,128)(2,1)} %param.15), kind=kOutput, calls=%fused_computation.20 | convolution fusion | flops 33947584 | bytes 4751616 | tf_op jit(solution)/shard_map/bhe,bte->bht/dot_general | solution.py:198
  37.8 2.9 %fusion.17 = f32[8,8,128]{2,1,0:T(8,128)S(1)} fusion(bf16[1,8,2048,128]{3,2,1,0:T(8,128)(2,1)} %param.16, f32[8,8,2048]{2,1,0:T(8,128)S(1)} %get-tuple-element.47, f32[8,8]{1,0:T(8,128)S(1)} %fusion.49, pred[8,2048]{1,0:T(8,128)(4,1)S(1)} %iota_compare_fusion.1, f32[8,128]{1,0:T(8,128)S(1)} %get-tuple-element.43, f32[8,8]{1,0:T(8,128)S(1)} %convert_element_type.79), kind=kOutput, calls=%fused_computation.14 | convolution fusion | flops 33964032 | bytes 4772352 | tf_op jit(solution)/shard_map/bht,bte->bhe/dot_general | solution.py:211
  40.8 2.5 %collective-permute-start.12 = (f32[8,5,128]{2,0,1:T(8,128)S(1)}, f32[8,5,128]{2,0,1:T(8,128)S(1)}, u32[]{:S(2)}, u32[]{:S(2)}) collective-permute-start(f32[8,5,128]{2,0,1:T(8,128)S(1)} %pad_maximum_fusion.4), channel_id=1, source_target_pairs={{0,1},{1,0},{2,3},{3,2},{4,5},{5,4},{6,7},{7,6},{8,9},{9,8},{10,11... | collective-permute-start | bytes 61448 | tf_op jit(solution)/shard_map/ppermute | solution.py:19
  44.5 2.2 %collective-permute-start.15 = (f32[8,128]{1,0:T(8,128)S(1)}, f32[8,128]{1,0:T(8,128)S(1)}, u32[]{:S(2)}, u32[]{:S(2)}) collective-permute-start(f32[8,128]{1,0:T(8,128)S(1)} %get-tuple-element.30), channel_id=1, source_target_pairs={{0,12},{1,13},{2,14},{3,15},{4,8},{5,9},{6,10},{7,11},{8,4},{9,5},... | collective-permute-start | bytes 12296 | tf_op jit(solution)/shard_map/ppermute | solution.py:101
  48.8 1.2 %collective-permute-done.14 = f32[8,128]{1,0:T(8,128)S(1)} collective-permute-done((f32[8,128]{1,0:T(8,128)S(1)}, f32[8,128]{1,0:T(8,128)S(1)}, u32[]{:S(2)}, u32[]{:S(2)}) %collective-permute-start.14) | collective-permute-done | bytes 4128 | tf_op jit(solution)/shard_map/ppermute | solution.py:101
  50.2 2.0 %collective-permute-start.18 = (f32[4,8,128]{2,1,0:T(8,128)S(1)}, f32[4,8,128]{2,1,0:T(8,128)S(1)}, u32[]{:S(2)}, u32[]{:S(2)}) collective-permute-start(f32[4,8,128]{2,1,0:T(8,128)S(1)} %select_reduce_fusion.8), channel_id=1, source_target_pairs={{0,3},{1,2},{2,1},{3,0},{4,7},{5,6},{6,5},{7,4},{8,11},{9,10},{10,... | collective-permute-start | bytes 49160 | tf_op jit(solution)/shard_map/ppermute | solution.py:105
  52.2 1.2 %collective-permute-start.17 = (f32[4,8,128]{2,1,0:T(8,128)S(1)}, f32[4,8,128]{2,1,0:T(8,128)S(1)}, u32[]{:S(2)}, u32[]{:S(2)}) collective-permute-start(f32[4,8,128]{2,1,0:T(8,128)S(1)} %select_reduce_fusion.8), channel_id=1, source_target_pairs={{0,2},{1,3},{2,0},{3,1},{4,6},{5,7},{6,4},{7,5},{8,10},{9,11},{10,... | collective-permute-start | bytes 49160 | tf_op jit(solution)/shard_map/ppermute | solution.py:105
  53.6 1.2 %collective-permute-done.17 = f32[4,8,128]{2,1,0:T(8,128)S(1)} collective-permute-done((f32[4,8,128]{2,1,0:T(8,128)S(1)}, f32[4,8,128]{2,1,0:T(8,128)S(1)}, u32[]{:S(2)}, u32[]{:S(2)}) %collective-permute-start.17) | collective-permute-done | bytes 16416 | tf_op jit(solution)/shard_map/ppermute | solution.py:105
  55.3 5.6 %fusion.11 = f32[8,4,512]{2,0,1:T(8,128)S(1)} fusion(bf16[4,512,16,128]{3,2,1,0:T(8,128)(2,1)} %bitcast.178, bf16[16,8,128]{2,1,0:T(8,128)(2,1)S(1)} %select_reduce_fusion), kind=kOutput, calls=%fused_computation.11 | convolution fusion | flops 67108864 | bytes 8486912 | tf_op jit(solution)/shard_map/gabe,cae->gbc/dot_general | solution.py:260
  61.0 2.1 %collective-permute-start.20 = (f32[8,512]{1,0:T(8,128)S(1)}, f32[8,512]{1,0:T(8,128)S(1)}, u32[]{:S(2)}, u32[]{:S(2)}) collective-permute-start(f32[8,512]{1,0:T(8,128)S(1)} %get-tuple-element.17), channel_id=1, source_target_pairs={{0,1},{1,5},{2,9},{3,13},{4,0},{5,4},{6,8},{7,12},{8,3},{9,7},{10,... | collective-permute-start | bytes 49160 | tf_op jit(solution)/shard_map/ppermute | solution.py:267
  63.2 2.8 %collective-permute-start.21 = (f32[8,512]{1,0:T(8,128)S(1)}, f32[8,512]{1,0:T(8,128)S(1)}, u32[]{:S(2)}, u32[]{:S(2)}) collective-permute-start(f32[8,512]{1,0:T(8,128)S(1)} %get-tuple-element.19), channel_id=1, source_target_pairs={{0,2},{1,6},{2,10},{3,14},{4,3},{5,7},{6,11},{7,15},{8,0},{9,4},{1... | collective-permute-start | bytes 49160 | tf_op jit(solution)/shard_map/ppermute | solution.py:267
  66.0 3.7 %collective-permute-start.19 = (f32[8,512]{1,0:T(8,128)S(1)}, f32[8,512]{1,0:T(8,128)S(1)}, u32[]{:S(2)}, u32[]{:S(2)}) collective-permute-start(f32[8,512]{1,0:T(8,128)S(1)} %get-tuple-element.20), channel_id=1, source_target_pairs={{0,0},{1,4},{2,8},{3,12},{4,1},{5,5},{6,9},{7,13},{8,2},{9,6},{10,... | collective-permute-start | bytes 49160 | tf_op jit(solution)/shard_map/ppermute | solution.py:267
  69.8 4.0 %collective-permute-done.19 = f32[8,512]{1,0:T(8,128)S(1)} collective-permute-done((f32[8,512]{1,0:T(8,128)S(1)}, f32[8,512]{1,0:T(8,128)S(1)}, u32[]{:S(2)}, u32[]{:S(2)}) %collective-permute-start.19) | collective-permute-done | bytes 16416 | tf_op jit(solution)/shard_map/ppermute | solution.py:267
  (103 shorter events, 14.6 us)
Async XLA Ops:
  0.0 14.9 %copy-start = (bf16[2,1024,512]{2,1,0:T(8,128)(2,1)S(1)}, bf16[2,1024,512]{2,1,0:T(8,128)(2,1)}, u32[]{:S(2)}) copy-start(bf16[2,1024,512]{2,1,0:T(8,128)(2,1)} %param.13) | copy-start | bytes 6291460
  0.0 5.4 %collective-permute-start.2 = (bf16[8,512]{1,0:T(8,128)(2,1)}, bf16[8,512]{1,0:T(8,128)(2,1)S(1)}, u32[]{:S(2)}, u32[]{:S(2)}) collective-permute-start(bf16[8,512]{1,0:T(8,128)(2,1)} %bitcast.204), channel_id=1, source_target_pairs={{0,3},{1,2},{2,1},{3,0},{4,7},{5,6},{6,5},{7,4},{8,11},{9,10},{10,... | collective-permute-start | bytes 24584 | tf_op jit(solution)/shard_map/ppermute | solution.py:105
  0.0 5.4 %collective-permute-start.1 = (bf16[8,512]{1,0:T(8,128)(2,1)}, bf16[8,512]{1,0:T(8,128)(2,1)S(1)}, u32[]{:S(2)}, u32[]{:S(2)}) collective-permute-start(bf16[8,512]{1,0:T(8,128)(2,1)} %bitcast.205), channel_id=1, source_target_pairs={{0,2},{1,3},{2,0},{3,1},{4,6},{5,7},{6,4},{7,5},{8,10},{9,11},{10,... | collective-permute-start | bytes 24584 | tf_op jit(solution)/shard_map/ppermute | solution.py:105
  2.0 3.4 %collective-permute-start = (bf16[8,512]{1,0:T(8,128)(2,1)}, bf16[8,512]{1,0:T(8,128)(2,1)S(1)}, u32[]{:S(2)}, u32[]{:S(2)}) collective-permute-start(bf16[8,512]{1,0:T(8,128)(2,1)} %bitcast.206), channel_id=1, source_target_pairs={{0,1},{1,0},{2,3},{3,2},{4,5},{5,4},{6,7},{7,6},{8,9},{9,8},{10,11... | collective-permute-start | bytes 24584 | tf_op jit(solution)/shard_map/ppermute | solution.py:105
  6.2 4.7 %collective-permute-start.5 = (bf16[4,8,512]{2,1,0:T(8,128)(2,1)S(1)}, bf16[4,8,512]{2,1,0:T(8,128)(2,1)S(1)}, u32[]{:S(2)}, u32[]{:S(2)}) collective-permute-start(bf16[4,8,512]{2,1,0:T(8,128)(2,1)S(1)} %select_reduce_fusion.7), channel_id=1, source_target_pairs={{0,12},{1,13},{2,14},{3,15},{4,8},{5,9},{6,10},{7,11},{8,4},{9,5},... | collective-permute-start | bytes 98312 | tf_op jit(solution)/shard_map/ppermute | solution.py:101
  9.6 4.0 %collective-permute-start.4 = (bf16[4,8,512]{2,1,0:T(8,128)(2,1)S(1)}, bf16[4,8,512]{2,1,0:T(8,128)(2,1)S(1)}, u32[]{:S(2)}, u32[]{:S(2)}) collective-permute-start(bf16[4,8,512]{2,1,0:T(8,128)(2,1)S(1)} %select_reduce_fusion.7), channel_id=1, source_target_pairs={{0,8},{1,9},{2,10},{3,11},{4,12},{5,13},{6,14},{7,15},{8,0},{9,1},... | collective-permute-start | bytes 98312 | tf_op jit(solution)/shard_map/ppermute | solution.py:101
  9.6 4.0 %collective-permute-start.3 = (bf16[4,8,512]{2,1,0:T(8,128)(2,1)S(1)}, bf16[4,8,512]{2,1,0:T(8,128)(2,1)S(1)}, u32[]{:S(2)}, u32[]{:S(2)}) collective-permute-start(bf16[4,8,512]{2,1,0:T(8,128)(2,1)S(1)} %select_reduce_fusion.7), channel_id=1, source_target_pairs={{0,4},{1,5},{2,6},{3,7},{4,0},{5,1},{6,2},{7,3},{8,12},{9,13},{10,... | collective-permute-start | bytes 98312 | tf_op jit(solution)/shard_map/ppermute | solution.py:101
  22.2 3.1 %collective-permute-start.6 = (f32[4,8,512]{2,1,0:T(8,128)S(1)}, f32[4,8,512]{2,1,0:T(8,128)S(1)}, u32[]{:S(2)}, u32[]{:S(2)}) collective-permute-start(f32[4,8,512]{2,1,0:T(8,128)S(1)} %get-tuple-element.14), channel_id=1, source_target_pairs={{0,1},{1,0},{2,3},{3,2},{4,5},{5,4},{6,7},{7,6},{8,9},{9,8},{10,11... | collective-permute-start | bytes 196616 | tf_op jit(solution)/shard_map/ppermute | solution.py:105
  23.7 4.3 %collective-permute-start.8 = (f32[4,8,512]{2,1,0:T(8,128)S(1)}, f32[4,8,512]{2,1,0:T(8,128)S(1)}, u32[]{:S(2)}, u32[]{:S(2)}) collective-permute-start(f32[4,8,512]{2,1,0:T(8,128)S(1)} %get-tuple-element.15), channel_id=1, source_target_pairs={{0,3},{1,2},{2,1},{3,0},{4,7},{5,6},{6,5},{7,4},{8,11},{9,10},{10,... | collective-permute-start | bytes 196616 | tf_op jit(solution)/shard_map/ppermute | solution.py:105
  24.0 4.7 %collective-permute-start.7 = (f32[4,8,512]{2,1,0:T(8,128)S(1)}, f32[4,8,512]{2,1,0:T(8,128)S(1)}, u32[]{:S(2)}, u32[]{:S(2)}) collective-permute-start(f32[4,8,512]{2,1,0:T(8,128)S(1)} %get-tuple-element.16), channel_id=1, source_target_pairs={{0,2},{1,3},{2,0},{3,1},{4,6},{5,7},{6,4},{7,5},{8,10},{9,11},{10,... | collective-permute-start | bytes 196616 | tf_op jit(solution)/shard_map/ppermute | solution.py:105
  28.7 4.5 %collective-permute-start.11 = (f32[8,512]{1,0:T(8,128)S(1)}, f32[8,512]{1,0:T(8,128)S(1)}, u32[]{:S(2)}, u32[]{:S(2)}) collective-permute-start(f32[8,512]{1,0:T(8,128)S(1)} %get-tuple-element.22), channel_id=1, source_target_pairs={{0,12},{1,13},{2,14},{3,15},{4,8},{5,9},{6,10},{7,11},{8,4},{9,5},... | collective-permute-start | bytes 49160 | tf_op jit(solution)/shard_map/ppermute | solution.py:101
  29.9 3.5 %collective-permute-start.10 = (f32[8,512]{1,0:T(8,128)S(1)}, f32[8,512]{1,0:T(8,128)S(1)}, u32[]{:S(2)}, u32[]{:S(2)}) collective-permute-start(f32[8,512]{1,0:T(8,128)S(1)} %get-tuple-element.23), channel_id=1, source_target_pairs={{0,8},{1,9},{2,10},{3,11},{4,12},{5,13},{6,14},{7,15},{8,0},{9,1},... | collective-permute-start | bytes 49160 | tf_op jit(solution)/shard_map/ppermute | solution.py:101
  30.6 3.0 %collective-permute-start.9 = (f32[8,512]{1,0:T(8,128)S(1)}, f32[8,512]{1,0:T(8,128)S(1)}, u32[]{:S(2)}, u32[]{:S(2)}) collective-permute-start(f32[8,512]{1,0:T(8,128)S(1)} %get-tuple-element.24), channel_id=1, source_target_pairs={{0,4},{1,5},{2,6},{3,7},{4,0},{5,1},{6,2},{7,3},{8,12},{9,13},{10,... | collective-permute-start | bytes 49160 | tf_op jit(solution)/shard_map/ppermute | solution.py:101
  40.8 3.3 %collective-permute-start.12 = (f32[8,5,128]{2,0,1:T(8,128)S(1)}, f32[8,5,128]{2,0,1:T(8,128)S(1)}, u32[]{:S(2)}, u32[]{:S(2)}) collective-permute-start(f32[8,5,128]{2,0,1:T(8,128)S(1)} %pad_maximum_fusion.4), channel_id=1, source_target_pairs={{0,1},{1,0},{2,3},{3,2},{4,5},{5,4},{6,7},{7,6},{8,9},{9,8},{10,11... | collective-permute-start | bytes 61448 | tf_op jit(solution)/shard_map/ppermute | solution.py:19
  44.5 4.3 %collective-permute-start.15 = (f32[8,128]{1,0:T(8,128)S(1)}, f32[8,128]{1,0:T(8,128)S(1)}, u32[]{:S(2)}, u32[]{:S(2)}) collective-permute-start(f32[8,128]{1,0:T(8,128)S(1)} %get-tuple-element.30), channel_id=1, source_target_pairs={{0,12},{1,13},{2,14},{3,15},{4,8},{5,9},{6,10},{7,11},{8,4},{9,5},... | collective-permute-start | bytes 12296 | tf_op jit(solution)/shard_map/ppermute | solution.py:101
  46.7 3.4 %collective-permute-start.14 = (f32[8,128]{1,0:T(8,128)S(1)}, f32[8,128]{1,0:T(8,128)S(1)}, u32[]{:S(2)}, u32[]{:S(2)}) collective-permute-start(f32[8,128]{1,0:T(8,128)S(1)} %get-tuple-element.31), channel_id=1, source_target_pairs={{0,8},{1,9},{2,10},{3,11},{4,12},{5,13},{6,14},{7,15},{8,0},{9,1},... | collective-permute-start | bytes 12296 | tf_op jit(solution)/shard_map/ppermute | solution.py:101
  47.3 2.7 %collective-permute-start.13 = (f32[8,128]{1,0:T(8,128)S(1)}, f32[8,128]{1,0:T(8,128)S(1)}, u32[]{:S(2)}, u32[]{:S(2)}) collective-permute-start(f32[8,128]{1,0:T(8,128)S(1)} %get-tuple-element.32), channel_id=1, source_target_pairs={{0,4},{1,5},{2,6},{3,7},{4,0},{5,1},{6,2},{7,3},{8,12},{9,13},{10,... | collective-permute-start | bytes 12296 | tf_op jit(solution)/shard_map/ppermute | solution.py:101
  50.2 3.5 %collective-permute-start.18 = (f32[4,8,128]{2,1,0:T(8,128)S(1)}, f32[4,8,128]{2,1,0:T(8,128)S(1)}, u32[]{:S(2)}, u32[]{:S(2)}) collective-permute-start(f32[4,8,128]{2,1,0:T(8,128)S(1)} %select_reduce_fusion.8), channel_id=1, source_target_pairs={{0,3},{1,2},{2,1},{3,0},{4,7},{5,6},{6,5},{7,4},{8,11},{9,10},{10,... | collective-permute-start | bytes 49160 | tf_op jit(solution)/shard_map/ppermute | solution.py:105
  52.2 2.6 %collective-permute-start.17 = (f32[4,8,128]{2,1,0:T(8,128)S(1)}, f32[4,8,128]{2,1,0:T(8,128)S(1)}, u32[]{:S(2)}, u32[]{:S(2)}) collective-permute-start(f32[4,8,128]{2,1,0:T(8,128)S(1)} %select_reduce_fusion.8), channel_id=1, source_target_pairs={{0,2},{1,3},{2,0},{3,1},{4,6},{5,7},{6,4},{7,5},{8,10},{9,11},{10,... | collective-permute-start | bytes 49160 | tf_op jit(solution)/shard_map/ppermute | solution.py:105
  53.4 1.4 %collective-permute-start.16 = (f32[4,8,128]{2,1,0:T(8,128)S(1)}, f32[4,8,128]{2,1,0:T(8,128)S(1)}, u32[]{:S(2)}, u32[]{:S(2)}) collective-permute-start(f32[4,8,128]{2,1,0:T(8,128)S(1)} %select_reduce_fusion.8), channel_id=1, source_target_pairs={{0,1},{1,0},{2,3},{3,2},{4,5},{5,4},{6,7},{7,6},{8,9},{9,8},{10,11... | collective-permute-start | bytes 49160 | tf_op jit(solution)/shard_map/ppermute | solution.py:105
  61.0 8.8 %collective-permute-start.20 = (f32[8,512]{1,0:T(8,128)S(1)}, f32[8,512]{1,0:T(8,128)S(1)}, u32[]{:S(2)}, u32[]{:S(2)}) collective-permute-start(f32[8,512]{1,0:T(8,128)S(1)} %get-tuple-element.17), channel_id=1, source_target_pairs={{0,1},{1,5},{2,9},{3,13},{4,0},{5,4},{6,8},{7,12},{8,3},{9,7},{10,... | collective-permute-start | bytes 49160 | tf_op jit(solution)/shard_map/ppermute | solution.py:267
  63.1 6.7 %collective-permute-start.22 = (f32[8,512]{1,0:T(8,128)S(1)}, f32[8,512]{1,0:T(8,128)S(1)}, u32[]{:S(2)}, u32[]{:S(2)}) collective-permute-start(f32[8,512]{1,0:T(8,128)S(1)} %get-tuple-element.18), channel_id=1, source_target_pairs={{0,3},{1,7},{2,11},{3,15},{4,2},{5,6},{6,10},{7,14},{8,1},{9,5},{1... | collective-permute-start | bytes 49160 | tf_op jit(solution)/shard_map/ppermute | solution.py:267
  63.2 6.6 %collective-permute-start.21 = (f32[8,512]{1,0:T(8,128)S(1)}, f32[8,512]{1,0:T(8,128)S(1)}, u32[]{:S(2)}, u32[]{:S(2)}) collective-permute-start(f32[8,512]{1,0:T(8,128)S(1)} %get-tuple-element.19), channel_id=1, source_target_pairs={{0,2},{1,6},{2,10},{3,14},{4,3},{5,7},{6,11},{7,15},{8,0},{9,4},{1... | collective-permute-start | bytes 49160 | tf_op jit(solution)/shard_map/ppermute | solution.py:267
  66.0 7.7 %collective-permute-start.19 = (f32[8,512]{1,0:T(8,128)S(1)}, f32[8,512]{1,0:T(8,128)S(1)}, u32[]{:S(2)}, u32[]{:S(2)}) collective-permute-start(f32[8,512]{1,0:T(8,128)S(1)} %get-tuple-element.20), channel_id=1, source_target_pairs={{0,0},{1,4},{2,8},{3,12},{4,1},{5,5},{6,9},{7,13},{8,2},{9,6},{10,... | collective-permute-start | bytes 49160 | tf_op jit(solution)/shard_map/ppermute | solution.py:267
  (1 other events, 9.6 us)
